TPU v7x, 32 devices: a whole 2x2x4 slice. The times are simulated.
32 devices in a mesh: pipe: 4 (over x, core), seq: 8 (over z, y).
Axes of the slice: x: 2, y: 2, z: 4, core: 2. Of those that a mesh axis runs over, the one named last changes fastest.
Arguments:
- queries: bfloat16 [4, 1024, 4096], P('pipe', 'seq'), may hold values from -6 to 6
- key_heads: bfloat16 [4, 1024, 512], P('pipe', 'seq'), may hold values from -6 to 6
- inputs: bfloat16 [4, 1024, 4096], P('pipe', 'seq'), may hold values from -6 to 6
- cotangent: bfloat16 [1024, 4096], P('seq'), may hold values from -6 to 6
- lengths: int32 [8], replicated, may hold values from 1 to 128, 768 in all
Outputs:
- grad_queries: bfloat16 [4, 1024, 4096], P('pipe', 'seq')
- grad_keys: bfloat16 [4, 1024, 512], P('pipe', 'seq')
- grad_inputs: bfloat16 [4, 1024, 4096], P('pipe', 'seq')
Inputs may be any that keep to these rules, and one draw needn't show every extreme that they name: lengths sum to 768 and one of them equals 128.
All inputs are finite; a program needn't handle non-finite values.
Results may differ from a plain program's by a relative error of at most 0.013.
Values may be sent and summed in bfloat16 or wider, within the bound.
No kernel may reach another device: no remote copies, remote signals or barrier semaphores. Data moves between devices by JAX's collectives and lax.ppermute only.
A program may use at most 64 MiB of HBM per device.

v0:
```python
import jax
import jax.numpy as jnp
from jax import lax
from jax.sharding import PartitionSpec as P

DH = 128
BLK = 128


def from_behind(value, axis, steps):
    count = lax.axis_size(axis)
    leading, last = (max(0, -steps), min(count, count - steps))
    return lax.ppermute(value, axis, [(source, source + steps) for source in range(leading, last)])


def key_pair(block_rows):
    first_block = jnp.broadcast_to(block_rows[:1], block_rows.shape)
    return jnp.concatenate([first_block, block_rows], axis=1)


def visible(lengths, block_count, block_len):
    shape = (block_count, block_len, 2 * block_len)
    row_index = lax.broadcasted_iota(jnp.int32, shape, 1)
    col_index = lax.broadcasted_iota(jnp.int32, shape, 2)
    block_index = lax.broadcasted_iota(jnp.int32, shape, 0)
    in_first = col_index < block_len
    offset = jnp.where(in_first, col_index, col_index - block_len)
    own_len = lengths[:, None, None]
    first_ok = in_first & (offset < lengths[0]) & ((block_index > 0) | (offset <= row_index))
    own_ok = (
        jnp.logical_not(in_first) & (block_index > 0) & (offset <= row_index) & (offset < own_len)
    )
    return (first_ok | own_ok)[:, None]


def fold_keys(key_terms, block_len):
    own_part = key_terms[:, block_len:]
    first_part = jnp.sum(key_terms[:, :block_len], axis=0)
    return own_part.at[0].add(first_part)


def fold_value(key_terms, block_len, groups):
    own_part = key_terms[:, block_len:]
    first_terms = key_terms[:, :block_len]
    grouped = first_terms.reshape((groups, first_terms.shape[0] // groups) + first_terms.shape[1:])
    partial_low = lax.optimization_barrier(jnp.sum(grouped, axis=1).astype(jnp.bfloat16))
    first_part = jnp.sum(partial_low.astype(jnp.float32), axis=0)
    return own_part.at[0].add(first_part)


def probabilities(query_blocks, keys_both, allowed, score_scale):
    scores = (
        jnp.einsum("bihd,bjhd->bhij", query_blocks, keys_both, preferred_element_type=jnp.float32)
        * score_scale
    )
    scores = jnp.where(allowed, scores, -jnp.inf)
    row_max = jnp.max(scores, axis=-1, keepdims=True)
    exp_scores = jnp.exp(scores - row_max)
    return exp_scores / jnp.sum(exp_scores, axis=-1, keepdims=True)


def value_grad(probs_low, grad_blocks, block_len, groups):
    key_terms = jnp.einsum(
        "bhij,bihd->bjhd", probs_low, grad_blocks, preferred_element_type=jnp.float32
    )
    return (grad_blocks.astype(jnp.float32) + fold_value(key_terms, block_len, groups)).astype(
        jnp.bfloat16
    )


def score_grads(
    softmax_probs, probs_low, query_blocks, keys_both, values_both, grad_blocks, score_scale
):
    output = jnp.einsum(
        "bhij,bjhd->bihd", probs_low, values_both, preferred_element_type=jnp.float32
    )
    row_dot = jnp.transpose(jnp.sum(grad_blocks.astype(jnp.float32) * output, axis=-1), (0, 2, 1))[
        ..., None
    ]
    grad_probs = jnp.einsum(
        "bihd,bjhd->bhij", grad_blocks, values_both, preferred_element_type=jnp.float32
    )
    grad_scores = (softmax_probs * (grad_probs - row_dot)).astype(jnp.bfloat16)
    grad_query = (
        jnp.einsum("bhij,bjhd->bihd", grad_scores, keys_both, preferred_element_type=jnp.float32)
        * score_scale
    ).astype(jnp.bfloat16)
    key_terms = jnp.einsum(
        "bhij,bihd->bjhd", grad_scores, query_blocks, preferred_element_type=jnp.float32
    )
    return (grad_query, key_terms)


def weight_grads(
    softmax_probs,
    probs_low,
    query_blocks,
    keys_both,
    values_both,
    grad_blocks,
    score_scale,
    block_len,
):
    grad_query, key_terms = score_grads(
        softmax_probs, probs_low, query_blocks, keys_both, values_both, grad_blocks, score_scale
    )
    grad_key = (fold_keys(key_terms, block_len) * score_scale).astype(jnp.bfloat16)
    return (grad_query, grad_key)


def on_device(queries, key_heads, inputs, cotangent, lengths):
    section_count = lax.axis_size("pipe")
    section_index = lax.axis_index("pipe")
    seq_ways = lax.axis_size("seq")
    tok_rows = queries.shape[1]
    full_width = queries.shape[2]
    head_count = full_width // DH
    kv_count = key_heads.shape[2] // DH
    group_size = head_count // kv_count
    seq_len = tok_rows * seq_ways
    block_count = seq_len // BLK
    local_heads = head_count // seq_ways
    score_scale = DH ** (-0.5)
    last_section = section_count - 1
    live_tick = last_section - section_index

    def to_heads(flat_rows):
        return flat_rows.reshape(block_count, BLK, local_heads, DH)

    def to_flat(block_rows):
        return block_rows.reshape(seq_len, local_heads * DH)

    def hand_down(grad_rows):
        return from_behind(grad_rows, "pipe", -1)

    def section_work(context, grad_head, active, held_pair):
        softmax_probs, probs_low, query_blocks, keys_both, values_both = context
        new_grad = value_grad(probs_low, grad_head, BLK, seq_ways)
        grad_query, grad_key = weight_grads(
            softmax_probs,
            probs_low,
            query_blocks,
            keys_both,
            values_both,
            grad_head,
            score_scale,
            BLK,
        )
        held_pair = (
            jnp.where(active, grad_query, held_pair[0]),
            jnp.where(active, grad_key, held_pair[1]),
        )
        return (new_grad, held_pair)

    zero_blocks = jnp.zeros((block_count, BLK, local_heads, DH), jnp.bfloat16)
    zero_rows = jnp.zeros((tok_rows, full_width), jnp.bfloat16)
    spread_keys = jnp.broadcast_to(
        key_heads[0].reshape(tok_rows, kv_count, 1, DH), (tok_rows, kv_count, group_size, DH)
    ).reshape(tok_rows, full_width)
    query_flat = lax.all_to_all(queries[0], "seq", split_axis=1, concat_axis=0, tiled=True)
    input_flat = lax.all_to_all(inputs[0], "seq", split_axis=1, concat_axis=0, tiled=True)
    key_flat = lax.all_to_all(spread_keys, "seq", split_axis=1, concat_axis=0, tiled=True)
    query_blocks = to_heads(query_flat)
    keys_both = key_pair(to_heads(key_flat))
    values_both = key_pair(to_heads(input_flat))
    allowed = visible(lengths, block_count, BLK)
    softmax_probs = probabilities(query_blocks, keys_both, allowed, score_scale)
    context = (
        softmax_probs,
        softmax_probs.astype(jnp.bfloat16),
        query_blocks,
        keys_both,
        values_both,
    )

    def tick_seq(tick_num, state_carry):
        arrived, out_grad, held_pair = state_carry
        incoming = jnp.where(section_index == last_section, cotangent, arrived)
        grad_head = to_heads(
            lax.all_to_all(incoming, "seq", split_axis=1, concat_axis=0, tiled=True)
        )
        active = tick_num == live_tick
        new_grad, held_pair = section_work(context, grad_head, active, held_pair)
        new_seq = lax.all_to_all(to_flat(new_grad), "seq", split_axis=0, concat_axis=1, tiled=True)
        out_grad = jnp.where(active, new_seq, out_grad)
        return (hand_down(new_seq), out_grad, held_pair)

    unused_rows, grad_inputs, held_pair = lax.fori_loop(
        0, section_count, tick_seq, (zero_rows, zero_rows, (zero_blocks, zero_blocks))
    )
    softmax_probs, probs_low, query_blocks, keys_both, values_both = context
    grad_query, grad_key = held_pair
    query_out, key_out = (
        lax.all_to_all(to_flat(grad_query), "seq", split_axis=0, concat_axis=1, tiled=True),
        lax.all_to_all(to_flat(grad_key), "seq", split_axis=0, concat_axis=1, tiled=True),
    )
    key_sum = jnp.sum(
        key_out.reshape(tok_rows, kv_count, group_size, DH).astype(jnp.float32), axis=2
    )
    key_final = key_sum.astype(jnp.bfloat16).reshape(tok_rows, kv_count * DH)
    return (query_out[None], key_final[None], grad_inputs[None])


def solution(mesh):
    placed = (
        P("pipe", "seq", None),
        P("pipe", "seq", None),
        P("pipe", "seq", None),
        P("seq", None),
        P(),
    )
    return jax.shard_map(
        on_device,
        mesh=mesh,
        in_specs=placed,
        out_specs=(P("pipe", "seq", None), P("pipe", "seq", None), P("pipe", "seq", None)),
        check_vma=False,
    )
```

profile of v0, /device:TPU:15, one launch (start us, length us, event | category | flops | bytes accessed | tf_op | source)
XLA Modules:
  0.0 460.3 jit_solution(4048004962747570211)
XLA Ops:
  3.0 5.7 %all-to-all-start.2 = ((bf16[128,8,512]{0,2,1:T(8,128)(2,1)}), bf16[128,8,512]{0,2,1:T(8,128)(2,1)S(1)}, u32[]{:S(2)}, u32[]{:S(2)}) async-start(bf16[128,8,512]{0,2,1:T(8,128)(2,1)} %bitcast.2), calls=%async_computation.2 | async-start | bytes 2097152 | tf_op jit(solution)/shard_map/all_to_all | solution.py:162
  9.9 21.9 %all-to-all-done.2 = bf16[128,8,512]{0,2,1:T(8,128)(2,1)S(1)} async-done(((bf16[128,8,512]{0,2,1:T(8,128)(2,1)}), bf16[128,8,512]{0,2,1:T(8,128)(2,1)S(1)}, u32[]{:S(2)}, u32[]{:S(2)}) %all-to-all-start.2) | async-done | bytes 1048608 | tf_op jit(solution)/shard_map/all_to_all | solution.py:162
  31.8 6.3 %all-to-all-start.3 = ((bf16[128,8,512]{0,2,1:T(8,128)(2,1)}), bf16[128,8,512]{0,2,1:T(8,128)(2,1)S(1)}, u32[]{:S(2)}, u32[]{:S(2)}) async-start(bf16[128,8,512]{0,2,1:T(8,128)(2,1)} %bitcast.6), calls=%async_computation.3 | async-start | bytes 2097152 | tf_op jit(solution)/shard_map/all_to_all | solution.py:160
  39.5 21.9 %all-to-all-done.3 = bf16[128,8,512]{0,2,1:T(8,128)(2,1)S(1)} async-done(((bf16[128,8,512]{0,2,1:T(8,128)(2,1)}), bf16[128,8,512]{0,2,1:T(8,128)(2,1)S(1)}, u32[]{:S(2)}, u32[]{:S(2)}) %all-to-all-start.3) | async-done | bytes 1048608 | tf_op jit(solution)/shard_map/all_to_all | solution.py:160
  61.4 6.5 %all-to-all-start.4 = ((bf16[128,8,512]{0,2,1:T(8,128)(2,1)}), bf16[128,8,512]{0,2,1:T(8,128)(2,1)S(1)}, u32[]{:S(2)}, u32[]{:S(2)}) async-start(bf16[128,8,512]{0,2,1:T(8,128)(2,1)} %bitcast.127), calls=%async_computation.4 | async-start | bytes 2097152 | tf_op jit(solution)/shard_map/all_to_all | solution.py:161
  73.9 17.3 %all-to-all-done.4 = bf16[128,8,512]{0,2,1:T(8,128)(2,1)S(1)} async-done(((bf16[128,8,512]{0,2,1:T(8,128)(2,1)}), bf16[128,8,512]{0,2,1:T(8,128)(2,1)S(1)}, u32[]{:S(2)}, u32[]{:S(2)}) %all-to-all-start.4) | async-done | bytes 1048608 | tf_op jit(solution)/shard_map/all_to_all | solution.py:161
  94.0 5.4 %fusion.27 = (f32[8,4,128]{2,1,0:T(4,128)S(1)}, f32[8,4,128,256]{2,3,1,0:T(8,128)}) fusion(pred[8,128,256]{1,2,0:T(8,128)(4,1)} %fusion.17, bf16[8,128,4,128]{1,3,2,0:T(8,128)(2,1)} %bitcast.126, bf16[8,128,4,128]{3,1,2,0:T(8,128)(2,1)} %copy.39, bf16[8,128,4,128]{3,1,2,0:T(8,128)(2,1)} %copy-done.13), kind=kOutput, calls=%fused_computation.50 | convolution fusion | flops 276824320 | bytes 7618560 | tf_op jit(solution)/shard_map/sub | solution.py:58
  112.8 3.9 copy.46
  116.8 5.4 %copy.47 = f32[8,4,128,256]{3,2,1,0:T(8,128)} copy(f32[8,4,128,256]{2,3,1,0:T(8,128)} %get-tuple-element.491) | data formatting | bytes 8388608
  123.2 278.9 %while.24 = (s32[]{:T(128)}, bf16[128,4096]{0,1:T(8,128)(2,1)}, bf16[128,4096]{0,1:T(8,128)(2,1)}, bf16[8,128,4,128]{3,1,2,0:T(8,128)(2,1)}, bf16[8,128,4,128]{3...) while((s32[]{:T(128)}, bf16[128,4096]{0,1:T(8,128)(2,1)}, ...), condition=%wide.region_6.7_spmd.clone, body=%wide.region_2.6_spmd.clone.sunk | while | flops 1087369216 | bytes 116425216 | solution.py:188
  124.6 6.3 %all-to-all-start = ((bf16[128,8,512]{0,2,1:T(8,128)(2,1)}), bf16[128,8,512]{0,2,1:T(8,128)(2,1)S(1)}, u32[]{:S(2)}, u32[]{:S(2)}) async-start(bf16[128,8,512]{0,2,1:T(8,128)(2,1)} %bitcast.111), calls=%async_computation | async-start | bytes 2097152 | tf_op jit(solution)/shard_map/while/body/eval_jaxpr/all_to_all | solution.py:180
  130.9 23.2 %all-to-all-done = bf16[128,8,512]{0,2,1:T(8,128)(2,1)S(1)} async-done(((bf16[128,8,512]{0,2,1:T(8,128)(2,1)}), bf16[128,8,512]{0,2,1:T(8,128)(2,1)S(1)}, u32[]{:S(2)}, u32[]{:S(2)}) %all-to-all-start) | async-done | bytes 1048608 | tf_op jit(solution)/shard_map/while/body/eval_jaxpr/all_to_all | solution.py:180
  158.2 6.3 %all-to-all-start.1 = ((bf16[8,128,512]{1,2,0:T(8,128)(2,1)}), bf16[8,128,512]{1,2,0:T(8,128)(2,1)S(1)}, u32[]{:S(2)}, u32[]{:S(2)}) async-start(bf16[8,128,512]{1,2,0:T(8,128)(2,1)} %bitcast.113), calls=%async_computation.1 | async-start | bytes 2097152 | tf_op jit(solution)/shard_map/while/body/eval_jaxpr/all_to_all | solution.py:184
  173.8 14.1 %all-to-all-done.1 = bf16[8,128,512]{1,2,0:T(8,128)(2,1)S(1)} async-done(((bf16[8,128,512]{1,2,0:T(8,128)(2,1)}), bf16[8,128,512]{1,2,0:T(8,128)(2,1)S(1)}, u32[]{:S(2)}, u32[]{:S(2)}) %all-to-all-start.1) | async-done | bytes 1048608 | tf_op jit(solution)/shard_map/while/body/eval_jaxpr/all_to_all | solution.py:184
  195.6 6.5 %all-to-all-start = ((bf16[128,8,512]{0,2,1:T(8,128)(2,1)}), bf16[128,8,512]{0,2,1:T(8,128)(2,1)S(1)}, u32[]{:S(2)}, u32[]{:S(2)}) async-start(bf16[128,8,512]{0,2,1:T(8,128)(2,1)} %bitcast.111), calls=%async_computation | async-start | bytes 2097152 | tf_op jit(solution)/shard_map/while/body/eval_jaxpr/all_to_all | solution.py:180
  202.0 12.1 %all-to-all-done = bf16[128,8,512]{0,2,1:T(8,128)(2,1)S(1)} async-done(((bf16[128,8,512]{0,2,1:T(8,128)(2,1)}), bf16[128,8,512]{0,2,1:T(8,128)(2,1)S(1)}, u32[]{:S(2)}, u32[]{:S(2)}) %all-to-all-start) | async-done | bytes 1048608 | tf_op jit(solution)/shard_map/while/body/eval_jaxpr/all_to_all | solution.py:180
  218.3 6.4 %all-to-all-start.1 = ((bf16[8,128,512]{1,2,0:T(8,128)(2,1)}), bf16[8,128,512]{1,2,0:T(8,128)(2,1)S(1)}, u32[]{:S(2)}, u32[]{:S(2)}) async-start(bf16[8,128,512]{1,2,0:T(8,128)(2,1)} %bitcast.113), calls=%async_computation.1 | async-start | bytes 2097152 | tf_op jit(solution)/shard_map/while/body/eval_jaxpr/all_to_all | solution.py:184
  238.1 21.3 %collective-permute-start = (bf16[128,4096]{0,1:T(8,128)(2,1)S(1)}, bf16[128,4096]{0,1:T(8,128)(2,1)}, u32[]{:S(2)}, u32[]{:S(2)}) collective-permute-start(bf16[128,4096]{0,1:T(8,128)(2,1)S(1)} %bitcast.119), channel_id=1, source_target_pairs={{8,0},{16,8},{24,16},{9,1},{17,9},{25,17},{10,2},{18,10},{26,18},{... | collective-permute-start | bytes 3145736 | tf_op jit(solution)/shard_map/while/body/eval_jaxpr/ppermute | solution.py:13
  265.2 6.9 %all-to-all-start = ((bf16[128,8,512]{0,2,1:T(8,128)(2,1)}), bf16[128,8,512]{0,2,1:T(8,128)(2,1)S(1)}, u32[]{:S(2)}, u32[]{:S(2)}) async-start(bf16[128,8,512]{0,2,1:T(8,128)(2,1)} %bitcast.111), calls=%async_computation | async-start | bytes 2097152 | tf_op jit(solution)/shard_map/while/body/eval_jaxpr/all_to_all | solution.py:180
  272.0 19.8 %all-to-all-done = bf16[128,8,512]{0,2,1:T(8,128)(2,1)S(1)} async-done(((bf16[128,8,512]{0,2,1:T(8,128)(2,1)}), bf16[128,8,512]{0,2,1:T(8,128)(2,1)S(1)}, u32[]{:S(2)}, u32[]{:S(2)}) %all-to-all-start) | async-done | bytes 1048608 | tf_op jit(solution)/shard_map/while/body/eval_jaxpr/all_to_all | solution.py:180
  296.0 6.1 %all-to-all-start.1 = ((bf16[8,128,512]{1,2,0:T(8,128)(2,1)}), bf16[8,128,512]{1,2,0:T(8,128)(2,1)S(1)}, u32[]{:S(2)}, u32[]{:S(2)}) async-start(bf16[8,128,512]{1,2,0:T(8,128)(2,1)} %bitcast.113), calls=%async_computation.1 | async-start | bytes 2097152 | tf_op jit(solution)/shard_map/while/body/eval_jaxpr/all_to_all | solution.py:184
  312.4 11.4 %all-to-all-done.1 = bf16[8,128,512]{1,2,0:T(8,128)(2,1)S(1)} async-done(((bf16[8,128,512]{1,2,0:T(8,128)(2,1)}), bf16[8,128,512]{1,2,0:T(8,128)(2,1)S(1)}, u32[]{:S(2)}, u32[]{:S(2)}) %all-to-all-start.1) | async-done | bytes 1048608 | tf_op jit(solution)/shard_map/while/body/eval_jaxpr/all_to_all | solution.py:184
  323.8 4.9 %collective-permute-start = (bf16[128,4096]{0,1:T(8,128)(2,1)S(1)}, bf16[128,4096]{0,1:T(8,128)(2,1)}, u32[]{:S(2)}, u32[]{:S(2)}) collective-permute-start(bf16[128,4096]{0,1:T(8,128)(2,1)S(1)} %bitcast.119), channel_id=1, source_target_pairs={{8,0},{16,8},{24,16},{9,1},{17,9},{25,17},{10,2},{18,10},{26,18},{... | collective-permute-start | bytes 3145736 | tf_op jit(solution)/shard_map/while/body/eval_jaxpr/ppermute | solution.py:13
  334.4 6.7 %all-to-all-start = ((bf16[128,8,512]{0,2,1:T(8,128)(2,1)}), bf16[128,8,512]{0,2,1:T(8,128)(2,1)S(1)}, u32[]{:S(2)}, u32[]{:S(2)}) async-start(bf16[128,8,512]{0,2,1:T(8,128)(2,1)} %bitcast.111), calls=%async_computation | async-start | bytes 2097152 | tf_op jit(solution)/shard_map/while/body/eval_jaxpr/all_to_all | solution.py:180
  341.1 19.8 %all-to-all-done = bf16[128,8,512]{0,2,1:T(8,128)(2,1)S(1)} async-done(((bf16[128,8,512]{0,2,1:T(8,128)(2,1)}), bf16[128,8,512]{0,2,1:T(8,128)(2,1)S(1)}, u32[]{:S(2)}, u32[]{:S(2)}) %all-to-all-start) | async-done | bytes 1048608 | tf_op jit(solution)/shard_map/while/body/eval_jaxpr/all_to_all | solution.py:180
  365.0 6.1 %all-to-all-start.1 = ((bf16[8,128,512]{1,2,0:T(8,128)(2,1)}), bf16[8,128,512]{1,2,0:T(8,128)(2,1)S(1)}, u32[]{:S(2)}, u32[]{:S(2)}) async-start(bf16[8,128,512]{1,2,0:T(8,128)(2,1)} %bitcast.113), calls=%async_computation.1 | async-start | bytes 2097152 | tf_op jit(solution)/shard_map/while/body/eval_jaxpr/all_to_all | solution.py:184
  381.5 11.4 %all-to-all-done.1 = bf16[8,128,512]{1,2,0:T(8,128)(2,1)S(1)} async-done(((bf16[8,128,512]{1,2,0:T(8,128)(2,1)}), bf16[8,128,512]{1,2,0:T(8,128)(2,1)S(1)}, u32[]{:S(2)}, u32[]{:S(2)}) %all-to-all-start.1) | async-done | bytes 1048608 | tf_op jit(solution)/shard_map/while/body/eval_jaxpr/all_to_all | solution.py:184
  392.9 4.9 %collective-permute-start = (bf16[128,4096]{0,1:T(8,128)(2,1)S(1)}, bf16[128,4096]{0,1:T(8,128)(2,1)}, u32[]{:S(2)}, u32[]{:S(2)}) collective-permute-start(bf16[128,4096]{0,1:T(8,128)(2,1)S(1)} %bitcast.119), channel_id=1, source_target_pairs={{8,0},{16,8},{24,16},{9,1},{17,9},{25,17},{10,2},{18,10},{26,18},{... | collective-permute-start | bytes 3145736 | tf_op jit(solution)/shard_map/while/body/eval_jaxpr/ppermute | solution.py:13
  404.5 6.7 %all-to-all-start.5 = ((bf16[8,128,512]{1,2,0:T(8,128)(2,1)}), bf16[8,128,512]{1,2,0:T(8,128)(2,1)S(1)}, u32[]{:S(2)}, u32[]{:S(2)}) async-start(bf16[8,128,512]{1,2,0:T(8,128)(2,1)} %bitcast.15), calls=%async_computation.5 | async-start | bytes 2097152 | tf_op jit(solution)/shard_map/all_to_all | solution.py:194
  412.5 19.0 %all-to-all-done.5 = bf16[8,128,512]{1,2,0:T(8,128)(2,1)S(1)} async-done(((bf16[8,128,512]{1,2,0:T(8,128)(2,1)}), bf16[8,128,512]{1,2,0:T(8,128)(2,1)S(1)}, u32[]{:S(2)}, u32[]{:S(2)}) %all-to-all-start.5) | async-done | bytes 1048608 | tf_op jit(solution)/shard_map/all_to_all | solution.py:194
  431.5 6.1 %all-to-all-start.6 = ((bf16[8,128,512]{1,2,0:T(8,128)(2,1)}), bf16[8,128,512]{1,2,0:T(8,128)(2,1)S(1)}, u32[]{:S(2)}, u32[]{:S(2)}) async-start(bf16[8,128,512]{1,2,0:T(8,128)(2,1)} %bitcast.129), calls=%async_computation.6 | async-start | bytes 2097152 | tf_op jit(solution)/shard_map/all_to_all | solution.py:195
  440.2 19.2 %all-to-all-done.6 = bf16[8,128,512]{1,2,0:T(8,128)(2,1)S(1)} async-done(((bf16[8,128,512]{1,2,0:T(8,128)(2,1)}), bf16[8,128,512]{1,2,0:T(8,128)(2,1)S(1)}, u32[]{:S(2)}, u32[]{:S(2)}) %all-to-all-start.6) | async-done | bytes 1048608 | tf_op jit(solution)/shard_map/all_to_all | solution.py:195
  (181 shorter events, 120.0 us)
Async XLA Ops:
  0.6 8.0 %copy-start.15 = (bf16[1,128,4096]{2,1,0:T(8,128)(2,1)S(1)}, bf16[1,128,4096]{2,1,0:T(8,128)(2,1)}, u32[]{:S(2)}) copy-start(bf16[1,128,4096]{2,1,0:T(8,128)(2,1)} %param.11) | copy-start | bytes 3145732
  3.0 28.9 %all-to-all-start.2 = ((bf16[128,8,512]{0,2,1:T(8,128)(2,1)}), bf16[128,8,512]{0,2,1:T(8,128)(2,1)S(1)}, u32[]{:S(2)}, u32[]{:S(2)}) async-start(bf16[128,8,512]{0,2,1:T(8,128)(2,1)} %bitcast.2), calls=%async_computation.2 | async-start | bytes 2097152 | tf_op jit(solution)/shard_map/all_to_all | solution.py:162
  8.6 29.5 %copy-start.16 = (bf16[1,128,4096]{2,1,0:T(8,128)(2,1)S(1)}, bf16[1,128,4096]{2,1,0:T(8,128)(2,1)}, u32[]{:S(2)}) copy-start(bf16[1,128,4096]{2,1,0:T(8,128)(2,1)} %param.13) | copy-start | bytes 3145732
  31.8 29.6 %all-to-all-start.3 = ((bf16[128,8,512]{0,2,1:T(8,128)(2,1)}), bf16[128,8,512]{0,2,1:T(8,128)(2,1)S(1)}, u32[]{:S(2)}, u32[]{:S(2)}) async-start(bf16[128,8,512]{0,2,1:T(8,128)(2,1)} %bitcast.6), calls=%async_computation.3 | async-start | bytes 2097152 | tf_op jit(solution)/shard_map/all_to_all | solution.py:160
  61.4 6.5 %copy-start.11 = (bf16[128,8,512]{0,2,1:T(8,128)(2,1)}, bf16[128,8,512]{0,2,1:T(8,128)(2,1)S(1)}, u32[]{:S(2)}) copy-start(bf16[128,8,512]{0,2,1:T(8,128)(2,1)S(1)} %all-to-all-done.3) | copy-start | bytes 3145732
  61.4 8.2 %copy-start.17 = (s32[8]{0:T(128)S(1)}, s32[8]{0:T(128)}, u32[]{:S(2)}) copy-start(s32[8]{0:T(128)} %param.15) | copy-start | bytes 100
  61.4 29.7 %all-to-all-start.4 = ((bf16[128,8,512]{0,2,1:T(8,128)(2,1)}), bf16[128,8,512]{0,2,1:T(8,128)(2,1)S(1)}, u32[]{:S(2)}, u32[]{:S(2)}) async-start(bf16[128,8,512]{0,2,1:T(8,128)(2,1)} %bitcast.127), calls=%async_computation.4 | async-start | bytes 2097152 | tf_op jit(solution)/shard_map/all_to_all | solution.py:161
  99.6 2.9 copy-start.10
  123.2 46.4 %copy-start.1 = (bf16[8,128,4,128]{3,1,2,0:T(8,128)(2,1)}, bf16[8,128,4,128]{3,1,2,0:T(8,128)(2,1)S(1)}, u32[]{:S(2)}) copy-start(bf16[8,128,4,128]{3,1,2,0:T(8,128)(2,1)S(1)} %get-tuple-element.632) | copy-start | bytes 3145732 | tf_op jit(solution)/shard_map/while
  124.6 29.5 %all-to-all-start = ((bf16[128,8,512]{0,2,1:T(8,128)(2,1)}), bf16[128,8,512]{0,2,1:T(8,128)(2,1)S(1)}, u32[]{:S(2)}, u32[]{:S(2)}) async-start(bf16[128,8,512]{0,2,1:T(8,128)(2,1)} %bitcast.111), calls=%async_computation | async-start | bytes 2097152 | tf_op jit(solution)/shard_map/while/body/eval_jaxpr/all_to_all | solution.py:180
  158.2 29.6 %all-to-all-start.1 = ((bf16[8,128,512]{1,2,0:T(8,128)(2,1)}), bf16[8,128,512]{1,2,0:T(8,128)(2,1)S(1)}, u32[]{:S(2)}, u32[]{:S(2)}) async-start(bf16[8,128,512]{1,2,0:T(8,128)(2,1)} %bitcast.113), calls=%async_computation.1 | async-start | bytes 2097152 | tf_op jit(solution)/shard_map/while/body/eval_jaxpr/all_to_all | solution.py:184
  164.6 2.2 copy-start
  187.8 5.1 %collective-permute-start = (bf16[128,4096]{0,1:T(8,128)(2,1)S(1)}, bf16[128,4096]{0,1:T(8,128)(2,1)}, u32[]{:S(2)}, u32[]{:S(2)}) collective-permute-start(bf16[128,4096]{0,1:T(8,128)(2,1)S(1)} %bitcast.119), channel_id=1, source_target_pairs={{8,0},{16,8},{24,16},{9,1},{17,9},{25,17},{10,2},{18,10},{26,18},{... | collective-permute-start | bytes 3145736 | tf_op jit(solution)/shard_map/while/body/eval_jaxpr/ppermute | solution.py:13
  194.3 35.4 %copy-start.1 = (bf16[8,128,4,128]{3,1,2,0:T(8,128)(2,1)}, bf16[8,128,4,128]{3,1,2,0:T(8,128)(2,1)S(1)}, u32[]{:S(2)}) copy-start(bf16[8,128,4,128]{3,1,2,0:T(8,128)(2,1)S(1)} %get-tuple-element.632) | copy-start | bytes 3145732 | tf_op jit(solution)/shard_map/while
  195.6 18.6 %all-to-all-start = ((bf16[128,8,512]{0,2,1:T(8,128)(2,1)}), bf16[128,8,512]{0,2,1:T(8,128)(2,1)S(1)}, u32[]{:S(2)}, u32[]{:S(2)}) async-start(bf16[128,8,512]{0,2,1:T(8,128)(2,1)} %bitcast.111), calls=%async_computation | async-start | bytes 2097152 | tf_op jit(solution)/shard_map/while/body/eval_jaxpr/all_to_all | solution.py:180
  218.3 19.8 %all-to-all-start.1 = ((bf16[8,128,512]{1,2,0:T(8,128)(2,1)}), bf16[8,128,512]{1,2,0:T(8,128)(2,1)S(1)}, u32[]{:S(2)}, u32[]{:S(2)}) async-start(bf16[8,128,512]{1,2,0:T(8,128)(2,1)} %bitcast.113), calls=%async_computation.1 | async-start | bytes 2097152 | tf_op jit(solution)/shard_map/while/body/eval_jaxpr/all_to_all | solution.py:184
  238.1 24.2 %collective-permute-start = (bf16[128,4096]{0,1:T(8,128)(2,1)S(1)}, bf16[128,4096]{0,1:T(8,128)(2,1)}, u32[]{:S(2)}, u32[]{:S(2)}) collective-permute-start(bf16[128,4096]{0,1:T(8,128)(2,1)S(1)} %bitcast.119), channel_id=1, source_target_pairs={{8,0},{16,8},{24,16},{9,1},{17,9},{25,17},{10,2},{18,10},{26,18},{... | collective-permute-start | bytes 3145736 | tf_op jit(solution)/shard_map/while/body/eval_jaxpr/ppermute | solution.py:13
  259.4 2.5 copy-start.6
  263.8 43.2 %copy-start.1 = (bf16[8,128,4,128]{3,1,2,0:T(8,128)(2,1)}, bf16[8,128,4,128]{3,1,2,0:T(8,128)(2,1)S(1)}, u32[]{:S(2)}) copy-start(bf16[8,128,4,128]{3,1,2,0:T(8,128)(2,1)S(1)} %get-tuple-element.632) | copy-start | bytes 3145732 | tf_op jit(solution)/shard_map/while
  265.2 26.7 %all-to-all-start = ((bf16[128,8,512]{0,2,1:T(8,128)(2,1)}), bf16[128,8,512]{0,2,1:T(8,128)(2,1)S(1)}, u32[]{:S(2)}, u32[]{:S(2)}) async-start(bf16[128,8,512]{0,2,1:T(8,128)(2,1)} %bitcast.111), calls=%async_computation | async-start | bytes 2097152 | tf_op jit(solution)/shard_map/while/body/eval_jaxpr/all_to_all | solution.py:180
  296.0 27.8 %all-to-all-start.1 = ((bf16[8,128,512]{1,2,0:T(8,128)(2,1)}), bf16[8,128,512]{1,2,0:T(8,128)(2,1)S(1)}, u32[]{:S(2)}, u32[]{:S(2)}) async-start(bf16[8,128,512]{1,2,0:T(8,128)(2,1)} %bitcast.113), calls=%async_computation.1 | async-start | bytes 2097152 | tf_op jit(solution)/shard_map/while/body/eval_jaxpr/all_to_all | solution.py:184
  323.8 7.7 %collective-permute-start = (bf16[128,4096]{0,1:T(8,128)(2,1)S(1)}, bf16[128,4096]{0,1:T(8,128)(2,1)}, u32[]{:S(2)}, u32[]{:S(2)}) collective-permute-start(bf16[128,4096]{0,1:T(8,128)(2,1)S(1)} %bitcast.119), channel_id=1, source_target_pairs={{8,0},{16,8},{24,16},{9,1},{17,9},{25,17},{10,2},{18,10},{26,18},{... | collective-permute-start | bytes 3145736 | tf_op jit(solution)/shard_map/while/body/eval_jaxpr/ppermute | solution.py:13
  328.7 2.5 copy-start.6
  333.1 43.0 %copy-start.1 = (bf16[8,128,4,128]{3,1,2,0:T(8,128)(2,1)}, bf16[8,128,4,128]{3,1,2,0:T(8,128)(2,1)S(1)}, u32[]{:S(2)}) copy-start(bf16[8,128,4,128]{3,1,2,0:T(8,128)(2,1)S(1)} %get-tuple-element.632) | copy-start | bytes 3145732 | tf_op jit(solution)/shard_map/while
  334.4 26.5 %all-to-all-start = ((bf16[128,8,512]{0,2,1:T(8,128)(2,1)}), bf16[128,8,512]{0,2,1:T(8,128)(2,1)S(1)}, u32[]{:S(2)}, u32[]{:S(2)}) async-start(bf16[128,8,512]{0,2,1:T(8,128)(2,1)} %bitcast.111), calls=%async_computation | async-start | bytes 2097152 | tf_op jit(solution)/shard_map/while/body/eval_jaxpr/all_to_all | solution.py:180
  365.0 27.8 %all-to-all-start.1 = ((bf16[8,128,512]{1,2,0:T(8,128)(2,1)}), bf16[8,128,512]{1,2,0:T(8,128)(2,1)S(1)}, u32[]{:S(2)}, u32[]{:S(2)}) async-start(bf16[8,128,512]{1,2,0:T(8,128)(2,1)} %bitcast.113), calls=%async_computation.1 | async-start | bytes 2097152 | tf_op jit(solution)/shard_map/while/body/eval_jaxpr/all_to_all | solution.py:184
  392.9 7.7 %collective-permute-start = (bf16[128,4096]{0,1:T(8,128)(2,1)S(1)}, bf16[128,4096]{0,1:T(8,128)(2,1)}, u32[]{:S(2)}, u32[]{:S(2)}) collective-permute-start(bf16[128,4096]{0,1:T(8,128)(2,1)S(1)} %bitcast.119), channel_id=1, source_target_pairs={{8,0},{16,8},{24,16},{9,1},{17,9},{25,17},{10,2},{18,10},{26,18},{... | collective-permute-start | bytes 3145736 | tf_op jit(solution)/shard_map/while/body/eval_jaxpr/ppermute | solution.py:13
  397.7 2.5 copy-start.6
  402.1 9.1 %copy-start.3 = (bf16[8,128,4,128]{3,1,2,0:T(8,128)(2,1)S(1)}, bf16[8,128,4,128]{3,1,2,0:T(8,128)(2,1)}, u32[]{:S(2)}) copy-start(bf16[8,128,4,128]{3,1,2,0:T(8,128)(2,1)} %get-tuple-element.367) | copy-start | bytes 3145732
  404.5 27.0 %all-to-all-start.5 = ((bf16[8,128,512]{1,2,0:T(8,128)(2,1)}), bf16[8,128,512]{1,2,0:T(8,128)(2,1)S(1)}, u32[]{:S(2)}, u32[]{:S(2)}) async-start(bf16[8,128,512]{1,2,0:T(8,128)(2,1)} %bitcast.15), calls=%async_computation.5 | async-start | bytes 2097152 | tf_op jit(solution)/shard_map/all_to_all | solution.py:194
  411.2 26.4 %copy-start.8 = (bf16[128,4096]{0,1:T(8,128)(2,1)S(1)}, bf16[128,4096]{0,1:T(8,128)(2,1)}, u32[]{:S(2)}) copy-start(bf16[128,4096]{0,1:T(8,128)(2,1)} %get-tuple-element.368) | copy-start | bytes 3145732
  431.5 27.8 %all-to-all-start.6 = ((bf16[8,128,512]{1,2,0:T(8,128)(2,1)}), bf16[8,128,512]{1,2,0:T(8,128)(2,1)S(1)}, u32[]{:S(2)}, u32[]{:S(2)}) async-start(bf16[8,128,512]{1,2,0:T(8,128)(2,1)} %bitcast.129), calls=%async_computation.6 | async-start | bytes 2097152 | tf_op jit(solution)/shard_map/all_to_all | solution.py:195
  (27 other events, 40.2 us)
where the time goes:
time: 467 us; the launch traced here: 460 us
  waiting for transfers between devices  214 us (46%)
  starting transfers between devices  117 us (25%)
  local copies, waits for them, and re-layouts  49.1 us (11%)
  matrix products  41.6 us (9%)
  other arithmetic  37.6 us (8%)
    all_to_all x4, waiting for transfers between devices, tick_seq(): lax.all_to_all(incoming, 'seq', split_axis=1, concat_axis=0, tiled=True)  74.9 us
    all_to_all x4, waiting for transfers between devices, tick_seq(): lax.all_to_all(to_flat(new_grad), 'seq', split_axis=0, concat_axis=1, til...  39.8 us
    ppermute x4, starting transfers between devices, from_behind(): lax.ppermute(value, axis, [(source, source + steps) for source in range(l...  34.4 us
    all_to_all x4, starting transfers between devices, tick_seq(): lax.all_to_all(incoming, 'seq', split_axis=1, concat_axis=0, tiled=True)  26.3 us
    all_to_all x4, starting transfers between devices, tick_seq(): lax.all_to_all(to_flat(new_grad), 'seq', split_axis=0, concat_axis=1, til...  24.8 us
    unnamed x28, local copies, waits for them, and re-layouts  23.6 us
    all_to_all x1, waiting for transfers between devices, on_device(): lax.all_to_all(queries[0], 'seq', split_axis=1, concat_axis=0, tiled=True)  21.9 us
    all_to_all x1, waiting for transfers between devices, on_device(): lax.all_to_all(spread_keys, 'seq', split_axis=1, concat_axis=0, tiled=True)  21.9 us
  transfers between devices with their start and end apart: 17, of which 13 were waited for; matrix products, arithmetic and copies ran while one was open for 12% of the time, Pallas kernels for 0%

commit v1 on v0

--- a/solution.py
+++ b/solution.py
@@ -130,75 +130,58 @@
     def to_flat(block_rows):
         return block_rows.reshape(seq_len, local_heads * DH)
 
-    def hand_down(grad_rows):
-        return from_behind(grad_rows, "pipe", -1)
-
-    def section_work(context, grad_head, active, held_pair):
-        softmax_probs, probs_low, query_blocks, keys_both, values_both = context
-        new_grad = value_grad(probs_low, grad_head, BLK, seq_ways)
-        grad_query, grad_key = weight_grads(
-            softmax_probs,
-            probs_low,
-            query_blocks,
-            keys_both,
-            values_both,
-            grad_head,
-            score_scale,
-            BLK,
-        )
-        held_pair = (
-            jnp.where(active, grad_query, held_pair[0]),
-            jnp.where(active, grad_key, held_pair[1]),
-        )
-        return (new_grad, held_pair)
-
-    zero_blocks = jnp.zeros((block_count, BLK, local_heads, DH), jnp.bfloat16)
-    zero_rows = jnp.zeros((tok_rows, full_width), jnp.bfloat16)
-    spread_keys = jnp.broadcast_to(
-        key_heads[0].reshape(tok_rows, kv_count, 1, DH), (tok_rows, kv_count, group_size, DH)
-    ).reshape(tok_rows, full_width)
-    query_flat = lax.all_to_all(queries[0], "seq", split_axis=1, concat_axis=0, tiled=True)
-    input_flat = lax.all_to_all(inputs[0], "seq", split_axis=1, concat_axis=0, tiled=True)
-    key_flat = lax.all_to_all(spread_keys, "seq", split_axis=1, concat_axis=0, tiled=True)
+    stacked = jnp.stack([queries[0], inputs[0], cotangent])
+    stacked_heads = lax.all_to_all(stacked, "seq", split_axis=2, concat_axis=1, tiled=True)
+    query_flat, input_flat, cot_flat = stacked_heads[0], stacked_heads[1], stacked_heads[2]
+    kv_pick = (jnp.arange(seq_ways) * local_heads) // group_size
+    key_rows = key_heads[0].reshape(tok_rows, kv_count, DH)[:, kv_pick, :]
+    key_flat = lax.all_to_all(key_rows, "seq", split_axis=1, concat_axis=0, tiled=True)
+    key_blocks = jnp.broadcast_to(
+        key_flat.reshape(block_count, BLK, 1, DH), (block_count, BLK, local_heads, DH)
+    )
     query_blocks = to_heads(query_flat)
-    keys_both = key_pair(to_heads(key_flat))
+    keys_both = key_pair(key_blocks)
     values_both = key_pair(to_heads(input_flat))
     allowed = visible(lengths, block_count, BLK)
     softmax_probs = probabilities(query_blocks, keys_both, allowed, score_scale)
-    context = (
+    probs_low = softmax_probs.astype(jnp.bfloat16)
+
+    arrived = jnp.zeros_like(cot_flat)
+    held_in = cot_flat
+    held_out = cot_flat
+    for tick in range(section_count):
+        sender = last_section - tick
+        grad_in = jnp.where(section_index == last_section, cot_flat, arrived)
+        new_grad = to_flat(value_grad(probs_low, to_heads(grad_in), BLK, seq_ways))
+        active = tick == live_tick
+        held_in = jnp.where(active, grad_in, held_in)
+        held_out = jnp.where(active, new_grad, held_out)
+        if sender > 0:
+            arrived = lax.ppermute(new_grad, "pipe", [(sender, sender - 1)])
+
+    grad_query, grad_key = weight_grads(
         softmax_probs,
-        softmax_probs.astype(jnp.bfloat16),
+        probs_low,
         query_blocks,
         keys_both,
         values_both,
-    )
-
-    def tick_seq(tick_num, state_carry):
-        arrived, out_grad, held_pair = state_carry
-        incoming = jnp.where(section_index == last_section, cotangent, arrived)
-        grad_head = to_heads(
-            lax.all_to_all(incoming, "seq", split_axis=1, concat_axis=0, tiled=True)
-        )
-        active = tick_num == live_tick
-        new_grad, held_pair = section_work(context, grad_head, active, held_pair)
-        new_seq = lax.all_to_all(to_flat(new_grad), "seq", split_axis=0, concat_axis=1, tiled=True)
-        out_grad = jnp.where(active, new_seq, out_grad)
-        return (hand_down(new_seq), out_grad, held_pair)
-
-    unused_rows, grad_inputs, held_pair = lax.fori_loop(
-        0, section_count, tick_seq, (zero_rows, zero_rows, (zero_blocks, zero_blocks))
-    )
-    softmax_probs, probs_low, query_blocks, keys_both, values_both = context
-    grad_query, grad_key = held_pair
-    query_out, key_out = (
-        lax.all_to_all(to_flat(grad_query), "seq", split_axis=0, concat_axis=1, tiled=True),
-        lax.all_to_all(to_flat(grad_key), "seq", split_axis=0, concat_axis=1, tiled=True),
-    )
+        to_heads(held_in),
+        score_scale,
+        BLK,
+    )
+    pair_out = lax.all_to_all(
+        jnp.stack([to_flat(grad_query), held_out]), "seq", split_axis=1, concat_axis=2, tiled=True
+    )
+    if local_heads == 1:
+        key_part = grad_key.reshape(seq_len, DH)
+    else:
+        key_part = jnp.sum(grad_key.astype(jnp.float32), axis=2).reshape(seq_len, DH)
+    key_out = lax.all_to_all(key_part[:, None, :], "seq", split_axis=0, concat_axis=1, tiled=True)
     key_sum = jnp.sum(
-        key_out.reshape(tok_rows, kv_count, group_size, DH).astype(jnp.float32), axis=2
+        key_out.reshape(tok_rows, kv_count, seq_ways // kv_count, DH).astype(jnp.float32), axis=2
     )
     key_final = key_sum.astype(jnp.bfloat16).reshape(tok_rows, kv_count * DH)
-    return (query_out[None], key_final[None], grad_inputs[None])
+    return (pair_out[0][None], key_final[None], pair_out[1][None])
 
 
 def solution(mesh):

time: 467 us -> 298 us (0.64)
  the two profiles are of different devices: /device:TPU:15 before, /device:TPU:1 now
where the time goes in v1:
time: 298 us; the launch traced here: 297 us
  waiting for transfers between devices  142 us (48%)
  local copies, waits for them, and re-layouts  88.7 us (30%)
  starting transfers between devices  26.3 us (9%)
  other arithmetic  23.3 us (8%)
  matrix products  14.9 us (5%)
    all_to_all x1, waiting for transfers between devices, on_device(): lax.all_to_all(stacked, 'seq', split_axis=2, concat_axis=1, tiled=True)  91.2 us
    all_to_all x1, waiting for transfers between devices, on_device(): lax.all_to_all(jnp.stack([to_flat(grad_query), held_out]), 'seq', split_a...  32.8 us
    unnamed x51, local copies, waits for them, and re-layouts  20.6 us
    ppermute x3, waiting for transfers between devices, on_device(): arrived = lax.ppermute(new_grad, 'pipe', [(sender, sender - 1)])  17.9 us
    reshape x7, local copies, waits for them, and re-layouts, to_flat(): return block_rows.reshape(seq_len, local_heads * DH)  14.4 us
    reshape x8, local copies, waits for them, and re-layouts, to_heads(): return flat_rows.reshape(block_count, BLK, local_heads, DH)  14.3 us
    convert_element_type x4, local copies, waits for them, and re-layouts, value_grad(): (grad_blocks.astype(jnp.float32) + fold_value(key_terms, block_len, group...  9.32 us
    all_to_all x1, starting transfers between devices, on_device(): lax.all_to_all(key_rows, 'seq', split_axis=1, concat_axis=0, tiled=True)  6.38 us
  transfers between devices with their start and end apart: 7, of which 4 were waited for; matrix products, arithmetic and copies ran while one was open for 15% of the time, Pallas kernels for 0%

profile of v1, /device:TPU:1, one launch (start us, length us, event | category | flops | bytes accessed | tf_op | source)
XLA Modules:
  0.0 296.7 jit_solution(6301174754206961210)
XLA Ops:
  3.1 6.4 %all-to-all-start = ((bf16[128,8,128]{2,0,1:T(8,128)(2,1)}), bf16[128,8,128]{2,0,1:T(8,128)(2,1)S(1)}, u32[]{:S(2)}, u32[]{:S(2)}) async-start(bf16[128,8,128]{2,0,1:T(8,128)(2,1)} %bitcast.2), calls=%async_computation | async-start | bytes 524288 | tf_op jit(solution)/shard_map/all_to_all | solution.py:138
  9.5 2.2 pad_maximum_fusion
  11.7 4.8 %copy.217 = bf16[3,128,4096]{1,0,2:T(4,128)(2,1)} copy(bf16[3,128,4096]{2,1,0:T(8,128)(2,1)S(1)} %pad_maximum_fusion) | data formatting | bytes 6291456 | tf_op jit(solution)/shard_map/stack | solution.py:133
  16.9 5.2 %all-to-all-start.1 = ((bf16[3,128,4096]{1,0,2:T(4,128)(2,1)}), bf16[3,128,4096]{1,0,2:T(4,128)(2,1)}, u32[]{:S(2)}, u32[]{:S(2)}) async-start(bf16[3,128,4096]{1,0,2:T(4,128)(2,1)} %copy.217), calls=%async_computation.1 | async-start | bytes 8388608 | tf_op jit(solution)/shard_map/all_to_all | solution.py:134
  22.5 91.2 %all-to-all-done.1 = bf16[3,128,4096]{1,0,2:T(4,128)(2,1)} async-done(((bf16[3,128,4096]{1,0,2:T(4,128)(2,1)}), bf16[3,128,4096]{1,0,2:T(4,128)(2,1)}, u32[]{:S(2)}, u32[]{:S(2)}) %all-to-all-start.1) | async-done | bytes 3145760 | tf_op jit(solution)/shard_map/all_to_all | solution.py:134
  113.7 2.6 copy.218
  121.1 2.2 fusion.37
  128.4 2.4 copy.289
  134.0 2.3 bitcast_select_fusion.2
  138.5 2.3 copy.224
  145.3 2.4 copy.267
  150.4 17.9 %collective-permute-done.1 = bf16[1024,512]{1,0:T(8,128)(2,1)S(1)} collective-permute-done((bf16[1024,512]{1,0:T(8,128)(2,1)S(1)}, bf16[1024,512]{1,0:T(8,128)(2,1)S(1)}, u32[]{:S(2)}, u32[]{:S(2)}) %collective-permute-start.1) | collective-permute-done | bytes 1048608 | tf_op jit(solution)/shard_map/ppermute | solution.py:160
  172.6 2.3 copy.229
  179.6 2.4 copy.271
  182.0 2.4 copy.287
  184.3 2.3 collective-permute-start.2
  187.5 2.9 copy.221
  190.6 2.3 copy.235
  194.1 2.3 reshape.399
  196.4 2.9 copy.226
  199.3 2.3 reshape.398
  201.6 2.9 copy.231
  204.5 2.3 reshape.397
  206.8 3.5 %fusion.13 = (bf16[1024,512]{1,0:T(8,128)(2,1)}, bf16[1024,512]{1,0:T(8,128)(2,1)}) fusion(bf16[1,8,128,512]{3,2,1,0:T(8,128)(2,1)S(1)} %copy.220, pred[]{:T(512)S(6)} %eq.22, pred[]{:T(512)S(6)} %eq.21, pred[]{:T(512)S(6)} %eq.20, pred[]{:T(512)S(6)} %eq.19, pred[]{:T(512)S(6)} %eq.18, bf16[1024,512]{1,0:T(8,128)(2,1)} %collective-permute-done, ...), kind=kLoop, calls=%fused_computation.45 | loop fusion | flops 4194304 | bytes 6291461 | tf_op jit(solution)/shard_map/jit(_where)/select_n | solution.py:157
  213.2 2.5 fusion.4
  220.4 2.7 convolution_bitcast_fusion
  233.6 4.4 %all-to-all-start.3 = ((f32[1024,1,128]{2,1,0:T(1,128)}), f32[1024,1,128]{2,1,0:T(1,128)}, u32[]{:S(2)}, u32[]{:S(2)}) async-start(f32[1024,1,128]{2,1,0:T(1,128)} %bitcast.137), calls=%async_computation.3 | async-start | bytes 1048576 | tf_op jit(solution)/shard_map/all_to_all | solution.py:179
  238.9 2.9 copy.240
  241.8 2.3 stack_reshape.3
  248.2 4.1 %copy.250 = bf16[2,1024,512]{2,0,1:T(2,128)(2,1)} copy(bf16[2,1024,512]{1,2,0:T(8,128)(2,1)S(1)} %pad_maximum_fusion.5) | data formatting | bytes 4194304 | tf_op jit(solution)/shard_map/stack | solution.py:173
  252.2 5.1 %all-to-all-start.2 = ((bf16[2,1024,512]{2,0,1:T(2,128)(2,1)}), bf16[2,1024,512]{2,0,1:T(2,128)(2,1)S(1)}, u32[]{:S(2)}, u32[]{:S(2)}) async-start(bf16[2,1024,512]{2,0,1:T(2,128)(2,1)} %copy.250), calls=%async_computation.2 | async-start | bytes 4194304 | tf_op jit(solution)/shard_map/all_to_all | solution.py:172
  259.3 32.8 %all-to-all-done.2 = bf16[2,1024,512]{2,0,1:T(2,128)(2,1)S(1)} async-done(((bf16[2,1024,512]{2,0,1:T(2,128)(2,1)}), bf16[2,1024,512]{2,0,1:T(2,128)(2,1)S(1)}, u32[]{:S(2)}, u32[]{:S(2)}) %all-to-all-start.2) | async-done | bytes 2097184 | tf_op jit(solution)/shard_map/all_to_all | solution.py:172
  (123 shorter events, 66.1 us)
Async XLA Ops:
  3.1 13.7 %all-to-all-start = ((bf16[128,8,128]{2,0,1:T(8,128)(2,1)}), bf16[128,8,128]{2,0,1:T(8,128)(2,1)S(1)}, u32[]{:S(2)}, u32[]{:S(2)}) async-start(bf16[128,8,128]{2,0,1:T(8,128)(2,1)} %bitcast.2), calls=%async_computation | async-start | bytes 524288 | tf_op jit(solution)/shard_map/all_to_all | solution.py:138
  16.5 5.6 %copy-start.21 = (s32[8]{0:T(128)S(1)}, s32[8]{0:T(128)}, u32[]{:S(2)}) copy-start(s32[8]{0:T(128)} %param.19) | copy-start | bytes 100
  16.9 96.9 %all-to-all-start.1 = ((bf16[3,128,4096]{1,0,2:T(4,128)(2,1)}), bf16[3,128,4096]{1,0,2:T(4,128)(2,1)}, u32[]{:S(2)}, u32[]{:S(2)}) async-start(bf16[3,128,4096]{1,0,2:T(4,128)(2,1)} %copy.217), calls=%async_computation.1 | async-start | bytes 8388608 | tf_op jit(solution)/shard_map/all_to_all | solution.py:134
  116.4 2.4 copy-start.2
  118.7 1.0 copy-start.5
  119.0 1.1 copy-start.10
  119.2 1.1 copy-start.8
  123.4 2.0 copy-start.12
  126.9 3.9 %copy-start.7 = (bf16[8,128,4,128]{1,3,2,0:T(8,128)(2,1)}, bf16[8,128,4,128]{1,3,2,0:T(8,128)(2,1)S(1)}, u32[]{:S(2)}) copy-start(bf16[8,128,4,128]{1,3,2,0:T(8,128)(2,1)S(1)} %add_convert_fusion.3) | copy-start | bytes 3145732
  130.8 3.2 %collective-permute-start = (bf16[1024,512]{1,0:T(8,128)(2,1)}, bf16[1024,512]{1,0:T(8,128)(2,1)}, u32[]{:S(2)}, u32[]{:S(2)}) collective-permute-start(bf16[1024,512]{1,0:T(8,128)(2,1)} %bitcast.121), channel_id=1, source_target_pairs={{24,16},{25,17},{26,18},{27,19},{28,20},{29,21},{30,22},{31,23}} | collective-permute-start | bytes 3145736 | tf_op jit(solution)/shard_map/ppermute | solution.py:160
  142.8 1.2 copy-start.3
  149.1 19.2 %collective-permute-start.1 = (bf16[1024,512]{1,0:T(8,128)(2,1)S(1)}, bf16[1024,512]{1,0:T(8,128)(2,1)S(1)}, u32[]{:S(2)}, u32[]{:S(2)}) collective-permute-start(bf16[1024,512]{1,0:T(8,128)(2,1)S(1)} %bitcast.140), channel_id=1, source_target_pairs={{16,8},{17,9},{18,10},{19,11},{20,12},{21,13},{22,14},{23,15}} | collective-permute-start | bytes 3145736 | tf_op jit(solution)/shard_map/ppermute | solution.py:160
  168.3 1.0 copy-start.16
  177.1 1.2 copy-start.4
  184.3 22.4 %collective-permute-start.2 = (bf16[1024,512]{1,0:T(8,128)(2,1)}, bf16[1024,512]{1,0:T(8,128)(2,1)}, u32[]{:S(2)}, u32[]{:S(2)}) collective-permute-start(bf16[1024,512]{1,0:T(8,128)(2,1)} %bitcast.119), channel_id=1, source_target_pairs={{8,0},{9,1},{10,2},{11,3},{12,4},{13,5},{14,6},{15,7}} | collective-permute-start | bytes 3145736 | tf_op jit(solution)/shard_map/ppermute | solution.py:160
  213.2 2.8 copy-start.13
  213.2 3.1 %copy-start.19 = (bf16[8,128,4,128]{3,1,2,0:T(8,128)(2,1)S(1)}, bf16[8,128,4,128]{3,1,2,0:T(8,128)(2,1)}, u32[]{:S(2)}) copy-start(bf16[8,128,4,128]{3,1,2,0:T(8,128)(2,1)} %copy.235) | copy-start | bytes 3145732
  213.2 3.4 %copy-start.20 = (bf16[8,128,4,128]{1,3,2,0:T(8,128)(2,1)S(1)}, bf16[8,128,4,128]{1,3,2,0:T(8,128)(2,1)}, u32[]{:S(2)}) copy-start(bf16[8,128,4,128]{1,3,2,0:T(8,128)(2,1)} %copy.237) | copy-start | bytes 3145732
  216.7 2.0 copy-start.9
  216.7 2.0 copy-start.11
  218.6 1.8 copy-start.6
  220.4 2.7 copy-start.17
  226.5 2.1 copy-start.1
  226.7 3.5 %copy-start = (f32[8,256,4,128]{1,3,2,0:T(8,128)S(1)}, f32[8,256,4,128]{1,3,2,0:T(8,128)}, u32[]{:S(2)}) copy-start(f32[8,256,4,128]{1,3,2,0:T(8,128)} %convolution_bitcast_fusion) | copy-start | bytes 12582916
  230.5 7.4 %slice-start = ((f32[8,256,4,128]{1,3,2,0:T(8,128)}), f32[8,128,4,128]{1,3,2,0:T(8,128)S(1)}, s32[]{:S(2)}) async-start(f32[8,256,4,128]{1,3,2,0:T(8,128)} %copy-done.1), calls=%async_computation.4 | async-start | bytes 4194304 | tf_op jit(solution)/shard_map/slice | solution.py:43
  233.6 18.7 %all-to-all-start.3 = ((f32[1024,1,128]{2,1,0:T(1,128)}), f32[1024,1,128]{2,1,0:T(1,128)}, u32[]{:S(2)}, u32[]{:S(2)}) async-start(f32[1024,1,128]{2,1,0:T(1,128)} %bitcast.137), calls=%async_computation.3 | async-start | bytes 1048576 | tf_op jit(solution)/shard_map/all_to_all | solution.py:179
  244.4 2.0 copy-start.14
  244.4 2.0 copy-start.15
  246.4 1.6 copy-start.18
  252.2 39.9 %all-to-all-start.2 = ((bf16[2,1024,512]{2,0,1:T(2,128)(2,1)}), bf16[2,1024,512]{2,0,1:T(2,128)(2,1)S(1)}, u32[]{:S(2)}, u32[]{:S(2)}) async-start(bf16[2,1024,512]{2,0,1:T(2,128)(2,1)} %copy.250), calls=%async_computation.2 | async-start | bytes 4194304 | tf_op jit(solution)/shard_map/all_to_all | solution.py:172

commit v2 on v1

v2 whole, which is shorter than its diff:
```python
import jax
import jax.numpy as jnp
from jax import lax
from jax.sharding import PartitionSpec as P

DH = 128
BLK = 128


def key_pair(block_rows):
    first_block = jnp.broadcast_to(block_rows[:, :1], block_rows.shape)
    return jnp.concatenate([first_block, block_rows], axis=2)


def visible(lengths, block_count, block_len):
    shape = (block_count, block_len, 2 * block_len)
    row_index = lax.broadcasted_iota(jnp.int32, shape, 1)
    col_index = lax.broadcasted_iota(jnp.int32, shape, 2)
    block_index = lax.broadcasted_iota(jnp.int32, shape, 0)
    in_first = col_index < block_len
    offset = jnp.where(in_first, col_index, col_index - block_len)
    own_len = lengths[:, None, None]
    first_ok = in_first & (offset < lengths[0]) & ((block_index > 0) | (offset <= row_index))
    own_ok = (
        jnp.logical_not(in_first) & (block_index > 0) & (offset <= row_index) & (offset < own_len)
    )
    return (first_ok | own_ok)[None]


def fold_keys(key_terms, block_len):
    own_part = key_terms[:, :, block_len:]
    first_part = jnp.sum(key_terms[:, :, :block_len], axis=1)
    return own_part.at[:, 0].add(first_part)


def fold_value(key_terms, block_len, groups):
    own_part = key_terms[:, :, block_len:]
    first_terms = key_terms[:, :, :block_len]
    heads, blocks = first_terms.shape[:2]
    grouped = first_terms.reshape((heads, groups, blocks // groups) + first_terms.shape[2:])
    partial_low = lax.optimization_barrier(jnp.sum(grouped, axis=2).astype(jnp.bfloat16))
    first_part = jnp.sum(partial_low.astype(jnp.float32), axis=1)
    return own_part.at[:, 0].add(first_part)


def probabilities(query_blocks, keys_both, allowed, score_scale):
    scores = (
        jnp.einsum("hbid,hbjd->hbij", query_blocks, keys_both, preferred_element_type=jnp.float32)
        * score_scale
    )
    scores = jnp.where(allowed, scores, -jnp.inf)
    row_max = jnp.max(scores, axis=-1, keepdims=True)
    exp_scores = jnp.exp(scores - row_max)
    return exp_scores / jnp.sum(exp_scores, axis=-1, keepdims=True)


def value_grad(probs_low, grad_blocks, block_len, groups):
    key_terms = jnp.einsum(
        "hbij,hbid->hbjd", probs_low, grad_blocks, preferred_element_type=jnp.float32
    )
    return (grad_blocks.astype(jnp.float32) + fold_value(key_terms, block_len, groups)).astype(
        jnp.bfloat16
    )


def weight_grads(
    softmax_probs, probs_low, query_blocks, keys_both, values_both, grad_blocks, score_scale, block_len
):
    output = jnp.einsum(
        "hbij,hbjd->hbid", probs_low, values_both, preferred_element_type=jnp.float32
    )
    row_dot = jnp.sum(grad_blocks.astype(jnp.float32) * output, axis=-1)[..., None]
    grad_probs = jnp.einsum(
        "hbid,hbjd->hbij", grad_blocks, values_both, preferred_element_type=jnp.float32
    )
    grad_scores = (softmax_probs * (grad_probs - row_dot)).astype(jnp.bfloat16)
    grad_query = (
        jnp.einsum("hbij,hbjd->hbid", grad_scores, keys_both, preferred_element_type=jnp.float32)
        * score_scale
    ).astype(jnp.bfloat16)
    key_terms = jnp.einsum(
        "hbij,hbid->hbjd", grad_scores, query_blocks, preferred_element_type=jnp.float32
    )
    grad_key = (fold_keys(key_terms, block_len) * score_scale).astype(jnp.bfloat16)
    return (grad_query, grad_key)


def on_device(queries, key_heads, inputs, cotangent, lengths):
    section_count = lax.axis_size("pipe")
    section_index = lax.axis_index("pipe")
    seq_ways = lax.axis_size("seq")
    tok_rows = queries.shape[1]
    full_width = queries.shape[2]
    head_count = full_width // DH
    kv_count = key_heads.shape[2] // DH
    group_size = head_count // kv_count
    seq_len = tok_rows * seq_ways
    block_count = seq_len // BLK
    local_heads = head_count // seq_ways
    score_scale = DH ** (-0.5)
    last_section = section_count - 1

    def to_blocks(head_rows):
        return head_rows.reshape(local_heads, block_count, BLK, DH)

    def head_major(rows):
        return jnp.transpose(rows.reshape(tok_rows, head_count, DH), (1, 0, 2))

    stacked = jnp.stack([head_major(queries[0]), head_major(inputs[0]), head_major(cotangent)])
    stacked_heads = lax.all_to_all(stacked, "seq", split_axis=1, concat_axis=2, tiled=True)
    query_blocks = to_blocks(stacked_heads[0])
    values_both = key_pair(to_blocks(stacked_heads[1]))
    cot_blocks = to_blocks(stacked_heads[2])
    kv_pick = (jnp.arange(seq_ways) * local_heads) // group_size
    key_rows = jnp.transpose(key_heads[0].reshape(tok_rows, kv_count, DH), (1, 0, 2))[kv_pick]
    key_flat = lax.all_to_all(key_rows, "seq", split_axis=0, concat_axis=1, tiled=True)
    key_blocks = jnp.broadcast_to(
        key_flat.reshape(1, block_count, BLK, DH), (local_heads, block_count, BLK, DH)
    )
    keys_both = key_pair(key_blocks)
    allowed = visible(lengths, block_count, BLK)
    softmax_probs = probabilities(query_blocks, keys_both, allowed, score_scale)
    probs_low = softmax_probs.astype(jnp.bfloat16)

    grad_ins = []
    grad_outs = []
    grad_in = cot_blocks
    for tick in range(section_count):
        sender = last_section - tick
        new_grad = value_grad(probs_low, grad_in, BLK, seq_ways)
        grad_ins.append(grad_in)
        grad_outs.append(new_grad)
        if sender > 0:
            grad_in = lax.ppermute(new_grad, "pipe", [(sender, sender - 1)])

    def by_section(per_tick):
        chosen = per_tick[0]
        for tick in range(1, section_count):
            chosen = jnp.where(section_index == last_section - tick, per_tick[tick], chosen)
        return chosen

    held_in = by_section(grad_ins)
    held_out = by_section(grad_outs)
    grad_query, grad_key = weight_grads(
        softmax_probs,
        probs_low,
        query_blocks,
        keys_both,
        values_both,
        held_in,
        score_scale,
        BLK,
    )
    pair = jnp.stack([grad_query, held_out]).reshape(2, local_heads, seq_len, DH)
    pair_out = lax.all_to_all(pair, "seq", split_axis=2, concat_axis=1, tiled=True)
    pair_rows = jnp.transpose(pair_out, (0, 2, 1, 3)).reshape(2, tok_rows, full_width)
    if local_heads == 1:
        key_part = grad_key.reshape(seq_len, DH)
    else:
        key_part = jnp.sum(grad_key.astype(jnp.float32), axis=0).reshape(seq_len, DH)
    key_out = lax.all_to_all(key_part[:, None, :], "seq", split_axis=0, concat_axis=1, tiled=True)
    key_sum = jnp.sum(
        key_out.reshape(tok_rows, kv_count, seq_ways // kv_count, DH).astype(jnp.float32), axis=2
    )
    key_final = key_sum.astype(jnp.bfloat16).reshape(tok_rows, kv_count * DH)
    return (pair_rows[0][None], key_final[None], pair_rows[1][None])


def solution(mesh):
    placed = (
        P("pipe", "seq", None),
        P("pipe", "seq", None),
        P("pipe", "seq", None),
        P("seq", None),
        P(),
    )
    return jax.shard_map(
        on_device,
        mesh=mesh,
        in_specs=placed,
        out_specs=(P("pipe", "seq", None), P("pipe", "seq", None), P("pipe", "seq", None)),
        check_vma=False,
    )
```

time: 298 us -> 229 us (0.77)
  the two profiles are of different devices: /device:TPU:1 before, /device:TPU:0 now
where the time goes in v2:
time: 229 us; the launch traced here: 228 us
  waiting for transfers between devices  147 us (64%)
  local copies, waits for them, and re-layouts  33.3 us (15%)
  starting transfers between devices  21.1 us (9%)
  other arithmetic  14.6 us (6%)
  matrix products  10.4 us (5%)
    all_to_all x1, waiting for transfers between devices, on_device(): lax.all_to_all(stacked, 'seq', split_axis=1, concat_axis=2, tiled=True)  69.2 us
    all_to_all x1, waiting for transfers between devices, on_device(): lax.all_to_all(pair, 'seq', split_axis=2, concat_axis=1, tiled=True)  47.5 us
    unnamed x51, local copies, waits for them, and re-layouts  19.2 us
    ppermute x3, waiting for transfers between devices, on_device(): grad_in = lax.ppermute(new_grad, 'pipe', [(sender, sender - 1)])  18.9 us
    all_to_all x1, waiting for transfers between devices, on_device(): lax.all_to_all(key_part[:, None, :], 'seq', split_axis=0, concat_axis=1,...  7.96 us
    all_to_all x1, starting transfers between devices, on_device(): lax.all_to_all(key_rows, 'seq', split_axis=0, concat_axis=1, tiled=True)  7.28 us
  transfers between devices with their start and end apart: 7, of which 5 were waited for; matrix products, arithmetic and copies ran while one was open for 7% of the time, Pallas kernels for 0%

profile of v2, /device:TPU:0, one launch (start us, length us, event | category | flops | bytes accessed | tf_op | source)
XLA Modules:
  0.0 227.7 jit_solution(16495156333464161144)
XLA Ops:
  0.7 1.2 copy.126
  2.0 1.3 gather_fusion
  3.3 7.3 %all-to-all-start.1 = ((bf16[8,128,128]{2,1,0:T(8,128)(2,1)}), bf16[8,128,128]{2,1,0:T(8,128)(2,1)S(1)}, u32[]{:S(2)}, u32[]{:S(2)}) async-start(bf16[8,128,128]{2,1,0:T(8,128)(2,1)} %gather_fusion), calls=%async_computation.1 | async-start | bytes 524288 | tf_op jit(solution)/shard_map/all_to_all | solution.py:116
  11.9 1.6 copy.122
  13.9 2.1 copy.123
  15.9 3.5 %all-to-all-done.1 = bf16[8,128,128]{2,1,0:T(8,128)(2,1)S(1)} async-done(((bf16[8,128,128]{2,1,0:T(8,128)(2,1)}), bf16[8,128,128]{2,1,0:T(8,128)(2,1)S(1)}, u32[]{:S(2)}, u32[]{:S(2)}) %all-to-all-start.1) | async-done | bytes 262176 | tf_op jit(solution)/shard_map/all_to_all | solution.py:116
  19.5 3.6 %all-to-all-start = ((bf16[3,32,128,128]{2,3,0,1:T(8,128)(2,1)}), bf16[3,32,128,128]{2,3,0,1:T(8,128)(2,1)S(1)}, u32[]{:S(2)}, u32[]{:S(2)}) async-start(bf16[3,32,128,128]{2,3,0,1:T(8,128)(2,1)} %copy.123), calls=%async_computation | async-start | bytes 6291456 | tf_op jit(solution)/shard_map/all_to_all | solution.py:110
  23.2 1.1 fusion.15
  24.2 69.2 %all-to-all-done = bf16[3,32,128,128]{2,3,0,1:T(8,128)(2,1)S(1)} async-done(((bf16[3,32,128,128]{2,3,0,1:T(8,128)(2,1)}), bf16[3,32,128,128]{2,3,0,1:T(8,128)(2,1)S(1)}, u32[]{:S(2)}, u32[]{:S(2)}) %all-to-all-start) | async-done | bytes 3145760 | tf_op jit(solution)/shard_map/all_to_all | solution.py:110
  93.4 1.6 copy-done.3
  95.1 3.5 %copy.125 = bf16[3,8,4,128,128]{4,3,1,2,0:T(8,128)(2,1)S(1)} copy(bf16[3,8,4,128,128]{3,4,0,2,1:T(8,128)(2,1)} %bitcast.84) | data formatting | bytes 6291456 | tf_op jit(solution)/shard_map/all_to_all | solution.py:110
  100.1 1.1 copy-done.6
  102.1 2.2 fusion.34
  105.0 1.4 copy-done.11
  106.4 1.3 copy-done.1
  114.3 1.3 add_convert_fusion.1
  115.6 1.5 collective-permute-start.2
  117.1 1.3 slice_bitcast_fusion
  118.4 18.9 %collective-permute-done.2 = bf16[4,8,128,128]{3,2,1,0:T(8,128)(2,1)} collective-permute-done((bf16[4,8,128,128]{3,2,1,0:T(8,128)(2,1)}, bf16[4,8,128,128]{3,2,1,0:T(8,128)(2,1)}, u32[]{:S(2)}, u32[]{:S(2)}) %collective-permute-start.2) | collective-permute-done | bytes 1048608 | tf_op jit(solution)/shard_map/ppermute | solution.py:134
  137.3 2.0 fusion.37
  141.2 1.1 copy-done.2
  142.2 3.3 %select_select_fusion = (bf16[4,8,128,128]{3,2,1,0:T(8,128)(2,1)S(1)}, bf16[4,8,128,128]{3,2,1,0:T(8,128)(2,1)}) fusion(bf16[4,8,128,128]{3,2,1,0:T(8,128)(2,1)} %collective-permute-done.2, bf16[4,8,128,128]{3,2,1,0:T(8,128)(2,1)S(1)} %copy-done.5, bf16[4,8,128,128]{3,2,1,0:T(8,128)(2,1)S(1)} %collective-permute-done, pred[]{:T(512)S(6)} %eq.14, ...), kind=kLoop, calls=%fused_computation.39 | loop fusion | flops 4718592 | bytes 11534339 | tf_op jit(solution)/shard_map/jit(_where)/select_n | solution.py:139
  146.6 1.4 copy-done.12
  148.0 1.5 multiply_convert_fusion
  152.2 3.7 %all-to-all-start.3 = ((f32[1024,1,128]{2,1,0:T(1,128)}), f32[1024,1,128]{2,1,0:T(1,128)S(1)}, u32[]{:S(2)}, u32[]{:S(2)}) async-start(f32[1024,1,128]{2,1,0:T(1,128)} %bitcast.32), calls=%async_computation.3 | async-start | bytes 1048576 | tf_op jit(solution)/shard_map/all_to_all | solution.py:161
  155.9 2.3 %multiply_convert_fusion.2 = bf16[4,8,128,128]{3,2,1,0:T(8,128)(2,1)S(1)} fusion(bf16[4,8,128,256]{3,2,1,0:T(8,128)(2,1)} %copy-done.17, bf16[4,8,128,128]{3,2,1,0:T(8,128)(2,1)S(1)} %copy-done.7, bf16[4,8,128,128]{3,2,1,0:T(8,128)(2,1)S(1)} %copy-done.9), kind=kOutput, calls=%fused_computation.21 | convolution fusion | flops 273678336 | bytes 5242880 | tf_op jit(solution)/shard_map/hbij,hbjd->hbid/dot_general | solution.py:78
  160.2 2.8 %pad_maximum_fusion.5 = bf16[2,4,1024,128]{3,1,0,2:T(4,128)(2,1)} fusion(bf16[1,4,1024,128]{3,1,0,2:T(4,128)(2,1)S(1)} %copy.135, bf16[1,4,1024,128]{3,1,0,2:T(4,128)(2,1)S(1)} %copy.134), kind=kLoop, calls=%fused_computation.16 | loop fusion | flops 1048576 | bytes 4194304 | tf_op jit(solution)/shard_map/stack | solution.py:154
  163.1 8.0 %all-to-all-done.3 = f32[1024,1,128]{2,1,0:T(1,128)S(1)} async-done(((f32[1024,1,128]{2,1,0:T(1,128)}), f32[1024,1,128]{2,1,0:T(1,128)S(1)}, u32[]{:S(2)}, u32[]{:S(2)}) %all-to-all-start.3) | async-done | bytes 524320 | tf_op jit(solution)/shard_map/all_to_all | solution.py:161
  171.0 3.6 %all-to-all-start.2 = ((bf16[2,4,1024,128]{3,1,0,2:T(4,128)(2,1)}), bf16[2,4,1024,128]{3,1,0,2:T(4,128)(2,1)S(1)}, u32[]{:S(2)}, u32[]{:S(2)}) async-start(bf16[2,4,1024,128]{3,1,0,2:T(4,128)(2,1)} %pad_maximum_fusion.5), calls=%async_computation.2 | async-start | bytes 4194304 | tf_op jit(solution)/shard_map/all_to_all | solution.py:155
  175.6 47.5 %all-to-all-done.2 = bf16[2,4,1024,128]{3,1,0,2:T(4,128)(2,1)S(1)} async-done(((bf16[2,4,1024,128]{3,1,0,2:T(4,128)(2,1)}), bf16[2,4,1024,128]{3,1,0,2:T(4,128)(2,1)S(1)}, u32[]{:S(2)}, u32[]{:S(2)}) %all-to-all-start.2) | async-done | bytes 2097184 | tf_op jit(solution)/shard_map/all_to_all | solution.py:155
  224.4 1.3 copy.142
  226.4 1.3 copy.144
  (94 shorter events, 22.0 us)
Async XLA Ops:
  0.6 9.9 %copy-start.18 = (bf16[1,128,4096]{2,1,0:T(8,128)(2,1)S(1)}, bf16[1,128,4096]{2,1,0:T(8,128)(2,1)}, u32[]{:S(2)}) copy-start(bf16[1,128,4096]{2,1,0:T(8,128)(2,1)} %param.15) | copy-start | bytes 3145732
  0.6 10.6 %copy-start.19 = (bf16[1,128,4096]{2,1,0:T(8,128)(2,1)S(1)}, bf16[1,128,4096]{2,1,0:T(8,128)(2,1)}, u32[]{:S(2)}) copy-start(bf16[1,128,4096]{2,1,0:T(8,128)(2,1)} %param.17) | copy-start | bytes 3145732
  3.3 16.2 %all-to-all-start.1 = ((bf16[8,128,128]{2,1,0:T(8,128)(2,1)}), bf16[8,128,128]{2,1,0:T(8,128)(2,1)S(1)}, u32[]{:S(2)}, u32[]{:S(2)}) async-start(bf16[8,128,128]{2,1,0:T(8,128)(2,1)} %gather_fusion), calls=%async_computation.1 | async-start | bytes 524288 | tf_op jit(solution)/shard_map/all_to_all | solution.py:116
  15.9 7.2 %copy-start.21 = (s32[8]{0:T(128)S(1)}, s32[8]{0:T(128)}, u32[]{:S(2)}) copy-start(s32[8]{0:T(128)} %param.19) | copy-start | bytes 100
  19.5 74.0 %all-to-all-start = ((bf16[3,32,128,128]{2,3,0,1:T(8,128)(2,1)}), bf16[3,32,128,128]{2,3,0,1:T(8,128)(2,1)S(1)}, u32[]{:S(2)}, u32[]{:S(2)}) async-start(bf16[3,32,128,128]{2,3,0,1:T(8,128)(2,1)} %copy.123), calls=%async_computation | async-start | bytes 6291456 | tf_op jit(solution)/shard_map/all_to_all | solution.py:110
  93.4 1.6 copy-start.3
  98.6 3.3 %copy-start = (bf16[3,8,4,128,128]{4,3,1,2,0:T(8,128)(2,1)}, bf16[3,8,4,128,128]{4,3,1,2,0:T(8,128)(2,1)S(1)}, u32[]{:S(2)}) copy-start(bf16[3,8,4,128,128]{4,3,1,2,0:T(8,128)(2,1)S(1)} %copy.125) | copy-start | bytes 9437188
  98.8 1.2 copy-start.8
  100.0 1.1 copy-start.6
  101.1 0.9 copy-start.20
  104.3 2.1 copy-start.11
  104.3 3.4 %copy-start.1 = (bf16[3,8,4,128,128]{4,3,1,2,0:T(8,128)(2,1)S(1)}, bf16[3,8,4,128,128]{4,3,1,2,0:T(8,128)(2,1)}, u32[]{:S(2)}) copy-start(bf16[3,8,4,128,128]{4,3,1,2,0:T(8,128)(2,1)} %copy-done) | copy-start | bytes 9437188
  109.3 1.0 copy-start.13
  109.3 1.0 collective-permute-start
  112.0 1.0 copy-start.15
  112.0 1.0 collective-permute-start.1
  113.0 1.4 copy-start.4
  115.6 21.7 %collective-permute-start.2 = (bf16[4,8,128,128]{3,2,1,0:T(8,128)(2,1)}, bf16[4,8,128,128]{3,2,1,0:T(8,128)(2,1)}, u32[]{:S(2)}, u32[]{:S(2)}) collective-permute-start(bf16[4,8,128,128]{3,2,1,0:T(8,128)(2,1)} %add_convert_fusion.1), channel_id=1, source_target_pairs={{8,0},{9,1},{10,2},{11,3},{12,4},{13,5},{14,6},{15,7}} | collective-permute-start | bytes 3145736 | tf_op jit(solution)/shard_map/ppermute | solution.py:134
  139.3 1.2 copy-start.5
  139.3 1.5 copy-start.14
  139.3 1.8 copy-start.16
  139.6 2.7 %copy-start.2 = (bf16[3,8,4,128,128]{4,3,1,2,0:T(8,128)(2,1)S(1)}, bf16[3,8,4,128,128]{4,3,1,2,0:T(8,128)(2,1)}, u32[]{:S(2)}) copy-start(bf16[3,8,4,128,128]{4,3,1,2,0:T(8,128)(2,1)} %copy-done) | copy-start | bytes 9437188
  145.8 2.2 copy-start.12
  149.5 1.3 copy-start.17
  151.2 4.7 %copy-start.7 = (bf16[4,8,128,128]{3,2,1,0:T(8,128)(2,1)S(1)}, bf16[4,8,128,128]{3,2,1,0:T(8,128)(2,1)}, u32[]{:S(2)}) copy-start(bf16[4,8,128,128]{3,2,1,0:T(8,128)(2,1)} %copy-done.6) | copy-start | bytes 3145732
  151.2 4.7 %copy-start.9 = (bf16[4,8,128,128]{3,2,1,0:T(8,128)(2,1)S(1)}, bf16[4,8,128,128]{3,2,1,0:T(8,128)(2,1)}, u32[]{:S(2)}) copy-start(bf16[4,8,128,128]{3,2,1,0:T(8,128)(2,1)} %copy-done.8) | copy-start | bytes 3145732
  152.2 18.8 %all-to-all-start.3 = ((f32[1024,1,128]{2,1,0:T(1,128)}), f32[1024,1,128]{2,1,0:T(1,128)S(1)}, u32[]{:S(2)}, u32[]{:S(2)}) async-start(f32[1024,1,128]{2,1,0:T(1,128)} %bitcast.32), calls=%async_computation.3 | async-start | bytes 1048576 | tf_op jit(solution)/shard_map/all_to_all | solution.py:161
  158.2 1.2 copy-start.10
  171.0 52.1 %all-to-all-start.2 = ((bf16[2,4,1024,128]{3,1,0,2:T(4,128)(2,1)}), bf16[2,4,1024,128]{3,1,0,2:T(4,128)(2,1)S(1)}, u32[]{:S(2)}, u32[]{:S(2)}) async-start(bf16[2,4,1024,128]{3,1,0,2:T(4,128)(2,1)} %pad_maximum_fusion.5), calls=%async_computation.2 | async-start | bytes 4194304 | tf_op jit(solution)/shard_map/all_to_all | solution.py:155

commit v3 on v2

--- a/solution.py
+++ b/solution.py
@@ -106,11 +106,12 @@
     def head_major(rows):
         return jnp.transpose(rows.reshape(tok_rows, head_count, DH), (1, 0, 2))
 
-    stacked = jnp.stack([head_major(queries[0]), head_major(inputs[0]), head_major(cotangent)])
+    stacked = jnp.stack([head_major(queries[0]), head_major(cotangent)])
     stacked_heads = lax.all_to_all(stacked, "seq", split_axis=1, concat_axis=2, tiled=True)
     query_blocks = to_blocks(stacked_heads[0])
-    values_both = key_pair(to_blocks(stacked_heads[1]))
-    cot_blocks = to_blocks(stacked_heads[2])
+    cot_blocks = to_blocks(stacked_heads[1])
+    input_heads = lax.all_to_all(head_major(inputs[0]), "seq", split_axis=0, concat_axis=1, tiled=True)
+    values_both = key_pair(to_blocks(input_heads))
     kv_pick = (jnp.arange(seq_ways) * local_heads) // group_size
     key_rows = jnp.transpose(key_heads[0].reshape(tok_rows, kv_count, DH), (1, 0, 2))[kv_pick]
     key_flat = lax.all_to_all(key_rows, "seq", split_axis=0, concat_axis=1, tiled=True)
@@ -141,6 +142,10 @@
 
     held_in = by_section(grad_ins)
     held_out = by_section(grad_outs)
+    grad_out = lax.all_to_all(
+        held_out.reshape(local_heads, seq_len, DH), "seq", split_axis=1, concat_axis=0, tiled=True
+    )
+    grad_rows = jnp.transpose(grad_out, (1, 0, 2)).reshape(tok_rows, full_width)
     grad_query, grad_key = weight_grads(
         softmax_probs,
         probs_low,
@@ -151,9 +156,10 @@
         score_scale,
         BLK,
     )
-    pair = jnp.stack([grad_query, held_out]).reshape(2, local_heads, seq_len, DH)
-    pair_out = lax.all_to_all(pair, "seq", split_axis=2, concat_axis=1, tiled=True)
-    pair_rows = jnp.transpose(pair_out, (0, 2, 1, 3)).reshape(2, tok_rows, full_width)
+    query_out = lax.all_to_all(
+        grad_query.reshape(local_heads, seq_len, DH), "seq", split_axis=1, concat_axis=0, tiled=True
+    )
+    query_rows = jnp.transpose(query_out, (1, 0, 2)).reshape(tok_rows, full_width)
     if local_heads == 1:
         key_part = grad_key.reshape(seq_len, DH)
     else:
@@ -163,7 +169,7 @@
         key_out.reshape(tok_rows, kv_count, seq_ways // kv_count, DH).astype(jnp.float32), axis=2
     )
     key_final = key_sum.astype(jnp.bfloat16).reshape(tok_rows, kv_count * DH)
-    return (pair_rows[0][None], key_final[None], pair_rows[1][None])
+    return (query_rows[None], key_final[None], grad_rows[None])
 
 
 def solution(mesh):

time: 229 us -> 224 us (0.978)
  the two profiles are of different devices: /device:TPU:0 before, /device:TPU:15 now
where the time goes in v3:
time: 224 us; the launch traced here: 220 us
  waiting for transfers between devices  116 us (52%)
  starting transfers between devices  43.9 us (20%)
  local copies, waits for them, and re-layouts  34 us (15%)
  other arithmetic  13.1 us (6%)
  matrix products  11.6 us (5%)
    all_to_all x1, waiting for transfers between devices, on_device(): lax.all_to_all(stacked, 'seq', split_axis=1, concat_axis=2, tiled=True)  45.3 us
    all_to_all x1, waiting for transfers between devices, on_device(): lax.all_to_all(grad_query.reshape(local_heads, seq_len, DH), 'seq', split...  21.5 us
    all_to_all x1, waiting for transfers between devices, on_device(): lax.all_to_all(held_out.reshape(local_heads, seq_len, DH), 'seq', split_a...  20.1 us
    unnamed x43, local copies, waits for them, and re-layouts  17.2 us
    all_to_all x1, waiting for transfers between devices, on_device(): lax.all_to_all(head_major(inputs[0]), 'seq', split_axis=0, concat_axis=1,...  16.4 us
    all_to_all x1, waiting for transfers between devices, on_device(): lax.all_to_all(key_part[:, None, :], 'seq', split_axis=0, concat_axis=1,...  7.79 us
    all_to_all x1, starting transfers between devices, on_device(): lax.all_to_all(head_major(inputs[0]), 'seq', split_axis=0, concat_axis=1,...  7.11 us
    all_to_all x1, starting transfers between devices, on_device(): lax.all_to_all(key_part[:, None, :], 'seq', split_axis=0, concat_axis=1,...  6.43 us
  transfers between devices with their start and end apart: 9, of which 7 were waited for; matrix products, arithmetic and copies ran while one was open for 10% of the time, Pallas kernels for 0%

profile of v3, /device:TPU:15, one launch (start us, length us, event | category | flops | bytes accessed | tf_op | source)
XLA Modules:
  0.0 219.9 jit_solution(1724287712987087750)
XLA Ops:
  3.3 5.7 %all-to-all-start.1 = ((bf16[8,128,128]{2,1,0:T(8,128)(2,1)}), bf16[8,128,128]{2,1,0:T(8,128)(2,1)S(1)}, u32[]{:S(2)}, u32[]{:S(2)}) async-start(bf16[8,128,128]{2,1,0:T(8,128)(2,1)} %gather_fusion), calls=%async_computation.1 | async-start | bytes 524288 | tf_op jit(solution)/shard_map/all_to_all | solution.py:117
  10.5 1.5 copy.140
  12.0 3.0 %all-to-all-done.1 = bf16[8,128,128]{2,1,0:T(8,128)(2,1)S(1)} async-done(((bf16[8,128,128]{2,1,0:T(8,128)(2,1)}), bf16[8,128,128]{2,1,0:T(8,128)(2,1)S(1)}, u32[]{:S(2)}, u32[]{:S(2)}) %all-to-all-start.1) | async-done | bytes 262176 | tf_op jit(solution)/shard_map/all_to_all | solution.py:117
  14.9 6.2 %all-to-all-start = ((bf16[2,32,128,128]{2,3,0,1:T(8,128)(2,1)}), bf16[2,32,128,128]{2,3,0,1:T(8,128)(2,1)S(1)}, u32[]{:S(2)}, u32[]{:S(2)}) async-start(bf16[2,32,128,128]{2,3,0,1:T(8,128)(2,1)} %copy.140), calls=%async_computation | async-start | bytes 4194304 | tf_op jit(solution)/shard_map/all_to_all | solution.py:110
  21.5 45.3 %all-to-all-done = bf16[2,32,128,128]{2,3,0,1:T(8,128)(2,1)S(1)} async-done(((bf16[2,32,128,128]{2,3,0,1:T(8,128)(2,1)}), bf16[2,32,128,128]{2,3,0,1:T(8,128)(2,1)S(1)}, u32[]{:S(2)}, u32[]{:S(2)}) %all-to-all-start) | async-done | bytes 2097184 | tf_op jit(solution)/shard_map/all_to_all | solution.py:110
  66.8 1.3 copy-done.3
  68.2 3.0 %copy.142 = bf16[2,8,4,128,128]{4,3,1,2,0:T(8,128)(2,1)S(1)} copy(bf16[2,8,4,128,128]{3,4,0,2,1:T(8,128)(2,1)} %bitcast.87) | data formatting | bytes 4194304 | tf_op jit(solution)/shard_map/all_to_all | solution.py:110
  74.4 2.2 %fusion.33 = (f32[4,8,128]{2,1,0:T(8,128)S(1)}, f32[4,8,128,256]{3,2,1,0:T(8,128)S(1)}) fusion(f32[4,8,128,256]{3,2,1,0:T(8,128)S(1)} %fusion.3, pred[8,128,256]{2,1,0:T(8,128)(4,1)S(1)} %fusion.15), kind=kOutput, calls=%fused_computation.79 | output fusion | flops 6291711 | bytes 8667136 | tf_op jit(solution)/shard_map/sub | solution.py:53
  77.4 1.4 copy-done.9
  81.4 2.5 %collective-permute-start = (bf16[4,8,128,128]{3,2,1,0:T(8,128)(2,1)S(1)}, bf16[4,8,128,128]{3,2,1,0:T(8,128)(2,1)S(1)}, u32[]{:S(2)}, u32[]{:S(2)}) collective-permute-start(bf16[4,8,128,128]{3,2,1,0:T(8,128)(2,1)S(1)} %add_convert_fusion.3), channel_id=1, source_target_pairs={{24,16},{25,17},{26,18},{27,19},{28,20},{29,21},{30,22},{31,23}} | collective-permute-start | bytes 3145736 | tf_op jit(solution)/shard_map/ppermute | solution.py:135
  83.8 2.2 collective-permute-done
  88.7 1.7 collective-permute-start.1
  90.4 2.3 %copy.148 = bf16[1,128,4096]{1,2,0:T(8,128)(2,1)} copy(bf16[1,128,4096]{2,1,0:T(8,128)(2,1)} %param.17) | data formatting | bytes 2097152 | tf_op args[2]
  92.6 7.1 %all-to-all-start.2 = ((bf16[32,128,128]{1,2,0:T(8,128)(2,1)}), bf16[32,128,128]{1,2,0:T(8,128)(2,1)}, u32[]{:S(2)}, u32[]{:S(2)}) async-start(bf16[32,128,128]{1,2,0:T(8,128)(2,1)} %bitcast.89), calls=%async_computation.2 | async-start | bytes 2097152 | tf_op jit(solution)/shard_map/all_to_all | solution.py:113
  99.8 2.0 fusion.35
  102.3 2.6 %add_convert_fusion.1 = bf16[4,8,128,128]{3,2,1,0:T(8,128)(2,1)} fusion(f32[4,8,128,128]{3,2,1,0:T(8,128)S(1)} %fusion.22, bf16[4,8,128,128]{3,2,1,0:T(8,128)(2,1)} %collective-permute-done.1), kind=kLoop, calls=%fused_computation.22 | loop fusion | flops 1572864 | bytes 4194304 | tf_op jit(solution)/shard_map/convert_element_type | solution.py:61
  104.9 1.6 collective-permute-start.2
  106.5 16.4 %all-to-all-done.2 = bf16[32,128,128]{1,2,0:T(8,128)(2,1)} async-done(((bf16[32,128,128]{1,2,0:T(8,128)(2,1)}), bf16[32,128,128]{1,2,0:T(8,128)(2,1)}, u32[]{:S(2)}, u32[]{:S(2)}) %all-to-all-start.2) | async-done | bytes 1048608 | tf_op jit(solution)/shard_map/all_to_all | solution.py:113
  122.9 2.3 %copy.150 = bf16[8,4,128,128]{3,2,0,1:T(8,128)(2,1)} copy(bf16[8,4,128,128]{2,3,1,0:T(8,128)(2,1)} %bitcast.20) | data formatting | bytes 2097152 | tf_op jit(solution)/shard_map/all_to_all | solution.py:113
  126.1 2.0 fusion.36
  130.2 3.2 %fusion.9 = (bf16[4,8,128,128]{3,2,1,0:T(8,128)(2,1)}, bf16[4,8,128,128]{3,2,1,0:T(8,128)(2,1)S(1)}) fusion(f32[4,8,128,128]{3,2,1,0:T(8,128)S(1)} %fusion.20, bf16[4,8,128,128]{3,2,1,0:T(8,128)(2,1)} %collective-permute-done.2, bf16[4,8,128,128]{3,2,1,0:T(8,128)(2,1)} %add_convert_fusion.1, bf16[4,8,128,128]{3,2,1,0:T(8,128)(2,1)} %add_convert_fusion.2, ...), kind=kLoop, calls=%fused_computation.34 | loop fusion | flops 4718592 | bytes 11534339 | tf_op jit(solution)/shard_map/jit(_where)/select_n | solution.py:140
  134.5 1.4 copy-done.10
  135.9 1.6 multiply_convert_fusion
  140.2 6.4 %all-to-all-start.4 = ((f32[1024,1,128]{2,1,0:T(1,128)}), f32[1024,1,128]{2,1,0:T(1,128)S(1)}, u32[]{:S(2)}, u32[]{:S(2)}) async-start(f32[1024,1,128]{2,1,0:T(1,128)} %bitcast.30), calls=%async_computation.4 | async-start | bytes 1048576 | tf_op jit(solution)/shard_map/all_to_all | solution.py:167
  146.6 2.3 %multiply_convert_fusion.2 = bf16[4,8,128,128]{3,2,1,0:T(8,128)(2,1)S(1)} fusion(bf16[4,8,128,256]{3,2,1,0:T(8,128)(2,1)} %copy-done.13, bf16[4,8,128,128]{3,2,1,0:T(8,128)(2,1)S(1)} %copy-done.5, bf16[4,8,128,128]{3,2,1,0:T(8,128)(2,1)S(1)} %copy-done.7), kind=kOutput, calls=%fused_computation.20 | convolution fusion | flops 273678336 | bytes 5242880 | tf_op jit(solution)/shard_map/hbij,hbjd->hbid/dot_general | solution.py:78
  148.9 1.8 copy.153
  150.7 7.8 %all-to-all-done.4 = f32[1024,1,128]{2,1,0:T(1,128)S(1)} async-done(((f32[1024,1,128]{2,1,0:T(1,128)}), f32[1024,1,128]{2,1,0:T(1,128)S(1)}, u32[]{:S(2)}, u32[]{:S(2)}) %all-to-all-start.4) | async-done | bytes 524320 | tf_op jit(solution)/shard_map/all_to_all | solution.py:167
  158.5 6.3 %all-to-all-start.3 = ((bf16[4,1024,128]{2,0,1:T(4,128)(2,1)}), bf16[4,1024,128]{2,0,1:T(4,128)(2,1)S(1)}, u32[]{:S(2)}, u32[]{:S(2)}) async-start(bf16[4,1024,128]{2,0,1:T(4,128)(2,1)} %copy.153), calls=%async_computation.3 | async-start | bytes 2097152 | tf_op jit(solution)/shard_map/all_to_all | solution.py:159
  164.8 1.8 copy.160
  166.6 21.5 %all-to-all-done.3 = bf16[4,1024,128]{2,0,1:T(4,128)(2,1)S(1)} async-done(((bf16[4,1024,128]{2,0,1:T(4,128)(2,1)}), bf16[4,1024,128]{2,0,1:T(4,128)(2,1)S(1)}, u32[]{:S(2)}, u32[]{:S(2)}) %all-to-all-start.3) | async-done | bytes 1048608 | tf_op jit(solution)/shard_map/all_to_all | solution.py:159
  188.1 6.3 %all-to-all-start.5 = ((bf16[4,1024,128]{2,0,1:T(4,128)(2,1)}), bf16[4,1024,128]{2,0,1:T(4,128)(2,1)S(1)}, u32[]{:S(2)}, u32[]{:S(2)}) async-start(bf16[4,1024,128]{2,0,1:T(4,128)(2,1)} %copy.160), calls=%async_computation.5 | async-start | bytes 2097152 | tf_op jit(solution)/shard_map/all_to_all | solution.py:145
  197.6 20.1 %all-to-all-done.5 = bf16[4,1024,128]{2,0,1:T(4,128)(2,1)S(1)} async-done(((bf16[4,1024,128]{2,0,1:T(4,128)(2,1)}), bf16[4,1024,128]{2,0,1:T(4,128)(2,1)S(1)}, u32[]{:S(2)}, u32[]{:S(2)}) %all-to-all-start.5) | async-done | bytes 1048608 | tf_op jit(solution)/shard_map/all_to_all | solution.py:145
  (90 shorter events, 26.2 us)
Async XLA Ops:
  0.6 8.3 %copy-start.15 = (bf16[1,128,4096]{2,1,0:T(8,128)(2,1)S(1)}, bf16[1,128,4096]{2,1,0:T(8,128)(2,1)}, u32[]{:S(2)}) copy-start(bf16[1,128,4096]{2,1,0:T(8,128)(2,1)} %param.15) | copy-start | bytes 3145732
  0.6 9.0 %copy-start.16 = (bf16[128,4096]{1,0:T(8,128)(2,1)S(1)}, bf16[128,4096]{1,0:T(8,128)(2,1)}, u32[]{:S(2)}) copy-start(bf16[128,4096]{1,0:T(8,128)(2,1)} %param.18) | copy-start | bytes 3145732
  3.3 11.7 %all-to-all-start.1 = ((bf16[8,128,128]{2,1,0:T(8,128)(2,1)}), bf16[8,128,128]{2,1,0:T(8,128)(2,1)S(1)}, u32[]{:S(2)}, u32[]{:S(2)}) async-start(bf16[8,128,128]{2,1,0:T(8,128)(2,1)} %gather_fusion), calls=%async_computation.1 | async-start | bytes 524288 | tf_op jit(solution)/shard_map/all_to_all | solution.py:117
  12.0 9.2 %copy-start.17 = (s32[8]{0:T(128)S(1)}, s32[8]{0:T(128)}, u32[]{:S(2)}) copy-start(s32[8]{0:T(128)} %param.19) | copy-start | bytes 100
  14.9 51.9 %all-to-all-start = ((bf16[2,32,128,128]{2,3,0,1:T(8,128)(2,1)}), bf16[2,32,128,128]{2,3,0,1:T(8,128)(2,1)S(1)}, u32[]{:S(2)}, u32[]{:S(2)}) async-start(bf16[2,32,128,128]{2,3,0,1:T(8,128)(2,1)} %copy.140), calls=%async_computation | async-start | bytes 4194304 | tf_op jit(solution)/shard_map/all_to_all | solution.py:110
  66.8 1.3 copy-start.3
  71.2 3.2 %copy-start = (bf16[2,8,4,128,128]{4,3,1,2,0:T(8,128)(2,1)}, bf16[2,8,4,128,128]{4,3,1,2,0:T(8,128)(2,1)S(1)}, u32[]{:S(2)}) copy-start(bf16[2,8,4,128,128]{4,3,1,2,0:T(8,128)(2,1)S(1)} %copy.142) | copy-start | bytes 6291460
  71.4 1.2 copy-start.6
  72.6 1.0 copy-start.4
  76.6 2.1 copy-start.9
  76.6 3.1 %copy-start.1 = (bf16[2,8,4,128,128]{4,3,1,2,0:T(8,128)(2,1)S(1)}, bf16[2,8,4,128,128]{4,3,1,2,0:T(8,128)(2,1)}, u32[]{:S(2)}) copy-start(bf16[2,8,4,128,128]{4,3,1,2,0:T(8,128)(2,1)} %copy-done) | copy-start | bytes 6291460
  81.3 2.5 %copy-start.11 = (bf16[4,8,128,128]{3,2,1,0:T(8,128)(2,1)}, bf16[4,8,128,128]{3,2,1,0:T(8,128)(2,1)S(1)}, u32[]{:S(2)}) copy-start(bf16[4,8,128,128]{3,2,1,0:T(8,128)(2,1)S(1)} %add_convert_fusion.3) | copy-start | bytes 3145732
  81.4 4.7 %collective-permute-start = (bf16[4,8,128,128]{3,2,1,0:T(8,128)(2,1)S(1)}, bf16[4,8,128,128]{3,2,1,0:T(8,128)(2,1)S(1)}, u32[]{:S(2)}, u32[]{:S(2)}) collective-permute-start(bf16[4,8,128,128]{3,2,1,0:T(8,128)(2,1)S(1)} %add_convert_fusion.3), channel_id=1, source_target_pairs={{24,16},{25,17},{26,18},{27,19},{28,20},{29,21},{30,22},{31,23}} | collective-permute-start | bytes 3145736 | tf_op jit(solution)/shard_map/ppermute | solution.py:135
  88.7 11.1 %collective-permute-start.1 = (bf16[4,8,128,128]{3,2,1,0:T(8,128)(2,1)}, bf16[4,8,128,128]{3,2,1,0:T(8,128)(2,1)}, u32[]{:S(2)}, u32[]{:S(2)}) collective-permute-start(bf16[4,8,128,128]{3,2,1,0:T(8,128)(2,1)} %add_convert_fusion.2), channel_id=1, source_target_pairs={{16,8},{17,9},{18,10},{19,11},{20,12},{21,13},{22,14},{23,15}} | collective-permute-start | bytes 3145736 | tf_op jit(solution)/shard_map/ppermute | solution.py:135
  92.6 30.3 %all-to-all-start.2 = ((bf16[32,128,128]{1,2,0:T(8,128)(2,1)}), bf16[32,128,128]{1,2,0:T(8,128)(2,1)}, u32[]{:S(2)}, u32[]{:S(2)}) async-start(bf16[32,128,128]{1,2,0:T(8,128)(2,1)} %bitcast.89), calls=%async_computation.2 | async-start | bytes 2097152 | tf_op jit(solution)/shard_map/all_to_all | solution.py:113
  104.9 21.2 %collective-permute-start.2 = (bf16[4,8,128,128]{3,2,1,0:T(8,128)(2,1)}, bf16[4,8,128,128]{3,2,1,0:T(8,128)(2,1)}, u32[]{:S(2)}, u32[]{:S(2)}) collective-permute-start(bf16[4,8,128,128]{3,2,1,0:T(8,128)(2,1)} %add_convert_fusion.1), channel_id=1, source_target_pairs={{8,0},{9,1},{10,2},{11,3},{12,4},{13,5},{14,6},{15,7}} | collective-permute-start | bytes 3145736 | tf_op jit(solution)/shard_map/ppermute | solution.py:135
  128.4 1.6 copy-start.2
  128.4 1.9 copy-start.12
  130.2 3.5 %copy-start.14 = (bf16[8,4,128,128]{3,2,0,1:T(8,128)(2,1)S(1)}, bf16[8,4,128,128]{3,2,0,1:T(8,128)(2,1)}, u32[]{:S(2)}) copy-start(bf16[8,4,128,128]{3,2,0,1:T(8,128)(2,1)} %copy.150) | copy-start | bytes 3145732
  133.7 2.2 copy-start.10
  137.4 1.3 copy-start.13
  139.1 7.5 %copy-start.5 = (bf16[4,8,128,128]{3,2,1,0:T(8,128)(2,1)S(1)}, bf16[4,8,128,128]{3,2,1,0:T(8,128)(2,1)}, u32[]{:S(2)}) copy-start(bf16[4,8,128,128]{3,2,1,0:T(8,128)(2,1)} %copy-done.4) | copy-start | bytes 3145732
  139.1 7.5 %copy-start.7 = (bf16[4,8,128,128]{3,2,1,0:T(8,128)(2,1)S(1)}, bf16[4,8,128,128]{3,2,1,0:T(8,128)(2,1)}, u32[]{:S(2)}) copy-start(bf16[4,8,128,128]{3,2,1,0:T(8,128)(2,1)} %copy-done.6) | copy-start | bytes 3145732
  140.2 18.3 %all-to-all-start.4 = ((f32[1024,1,128]{2,1,0:T(1,128)}), f32[1024,1,128]{2,1,0:T(1,128)S(1)}, u32[]{:S(2)}, u32[]{:S(2)}) async-start(f32[1024,1,128]{2,1,0:T(1,128)} %bitcast.30), calls=%async_computation.4 | async-start | bytes 1048576 | tf_op jit(solution)/shard_map/all_to_all | solution.py:167
  148.9 15.9 %copy-start.8 = (bf16[4,8,128,128]{3,2,1,0:T(8,128)(2,1)S(1)}, bf16[4,8,128,128]{3,2,1,0:T(8,128)(2,1)}, u32[]{:S(2)}) copy-start(bf16[4,8,128,128]{3,2,1,0:T(8,128)(2,1)} %get-tuple-element.74) | copy-start | bytes 3145732
  158.5 29.6 %all-to-all-start.3 = ((bf16[4,1024,128]{2,0,1:T(4,128)(2,1)}), bf16[4,1024,128]{2,0,1:T(4,128)(2,1)S(1)}, u32[]{:S(2)}, u32[]{:S(2)}) async-start(bf16[4,1024,128]{2,0,1:T(4,128)(2,1)} %copy.153), calls=%async_computation.3 | async-start | bytes 2097152 | tf_op jit(solution)/shard_map/all_to_all | solution.py:159
  188.1 29.6 %all-to-all-start.5 = ((bf16[4,1024,128]{2,0,1:T(4,128)(2,1)}), bf16[4,1024,128]{2,0,1:T(4,128)(2,1)S(1)}, u32[]{:S(2)}, u32[]{:S(2)}) async-start(bf16[4,1024,128]{2,0,1:T(4,128)(2,1)} %copy.160), calls=%async_computation.5 | async-start | bytes 2097152 | tf_op jit(solution)/shard_map/all_to_all | solution.py:145

commit v4 on v2

--- a/solution.py
+++ b/solution.py
@@ -100,17 +100,42 @@
     score_scale = DH ** (-0.5)
     last_section = section_count - 1
 
+    seq_index = lax.axis_index("seq")
+
+    def transpose_seq(value, split_axis, concat_axis):
+        if seq_ways > 8:
+            return lax.all_to_all(value, "seq", split_axis, concat_axis, tiled=True)
+        split_size = value.shape[split_axis] // seq_ways
+        concat_size = value.shape[concat_axis]
+        out_shape = list(value.shape)
+        out_shape[split_axis] = split_size
+        out_shape[concat_axis] = concat_size * seq_ways
+        result = jnp.zeros(out_shape, value.dtype)
+        for shift in range(seq_ways):
+            target = (seq_index + shift) % seq_ways
+            chunk = lax.dynamic_slice_in_dim(value, target * split_size, split_size, axis=split_axis)
+            if shift > 0:
+                chunk = lax.ppermute(
+                    chunk, "seq", [(s, (s + shift) % seq_ways) for s in range(seq_ways)]
+                )
+            source = (seq_index + seq_ways - shift) % seq_ways
+            result = lax.dynamic_update_slice_in_dim(
+                result, chunk, source * concat_size, axis=concat_axis
+            )
+        return result
+
     def to_blocks(head_rows):
         return head_rows.reshape(local_heads, block_count, BLK, DH)
 
     def head_major(rows):
         return jnp.transpose(rows.reshape(tok_rows, head_count, DH), (1, 0, 2))
 
-    stacked = jnp.stack([head_major(queries[0]), head_major(inputs[0]), head_major(cotangent)])
-    stacked_heads = lax.all_to_all(stacked, "seq", split_axis=1, concat_axis=2, tiled=True)
+    stacked = jnp.stack([head_major(queries[0]), head_major(cotangent)])
+    stacked_heads = transpose_seq(stacked, 1, 2)
     query_blocks = to_blocks(stacked_heads[0])
-    values_both = key_pair(to_blocks(stacked_heads[1]))
-    cot_blocks = to_blocks(stacked_heads[2])
+    cot_blocks = to_blocks(stacked_heads[1])
+    input_heads = lax.all_to_all(head_major(inputs[0]), "seq", split_axis=0, concat_axis=1, tiled=True)
+    values_both = key_pair(to_blocks(input_heads))
     kv_pick = (jnp.arange(seq_ways) * local_heads) // group_size
     key_rows = jnp.transpose(key_heads[0].reshape(tok_rows, kv_count, DH), (1, 0, 2))[kv_pick]
     key_flat = lax.all_to_all(key_rows, "seq", split_axis=0, concat_axis=1, tiled=True)
@@ -152,7 +177,7 @@
         BLK,
     )
     pair = jnp.stack([grad_query, held_out]).reshape(2, local_heads, seq_len, DH)
-    pair_out = lax.all_to_all(pair, "seq", split_axis=2, concat_axis=1, tiled=True)
+    pair_out = transpose_seq(pair, 2, 1)
     pair_rows = jnp.transpose(pair_out, (0, 2, 1, 3)).reshape(2, tok_rows, full_width)
     if local_heads == 1:
         key_part = grad_key.reshape(seq_len, DH)

time: 229 us -> 202 us (0.88)
  the two profiles are of different devices: /device:TPU:0 before, /device:TPU:26 now
where the time goes in v4:
time: 202 us; the launch traced here: 201 us
  starting transfers between devices  82.3 us (41%)
  waiting for transfers between devices  59.1 us (29%)
  local copies, waits for them, and re-layouts  33.8 us (17%)
  other arithmetic  14.8 us (7%)
  matrix products  10 us (5%)
    ppermute x14, starting transfers between devices, transpose_seq(): lax.ppermute(chunk, 'seq', [(s, (s + shift) % seq_ways) for s in range(se...  55.4 us
    ppermute x14, waiting for transfers between devices, transpose_seq(): lax.ppermute(chunk, 'seq', [(s, (s + shift) % seq_ways) for s in range(se...  37.6 us
    all_to_all x1, waiting for transfers between devices, on_device(): lax.all_to_all(head_major(inputs[0]), 'seq', split_axis=0, concat_axis=1,...  15.5 us
    unnamed x40, local copies, waits for them, and re-layouts  10.2 us
    dynamic_update_slice x15, local copies, waits for them, and re-layouts, transpose_seq(): lax.dynamic_update_slice_in_dim(result, chunk, source * concat_size, axis...  9.5 us
    all_to_all x1, starting transfers between devices, on_device(): lax.all_to_all(head_major(inputs[0]), 'seq', split_axis=0, concat_axis=1,...  8.63 us
    all_to_all x1, starting transfers between devices, on_device(): lax.all_to_all(key_part[:, None, :], 'seq', split_axis=0, concat_axis=1,...  7.13 us
    all_to_all x1, starting transfers between devices, on_device(): lax.all_to_all(key_rows, 'seq', split_axis=0, concat_axis=1, tiled=True)  5.82 us
  transfers between devices with their start and end apart: 20, of which 8 were waited for; matrix products, arithmetic and copies ran while one was open for 13% of the time, Pallas kernels for 0%

profile of v4, /device:TPU:26, one launch (start us, length us, event | category | flops | bytes accessed | tf_op | source)
XLA Modules:
  0.0 201.4 jit_solution(15154725630672977667)
XLA Ops:
  3.0 1.6 broadcast_in_dim.43
  5.9 1.5 collective-permute-start
  7.6 2.5 %collective-permute-start.2 = (bf16[2,4,128,128]{3,2,1,0:T(8,128)(2,1)}, bf16[2,4,128,128]{3,2,1,0:T(8,128)(2,1)S(1)}, u32[]{:S(2)}, u32[]{:S(2)}) collective-permute-start(bf16[2,4,128,128]{3,2,1,0:T(8,128)(2,1)} %get-tuple-element.84), channel_id=1, source_target_pairs={{0,3},{1,4},{2,5},{3,6},{4,7},{5,0},{6,1},{7,2},{8,11},{9,12},{10,... | collective-permute-start | bytes 786440 | tf_op jit(solution)/shard_map/ppermute | solution.py:118
  10.7 2.6 %collective-permute-start.4 = (bf16[2,4,128,128]{3,2,1,0:T(8,128)(2,1)S(1)}, bf16[2,4,128,128]{3,2,1,0:T(8,128)(2,1)S(1)}, u32[]{:S(2)}, u32[]{:S(2)}) collective-permute-start(bf16[2,4,128,128]{3,2,1,0:T(8,128)(2,1)S(1)} %get-tuple-element.87), channel_id=1, source_target_pairs={{0,5},{1,6},{2,7},{3,0},{4,1},{5,2},{6,3},{7,4},{8,13},{9,14},{10,... | collective-permute-start | bytes 786440 | tf_op jit(solution)/shard_map/ppermute | solution.py:118
  14.9 5.8 %all-to-all-start = ((bf16[8,128,128]{2,1,0:T(8,128)(2,1)}), bf16[8,128,128]{2,1,0:T(8,128)(2,1)S(1)}, u32[]{:S(2)}, u32[]{:S(2)}) async-start(bf16[8,128,128]{2,1,0:T(8,128)(2,1)} %gather_fusion), calls=%async_computation | async-start | bytes 524288 | tf_op jit(solution)/shard_map/all_to_all | solution.py:141
  21.8 1.7 constant_dynamic-update-slice_fusion.6
  23.5 18.8 %collective-permute-start.6 = (bf16[2,4,128,128]{3,2,1,0:T(8,128)(2,1)S(1)}, bf16[2,4,128,128]{3,2,1,0:T(8,128)(2,1)S(1)}, u32[]{:S(2)}, u32[]{:S(2)}) collective-permute-start(bf16[2,4,128,128]{3,2,1,0:T(8,128)(2,1)S(1)} %copy-done.15), channel_id=1, source_target_pairs={{0,7},{1,0},{2,1},{3,2},{4,3},{5,4},{6,5},{7,6},{8,15},{9,8},{10,9... | collective-permute-start | bytes 786440 | tf_op jit(solution)/shard_map/ppermute | solution.py:118
  42.3 1.7 constant_dynamic-update-slice_fusion.5
  44.0 8.6 %collective-permute-done.2 = bf16[2,4,128,128]{3,2,1,0:T(8,128)(2,1)S(1)} collective-permute-done((bf16[2,4,128,128]{3,2,1,0:T(8,128)(2,1)}, bf16[2,4,128,128]{3,2,1,0:T(8,128)(2,1)S(1)}, u32[]{:S(2)}, u32[]{:S(2)}) %collective-permute-start.2) | collective-permute-done | bytes 262176 | tf_op jit(solution)/shard_map/ppermute | solution.py:118
  56.4 1.7 fusion.49
  58.1 2.2 %all-to-all-done = bf16[8,128,128]{2,1,0:T(8,128)(2,1)S(1)} async-done(((bf16[8,128,128]{2,1,0:T(8,128)(2,1)}), bf16[8,128,128]{2,1,0:T(8,128)(2,1)S(1)}, u32[]{:S(2)}, u32[]{:S(2)}) %all-to-all-start) | async-done | bytes 262176 | tf_op jit(solution)/shard_map/all_to_all | solution.py:141
  62.4 2.2 %fusion.50 = (f32[4,8,128]{2,1,0:T(8,128)S(1)}, f32[4,8,128,256]{3,2,1,0:T(8,128)S(1)}) fusion(f32[4,8,128,256]{3,2,1,0:T(8,128)S(1)} %fusion.3, pred[8,128,256]{2,1,0:T(8,128)(4,1)S(1)} %fusion.15), kind=kOutput, calls=%fused_computation.142 | output fusion | flops 6291711 | bytes 8667136 | tf_op jit(solution)/shard_map/sub | solution.py:53
  69.6 3.2 %collective-permute-done.7 = bf16[4,8,128,128]{3,2,1,0:T(8,128)(2,1)S(1)} collective-permute-done((bf16[4,8,128,128]{3,2,1,0:T(8,128)(2,1)S(1)}, bf16[4,8,128,128]{3,2,1,0:T(8,128)(2,1)S(1)}, u32[]{:S(2)}, u32[]{:S(2)}) %collective-permute-start.7) | collective-permute-done | bytes 1048608 | tf_op jit(solution)/shard_map/ppermute | solution.py:159
  75.5 2.4 %collective-permute-start.8 = (bf16[4,8,128,128]{3,2,1,0:T(8,128)(2,1)}, bf16[4,8,128,128]{3,2,1,0:T(8,128)(2,1)}, u32[]{:S(2)}, u32[]{:S(2)}) collective-permute-start(bf16[4,8,128,128]{3,2,1,0:T(8,128)(2,1)} %add_convert_fusion.2), channel_id=1, source_target_pairs={{16,8},{17,9},{18,10},{19,11},{20,12},{21,13},{22,14},{23,15}} | collective-permute-start | bytes 3145736 | tf_op jit(solution)/shard_map/ppermute | solution.py:159
  77.9 2.3 %copy.116 = bf16[1,128,4096]{1,2,0:T(8,128)(2,1)} copy(bf16[1,128,4096]{2,1,0:T(8,128)(2,1)} %param.17) | data formatting | bytes 2097152 | tf_op args[2]
  80.2 8.6 %all-to-all-start.1 = ((bf16[32,128,128]{1,2,0:T(8,128)(2,1)}), bf16[32,128,128]{1,2,0:T(8,128)(2,1)}, u32[]{:S(2)}, u32[]{:S(2)}) async-start(bf16[32,128,128]{1,2,0:T(8,128)(2,1)} %bitcast.82), calls=%async_computation.1 | async-start | bytes 2097152 | tf_op jit(solution)/shard_map/all_to_all | solution.py:137
  89.4 2.0 fusion.53
  92.0 2.6 %add_convert_fusion.1 = bf16[4,8,128,128]{3,2,1,0:T(8,128)(2,1)} fusion(f32[4,8,128,128]{3,2,1,0:T(8,128)S(1)} %fusion.37, bf16[4,8,128,128]{3,2,1,0:T(8,128)(2,1)} %collective-permute-done.8), kind=kLoop, calls=%fused_computation.53 | loop fusion | flops 1572864 | bytes 4194304 | tf_op jit(solution)/shard_map/convert_element_type | solution.py:61
  94.5 1.6 collective-permute-start.9
  96.2 15.5 %all-to-all-done.1 = bf16[32,128,128]{1,2,0:T(8,128)(2,1)} async-done(((bf16[32,128,128]{1,2,0:T(8,128)(2,1)}), bf16[32,128,128]{1,2,0:T(8,128)(2,1)}, u32[]{:S(2)}, u32[]{:S(2)}) %all-to-all-start.1) | async-done | bytes 1048608 | tf_op jit(solution)/shard_map/all_to_all | solution.py:137
  111.6 2.3 %copy.118 = bf16[8,4,128,128]{3,2,0,1:T(8,128)(2,1)} copy(bf16[8,4,128,128]{2,3,1,0:T(8,128)(2,1)} %bitcast.16) | data formatting | bytes 2097152 | tf_op jit(solution)/shard_map/all_to_all | solution.py:137
  114.9 2.0 fusion.54
  118.6 2.6 %fusion.9 = (bf16[4,8,128,128]{3,2,1,0:T(8,128)(2,1)S(1)}, bf16[4,8,128,128]{3,2,1,0:T(8,128)(2,1)S(1)}) fusion(f32[4,8,128,128]{3,2,1,0:T(8,128)S(1)} %fusion.36, bf16[4,8,128,128]{3,2,1,0:T(8,128)(2,1)} %collective-permute-done.9, bf16[4,8,128,128]{3,2,1,0:T(8,128)(2,1)} %add_convert_fusion.1, bf16[4,8,128,128]{3,2,1,0:T(8,128)(2,1)} %add_convert_fusion.2, ...), kind=kLoop, calls=%fused_computation.65 | loop fusion | flops 4718592 | bytes 11534339 | tf_op jit(solution)/shard_map/jit(_where)/select_n | solution.py:164
  123.6 1.6 multiply_convert_fusion
  128.9 1.8 collective-permute-start.10
  130.7 7.1 %all-to-all-start.2 = ((f32[1024,1,128]{2,1,0:T(1,128)}), f32[1024,1,128]{2,1,0:T(1,128)}, u32[]{:S(2)}, u32[]{:S(2)}) async-start(f32[1024,1,128]{2,1,0:T(1,128)} %bitcast.24), calls=%async_computation.2 | async-start | bytes 1048576 | tf_op jit(solution)/shard_map/all_to_all | solution.py:186
  139.3 2.4 %collective-permute-start.11 = (bf16[2,4,128,128]{3,2,1,0:T(8,128)(2,1)S(1)}, bf16[2,4,128,128]{3,2,1,0:T(8,128)(2,1)S(1)}, u32[]{:S(2)}, u32[]{:S(2)}) collective-permute-start(bf16[2,4,128,128]{3,2,1,0:T(8,128)(2,1)S(1)} %get-tuple-element.73), channel_id=1, source_target_pairs={{0,2},{1,3},{2,4},{3,5},{4,6},{5,7},{6,0},{7,1},{8,10},{9,11},{10,... | collective-permute-start | bytes 786440 | tf_op jit(solution)/shard_map/ppermute | solution.py:118
  143.4 1.9 collective-permute-start.15
  145.6 13.3 %collective-permute-done.11 = bf16[2,4,128,128]{3,2,1,0:T(8,128)(2,1)S(1)} collective-permute-done((bf16[2,4,128,128]{3,2,1,0:T(8,128)(2,1)S(1)}, bf16[2,4,128,128]{3,2,1,0:T(8,128)(2,1)S(1)}, u32[]{:S(2)}, u32[]{:S(2)}) %collective-permute-start.11) | collective-permute-done | bytes 262176 | tf_op jit(solution)/shard_map/ppermute | solution.py:118
  158.9 20.1 %collective-permute-start.16 = (bf16[2,4,128,128]{3,2,1,0:T(8,128)(2,1)S(1)}, bf16[2,4,128,128]{3,2,1,0:T(8,128)(2,1)S(1)}, u32[]{:S(2)}, u32[]{:S(2)}) collective-permute-start(bf16[2,4,128,128]{3,2,1,0:T(8,128)(2,1)S(1)} %get-tuple-element.70), channel_id=1, source_target_pairs={{0,7},{1,0},{2,1},{3,2},{4,3},{5,4},{6,5},{7,6},{8,15},{9,8},{10,9... | collective-permute-start | bytes 786440 | tf_op jit(solution)/shard_map/ppermute | solution.py:118
  179.3 4.8 %collective-permute-done.12 = bf16[2,4,128,128]{3,2,1,0:T(8,128)(2,1)S(1)} collective-permute-done((bf16[2,4,128,128]{3,2,1,0:T(8,128)(2,1)S(1)}, bf16[2,4,128,128]{3,2,1,0:T(8,128)(2,1)S(1)}, u32[]{:S(2)}, u32[]{:S(2)}) %collective-permute-start.12) | collective-permute-done | bytes 262176 | tf_op jit(solution)/shard_map/ppermute | solution.py:118
  184.3 10.9 %collective-permute-done.13 = bf16[2,4,128,128]{3,2,1,0:T(8,128)(2,1)S(1)} collective-permute-done((bf16[2,4,128,128]{3,2,1,0:T(8,128)(2,1)S(1)}, bf16[2,4,128,128]{3,2,1,0:T(8,128)(2,1)S(1)}, u32[]{:S(2)}, u32[]{:S(2)}) %collective-permute-start.13) | collective-permute-done | bytes 262176 | tf_op jit(solution)/shard_map/ppermute | solution.py:118
  (125 shorter events, 40.2 us)
Async XLA Ops:
  0.6 2.0 %copy-start = (bf16[128,4096]{1,0:T(8,128)(2,1)S(1)}, bf16[128,4096]{1,0:T(8,128)(2,1)}, u32[]{:S(2)}) copy-start(bf16[128,4096]{1,0:T(8,128)(2,1)} %param.18) | copy-start | bytes 3145732
  5.9 7.4 %copy-start.16 = (bf16[1,128,512]{2,1,0:T(8,128)(2,1)S(1)}, bf16[1,128,512]{2,1,0:T(8,128)(2,1)}, u32[]{:S(2)}) copy-start(bf16[1,128,512]{2,1,0:T(8,128)(2,1)} %param.16) | copy-start | bytes 393220
  5.9 15.3 %collective-permute-start = (bf16[2,4,128,128]{3,2,1,0:T(8,128)(2,1)}, bf16[2,4,128,128]{3,2,1,0:T(8,128)(2,1)}, u32[]{:S(2)}, u32[]{:S(2)}) collective-permute-start(bf16[2,4,128,128]{3,2,1,0:T(8,128)(2,1)} %get-tuple-element.82), channel_id=1, source_target_pairs={{0,1},{1,2},{2,3},{3,4},{4,5},{5,6},{6,7},{7,0},{8,9},{9,10},{10,1... | collective-permute-start | bytes 786440 | tf_op jit(solution)/shard_map/ppermute | solution.py:118
  7.4 16.1 %collective-permute-start.1 = (bf16[2,4,128,128]{3,2,1,0:T(8,128)(2,1)}, bf16[2,4,128,128]{3,2,1,0:T(8,128)(2,1)}, u32[]{:S(2)}, u32[]{:S(2)}) collective-permute-start(bf16[2,4,128,128]{3,2,1,0:T(8,128)(2,1)} %get-tuple-element.83), channel_id=1, source_target_pairs={{0,2},{1,3},{2,4},{3,5},{4,6},{5,7},{6,0},{7,1},{8,10},{9,11},{10,... | collective-permute-start | bytes 786440 | tf_op jit(solution)/shard_map/ppermute | solution.py:118
  7.6 45.0 %collective-permute-start.2 = (bf16[2,4,128,128]{3,2,1,0:T(8,128)(2,1)}, bf16[2,4,128,128]{3,2,1,0:T(8,128)(2,1)S(1)}, u32[]{:S(2)}, u32[]{:S(2)}) collective-permute-start(bf16[2,4,128,128]{3,2,1,0:T(8,128)(2,1)} %get-tuple-element.84), channel_id=1, source_target_pairs={{0,3},{1,4},{2,5},{3,6},{4,7},{5,0},{6,1},{7,2},{8,11},{9,12},{10,... | collective-permute-start | bytes 786440 | tf_op jit(solution)/shard_map/ppermute | solution.py:118
  10.2 10.6 %copy-start.17 = (s32[8]{0:T(128)S(1)}, s32[8]{0:T(128)}, u32[]{:S(2)}) copy-start(s32[8]{0:T(128)} %param.19) | copy-start | bytes 100
  10.2 13.2 %copy-start.15 = (bf16[2,4,128,128]{3,2,1,0:T(8,128)(2,1)S(1)}, bf16[2,4,128,128]{3,2,1,0:T(8,128)(2,1)}, u32[]{:S(2)}) copy-start(bf16[2,4,128,128]{3,2,1,0:T(8,128)(2,1)} %get-tuple-element.80) | copy-start | bytes 786436
  10.3 43.1 %collective-permute-start.3 = (bf16[2,4,128,128]{3,2,1,0:T(8,128)(2,1)S(1)}, bf16[2,4,128,128]{3,2,1,0:T(8,128)(2,1)S(1)}, u32[]{:S(2)}, u32[]{:S(2)}) collective-permute-start(bf16[2,4,128,128]{3,2,1,0:T(8,128)(2,1)S(1)} %get-tuple-element.86), channel_id=1, source_target_pairs={{0,4},{1,5},{2,6},{3,7},{4,0},{5,1},{6,2},{7,3},{8,12},{9,13},{10,... | collective-permute-start | bytes 786440 | tf_op jit(solution)/shard_map/ppermute | solution.py:118
  10.7 43.5 %collective-permute-start.4 = (bf16[2,4,128,128]{3,2,1,0:T(8,128)(2,1)S(1)}, bf16[2,4,128,128]{3,2,1,0:T(8,128)(2,1)S(1)}, u32[]{:S(2)}, u32[]{:S(2)}) collective-permute-start(bf16[2,4,128,128]{3,2,1,0:T(8,128)(2,1)S(1)} %get-tuple-element.87), channel_id=1, source_target_pairs={{0,5},{1,6},{2,7},{3,0},{4,1},{5,2},{6,3},{7,4},{8,13},{9,14},{10,... | collective-permute-start | bytes 786440 | tf_op jit(solution)/shard_map/ppermute | solution.py:118
  14.9 45.3 %all-to-all-start = ((bf16[8,128,128]{2,1,0:T(8,128)(2,1)}), bf16[8,128,128]{2,1,0:T(8,128)(2,1)S(1)}, u32[]{:S(2)}, u32[]{:S(2)}) async-start(bf16[8,128,128]{2,1,0:T(8,128)(2,1)} %gather_fusion), calls=%async_computation | async-start | bytes 524288 | tf_op jit(solution)/shard_map/all_to_all | solution.py:141
  21.2 33.7 %collective-permute-start.5 = (bf16[2,4,128,128]{3,2,1,0:T(8,128)(2,1)S(1)}, bf16[2,4,128,128]{3,2,1,0:T(8,128)(2,1)S(1)}, u32[]{:S(2)}, u32[]{:S(2)}) collective-permute-start(bf16[2,4,128,128]{3,2,1,0:T(8,128)(2,1)S(1)} %get-tuple-element.85), channel_id=1, source_target_pairs={{0,6},{1,7},{2,0},{3,1},{4,2},{5,3},{6,4},{7,5},{8,14},{9,15},{10,... | collective-permute-start | bytes 786440 | tf_op jit(solution)/shard_map/ppermute | solution.py:118
  23.5 32.1 %collective-permute-start.6 = (bf16[2,4,128,128]{3,2,1,0:T(8,128)(2,1)S(1)}, bf16[2,4,128,128]{3,2,1,0:T(8,128)(2,1)S(1)}, u32[]{:S(2)}, u32[]{:S(2)}) collective-permute-start(bf16[2,4,128,128]{3,2,1,0:T(8,128)(2,1)S(1)} %copy-done.15), channel_id=1, source_target_pairs={{0,7},{1,0},{2,1},{3,2},{4,3},{5,4},{6,5},{7,6},{8,15},{9,8},{10,9... | collective-permute-start | bytes 786440 | tf_op jit(solution)/shard_map/ppermute | solution.py:118
  58.0 4.2 %copy-start.2 = (bf16[1,4,1024,128]{3,2,1,0:T(8,128)(2,1)}, bf16[1,4,1024,128]{3,2,1,0:T(8,128)(2,1)S(1)}, u32[]{:S(2)}) copy-start(bf16[1,4,1024,128]{3,2,1,0:T(8,128)(2,1)S(1)} %get-tuple-element.79) | copy-start | bytes 3145732
  64.7 1.9 copy-start.10
  68.3 4.6 %collective-permute-start.7 = (bf16[4,8,128,128]{3,2,1,0:T(8,128)(2,1)S(1)}, bf16[4,8,128,128]{3,2,1,0:T(8,128)(2,1)S(1)}, u32[]{:S(2)}, u32[]{:S(2)}) collective-permute-start(bf16[4,8,128,128]{3,2,1,0:T(8,128)(2,1)S(1)} %add_convert_fusion.3), channel_id=1, source_target_pairs={{24,16},{25,17},{26,18},{27,19},{28,20},{29,21},{30,22},{31,23}} | collective-permute-start | bytes 3145736 | tf_op jit(solution)/shard_map/ppermute | solution.py:159
  75.5 13.9 %collective-permute-start.8 = (bf16[4,8,128,128]{3,2,1,0:T(8,128)(2,1)}, bf16[4,8,128,128]{3,2,1,0:T(8,128)(2,1)}, u32[]{:S(2)}, u32[]{:S(2)}) collective-permute-start(bf16[4,8,128,128]{3,2,1,0:T(8,128)(2,1)} %add_convert_fusion.2), channel_id=1, source_target_pairs={{16,8},{17,9},{18,10},{19,11},{20,12},{21,13},{22,14},{23,15}} | collective-permute-start | bytes 3145736 | tf_op jit(solution)/shard_map/ppermute | solution.py:159
  80.2 31.5 %all-to-all-start.1 = ((bf16[32,128,128]{1,2,0:T(8,128)(2,1)}), bf16[32,128,128]{1,2,0:T(8,128)(2,1)}, u32[]{:S(2)}, u32[]{:S(2)}) async-start(bf16[32,128,128]{1,2,0:T(8,128)(2,1)} %bitcast.82), calls=%async_computation.1 | async-start | bytes 2097152 | tf_op jit(solution)/shard_map/all_to_all | solution.py:137
  94.5 20.3 %collective-permute-start.9 = (bf16[4,8,128,128]{3,2,1,0:T(8,128)(2,1)}, bf16[4,8,128,128]{3,2,1,0:T(8,128)(2,1)}, u32[]{:S(2)}, u32[]{:S(2)}) collective-permute-start(bf16[4,8,128,128]{3,2,1,0:T(8,128)(2,1)} %add_convert_fusion.1), channel_id=1, source_target_pairs={{8,0},{9,1},{10,2},{11,3},{12,4},{13,5},{14,6},{15,7}} | collective-permute-start | bytes 3145736 | tf_op jit(solution)/shard_map/ppermute | solution.py:159
  117.1 1.5 copy-start.13
  118.6 2.8 %copy-start.14 = (bf16[8,4,128,128]{3,2,0,1:T(8,128)(2,1)S(1)}, bf16[8,4,128,128]{3,2,0,1:T(8,128)(2,1)}, u32[]{:S(2)}) copy-start(bf16[8,4,128,128]{3,2,0,1:T(8,128)(2,1)} %copy.118) | copy-start | bytes 3145732
  121.4 2.2 %copy-start.11 = (f32[4,8,128,256]{3,2,1,0:T(8,128)S(1)}, f32[4,8,128,256]{3,2,1,0:T(8,128)}, u32[]{:S(2)}) copy-start(f32[4,8,128,256]{3,2,1,0:T(8,128)} %copy-done.10) | copy-start | bytes 12582916
  123.6 1.6 copy-start.3
  125.2 1.5 copy-start.9
  128.9 14.5 %collective-permute-start.10 = (bf16[2,4,128,128]{3,2,1,0:T(8,128)(2,1)S(1)}, bf16[2,4,128,128]{3,2,1,0:T(8,128)(2,1)S(1)}, u32[]{:S(2)}, u32[]{:S(2)}) collective-permute-start(bf16[2,4,128,128]{3,2,1,0:T(8,128)(2,1)S(1)} %get-tuple-element.72), channel_id=1, source_target_pairs={{0,1},{1,2},{2,3},{3,4},{4,5},{5,6},{6,7},{7,0},{8,9},{9,10},{10,1... | collective-permute-start | bytes 786440 | tf_op jit(solution)/shard_map/ppermute | solution.py:118
  130.7 68.6 %all-to-all-start.2 = ((f32[1024,1,128]{2,1,0:T(1,128)}), f32[1024,1,128]{2,1,0:T(1,128)}, u32[]{:S(2)}, u32[]{:S(2)}) async-start(f32[1024,1,128]{2,1,0:T(1,128)} %bitcast.24), calls=%async_computation.2 | async-start | bytes 1048576 | tf_op jit(solution)/shard_map/all_to_all | solution.py:186
  137.9 57.6 %collective-permute-start.14 = (bf16[2,4,128,128]{3,2,1,0:T(8,128)(2,1)S(1)}, bf16[2,4,128,128]{3,2,1,0:T(8,128)(2,1)S(1)}, u32[]{:S(2)}, u32[]{:S(2)}) collective-permute-start(bf16[2,4,128,128]{3,2,1,0:T(8,128)(2,1)S(1)} %get-tuple-element.77), channel_id=1, source_target_pairs={{0,5},{1,6},{2,7},{3,0},{4,1},{5,2},{6,3},{7,4},{8,13},{9,14},{10,... | collective-permute-start | bytes 786440 | tf_op jit(solution)/shard_map/ppermute | solution.py:118
  139.3 19.6 %collective-permute-start.11 = (bf16[2,4,128,128]{3,2,1,0:T(8,128)(2,1)S(1)}, bf16[2,4,128,128]{3,2,1,0:T(8,128)(2,1)S(1)}, u32[]{:S(2)}, u32[]{:S(2)}) collective-permute-start(bf16[2,4,128,128]{3,2,1,0:T(8,128)(2,1)S(1)} %get-tuple-element.73), channel_id=1, source_target_pairs={{0,2},{1,3},{2,4},{3,5},{4,6},{5,7},{6,0},{7,1},{8,10},{9,11},{10,... | collective-permute-start | bytes 786440 | tf_op jit(solution)/shard_map/ppermute | solution.py:118
  141.7 42.3 %collective-permute-start.12 = (bf16[2,4,128,128]{3,2,1,0:T(8,128)(2,1)S(1)}, bf16[2,4,128,128]{3,2,1,0:T(8,128)(2,1)S(1)}, u32[]{:S(2)}, u32[]{:S(2)}) collective-permute-start(bf16[2,4,128,128]{3,2,1,0:T(8,128)(2,1)S(1)} %get-tuple-element.74), channel_id=1, source_target_pairs={{0,3},{1,4},{2,5},{3,6},{4,7},{5,0},{6,1},{7,2},{8,11},{9,12},{10,... | collective-permute-start | bytes 786440 | tf_op jit(solution)/shard_map/ppermute | solution.py:118
  142.6 52.6 %collective-permute-start.13 = (bf16[2,4,128,128]{3,2,1,0:T(8,128)(2,1)S(1)}, bf16[2,4,128,128]{3,2,1,0:T(8,128)(2,1)S(1)}, u32[]{:S(2)}, u32[]{:S(2)}) collective-permute-start(bf16[2,4,128,128]{3,2,1,0:T(8,128)(2,1)S(1)} %get-tuple-element.75), channel_id=1, source_target_pairs={{0,4},{1,5},{2,6},{3,7},{4,0},{5,1},{6,2},{7,3},{8,12},{9,13},{10,... | collective-permute-start | bytes 786440 | tf_op jit(solution)/shard_map/ppermute | solution.py:118
  143.4 52.4 %collective-permute-start.15 = (bf16[2,4,128,128]{3,2,1,0:T(8,128)(2,1)S(1)}, bf16[2,4,128,128]{3,2,1,0:T(8,128)(2,1)S(1)}, u32[]{:S(2)}, u32[]{:S(2)}) collective-permute-start(bf16[2,4,128,128]{3,2,1,0:T(8,128)(2,1)S(1)} %get-tuple-element.76), channel_id=1, source_target_pairs={{0,6},{1,7},{2,0},{3,1},{4,2},{5,3},{6,4},{7,5},{8,14},{9,15},{10,... | collective-permute-start | bytes 786440 | tf_op jit(solution)/shard_map/ppermute | solution.py:118
  158.9 37.3 %collective-permute-start.16 = (bf16[2,4,128,128]{3,2,1,0:T(8,128)(2,1)S(1)}, bf16[2,4,128,128]{3,2,1,0:T(8,128)(2,1)S(1)}, u32[]{:S(2)}, u32[]{:S(2)}) collective-permute-start(bf16[2,4,128,128]{3,2,1,0:T(8,128)(2,1)S(1)} %get-tuple-element.70), channel_id=1, source_target_pairs={{0,7},{1,0},{2,1},{3,2},{4,3},{5,4},{6,5},{7,6},{8,15},{9,8},{10,9... | collective-permute-start | bytes 786440 | tf_op jit(solution)/shard_map/ppermute | solution.py:118
  196.8 4.5 %copy-start.1 = (bf16[128,4096]{1,0:T(8,128)(2,1)S(1)}, bf16[128,4096]{1,0:T(8,128)(2,1)}, u32[]{:S(2)}) copy-start(bf16[128,4096]{1,0:T(8,128)(2,1)} %param.18) | copy-start | bytes 3145732
  (6 other events, 7.1 us)

commit v5 on v4

--- a/solution.py
+++ b/solution.py
@@ -134,7 +134,7 @@
     stacked_heads = transpose_seq(stacked, 1, 2)
     query_blocks = to_blocks(stacked_heads[0])
     cot_blocks = to_blocks(stacked_heads[1])
-    input_heads = lax.all_to_all(head_major(inputs[0]), "seq", split_axis=0, concat_axis=1, tiled=True)
+    input_heads = transpose_seq(head_major(inputs[0]), 0, 1)
     values_both = key_pair(to_blocks(input_heads))
     kv_pick = (jnp.arange(seq_ways) * local_heads) // group_size
     key_rows = jnp.transpose(key_heads[0].reshape(tok_rows, kv_count, DH), (1, 0, 2))[kv_pick]

time: 202 us -> 195 us (0.965)
  the two profiles are of different devices: /device:TPU:26 before, /device:TPU:15 now
where the time goes in v5:
time: 195 us; the launch traced here: 192 us
  waiting for transfers between devices  66 us (34%)
  starting transfers between devices  55.2 us (28%)
  local copies, waits for them, and re-layouts  44.9 us (23%)
  other arithmetic  13 us (7%)
  matrix products  11.2 us (6%)
    ppermute x21, waiting for transfers between devices, transpose_seq(): lax.ppermute(chunk, 'seq', [(s, (s + shift) % seq_ways) for s in range(se...  63.8 us
    ppermute x21, starting transfers between devices, transpose_seq(): lax.ppermute(chunk, 'seq', [(s, (s + shift) % seq_ways) for s in range(se...  38.6 us
    dynamic_update_slice x23, local copies, waits for them, and re-layouts, transpose_seq(): lax.dynamic_update_slice_in_dim(result, chunk, source * concat_size, axis...  19.8 us
    unnamed x57, local copies, waits for them, and re-layouts  11.5 us
    all_to_all x1, starting transfers between devices, on_device(): lax.all_to_all(key_part[:, None, :], 'seq', split_axis=0, concat_axis=1,...  6.05 us
    all_to_all x1, starting transfers between devices, on_device(): lax.all_to_all(key_rows, 'seq', split_axis=0, concat_axis=1, tiled=True)  5.69 us
    ppermute x3, starting transfers between devices, on_device(): grad_in = lax.ppermute(new_grad, 'pipe', [(sender, sender - 1)])  4.85 us
    dot_general x4, matrix products, value_grad(): jnp.einsum('hbij,hbid->hbjd', probs_low, grad_blocks, preferred_element_t...  4.26 us
  transfers between devices with their start and end apart: 26, of which 12 were waited for; matrix products, arithmetic and copies ran while one was open for 19% of the time, Pallas kernels for 0%

profile of v5, /device:TPU:15, one launch (start us, length us, event | category | flops | bytes accessed | tf_op | source)
XLA Modules:
  0.0 191.7 jit_solution(6163702587218087063)
XLA Ops:
  0.7 1.5 copy.184
  3.0 1.6 broadcast_in_dim.46
  13.6 5.7 %all-to-all-start = ((bf16[8,128,128]{2,1,0:T(8,128)(2,1)}), bf16[8,128,128]{2,1,0:T(8,128)(2,1)S(1)}, u32[]{:S(2)}, u32[]{:S(2)}) async-start(bf16[8,128,128]{2,1,0:T(8,128)(2,1)} %gather_fusion), calls=%async_computation | async-start | bytes 524288 | tf_op jit(solution)/shard_map/all_to_all | solution.py:141
  20.6 1.7 constant_dynamic-update-slice_fusion.13
  22.5 1.7 constant_dynamic-update-slice_fusion.12
  24.2 24.8 %collective-permute-done.2 = bf16[2,4,128,128]{3,2,1,0:T(8,128)(2,1)} collective-permute-done((bf16[2,4,128,128]{3,2,1,0:T(8,128)(2,1)}, bf16[2,4,128,128]{3,2,1,0:T(8,128)(2,1)}, u32[]{:S(2)}, u32[]{:S(2)}) %collective-permute-start.2) | collective-permute-done | bytes 262176 | tf_op jit(solution)/shard_map/ppermute | solution.py:118
  49.0 1.7 constant_dynamic-update-slice_fusion.11
  50.7 3.8 %collective-permute-done.3 = bf16[2,4,128,128]{3,2,1,0:T(8,128)(2,1)S(1)} collective-permute-done((bf16[2,4,128,128]{3,2,1,0:T(8,128)(2,1)S(1)}, bf16[2,4,128,128]{3,2,1,0:T(8,128)(2,1)S(1)}, u32[]{:S(2)}, u32[]{:S(2)}) %collective-permute-start.3) | collective-permute-done | bytes 262176 | tf_op jit(solution)/shard_map/ppermute | solution.py:118
  56.1 4.2 %collective-permute-done.5 = bf16[2,4,128,128]{3,2,1,0:T(8,128)(2,1)S(1)} collective-permute-done((bf16[2,4,128,128]{3,2,1,0:T(8,128)(2,1)S(1)}, bf16[2,4,128,128]{3,2,1,0:T(8,128)(2,1)S(1)}, u32[]{:S(2)}, u32[]{:S(2)}) %collective-permute-start.5) | collective-permute-done | bytes 262176 | tf_op jit(solution)/shard_map/ppermute | solution.py:118
  62.1 1.7 fusion.50
  66.3 2.2 %fusion.51 = (f32[4,8,128]{2,1,0:T(8,128)S(1)}, f32[4,8,128,256]{3,2,1,0:T(8,128)S(1)}) fusion(f32[4,8,128,256]{3,2,1,0:T(8,128)S(1)} %fusion.3, pred[8,128,256]{2,1,0:T(8,128)(4,1)S(1)} %copy-done.19), kind=kOutput, calls=%fused_computation.166 | output fusion | flops 6291711 | bytes 8667136 | tf_op jit(solution)/shard_map/sub | solution.py:53
  72.1 2.5 %collective-permute-start.7 = (bf16[4,8,128,128]{3,2,1,0:T(8,128)(2,1)S(1)}, bf16[4,8,128,128]{3,2,1,0:T(8,128)(2,1)S(1)}, u32[]{:S(2)}, u32[]{:S(2)}) collective-permute-start(bf16[4,8,128,128]{3,2,1,0:T(8,128)(2,1)S(1)} %add_convert_fusion.3), channel_id=1, source_target_pairs={{24,16},{25,17},{26,18},{27,19},{28,20},{29,21},{30,22},{31,23}} | collective-permute-start | bytes 3145736 | tf_op jit(solution)/shard_map/ppermute | solution.py:159
  74.6 2.2 %collective-permute-done.7 = bf16[4,8,128,128]{3,2,1,0:T(8,128)(2,1)S(1)} collective-permute-done((bf16[4,8,128,128]{3,2,1,0:T(8,128)(2,1)S(1)}, bf16[4,8,128,128]{3,2,1,0:T(8,128)(2,1)S(1)}, u32[]{:S(2)}, u32[]{:S(2)}) %collective-permute-start.7) | collective-permute-done | bytes 1048608 | tf_op jit(solution)/shard_map/ppermute | solution.py:159
  82.3 2.7 %collective-permute-start.12 = (bf16[4,128,128]{2,1,0:T(8,128)(2,1)}, bf16[4,128,128]{2,1,0:T(8,128)(2,1)}, u32[]{:S(2)}, u32[]{:S(2)}) collective-permute-start(bf16[4,128,128]{2,1,0:T(8,128)(2,1)} %bitcast.92), channel_id=1, source_target_pairs={{0,3},{1,4},{2,5},{3,6},{4,7},{5,0},{6,1},{7,2},{8,11},{9,12},{10,... | collective-permute-start | bytes 393224 | tf_op jit(solution)/shard_map/ppermute | solution.py:118
  89.2 1.7 collective-permute-start.9
  94.5 1.6 constant_dynamic-update-slice_fusion.6
  96.0 1.9 %collective-permute-start.15 = (bf16[4,128,128]{2,1,0:T(8,128)(2,1)S(1)}, bf16[4,128,128]{2,1,0:T(8,128)(2,1)S(1)}, u32[]{:S(2)}, u32[]{:S(2)}) collective-permute-start(bf16[4,128,128]{2,1,0:T(8,128)(2,1)S(1)} %bitcast.116), channel_id=1, source_target_pairs={{0,6},{1,7},{2,0},{3,1},{4,2},{5,3},{6,4},{7,5},{8,14},{9,15},{10,... | collective-permute-start | bytes 393224 | tf_op jit(solution)/shard_map/ppermute | solution.py:118
  98.0 1.6 constant_dynamic-update-slice_fusion.5
  101.0 1.6 constant_dynamic-update-slice_fusion.4
  102.6 1.6 constant_dynamic-update-slice_fusion.3
  108.1 2.0 %fusion.55 = f32[4,8,256,128]{3,2,1,0:T(8,128)S(1)} fusion(bf16[4,8,128,256]{3,2,1,0:T(8,128)(2,1)S(1)} %fusion.8, bf16[4,8,128,128]{3,2,1,0:T(8,128)(2,1)} %collective-permute-done.9), kind=kOutput, calls=%fused_computation.170 | convolution fusion | flops 268435456 | bytes 7340032 | tf_op jit(solution)/shard_map/hbij,hbid->hbjd/dot_general | solution.py:58
  112.5 2.2 %fusion.9 = (bf16[4,8,128,128]{3,2,1,0:T(8,128)(2,1)S(1)}, bf16[4,8,128,128]{3,2,1,0:T(8,128)(2,1)S(1)}) fusion(f32[4,8,128,128]{3,2,1,0:T(8,128)S(1)} %fusion.36, bf16[4,8,128,128]{3,2,1,0:T(8,128)(2,1)} %collective-permute-done.9, bf16[4,8,128,128]{3,2,1,0:T(8,128)(2,1)} %add_convert_fusion.1, bf16[4,8,128,128]{3,2,1,0:T(8,128)(2,1)S(1)} %copy-done.17, ...), kind=kLoop, calls=%fused_computation.65 | loop fusion | flops 4718592 | bytes 11534339 | tf_op jit(solution)/shard_map/jit(_where)/select_n | solution.py:164
  115.0 2.2 %multiply_reduce_fusion = f32[4,8,128]{2,1,0:T(8,128)S(1)} fusion(bf16[4,8,128,128]{3,2,1,0:T(8,128)(2,1)S(1)} %get-tuple-element.89, bf16[4,8,128,256]{3,2,1,0:T(8,128)(2,1)S(1)} %fusion.8, bf16[4,8,128,128]{3,2,1,0:T(8,128)(2,1)} %bitcast.22, bf16[4,8,128,128]{3,2,1,0:T(8,128)(2,1)S(1)} %broadcast_in_dim.52), kind=kOutput, calls=%fused_computation.52 | convolution fusion | flops 274198528 | bytes 5259264 | tf_op jit(solution)/shard_map/hbij,hbjd->hbid/dot_general | solution.py:69
  117.5 2.5 %multiply_convert_fusion = bf16[4,8,128,256]{3,2,1,0:T(8,128)(2,1)S(1)} fusion(bf16[4,8,128,128]{3,2,1,0:T(8,128)(2,1)S(1)} %get-tuple-element.89, f32[4,8,128]{2,1,0:T(8,128)S(1)} %multiply_reduce_fusion, bf16[4,8,128,128]{3,2,1,0:T(8,128)(2,1)} %bitcast.22, bf16[4,8,128,128]{3,2,1,0:T(8,128)(2,1)S(1)} %broadcast_in_dim.52, ...), kind=kOutput, calls=%fused_computation.2 | convolution fusion | flops 276824064 | bytes 9469952 | tf_op jit(solution)/shard_map/hbid,hbjd->hbij/dot_general | solution.py:73
  123.9 6.1 %all-to-all-start.1 = ((f32[1024,1,128]{2,1,0:T(1,128)}), f32[1024,1,128]{2,1,0:T(1,128)}, u32[]{:S(2)}, u32[]{:S(2)}) async-start(f32[1024,1,128]{2,1,0:T(1,128)} %bitcast.29), calls=%async_computation.1 | async-start | bytes 1048576 | tf_op jit(solution)/shard_map/all_to_all | solution.py:186
  131.5 3.9 %collective-permute-start.19 = (bf16[2,4,128,128]{3,2,1,0:T(8,128)(2,1)S(1)}, bf16[2,4,128,128]{3,2,1,0:T(8,128)(2,1)S(1)}, u32[]{:S(2)}, u32[]{:S(2)}) collective-permute-start(bf16[2,4,128,128]{3,2,1,0:T(8,128)(2,1)S(1)} %get-tuple-element.74), channel_id=1, source_target_pairs={{0,3},{1,4},{2,5},{3,6},{4,7},{5,0},{6,1},{7,2},{8,11},{9,12},{10,... | collective-permute-start | bytes 786440 | tf_op jit(solution)/shard_map/ppermute | solution.py:118
  136.0 1.5 collective-permute-start.22
  137.8 18.9 %collective-permute-done.18 = bf16[2,4,128,128]{3,2,1,0:T(8,128)(2,1)S(1)} collective-permute-done((bf16[2,4,128,128]{3,2,1,0:T(8,128)(2,1)S(1)}, bf16[2,4,128,128]{3,2,1,0:T(8,128)(2,1)S(1)}, u32[]{:S(2)}, u32[]{:S(2)}) %collective-permute-start.18) | collective-permute-done | bytes 262176 | tf_op jit(solution)/shard_map/ppermute | solution.py:118
  156.7 17.4 %collective-permute-start.23 = (bf16[2,4,128,128]{3,2,1,0:T(8,128)(2,1)S(1)}, bf16[2,4,128,128]{3,2,1,0:T(8,128)(2,1)S(1)}, u32[]{:S(2)}, u32[]{:S(2)}) collective-permute-start(bf16[2,4,128,128]{3,2,1,0:T(8,128)(2,1)S(1)} %get-tuple-element.70), channel_id=1, source_target_pairs={{0,7},{1,0},{2,1},{3,2},{4,3},{5,4},{6,5},{7,6},{8,15},{9,8},{10,9... | collective-permute-start | bytes 786440 | tf_op jit(solution)/shard_map/ppermute | solution.py:118
  176.0 5.3 %collective-permute-done.20 = bf16[2,4,128,128]{3,2,1,0:T(8,128)(2,1)S(1)} collective-permute-done((bf16[2,4,128,128]{3,2,1,0:T(8,128)(2,1)S(1)}, bf16[2,4,128,128]{3,2,1,0:T(8,128)(2,1)S(1)}, u32[]{:S(2)}, u32[]{:S(2)}) %collective-permute-start.20) | collective-permute-done | bytes 262176 | tf_op jit(solution)/shard_map/ppermute | solution.py:118
  181.9 1.6 collective-permute-done.22
  183.9 2.6 %collective-permute-done.23 = bf16[2,4,128,128]{3,2,1,0:T(8,128)(2,1)S(1)} collective-permute-done((bf16[2,4,128,128]{3,2,1,0:T(8,128)(2,1)S(1)}, bf16[2,4,128,128]{3,2,1,0:T(8,128)(2,1)S(1)}, u32[]{:S(2)}, u32[]{:S(2)}) %collective-permute-start.23) | collective-permute-done | bytes 262176 | tf_op jit(solution)/shard_map/ppermute | solution.py:118
  (163 shorter events, 56.0 us)
Async XLA Ops:
  5.9 6.0 %copy-start.21 = (bf16[1,128,512]{2,1,0:T(8,128)(2,1)S(1)}, bf16[1,128,512]{2,1,0:T(8,128)(2,1)}, u32[]{:S(2)}) copy-start(bf16[1,128,512]{2,1,0:T(8,128)(2,1)} %param.16) | copy-start | bytes 393220
  5.9 14.4 %collective-permute-start = (bf16[2,4,128,128]{3,2,1,0:T(8,128)(2,1)}, bf16[2,4,128,128]{3,2,1,0:T(8,128)(2,1)}, u32[]{:S(2)}, u32[]{:S(2)}) collective-permute-start(bf16[2,4,128,128]{3,2,1,0:T(8,128)(2,1)} %get-tuple-element.82), channel_id=1, source_target_pairs={{0,1},{1,2},{2,3},{3,4},{4,5},{5,6},{6,7},{7,0},{8,9},{9,10},{10,1... | collective-permute-start | bytes 786440 | tf_op jit(solution)/shard_map/ppermute | solution.py:118
  7.2 15.2 %collective-permute-start.1 = (bf16[2,4,128,128]{3,2,1,0:T(8,128)(2,1)}, bf16[2,4,128,128]{3,2,1,0:T(8,128)(2,1)}, u32[]{:S(2)}, u32[]{:S(2)}) collective-permute-start(bf16[2,4,128,128]{3,2,1,0:T(8,128)(2,1)} %get-tuple-element.83), channel_id=1, source_target_pairs={{0,2},{1,3},{2,4},{3,5},{4,6},{5,7},{6,0},{7,1},{8,10},{9,11},{10,... | collective-permute-start | bytes 786440 | tf_op jit(solution)/shard_map/ppermute | solution.py:118
  8.5 40.5 %collective-permute-start.2 = (bf16[2,4,128,128]{3,2,1,0:T(8,128)(2,1)}, bf16[2,4,128,128]{3,2,1,0:T(8,128)(2,1)}, u32[]{:S(2)}, u32[]{:S(2)}) collective-permute-start(bf16[2,4,128,128]{3,2,1,0:T(8,128)(2,1)} %get-tuple-element.84), channel_id=1, source_target_pairs={{0,3},{1,4},{2,5},{3,6},{4,7},{5,0},{6,1},{7,2},{8,11},{9,12},{10,... | collective-permute-start | bytes 786440 | tf_op jit(solution)/shard_map/ppermute | solution.py:118
  9.4 9.8 %copy-start.22 = (s32[8]{0:T(128)S(1)}, s32[8]{0:T(128)}, u32[]{:S(2)}) copy-start(s32[8]{0:T(128)} %param.19) | copy-start | bytes 100
  9.5 12.9 %copy-start.20 = (bf16[2,4,128,128]{3,2,1,0:T(8,128)(2,1)S(1)}, bf16[2,4,128,128]{3,2,1,0:T(8,128)(2,1)}, u32[]{:S(2)}) copy-start(bf16[2,4,128,128]{3,2,1,0:T(8,128)(2,1)} %get-tuple-element.80) | copy-start | bytes 786436
  9.5 45.0 %collective-permute-start.3 = (bf16[2,4,128,128]{3,2,1,0:T(8,128)(2,1)S(1)}, bf16[2,4,128,128]{3,2,1,0:T(8,128)(2,1)S(1)}, u32[]{:S(2)}, u32[]{:S(2)}) collective-permute-start(bf16[2,4,128,128]{3,2,1,0:T(8,128)(2,1)S(1)} %get-tuple-element.86), channel_id=1, source_target_pairs={{0,4},{1,5},{2,6},{3,7},{4,0},{5,1},{6,2},{7,3},{8,12},{9,13},{10,... | collective-permute-start | bytes 786440 | tf_op jit(solution)/shard_map/ppermute | solution.py:118
  10.9 44.4 %collective-permute-start.4 = (bf16[2,4,128,128]{3,2,1,0:T(8,128)(2,1)S(1)}, bf16[2,4,128,128]{3,2,1,0:T(8,128)(2,1)S(1)}, u32[]{:S(2)}, u32[]{:S(2)}) collective-permute-start(bf16[2,4,128,128]{3,2,1,0:T(8,128)(2,1)S(1)} %get-tuple-element.87), channel_id=1, source_target_pairs={{0,5},{1,6},{2,7},{3,0},{4,1},{5,2},{6,3},{7,4},{8,13},{9,14},{10,... | collective-permute-start | bytes 786440 | tf_op jit(solution)/shard_map/ppermute | solution.py:118
  13.6 50.3 %all-to-all-start = ((bf16[8,128,128]{2,1,0:T(8,128)(2,1)}), bf16[8,128,128]{2,1,0:T(8,128)(2,1)S(1)}, u32[]{:S(2)}, u32[]{:S(2)}) async-start(bf16[8,128,128]{2,1,0:T(8,128)(2,1)} %gather_fusion), calls=%async_computation | async-start | bytes 524288 | tf_op jit(solution)/shard_map/all_to_all | solution.py:141
  20.4 39.9 %collective-permute-start.5 = (bf16[2,4,128,128]{3,2,1,0:T(8,128)(2,1)S(1)}, bf16[2,4,128,128]{3,2,1,0:T(8,128)(2,1)S(1)}, u32[]{:S(2)}, u32[]{:S(2)}) collective-permute-start(bf16[2,4,128,128]{3,2,1,0:T(8,128)(2,1)S(1)} %get-tuple-element.85), channel_id=1, source_target_pairs={{0,6},{1,7},{2,0},{3,1},{4,2},{5,3},{6,4},{7,5},{8,14},{9,15},{10,... | collective-permute-start | bytes 786440 | tf_op jit(solution)/shard_map/ppermute | solution.py:118
  22.4 39.0 %collective-permute-start.6 = (bf16[2,4,128,128]{3,2,1,0:T(8,128)(2,1)S(1)}, bf16[2,4,128,128]{3,2,1,0:T(8,128)(2,1)S(1)}, u32[]{:S(2)}, u32[]{:S(2)}) collective-permute-start(bf16[2,4,128,128]{3,2,1,0:T(8,128)(2,1)S(1)} %copy-done.20), channel_id=1, source_target_pairs={{0,7},{1,0},{2,1},{3,2},{4,3},{5,4},{6,5},{7,6},{8,15},{9,8},{10,9... | collective-permute-start | bytes 786440 | tf_op jit(solution)/shard_map/ppermute | solution.py:118
  72.1 4.7 %collective-permute-start.7 = (bf16[4,8,128,128]{3,2,1,0:T(8,128)(2,1)S(1)}, bf16[4,8,128,128]{3,2,1,0:T(8,128)(2,1)S(1)}, u32[]{:S(2)}, u32[]{:S(2)}) collective-permute-start(bf16[4,8,128,128]{3,2,1,0:T(8,128)(2,1)S(1)} %add_convert_fusion.3), channel_id=1, source_target_pairs={{24,16},{25,17},{26,18},{27,19},{28,20},{29,21},{30,22},{31,23}} | collective-permute-start | bytes 3145736 | tf_op jit(solution)/shard_map/ppermute | solution.py:159
  78.6 7.9 %collective-permute-start.8 = (bf16[4,8,128,128]{3,2,1,0:T(8,128)(2,1)S(1)}, bf16[4,8,128,128]{3,2,1,0:T(8,128)(2,1)S(1)}, u32[]{:S(2)}, u32[]{:S(2)}) collective-permute-start(bf16[4,8,128,128]{3,2,1,0:T(8,128)(2,1)S(1)} %add_convert_fusion.2), channel_id=1, source_target_pairs={{16,8},{17,9},{18,10},{19,11},{20,12},{21,13},{22,14},{23,15}} | collective-permute-start | bytes 3145736 | tf_op jit(solution)/shard_map/ppermute | solution.py:159
  80.9 12.5 %collective-permute-start.10 = (bf16[4,128,128]{2,1,0:T(8,128)(2,1)}, bf16[4,128,128]{2,1,0:T(8,128)(2,1)}, u32[]{:S(2)}, u32[]{:S(2)}) collective-permute-start(bf16[4,128,128]{2,1,0:T(8,128)(2,1)} %bitcast.94), channel_id=1, source_target_pairs={{0,1},{1,2},{2,3},{3,4},{4,5},{5,6},{6,7},{7,0},{8,9},{9,10},{10,1... | collective-permute-start | bytes 393224 | tf_op jit(solution)/shard_map/ppermute | solution.py:118
  81.6 14.4 %collective-permute-start.11 = (bf16[4,128,128]{2,1,0:T(8,128)(2,1)}, bf16[4,128,128]{2,1,0:T(8,128)(2,1)}, u32[]{:S(2)}, u32[]{:S(2)}) collective-permute-start(bf16[4,128,128]{2,1,0:T(8,128)(2,1)} %bitcast.93), channel_id=1, source_target_pairs={{0,2},{1,3},{2,4},{3,5},{4,6},{5,7},{6,0},{7,1},{8,10},{9,11},{10,... | collective-permute-start | bytes 393224 | tf_op jit(solution)/shard_map/ppermute | solution.py:118
  82.3 17.3 %collective-permute-start.12 = (bf16[4,128,128]{2,1,0:T(8,128)(2,1)}, bf16[4,128,128]{2,1,0:T(8,128)(2,1)}, u32[]{:S(2)}, u32[]{:S(2)}) collective-permute-start(bf16[4,128,128]{2,1,0:T(8,128)(2,1)} %bitcast.92), channel_id=1, source_target_pairs={{0,3},{1,4},{2,5},{3,6},{4,7},{5,0},{6,1},{7,2},{8,11},{9,12},{10,... | collective-permute-start | bytes 393224 | tf_op jit(solution)/shard_map/ppermute | solution.py:118
  85.7 17.0 %collective-permute-start.13 = (bf16[4,128,128]{2,1,0:T(8,128)(2,1)}, bf16[4,128,128]{2,1,0:T(8,128)(2,1)}, u32[]{:S(2)}, u32[]{:S(2)}) collective-permute-start(bf16[4,128,128]{2,1,0:T(8,128)(2,1)} %bitcast.91), channel_id=1, source_target_pairs={{0,4},{1,5},{2,6},{3,7},{4,0},{5,1},{6,2},{7,3},{8,12},{9,13},{10,... | collective-permute-start | bytes 393224 | tf_op jit(solution)/shard_map/ppermute | solution.py:118
  89.2 18.9 %collective-permute-start.9 = (bf16[4,8,128,128]{3,2,1,0:T(8,128)(2,1)}, bf16[4,8,128,128]{3,2,1,0:T(8,128)(2,1)}, u32[]{:S(2)}, u32[]{:S(2)}) collective-permute-start(bf16[4,8,128,128]{3,2,1,0:T(8,128)(2,1)} %add_convert_fusion.1), channel_id=1, source_target_pairs={{8,0},{9,1},{10,2},{11,3},{12,4},{13,5},{14,6},{15,7}} | collective-permute-start | bytes 3145736 | tf_op jit(solution)/shard_map/ppermute | solution.py:159
  93.4 10.8 %collective-permute-start.14 = (bf16[4,128,128]{2,1,0:T(8,128)(2,1)}, bf16[4,128,128]{2,1,0:T(8,128)(2,1)S(1)}, u32[]{:S(2)}, u32[]{:S(2)}) collective-permute-start(bf16[4,128,128]{2,1,0:T(8,128)(2,1)} %bitcast.117), channel_id=1, source_target_pairs={{0,5},{1,6},{2,7},{3,0},{4,1},{5,2},{6,3},{7,4},{8,13},{9,14},{10,... | collective-permute-start | bytes 393224 | tf_op jit(solution)/shard_map/ppermute | solution.py:118
  96.0 9.5 %collective-permute-start.15 = (bf16[4,128,128]{2,1,0:T(8,128)(2,1)S(1)}, bf16[4,128,128]{2,1,0:T(8,128)(2,1)S(1)}, u32[]{:S(2)}, u32[]{:S(2)}) collective-permute-start(bf16[4,128,128]{2,1,0:T(8,128)(2,1)S(1)} %bitcast.116), channel_id=1, source_target_pairs={{0,6},{1,7},{2,0},{3,1},{4,2},{5,3},{6,4},{7,5},{8,14},{9,15},{10,... | collective-permute-start | bytes 393224 | tf_op jit(solution)/shard_map/ppermute | solution.py:118
  99.6 6.9 %collective-permute-start.16 = (bf16[4,128,128]{2,1,0:T(8,128)(2,1)S(1)}, bf16[4,128,128]{2,1,0:T(8,128)(2,1)S(1)}, u32[]{:S(2)}, u32[]{:S(2)}) collective-permute-start(bf16[4,128,128]{2,1,0:T(8,128)(2,1)S(1)} %bitcast.115), channel_id=1, source_target_pairs={{0,7},{1,0},{2,1},{3,2},{4,3},{5,4},{6,5},{7,6},{8,15},{9,8},{10,9... | collective-permute-start | bytes 393224 | tf_op jit(solution)/shard_map/ppermute | solution.py:118
  115.0 2.5 %copy-start.13 = (f32[4,8,128,256]{3,2,1,0:T(8,128)S(1)}, f32[4,8,128,256]{3,2,1,0:T(8,128)}, u32[]{:S(2)}) copy-start(f32[4,8,128,256]{3,2,1,0:T(8,128)} %copy-done.12) | copy-start | bytes 12582916
  117.5 2.5 %copy-start.3 = (bf16[1,4,1024,128]{3,2,1,0:T(8,128)(2,1)S(1)}, bf16[1,4,1024,128]{3,2,1,0:T(8,128)(2,1)}, u32[]{:S(2)}) copy-start(bf16[1,4,1024,128]{3,2,1,0:T(8,128)(2,1)} %copy-done.2) | copy-start | bytes 3145732
  123.8 12.1 %collective-permute-start.17 = (bf16[2,4,128,128]{3,2,1,0:T(8,128)(2,1)S(1)}, bf16[2,4,128,128]{3,2,1,0:T(8,128)(2,1)S(1)}, u32[]{:S(2)}, u32[]{:S(2)}) collective-permute-start(bf16[2,4,128,128]{3,2,1,0:T(8,128)(2,1)S(1)} %get-tuple-element.72), channel_id=1, source_target_pairs={{0,1},{1,2},{2,3},{3,4},{4,5},{5,6},{6,7},{7,0},{8,9},{9,10},{10,1... | collective-permute-start | bytes 786440 | tf_op jit(solution)/shard_map/ppermute | solution.py:118
  123.9 65.7 %all-to-all-start.1 = ((f32[1024,1,128]{2,1,0:T(1,128)}), f32[1024,1,128]{2,1,0:T(1,128)}, u32[]{:S(2)}, u32[]{:S(2)}) async-start(f32[1024,1,128]{2,1,0:T(1,128)} %bitcast.29), calls=%async_computation.1 | async-start | bytes 1048576 | tf_op jit(solution)/shard_map/all_to_all | solution.py:186
  130.0 51.6 %collective-permute-start.21 = (bf16[2,4,128,128]{3,2,1,0:T(8,128)(2,1)S(1)}, bf16[2,4,128,128]{3,2,1,0:T(8,128)(2,1)S(1)}, u32[]{:S(2)}, u32[]{:S(2)}) collective-permute-start(bf16[2,4,128,128]{3,2,1,0:T(8,128)(2,1)S(1)} %get-tuple-element.77), channel_id=1, source_target_pairs={{0,5},{1,6},{2,7},{3,0},{4,1},{5,2},{6,3},{7,4},{8,13},{9,14},{10,... | collective-permute-start | bytes 786440 | tf_op jit(solution)/shard_map/ppermute | solution.py:118
  130.2 26.5 %collective-permute-start.18 = (bf16[2,4,128,128]{3,2,1,0:T(8,128)(2,1)S(1)}, bf16[2,4,128,128]{3,2,1,0:T(8,128)(2,1)S(1)}, u32[]{:S(2)}, u32[]{:S(2)}) collective-permute-start(bf16[2,4,128,128]{3,2,1,0:T(8,128)(2,1)S(1)} %get-tuple-element.73), channel_id=1, source_target_pairs={{0,2},{1,3},{2,4},{3,5},{4,6},{5,7},{6,0},{7,1},{8,10},{9,11},{10,... | collective-permute-start | bytes 786440 | tf_op jit(solution)/shard_map/ppermute | solution.py:118
  131.5 44.2 %collective-permute-start.19 = (bf16[2,4,128,128]{3,2,1,0:T(8,128)(2,1)S(1)}, bf16[2,4,128,128]{3,2,1,0:T(8,128)(2,1)S(1)}, u32[]{:S(2)}, u32[]{:S(2)}) collective-permute-start(bf16[2,4,128,128]{3,2,1,0:T(8,128)(2,1)S(1)} %get-tuple-element.74), channel_id=1, source_target_pairs={{0,3},{1,4},{2,5},{3,6},{4,7},{5,0},{6,1},{7,2},{8,11},{9,12},{10,... | collective-permute-start | bytes 786440 | tf_op jit(solution)/shard_map/ppermute | solution.py:118
  135.4 46.0 %collective-permute-start.20 = (bf16[2,4,128,128]{3,2,1,0:T(8,128)(2,1)S(1)}, bf16[2,4,128,128]{3,2,1,0:T(8,128)(2,1)S(1)}, u32[]{:S(2)}, u32[]{:S(2)}) collective-permute-start(bf16[2,4,128,128]{3,2,1,0:T(8,128)(2,1)S(1)} %get-tuple-element.75), channel_id=1, source_target_pairs={{0,4},{1,5},{2,6},{3,7},{4,0},{5,1},{6,2},{7,3},{8,12},{9,13},{10,... | collective-permute-start | bytes 786440 | tf_op jit(solution)/shard_map/ppermute | solution.py:118
  136.0 47.6 %collective-permute-start.22 = (bf16[2,4,128,128]{3,2,1,0:T(8,128)(2,1)S(1)}, bf16[2,4,128,128]{3,2,1,0:T(8,128)(2,1)S(1)}, u32[]{:S(2)}, u32[]{:S(2)}) collective-permute-start(bf16[2,4,128,128]{3,2,1,0:T(8,128)(2,1)S(1)} %get-tuple-element.76), channel_id=1, source_target_pairs={{0,6},{1,7},{2,0},{3,1},{4,2},{5,3},{6,4},{7,5},{8,14},{9,15},{10,... | collective-permute-start | bytes 786440 | tf_op jit(solution)/shard_map/ppermute | solution.py:118
  156.7 29.7 %collective-permute-start.23 = (bf16[2,4,128,128]{3,2,1,0:T(8,128)(2,1)S(1)}, bf16[2,4,128,128]{3,2,1,0:T(8,128)(2,1)S(1)}, u32[]{:S(2)}, u32[]{:S(2)}) collective-permute-start(bf16[2,4,128,128]{3,2,1,0:T(8,128)(2,1)S(1)} %get-tuple-element.70), channel_id=1, source_target_pairs={{0,7},{1,0},{2,1},{3,2},{4,3},{5,4},{6,5},{7,6},{8,15},{9,8},{10,9... | collective-permute-start | bytes 786440 | tf_op jit(solution)/shard_map/ppermute | solution.py:118
  187.1 4.5 %copy-start.1 = (bf16[128,4096]{1,0:T(8,128)(2,1)S(1)}, bf16[128,4096]{1,0:T(8,128)(2,1)}, u32[]{:S(2)}) copy-start(bf16[128,4096]{1,0:T(8,128)(2,1)} %param.18) | copy-start | bytes 3145732
  (17 other events, 26.9 us)

commit v6 on v5

--- a/solution.py
+++ b/solution.py
@@ -107,10 +107,7 @@
             return lax.all_to_all(value, "seq", split_axis, concat_axis, tiled=True)
         split_size = value.shape[split_axis] // seq_ways
         concat_size = value.shape[concat_axis]
-        out_shape = list(value.shape)
-        out_shape[split_axis] = split_size
-        out_shape[concat_axis] = concat_size * seq_ways
-        result = jnp.zeros(out_shape, value.dtype)
+        received = []
         for shift in range(seq_ways):
             target = (seq_index + shift) % seq_ways
             chunk = lax.dynamic_slice_in_dim(value, target * split_size, split_size, axis=split_axis)
@@ -118,11 +115,11 @@
                 chunk = lax.ppermute(
                     chunk, "seq", [(s, (s + shift) % seq_ways) for s in range(seq_ways)]
                 )
-            source = (seq_index + seq_ways - shift) % seq_ways
-            result = lax.dynamic_update_slice_in_dim(
-                result, chunk, source * concat_size, axis=concat_axis
-            )
-        return result
+            received.append(chunk)
+        rising = [received[(seq_ways - k) % seq_ways] for k in range(seq_ways)]
+        doubled = jnp.concatenate(rising + rising, axis=concat_axis)
+        start = ((seq_ways - seq_index) % seq_ways) * concat_size
+        return lax.dynamic_slice_in_dim(doubled, start, seq_ways * concat_size, axis=concat_axis)
 
     def to_blocks(head_rows):
         return head_rows.reshape(local_heads, block_count, BLK, DH)

time: 195 us -> 211 us (1.082)
  the two profiles are of different devices: /device:TPU:15 before, /device:TPU:0 now
where the time goes in v6:
time: 211 us; the launch traced here: 210 us
  waiting for transfers between devices  73.3 us (35%)
  local copies, waits for them, and re-layouts  56.5 us (27%)
  starting transfers between devices  53.4 us (25%)
  other arithmetic  16.5 us (8%)
  matrix products  8.87 us (4%)
    ppermute x21, waiting for transfers between devices, transpose_seq(): lax.ppermute(chunk, 'seq', [(s, (s + shift) % seq_ways) for s in range(se...  73 us
    unnamed x89, local copies, waits for them, and re-layouts  43.3 us
    ppermute x21, starting transfers between devices, transpose_seq(): lax.ppermute(chunk, 'seq', [(s, (s + shift) % seq_ways) for s in range(se...  40.1 us
    all_to_all x1, starting transfers between devices, on_device(): lax.all_to_all(key_rows, 'seq', split_axis=0, concat_axis=1, tiled=True)  6.05 us
    dot_general x4, matrix products, value_grad(): jnp.einsum('hbij,hbid->hbjd', probs_low, grad_blocks, preferred_element_t...  4.26 us
  transfers between devices with their start and end apart: 26, of which 6 were waited for; matrix products, arithmetic and copies ran while one was open for 26% of the time, Pallas kernels for 0%

profile of v6, /device:TPU:0, one launch (start us, length us, event | category | flops | bytes accessed | tf_op | source)
XLA Modules:
  0.0 210.2 jit_solution(16831356191936724999)
XLA Ops:
  0.7 1.5 copy.150
  4.4 6.0 %collective-permute-start = (bf16[2,4,128,128]{3,2,1,0:T(8,128)(2,1)}, bf16[2,4,128,128]{3,2,1,0:T(8,128)(2,1)S(1)}, u32[]{:S(2)}, u32[]{:S(2)}) collective-permute-start(bf16[2,4,128,128]{3,2,1,0:T(8,128)(2,1)} %get-tuple-element.82), channel_id=1, source_target_pairs={{0,7},{1,0},{2,1},{3,2},{4,3},{5,4},{6,5},{7,6},{8,15},{9,8},{10,9... | collective-permute-start | bytes 786440 | tf_op jit(solution)/shard_map/ppermute | solution.py:115
  10.9 3.0 %collective-permute-start.3 = (bf16[2,4,128,128]{3,2,1,0:T(8,128)(2,1)}, bf16[2,4,128,128]{3,2,1,0:T(8,128)(2,1)}, u32[]{:S(2)}, u32[]{:S(2)}) collective-permute-start(bf16[2,4,128,128]{3,2,1,0:T(8,128)(2,1)} %get-tuple-element.85), channel_id=1, source_target_pairs={{0,4},{1,5},{2,6},{3,7},{4,0},{5,1},{6,2},{7,3},{8,12},{9,13},{10,... | collective-permute-start | bytes 786440 | tf_op jit(solution)/shard_map/ppermute | solution.py:115
  16.3 6.1 %all-to-all-start = ((bf16[8,128,128]{2,1,0:T(8,128)(2,1)}), bf16[8,128,128]{2,1,0:T(8,128)(2,1)S(1)}, u32[]{:S(2)}, u32[]{:S(2)}) async-start(bf16[8,128,128]{2,1,0:T(8,128)(2,1)} %gather_fusion), calls=%async_computation | async-start | bytes 524288 | tf_op jit(solution)/shard_map/all_to_all | solution.py:138
  23.5 2.0 collective-permute-start.5
  26.2 1.5 collective-permute-start.6
  29.6 29.9 %collective-permute-done.3 = bf16[2,4,128,128]{3,2,1,0:T(8,128)(2,1)} collective-permute-done((bf16[2,4,128,128]{3,2,1,0:T(8,128)(2,1)}, bf16[2,4,128,128]{3,2,1,0:T(8,128)(2,1)}, u32[]{:S(2)}, u32[]{:S(2)}) %collective-permute-start.3) | collective-permute-done | bytes 262176 | tf_op jit(solution)/shard_map/ppermute | solution.py:115
  59.5 1.7 constant_dynamic-update-slice_fusion.11
  61.2 1.7 constant_dynamic-update-slice_fusion.10
  67.3 1.7 constant_dynamic-update-slice_fusion.3
  69.0 1.7 constant_dynamic-update-slice_fusion.2
  72.2 1.7 constant_dynamic-slice_fusion.9
  76.4 2.2 %fusion.49 = (f32[4,8,128]{2,1,0:T(8,128)S(1)}, f32[4,8,128,256]{3,2,1,0:T(8,128)S(1)}) fusion(f32[4,8,128,256]{3,2,1,0:T(8,128)S(1)} %fusion.3, pred[8,128,256]{2,1,0:T(8,128)(4,1)S(1)} %copy-done.13), kind=kOutput, calls=%fused_computation.196 | output fusion | flops 6291711 | bytes 8667136 | tf_op jit(solution)/shard_map/sub | solution.py:53
  83.3 1.6 collective-permute-start.7
  88.4 3.2 %collective-permute-start.12 = (bf16[4,128,128]{2,1,0:T(8,128)(2,1)}, bf16[4,128,128]{2,1,0:T(8,128)(2,1)}, u32[]{:S(2)}, u32[]{:S(2)}) collective-permute-start(bf16[4,128,128]{2,1,0:T(8,128)(2,1)} %bitcast.101), channel_id=1, source_target_pairs={{0,5},{1,6},{2,7},{3,0},{4,1},{5,2},{6,3},{7,4},{8,13},{9,14},{10,... | collective-permute-start | bytes 393224 | tf_op jit(solution)/shard_map/ppermute | solution.py:115
  93.5 1.6 copy.173
  96.7 2.0 fusion.51
  99.3 1.6 add_convert_fusion.2
  102.6 2.6 %collective-permute-start.15 = (bf16[4,128,128]{2,1,0:T(8,128)(2,1)S(1)}, bf16[4,128,128]{2,1,0:T(8,128)(2,1)S(1)}, u32[]{:S(2)}, u32[]{:S(2)}) collective-permute-start(bf16[4,128,128]{2,1,0:T(8,128)(2,1)S(1)} %bitcast.133), channel_id=1, source_target_pairs={{0,2},{1,3},{2,4},{3,5},{4,6},{5,7},{6,0},{7,1},{8,10},{9,11},{10,... | collective-permute-start | bytes 393224 | tf_op jit(solution)/shard_map/ppermute | solution.py:115
  106.2 5.6 %collective-permute-start.16 = (bf16[4,128,128]{2,1,0:T(8,128)(2,1)S(1)}, bf16[4,128,128]{2,1,0:T(8,128)(2,1)S(1)}, u32[]{:S(2)}, u32[]{:S(2)}) collective-permute-start(bf16[4,128,128]{2,1,0:T(8,128)(2,1)S(1)} %bitcast.132), channel_id=1, source_target_pairs={{0,1},{1,2},{2,3},{3,4},{4,5},{5,6},{6,7},{7,0},{8,9},{9,10},{10,1... | collective-permute-start | bytes 393224 | tf_op jit(solution)/shard_map/ppermute | solution.py:115
  122.9 1.9 select_select_fusion
  125.9 1.5 copy-done.11
  127.4 1.5 multiply_convert_fusion
  131.6 1.4 fusion.18
  133.0 4.0 %collective-permute-start.17 = (bf16[2,4,128,128]{3,2,1,0:T(8,128)(2,1)}, bf16[2,4,128,128]{3,2,1,0:T(8,128)(2,1)S(1)}, u32[]{:S(2)}, u32[]{:S(2)}) collective-permute-start(bf16[2,4,128,128]{3,2,1,0:T(8,128)(2,1)} %get-tuple-element.74), channel_id=1, source_target_pairs={{0,7},{1,0},{2,1},{3,2},{4,3},{5,4},{6,5},{7,6},{8,15},{9,8},{10,9... | collective-permute-start | bytes 786440 | tf_op jit(solution)/shard_map/ppermute | solution.py:115
  138.0 3.6 %all-to-all-start.1 = ((f32[1024,1,128]{2,1,0:T(1,128)}), f32[1024,1,128]{2,1,0:T(1,128)S(1)}, u32[]{:S(2)}, u32[]{:S(2)}) async-start(f32[1024,1,128]{2,1,0:T(1,128)} %bitcast.29), calls=%async_computation.1 | async-start | bytes 1048576 | tf_op jit(solution)/shard_map/all_to_all | solution.py:183
  141.6 3.8 %collective-permute-start.19 = (bf16[2,4,128,128]{3,2,1,0:T(8,128)(2,1)}, bf16[2,4,128,128]{3,2,1,0:T(8,128)(2,1)S(1)}, u32[]{:S(2)}, u32[]{:S(2)}) collective-permute-start(bf16[2,4,128,128]{3,2,1,0:T(8,128)(2,1)} %get-tuple-element.76), channel_id=1, source_target_pairs={{0,5},{1,6},{2,7},{3,0},{4,1},{5,2},{6,3},{7,4},{8,13},{9,14},{10,... | collective-permute-start | bytes 786440 | tf_op jit(solution)/shard_map/ppermute | solution.py:115
  145.5 2.0 collective-permute-start.20
  147.6 3.3 %collective-permute-start.22 = (bf16[2,4,128,128]{3,2,1,0:T(8,128)(2,1)S(1)}, bf16[2,4,128,128]{3,2,1,0:T(8,128)(2,1)S(1)}, u32[]{:S(2)}, u32[]{:S(2)}) collective-permute-start(bf16[2,4,128,128]{3,2,1,0:T(8,128)(2,1)S(1)} %get-tuple-element.78), channel_id=1, source_target_pairs={{0,2},{1,3},{2,4},{3,5},{4,6},{5,7},{6,0},{7,1},{8,10},{9,11},{10,... | collective-permute-start | bytes 786440 | tf_op jit(solution)/shard_map/ppermute | solution.py:115
  152.9 11.4 %collective-permute-done.19 = bf16[2,4,128,128]{3,2,1,0:T(8,128)(2,1)S(1)} collective-permute-done((bf16[2,4,128,128]{3,2,1,0:T(8,128)(2,1)}, bf16[2,4,128,128]{3,2,1,0:T(8,128)(2,1)S(1)}, u32[]{:S(2)}, u32[]{:S(2)}) %collective-permute-start.19) | collective-permute-done | bytes 262176 | tf_op jit(solution)/shard_map/ppermute | solution.py:115
  165.0 30.7 %collective-permute-done.20 = bf16[2,4,128,128]{3,2,1,0:T(8,128)(2,1)S(1)} collective-permute-done((bf16[2,4,128,128]{3,2,1,0:T(8,128)(2,1)S(1)}, bf16[2,4,128,128]{3,2,1,0:T(8,128)(2,1)S(1)}, u32[]{:S(2)}, u32[]{:S(2)}) %collective-permute-start.20) | collective-permute-done | bytes 262176 | tf_op jit(solution)/shard_map/ppermute | solution.py:115
  204.7 1.7 dynamic-slice_bitcast_fusion
  (175 shorter events, 63.1 us)
Async XLA Ops:
  4.4 10.3 %copy-start.15 = (bf16[1,128,512]{2,1,0:T(8,128)(2,1)S(1)}, bf16[1,128,512]{2,1,0:T(8,128)(2,1)}, u32[]{:S(2)}) copy-start(bf16[1,128,512]{2,1,0:T(8,128)(2,1)} %param.16) | copy-start | bytes 393220
  4.4 19.0 %collective-permute-start = (bf16[2,4,128,128]{3,2,1,0:T(8,128)(2,1)}, bf16[2,4,128,128]{3,2,1,0:T(8,128)(2,1)S(1)}, u32[]{:S(2)}, u32[]{:S(2)}) collective-permute-start(bf16[2,4,128,128]{3,2,1,0:T(8,128)(2,1)} %get-tuple-element.82), channel_id=1, source_target_pairs={{0,7},{1,0},{2,1},{3,2},{4,3},{5,4},{6,5},{7,6},{8,15},{9,8},{10,9... | collective-permute-start | bytes 786440 | tf_op jit(solution)/shard_map/ppermute | solution.py:115
  10.4 15.8 %collective-permute-start.1 = (bf16[2,4,128,128]{3,2,1,0:T(8,128)(2,1)}, bf16[2,4,128,128]{3,2,1,0:T(8,128)(2,1)S(1)}, u32[]{:S(2)}, u32[]{:S(2)}) collective-permute-start(bf16[2,4,128,128]{3,2,1,0:T(8,128)(2,1)} %get-tuple-element.83), channel_id=1, source_target_pairs={{0,6},{1,7},{2,0},{3,1},{4,2},{5,3},{6,4},{7,5},{8,14},{9,15},{10,... | collective-permute-start | bytes 786440 | tf_op jit(solution)/shard_map/ppermute | solution.py:115
  10.9 17.9 %collective-permute-start.2 = (bf16[2,4,128,128]{3,2,1,0:T(8,128)(2,1)}, bf16[2,4,128,128]{3,2,1,0:T(8,128)(2,1)S(1)}, u32[]{:S(2)}, u32[]{:S(2)}) collective-permute-start(bf16[2,4,128,128]{3,2,1,0:T(8,128)(2,1)} %get-tuple-element.84), channel_id=1, source_target_pairs={{0,5},{1,6},{2,7},{3,0},{4,1},{5,2},{6,3},{7,4},{8,13},{9,14},{10,... | collective-permute-start | bytes 786440 | tf_op jit(solution)/shard_map/ppermute | solution.py:115
  10.9 48.6 %collective-permute-start.3 = (bf16[2,4,128,128]{3,2,1,0:T(8,128)(2,1)}, bf16[2,4,128,128]{3,2,1,0:T(8,128)(2,1)}, u32[]{:S(2)}, u32[]{:S(2)}) collective-permute-start(bf16[2,4,128,128]{3,2,1,0:T(8,128)(2,1)} %get-tuple-element.85), channel_id=1, source_target_pairs={{0,4},{1,5},{2,6},{3,7},{4,0},{5,1},{6,2},{7,3},{8,12},{9,13},{10,... | collective-permute-start | bytes 786440 | tf_op jit(solution)/shard_map/ppermute | solution.py:115
  13.9 8.5 %copy-start.17 = (s32[8]{0:T(128)S(1)}, s32[8]{0:T(128)}, u32[]{:S(2)}) copy-start(s32[8]{0:T(128)} %param.19) | copy-start | bytes 100
  14.7 46.5 %collective-permute-start.4 = (bf16[2,4,128,128]{3,2,1,0:T(8,128)(2,1)}, bf16[2,4,128,128]{3,2,1,0:T(8,128)(2,1)}, u32[]{:S(2)}, u32[]{:S(2)}) collective-permute-start(bf16[2,4,128,128]{3,2,1,0:T(8,128)(2,1)} %get-tuple-element.87), channel_id=1, source_target_pairs={{0,3},{1,4},{2,5},{3,6},{4,7},{5,0},{6,1},{7,2},{8,11},{9,12},{10,... | collective-permute-start | bytes 786440 | tf_op jit(solution)/shard_map/ppermute | solution.py:115
  16.3 57.6 %all-to-all-start = ((bf16[8,128,128]{2,1,0:T(8,128)(2,1)}), bf16[8,128,128]{2,1,0:T(8,128)(2,1)S(1)}, u32[]{:S(2)}, u32[]{:S(2)}) async-start(bf16[8,128,128]{2,1,0:T(8,128)(2,1)} %gather_fusion), calls=%async_computation | async-start | bytes 524288 | tf_op jit(solution)/shard_map/all_to_all | solution.py:138
  23.5 39.4 %collective-permute-start.5 = (bf16[2,4,128,128]{3,2,1,0:T(8,128)(2,1)}, bf16[2,4,128,128]{3,2,1,0:T(8,128)(2,1)S(1)}, u32[]{:S(2)}, u32[]{:S(2)}) collective-permute-start(bf16[2,4,128,128]{3,2,1,0:T(8,128)(2,1)} %get-tuple-element.86), channel_id=1, source_target_pairs={{0,2},{1,3},{2,4},{3,5},{4,6},{5,7},{6,0},{7,1},{8,10},{9,11},{10,... | collective-permute-start | bytes 786440 | tf_op jit(solution)/shard_map/ppermute | solution.py:115
  26.2 37.4 %collective-permute-start.6 = (bf16[2,4,128,128]{3,2,1,0:T(8,128)(2,1)}, bf16[2,4,128,128]{3,2,1,0:T(8,128)(2,1)S(1)}, u32[]{:S(2)}, u32[]{:S(2)}) collective-permute-start(bf16[2,4,128,128]{3,2,1,0:T(8,128)(2,1)} %get-tuple-element.80), channel_id=1, source_target_pairs={{0,1},{1,2},{2,3},{3,4},{4,5},{5,6},{6,7},{7,0},{8,9},{9,10},{10,1... | collective-permute-start | bytes 786440 | tf_op jit(solution)/shard_map/ppermute | solution.py:115
  83.3 12.6 %collective-permute-start.7 = (bf16[4,8,128,128]{3,2,1,0:T(8,128)(2,1)}, bf16[4,8,128,128]{3,2,1,0:T(8,128)(2,1)}, u32[]{:S(2)}, u32[]{:S(2)}) collective-permute-start(bf16[4,8,128,128]{3,2,1,0:T(8,128)(2,1)} %add_convert_fusion.3), channel_id=1, source_target_pairs={{24,16},{25,17},{26,18},{27,19},{28,20},{29,21},{30,22},{31,23}} | collective-permute-start | bytes 3145736 | tf_op jit(solution)/shard_map/ppermute | solution.py:156
  87.1 13.8 %collective-permute-start.10 = (bf16[4,128,128]{2,1,0:T(8,128)(2,1)}, bf16[4,128,128]{2,1,0:T(8,128)(2,1)}, u32[]{:S(2)}, u32[]{:S(2)}) collective-permute-start(bf16[4,128,128]{2,1,0:T(8,128)(2,1)} %bitcast.103), channel_id=1, source_target_pairs={{0,7},{1,0},{2,1},{3,2},{4,3},{5,4},{6,5},{7,6},{8,15},{9,8},{10,9... | collective-permute-start | bytes 393224 | tf_op jit(solution)/shard_map/ppermute | solution.py:115
  87.8 14.8 %collective-permute-start.11 = (bf16[4,128,128]{2,1,0:T(8,128)(2,1)}, bf16[4,128,128]{2,1,0:T(8,128)(2,1)}, u32[]{:S(2)}, u32[]{:S(2)}) collective-permute-start(bf16[4,128,128]{2,1,0:T(8,128)(2,1)} %bitcast.102), channel_id=1, source_target_pairs={{0,6},{1,7},{2,0},{3,1},{4,2},{5,3},{6,4},{7,5},{8,14},{9,15},{10,... | collective-permute-start | bytes 393224 | tf_op jit(solution)/shard_map/ppermute | solution.py:115
  88.4 17.7 %collective-permute-start.12 = (bf16[4,128,128]{2,1,0:T(8,128)(2,1)}, bf16[4,128,128]{2,1,0:T(8,128)(2,1)}, u32[]{:S(2)}, u32[]{:S(2)}) collective-permute-start(bf16[4,128,128]{2,1,0:T(8,128)(2,1)} %bitcast.101), channel_id=1, source_target_pairs={{0,5},{1,6},{2,7},{3,0},{4,1},{5,2},{6,3},{7,4},{8,13},{9,14},{10,... | collective-permute-start | bytes 393224 | tf_op jit(solution)/shard_map/ppermute | solution.py:115
  92.3 20.4 %collective-permute-start.13 = (bf16[4,128,128]{2,1,0:T(8,128)(2,1)}, bf16[4,128,128]{2,1,0:T(8,128)(2,1)}, u32[]{:S(2)}, u32[]{:S(2)}) collective-permute-start(bf16[4,128,128]{2,1,0:T(8,128)(2,1)} %bitcast.100), channel_id=1, source_target_pairs={{0,4},{1,5},{2,6},{3,7},{4,0},{5,1},{6,2},{7,3},{8,12},{9,13},{10,... | collective-permute-start | bytes 393224 | tf_op jit(solution)/shard_map/ppermute | solution.py:115
  95.8 18.4 %collective-permute-start.14 = (bf16[4,128,128]{2,1,0:T(8,128)(2,1)}, bf16[4,128,128]{2,1,0:T(8,128)(2,1)S(1)}, u32[]{:S(2)}, u32[]{:S(2)}) collective-permute-start(bf16[4,128,128]{2,1,0:T(8,128)(2,1)} %bitcast.134), channel_id=1, source_target_pairs={{0,3},{1,4},{2,5},{3,6},{4,7},{5,0},{6,1},{7,2},{8,11},{9,12},{10,... | collective-permute-start | bytes 393224 | tf_op jit(solution)/shard_map/ppermute | solution.py:115
  100.9 14.4 %collective-permute-start.8 = (bf16[4,8,128,128]{3,2,1,0:T(8,128)(2,1)S(1)}, bf16[4,8,128,128]{3,2,1,0:T(8,128)(2,1)S(1)}, u32[]{:S(2)}, u32[]{:S(2)}) collective-permute-start(bf16[4,8,128,128]{3,2,1,0:T(8,128)(2,1)S(1)} %add_convert_fusion.2), channel_id=1, source_target_pairs={{16,8},{17,9},{18,10},{19,11},{20,12},{21,13},{22,14},{23,15}} | collective-permute-start | bytes 3145736 | tf_op jit(solution)/shard_map/ppermute | solution.py:156
  102.6 11.6 %collective-permute-start.15 = (bf16[4,128,128]{2,1,0:T(8,128)(2,1)S(1)}, bf16[4,128,128]{2,1,0:T(8,128)(2,1)S(1)}, u32[]{:S(2)}, u32[]{:S(2)}) collective-permute-start(bf16[4,128,128]{2,1,0:T(8,128)(2,1)S(1)} %bitcast.133), channel_id=1, source_target_pairs={{0,2},{1,3},{2,4},{3,5},{4,6},{5,7},{6,0},{7,1},{8,10},{9,11},{10,... | collective-permute-start | bytes 393224 | tf_op jit(solution)/shard_map/ppermute | solution.py:115
  106.2 8.1 %collective-permute-start.16 = (bf16[4,128,128]{2,1,0:T(8,128)(2,1)S(1)}, bf16[4,128,128]{2,1,0:T(8,128)(2,1)S(1)}, u32[]{:S(2)}, u32[]{:S(2)}) collective-permute-start(bf16[4,128,128]{2,1,0:T(8,128)(2,1)S(1)} %bitcast.132), channel_id=1, source_target_pairs={{0,1},{1,2},{2,3},{3,4},{4,5},{5,6},{6,7},{7,0},{8,9},{9,10},{10,1... | collective-permute-start | bytes 393224 | tf_op jit(solution)/shard_map/ppermute | solution.py:115
  117.0 4.6 %collective-permute-start.9 = (bf16[4,8,128,128]{3,2,1,0:T(8,128)(2,1)S(1)}, bf16[4,8,128,128]{3,2,1,0:T(8,128)(2,1)S(1)}, u32[]{:S(2)}, u32[]{:S(2)}) collective-permute-start(bf16[4,8,128,128]{3,2,1,0:T(8,128)(2,1)S(1)} %add_convert_fusion.1), channel_id=1, source_target_pairs={{8,0},{9,1},{10,2},{11,3},{12,4},{13,5},{14,6},{15,7}} | collective-permute-start | bytes 3145736 | tf_op jit(solution)/shard_map/ppermute | solution.py:156
  124.8 6.7 %copy-start.2 = (bf16[4,8,128,128]{3,2,1,0:T(8,128)(2,1)}, bf16[4,8,128,128]{3,2,1,0:T(8,128)(2,1)S(1)}, u32[]{:S(2)}) copy-start(bf16[4,8,128,128]{3,2,1,0:T(8,128)(2,1)S(1)} %get-tuple-element.97) | copy-start | bytes 3145732
  133.0 14.6 %collective-permute-start.17 = (bf16[2,4,128,128]{3,2,1,0:T(8,128)(2,1)}, bf16[2,4,128,128]{3,2,1,0:T(8,128)(2,1)S(1)}, u32[]{:S(2)}, u32[]{:S(2)}) collective-permute-start(bf16[2,4,128,128]{3,2,1,0:T(8,128)(2,1)} %get-tuple-element.74), channel_id=1, source_target_pairs={{0,7},{1,0},{2,1},{3,2},{4,3},{5,4},{6,5},{7,6},{8,15},{9,8},{10,9... | collective-permute-start | bytes 786440 | tf_op jit(solution)/shard_map/ppermute | solution.py:115
  137.0 14.6 %collective-permute-start.18 = (bf16[2,4,128,128]{3,2,1,0:T(8,128)(2,1)}, bf16[2,4,128,128]{3,2,1,0:T(8,128)(2,1)S(1)}, u32[]{:S(2)}, u32[]{:S(2)}) collective-permute-start(bf16[2,4,128,128]{3,2,1,0:T(8,128)(2,1)} %get-tuple-element.75), channel_id=1, source_target_pairs={{0,6},{1,7},{2,0},{3,1},{4,2},{5,3},{6,4},{7,5},{8,14},{9,15},{10,... | collective-permute-start | bytes 786440 | tf_op jit(solution)/shard_map/ppermute | solution.py:115
  137.0 8.4 %copy-start.3 = (bf16[4,8,128,128]{3,2,1,0:T(8,128)(2,1)S(1)}, bf16[4,8,128,128]{3,2,1,0:T(8,128)(2,1)}, u32[]{:S(2)}) copy-start(bf16[4,8,128,128]{3,2,1,0:T(8,128)(2,1)} %copy-done.2) | copy-start | bytes 3145732
  138.0 71.2 %all-to-all-start.1 = ((f32[1024,1,128]{2,1,0:T(1,128)}), f32[1024,1,128]{2,1,0:T(1,128)S(1)}, u32[]{:S(2)}, u32[]{:S(2)}) async-start(f32[1024,1,128]{2,1,0:T(1,128)} %bitcast.29), calls=%async_computation.1 | async-start | bytes 1048576 | tf_op jit(solution)/shard_map/all_to_all | solution.py:183
  141.6 3.9 %copy-start.14 = (bf16[2,4,128,128]{3,2,1,0:T(8,128)(2,1)S(1)}, bf16[2,4,128,128]{3,2,1,0:T(8,128)(2,1)}, u32[]{:S(2)}) copy-start(bf16[2,4,128,128]{3,2,1,0:T(8,128)(2,1)} %get-tuple-element.77) | copy-start | bytes 786436
  141.6 22.6 %collective-permute-start.19 = (bf16[2,4,128,128]{3,2,1,0:T(8,128)(2,1)}, bf16[2,4,128,128]{3,2,1,0:T(8,128)(2,1)S(1)}, u32[]{:S(2)}, u32[]{:S(2)}) collective-permute-start(bf16[2,4,128,128]{3,2,1,0:T(8,128)(2,1)} %get-tuple-element.76), channel_id=1, source_target_pairs={{0,5},{1,6},{2,7},{3,0},{4,1},{5,2},{6,3},{7,4},{8,13},{9,14},{10,... | collective-permute-start | bytes 786440 | tf_op jit(solution)/shard_map/ppermute | solution.py:115
  145.5 51.0 %collective-permute-start.21 = (bf16[2,4,128,128]{3,2,1,0:T(8,128)(2,1)S(1)}, bf16[2,4,128,128]{3,2,1,0:T(8,128)(2,1)S(1)}, u32[]{:S(2)}, u32[]{:S(2)}) collective-permute-start(bf16[2,4,128,128]{3,2,1,0:T(8,128)(2,1)S(1)} %get-tuple-element.79), channel_id=1, source_target_pairs={{0,3},{1,4},{2,5},{3,6},{4,7},{5,0},{6,1},{7,2},{8,11},{9,12},{10,... | collective-permute-start | bytes 786440 | tf_op jit(solution)/shard_map/ppermute | solution.py:115
  145.5 50.1 %collective-permute-start.20 = (bf16[2,4,128,128]{3,2,1,0:T(8,128)(2,1)S(1)}, bf16[2,4,128,128]{3,2,1,0:T(8,128)(2,1)S(1)}, u32[]{:S(2)}, u32[]{:S(2)}) collective-permute-start(bf16[2,4,128,128]{3,2,1,0:T(8,128)(2,1)S(1)} %copy-done.14), channel_id=1, source_target_pairs={{0,4},{1,5},{2,6},{3,7},{4,0},{5,1},{6,2},{7,3},{8,12},{9,13},{10,... | collective-permute-start | bytes 786440 | tf_op jit(solution)/shard_map/ppermute | solution.py:115
  147.6 49.6 %collective-permute-start.22 = (bf16[2,4,128,128]{3,2,1,0:T(8,128)(2,1)S(1)}, bf16[2,4,128,128]{3,2,1,0:T(8,128)(2,1)S(1)}, u32[]{:S(2)}, u32[]{:S(2)}) collective-permute-start(bf16[2,4,128,128]{3,2,1,0:T(8,128)(2,1)S(1)} %get-tuple-element.78), channel_id=1, source_target_pairs={{0,2},{1,3},{2,4},{3,5},{4,6},{5,7},{6,0},{7,1},{8,10},{9,11},{10,... | collective-permute-start | bytes 786440 | tf_op jit(solution)/shard_map/ppermute | solution.py:115
  151.6 46.4 %collective-permute-start.23 = (bf16[2,4,128,128]{3,2,1,0:T(8,128)(2,1)S(1)}, bf16[2,4,128,128]{3,2,1,0:T(8,128)(2,1)S(1)}, u32[]{:S(2)}, u32[]{:S(2)}) collective-permute-start(bf16[2,4,128,128]{3,2,1,0:T(8,128)(2,1)S(1)} %get-tuple-element.72), channel_id=1, source_target_pairs={{0,1},{1,2},{2,3},{3,4},{4,5},{5,6},{6,7},{7,0},{8,9},{9,10},{10,1... | collective-permute-start | bytes 786440 | tf_op jit(solution)/shard_map/ppermute | solution.py:115
  206.7 3.4 %copy-start.1 = (bf16[128,4096]{1,0:T(8,128)(2,1)S(1)}, bf16[128,4096]{1,0:T(8,128)(2,1)}, u32[]{:S(2)}) copy-start(bf16[128,4096]{1,0:T(8,128)(2,1)} %param.18) | copy-start | bytes 3145732
  (12 other events, 22.2 us)

commit v7 on v5

--- a/solution.py
+++ b/solution.py
@@ -130,15 +130,22 @@
     def head_major(rows):
         return jnp.transpose(rows.reshape(tok_rows, head_count, DH), (1, 0, 2))
 
-    stacked = jnp.stack([head_major(queries[0]), head_major(cotangent)])
-    stacked_heads = transpose_seq(stacked, 1, 2)
-    query_blocks = to_blocks(stacked_heads[0])
-    cot_blocks = to_blocks(stacked_heads[1])
+    kv_pick = (jnp.arange(seq_ways) * local_heads) // group_size
+    key_rows = jnp.transpose(key_heads[0].reshape(tok_rows, kv_count, DH), (1, 0, 2))[kv_pick]
+    per_target = jnp.concatenate(
+        [
+            head_major(queries[0]).reshape(seq_ways, local_heads, tok_rows, DH),
+            head_major(cotangent).reshape(seq_ways, local_heads, tok_rows, DH),
+            key_rows.reshape(seq_ways, 1, tok_rows, DH),
+        ],
+        axis=1,
+    ).reshape(seq_ways * (2 * local_heads + 1), tok_rows, DH)
+    stacked_heads = transpose_seq(per_target, 0, 1)
+    query_blocks = to_blocks(stacked_heads[:local_heads])
+    cot_blocks = to_blocks(stacked_heads[local_heads : 2 * local_heads])
+    key_flat = stacked_heads[2 * local_heads :]
     input_heads = transpose_seq(head_major(inputs[0]), 0, 1)
     values_both = key_pair(to_blocks(input_heads))
-    kv_pick = (jnp.arange(seq_ways) * local_heads) // group_size
-    key_rows = jnp.transpose(key_heads[0].reshape(tok_rows, kv_count, DH), (1, 0, 2))[kv_pick]
-    key_flat = lax.all_to_all(key_rows, "seq", split_axis=0, concat_axis=1, tiled=True)
     key_blocks = jnp.broadcast_to(
         key_flat.reshape(1, block_count, BLK, DH), (local_heads, block_count, BLK, DH)
     )
@@ -176,19 +183,36 @@
         score_scale,
         BLK,
     )
-    pair = jnp.stack([grad_query, held_out]).reshape(2, local_heads, seq_len, DH)
-    pair_out = transpose_seq(pair, 2, 1)
-    pair_rows = jnp.transpose(pair_out, (0, 2, 1, 3)).reshape(2, tok_rows, full_width)
     if local_heads == 1:
-        key_part = grad_key.reshape(seq_len, DH)
+        key_parts = [grad_key.reshape(1, seq_len, DH)]
     else:
-        key_part = jnp.sum(grad_key.astype(jnp.float32), axis=0).reshape(seq_len, DH)
-    key_out = lax.all_to_all(key_part[:, None, :], "seq", split_axis=0, concat_axis=1, tiled=True)
-    key_sum = jnp.sum(
-        key_out.reshape(tok_rows, kv_count, seq_ways // kv_count, DH).astype(jnp.float32), axis=2
-    )
-    key_final = key_sum.astype(jnp.bfloat16).reshape(tok_rows, kv_count * DH)
-    return (pair_rows[0][None], key_final[None], pair_rows[1][None])
+        key_sum_local = jnp.sum(grad_key.astype(jnp.float32), axis=0).reshape(seq_len, DH)
+        key_high = key_sum_local.astype(jnp.bfloat16)
+        key_low = (key_sum_local - key_high.astype(jnp.float32)).astype(jnp.bfloat16)
+        key_parts = [key_high[None], key_low[None]]
+    key_count = len(key_parts)
+    rows_out = jnp.concatenate(
+        [grad_query.reshape(local_heads, seq_len, DH), held_out.reshape(local_heads, seq_len, DH)]
+        + key_parts,
+        axis=0,
+    )
+    per_source = transpose_seq(rows_out, 1, 0).reshape(
+        seq_ways, 2 * local_heads + key_count, tok_rows, DH
+    )
+
+    def head_rows(part):
+        return jnp.transpose(part.reshape(head_count, tok_rows, DH), (1, 0, 2)).reshape(
+            tok_rows, full_width
+        )
+
+    query_rows = head_rows(per_source[:, :local_heads])
+    grad_rows = head_rows(per_source[:, local_heads : 2 * local_heads])
+    key_terms = jnp.sum(per_source[:, 2 * local_heads :].astype(jnp.float32), axis=1)
+    key_sum = jnp.sum(key_terms.reshape(kv_count, seq_ways // kv_count, tok_rows, DH), axis=1)
+    key_final = (
+        jnp.transpose(key_sum, (1, 0, 2)).astype(jnp.bfloat16).reshape(tok_rows, kv_count * DH)
+    )
+    return (query_rows[None], key_final[None], grad_rows[None])
 
 
 def solution(mesh):

time: 195 us -> 209 us (1.072); the launches traced: 192 us -> 208 us
  waiting for transfers between devices: 66 us -> 101 us
  starting transfers between devices: 55.2 us -> 27.1 us
  local copies, waits for them, and re-layouts: 44.9 us -> 53.8 us
    ppermute x21, waiting for transfers between devices: 63.8 us -> 98.4 us  [transpose_seq(): lax.ppermute(chunk, 'seq', [(s, (s + shift) % seq_ways) for s in range(se...]
    ppermute x21, starting transfers between devices: 38.6 us -> 21.3 us  [transpose_seq(): lax.ppermute(chunk, 'seq', [(s, (s + shift) % seq_ways) for s in range(se...]
    all_to_all x2 -> x0, starting transfers between devices: 11.7 us -> none  [the longest x1 6.05 us: on_device(): lax.all_to_all(key_part[:, None, :], 'seq', split_axis=0, concat_axis=1,...]
    another operation x3, local copies, waits for them, and re-layouts: 1.25 us -> 4.8 us  [the longest x2 2.55 us: on_device(): return (query_rows[None], key_final[None], grad_rows[None])]
    dynamic_slice x0 -> x2, local copies, waits for them, and re-layouts: none -> 2.69 us  [transpose_seq(): lax.dynamic_slice_in_dim(value, target * split_size, split_size, axis=spl...]
    unnamed x57 -> x46, local copies, waits for them, and re-layouts: 11.5 us -> 13.9 us
    convert_element_type x3, other arithmetic: 1.95 us -> 4.16 us  [value_grad(): (grad_blocks.astype(jnp.float32) + fold_value(key_terms, block_len, group...]
    dynamic_update_slice x23 -> x22, local copies, waits for them, and re-layouts: 19.8 us -> 18 us  [transpose_seq(): lax.dynamic_update_slice_in_dim(result, chunk, source * concat_size, axis...]
  transfers between devices with their start and end apart: 26 -> 24, of which waited for: 12 -> 14; matrix products, arithmetic and copies ran while one was open for 19% -> 16% of each run, Pallas kernels for 0% -> 0%
where the time goes in v7:
time: 209 us; the launch traced here: 208 us
  waiting for transfers between devices  101 us (48%)
  local copies, waits for them, and re-layouts  53.8 us (26%)
  starting transfers between devices  27.1 us (13%)
  other arithmetic  12.6 us (6%)
  matrix products  12.5 us (6%)
    ppermute x21, waiting for transfers between devices, transpose_seq(): lax.ppermute(chunk, 'seq', [(s, (s + shift) % seq_ways) for s in range(se...  98.4 us
    ppermute x21, starting transfers between devices, transpose_seq(): lax.ppermute(chunk, 'seq', [(s, (s + shift) % seq_ways) for s in range(se...  21.3 us
    dynamic_update_slice x22, local copies, waits for them, and re-layouts, transpose_seq(): lax.dynamic_update_slice_in_dim(result, chunk, source * concat_size, axis...  18 us
    unnamed x46, local copies, waits for them, and re-layouts  13.9 us
    ppermute x3, starting transfers between devices, on_device(): grad_in = lax.ppermute(new_grad, 'pipe', [(sender, sender - 1)])  5.8 us
    dot_general x4, matrix products, value_grad(): jnp.einsum('hbij,hbid->hbjd', probs_low, grad_blocks, preferred_element_t...  5.47 us
  transfers between devices with their start and end apart: 24, of which 14 were waited for; matrix products, arithmetic and copies ran while one was open for 16% of the time, Pallas kernels for 0%

profile of v7, /device:TPU:15, one launch (start us, length us, event | category | flops | bytes accessed | tf_op | source)
XLA Modules:
  0.0 208.0 jit_solution(3313775301469898993)
XLA Ops:
  4.9 1.8 broadcast_in_dim.50
  17.1 5.2 %collective-permute-done.1 = bf16[9,128,128]{2,1,0:T(8,128)(2,1)S(1)} collective-permute-done((bf16[9,128,128]{2,1,0:T(8,128)(2,1)S(1)}, bf16[9,128,128]{2,1,0:T(8,128)(2,1)S(1)}, u32[]{:S(2)}, u32[]{:S(2)}) %collective-permute-start.1) | collective-permute-done | bytes 294944 | tf_op jit(solution)/shard_map/ppermute | solution.py:118
  23.1 29.9 %collective-permute-done.2 = bf16[9,128,128]{2,1,0:T(8,128)(2,1)S(1)} collective-permute-done((bf16[9,128,128]{2,1,0:T(8,128)(2,1)S(1)}, bf16[9,128,128]{2,1,0:T(8,128)(2,1)S(1)}, u32[]{:S(2)}, u32[]{:S(2)}) %collective-permute-start.2) | collective-permute-done | bytes 294944 | tf_op jit(solution)/shard_map/ppermute | solution.py:118
  53.8 5.6 %collective-permute-done.3 = bf16[9,128,128]{2,1,0:T(8,128)(2,1)S(1)} collective-permute-done((bf16[9,128,128]{2,1,0:T(8,128)(2,1)S(1)}, bf16[9,128,128]{2,1,0:T(8,128)(2,1)S(1)}, u32[]{:S(2)}, u32[]{:S(2)}) %collective-permute-start.3) | collective-permute-done | bytes 294944 | tf_op jit(solution)/shard_map/ppermute | solution.py:118
  64.2 1.7 fusion.34
  71.0 2.2 %fusion.35 = (f32[4,8,128]{2,1,0:T(8,128)S(1)}, f32[4,8,128,256]{3,2,1,0:T(8,128)S(1)}) fusion(f32[4,8,128,256]{3,2,1,0:T(8,128)S(1)} %fusion.3, pred[8,128,256]{2,1,0:T(8,128)(4,1)S(1)} %copy-done.14), kind=kOutput, calls=%fused_computation.138 | output fusion | flops 6291711 | bytes 8667136 | tf_op jit(solution)/shard_map/sub | solution.py:53
  76.9 2.5 %collective-permute-start.7 = (bf16[4,8,128,128]{3,2,1,0:T(8,128)(2,1)S(1)}, bf16[4,8,128,128]{3,2,1,0:T(8,128)(2,1)S(1)}, u32[]{:S(2)}, u32[]{:S(2)}) collective-permute-start(bf16[4,8,128,128]{3,2,1,0:T(8,128)(2,1)S(1)} %add_convert_fusion.3), channel_id=1, source_target_pairs={{24,16},{25,17},{26,18},{27,19},{28,20},{29,21},{30,22},{31,23}} | collective-permute-start | bytes 3145736 | tf_op jit(solution)/shard_map/ppermute | solution.py:166
  79.4 2.2 %collective-permute-done.7 = bf16[4,8,128,128]{3,2,1,0:T(8,128)(2,1)S(1)} collective-permute-done((bf16[4,8,128,128]{3,2,1,0:T(8,128)(2,1)S(1)}, bf16[4,8,128,128]{3,2,1,0:T(8,128)(2,1)S(1)}, u32[]{:S(2)}, u32[]{:S(2)}) %collective-permute-start.7) | collective-permute-done | bytes 1048608 | tf_op jit(solution)/shard_map/ppermute | solution.py:166
  84.3 1.7 collective-permute-start.8
  86.0 2.4 %copy.131 = bf16[16,8,32,128]{3,2,1,0:T(8,128)(2,1)} copy(bf16[16,8,32,128]{3,1,2,0:T(8,128)(2,1)} %bitcast.126) | data formatting | bytes 2097152
  88.4 2.3 %constant_dynamic-slice_fusion.7 = (bf16[128,4,128]{2,1,0:T(4,128)(2,1)S(1)}, bf16[128,4,128]{2,1,0:T(4,128)(2,1)S(1)}, bf16[128,4,128]{2,1,0:T(4,128)(2,1)S(1)}...) fusion(bf16[128,32,128]{2,1,0:T(8,128)(2,1)} %bitcast.114, ...), kind=kLoop, calls=%fused_computation.91 | loop fusion | bytes 2097184 | tf_op jit(solution)/shard_map/dynamic-slice.43
  92.7 4.1 %collective-permute-start.12 = (bf16[4,128,128]{2,1,0:T(8,128)(2,1)}, bf16[4,128,128]{2,1,0:T(8,128)(2,1)}, u32[]{:S(2)}, u32[]{:S(2)}) collective-permute-start(bf16[4,128,128]{2,1,0:T(8,128)(2,1)} %bitcast.100), channel_id=1, source_target_pairs={{0,3},{1,4},{2,5},{3,6},{4,7},{5,0},{6,1},{7,2},{8,11},{9,12},{10,... | collective-permute-start | bytes 393224 | tf_op jit(solution)/shard_map/ppermute | solution.py:118
  97.4 2.0 fusion.38
  100.0 2.6 %add_convert_fusion.1 = bf16[4,8,128,128]{3,2,1,0:T(8,128)(2,1)} fusion(f32[4,8,128,128]{3,2,1,0:T(8,128)S(1)} %fusion.21, bf16[4,8,128,128]{3,2,1,0:T(8,128)(2,1)} %collective-permute-done.8), kind=kLoop, calls=%fused_computation.23 | loop fusion | flops 1572864 | bytes 4194304 | tf_op jit(solution)/shard_map/convert_element_type | solution.py:61
  102.6 1.6 collective-permute-start.9
  106.8 1.7 collective-permute-start.14
  108.4 1.6 constant_dynamic-update-slice_fusion.13
  110.0 1.9 collective-permute-start.15
  112.0 1.6 constant_dynamic-update-slice_fusion.12
  115.0 1.6 constant_dynamic-update-slice_fusion.11
  116.6 1.6 constant_dynamic-update-slice_fusion.10
  119.6 2.4 %collective-permute-done.16 = bf16[4,128,128]{2,1,0:T(8,128)(2,1)S(1)} collective-permute-done((bf16[4,128,128]{2,1,0:T(8,128)(2,1)S(1)}, bf16[4,128,128]{2,1,0:T(8,128)(2,1)S(1)}, u32[]{:S(2)}, u32[]{:S(2)}) %collective-permute-start.16) | collective-permute-done | bytes 131104 | tf_op jit(solution)/shard_map/ppermute | solution.py:118
  123.6 2.0 fusion.39
  127.4 2.2 %fusion.9 = (bf16[4,8,128,128]{3,2,1,0:T(8,128)(2,1)S(1)}, bf16[4,8,128,128]{3,2,1,0:T(8,128)(2,1)S(1)}) fusion(f32[4,8,128,128]{3,2,1,0:T(8,128)S(1)} %fusion.20, bf16[4,8,128,128]{3,2,1,0:T(8,128)(2,1)} %collective-permute-done.9, bf16[4,8,128,128]{3,2,1,0:T(8,128)(2,1)} %add_convert_fusion.1, bf16[4,8,128,128]{3,2,1,0:T(8,128)(2,1)} %add_convert_fusion.2, ...), kind=kLoop, calls=%fused_computation.35 | loop fusion | flops 4718592 | bytes 11534339 | tf_op jit(solution)/shard_map/jit(_where)/select_n | solution.py:171
  129.8 2.2 %multiply_reduce_fusion = f32[4,8,128]{2,1,0:T(8,128)S(1)} fusion(bf16[4,8,128,128]{3,2,1,0:T(8,128)(2,1)S(1)} %get-tuple-element.91, bf16[4,8,128,256]{3,2,1,0:T(8,128)(2,1)S(1)} %fusion.8, bf16[4,8,128,128]{3,2,1,0:T(8,128)(2,1)} %bitcast.26, bf16[4,8,128,128]{3,2,1,0:T(8,128)(2,1)S(1)} %broadcast_in_dim.57), kind=kOutput, calls=%fused_computation.22 | convolution fusion | flops 274198528 | bytes 5259264 | tf_op jit(solution)/shard_map/hbij,hbjd->hbid/dot_general | solution.py:69
  132.3 2.6 %multiply_convert_fusion = bf16[4,8,128,256]{3,2,1,0:T(8,128)(2,1)S(1)} fusion(bf16[4,8,128,128]{3,2,1,0:T(8,128)(2,1)S(1)} %get-tuple-element.91, f32[4,8,128]{2,1,0:T(8,128)S(1)} %multiply_reduce_fusion, bf16[4,8,128,128]{3,2,1,0:T(8,128)(2,1)} %bitcast.26, bf16[4,8,128,128]{3,2,1,0:T(8,128)(2,1)S(1)} %broadcast_in_dim.57, ...), kind=kOutput, calls=%fused_computation.2 | convolution fusion | flops 276824064 | bytes 9469952 | tf_op jit(solution)/shard_map/hbid,hbjd->hbij/dot_general | solution.py:73
  139.9 4.4 %collective-permute-start.19 = (bf16[10,128,128]{2,1,0:T(8,128)(2,1)}, bf16[10,128,128]{2,1,0:T(8,128)(2,1)}, u32[]{:S(2)}, u32[]{:S(2)}) collective-permute-start(bf16[10,128,128]{2,1,0:T(8,128)(2,1)} %get-tuple-element.76), channel_id=1, source_target_pairs={{0,3},{1,4},{2,5},{3,6},{4,7},{5,0},{6,1},{7,2},{8,11},{9,12},{10,... | collective-permute-start | bytes 983048 | tf_op jit(solution)/shard_map/ppermute | solution.py:118
  145.8 2.2 %collective-permute-done.17 = bf16[10,128,128]{2,1,0:T(8,128)(2,1)} collective-permute-done((bf16[10,128,128]{2,1,0:T(8,128)(2,1)}, bf16[10,128,128]{2,1,0:T(8,128)(2,1)}, u32[]{:S(2)}, u32[]{:S(2)}) %collective-permute-start.17) | collective-permute-done | bytes 327712 | tf_op jit(solution)/shard_map/ppermute | solution.py:118
  149.0 4.8 %collective-permute-done.18 = bf16[10,128,128]{2,1,0:T(8,128)(2,1)} collective-permute-done((bf16[10,128,128]{2,1,0:T(8,128)(2,1)}, bf16[10,128,128]{2,1,0:T(8,128)(2,1)}, u32[]{:S(2)}, u32[]{:S(2)}) %collective-permute-start.18) | collective-permute-done | bytes 327712 | tf_op jit(solution)/shard_map/ppermute | solution.py:118
  154.8 33.0 %collective-permute-done.19 = bf16[10,128,128]{2,1,0:T(8,128)(2,1)} collective-permute-done((bf16[10,128,128]{2,1,0:T(8,128)(2,1)}, bf16[10,128,128]{2,1,0:T(8,128)(2,1)}, u32[]{:S(2)}, u32[]{:S(2)}) %collective-permute-start.19) | collective-permute-done | bytes 327712 | tf_op jit(solution)/shard_map/ppermute | solution.py:118
  188.8 6.0 %collective-permute-done.20 = bf16[10,128,128]{2,1,0:T(8,128)(2,1)S(1)} collective-permute-done((bf16[10,128,128]{2,1,0:T(8,128)(2,1)}, bf16[10,128,128]{2,1,0:T(8,128)(2,1)S(1)}, u32[]{:S(2)}, u32[]{:S(2)}) %collective-permute-start.20) | collective-permute-done | bytes 327712 | tf_op jit(solution)/shard_map/ppermute | solution.py:118
  194.9 5.8 %collective-permute-done.22 = bf16[10,128,128]{2,1,0:T(8,128)(2,1)S(1)} collective-permute-done((bf16[10,128,128]{2,1,0:T(8,128)(2,1)S(1)}, bf16[10,128,128]{2,1,0:T(8,128)(2,1)S(1)}, u32[]{:S(2)}, u32[]{:S(2)}) %collective-permute-start.22) | collective-permute-done | bytes 327712 | tf_op jit(solution)/shard_map/ppermute | solution.py:118
  (152 shorter events, 61.5 us)
Async XLA Ops:
  0.6 2.1 %copy-start.13 = (bf16[128,4096]{1,0:T(8,128)(2,1)S(1)}, bf16[128,4096]{1,0:T(8,128)(2,1)}, u32[]{:S(2)}) copy-start(bf16[128,4096]{1,0:T(8,128)(2,1)} %param.18) | copy-start | bytes 3145732
  6.7 7.4 %copy-start.16 = (s32[8]{0:T(128)S(1)}, s32[8]{0:T(128)}, u32[]{:S(2)}) copy-start(s32[8]{0:T(128)} %param.19) | copy-start | bytes 100
  8.2 7.9 %collective-permute-start = (bf16[9,128,128]{2,1,0:T(8,128)(2,1)S(1)}, bf16[9,128,128]{2,1,0:T(8,128)(2,1)S(1)}, u32[]{:S(2)}, u32[]{:S(2)}) collective-permute-start(bf16[9,128,128]{2,1,0:T(8,128)(2,1)S(1)} %get-tuple-element.88), channel_id=1, source_target_pairs={{0,1},{1,2},{2,3},{3,4},{4,5},{5,6},{6,7},{7,0},{8,9},{9,10},{10,1... | collective-permute-start | bytes 884744 | tf_op jit(solution)/shard_map/ppermute | solution.py:118
  9.4 12.9 %collective-permute-start.1 = (bf16[9,128,128]{2,1,0:T(8,128)(2,1)S(1)}, bf16[9,128,128]{2,1,0:T(8,128)(2,1)S(1)}, u32[]{:S(2)}, u32[]{:S(2)}) collective-permute-start(bf16[9,128,128]{2,1,0:T(8,128)(2,1)S(1)} %get-tuple-element.87), channel_id=1, source_target_pairs={{0,2},{1,3},{2,4},{3,5},{4,6},{5,7},{6,0},{7,1},{8,10},{9,11},{10,... | collective-permute-start | bytes 884744 | tf_op jit(solution)/shard_map/ppermute | solution.py:118
  10.7 42.3 %collective-permute-start.2 = (bf16[9,128,128]{2,1,0:T(8,128)(2,1)S(1)}, bf16[9,128,128]{2,1,0:T(8,128)(2,1)S(1)}, u32[]{:S(2)}, u32[]{:S(2)}) collective-permute-start(bf16[9,128,128]{2,1,0:T(8,128)(2,1)S(1)} %get-tuple-element.86), channel_id=1, source_target_pairs={{0,3},{1,4},{2,5},{3,6},{4,7},{5,0},{6,1},{7,2},{8,11},{9,12},{10,... | collective-permute-start | bytes 884744 | tf_op jit(solution)/shard_map/ppermute | solution.py:118
  11.7 47.7 %collective-permute-start.3 = (bf16[9,128,128]{2,1,0:T(8,128)(2,1)S(1)}, bf16[9,128,128]{2,1,0:T(8,128)(2,1)S(1)}, u32[]{:S(2)}, u32[]{:S(2)}) collective-permute-start(bf16[9,128,128]{2,1,0:T(8,128)(2,1)S(1)} %get-tuple-element.85), channel_id=1, source_target_pairs={{0,4},{1,5},{2,6},{3,7},{4,0},{5,1},{6,2},{7,3},{8,12},{9,13},{10,... | collective-permute-start | bytes 884744 | tf_op jit(solution)/shard_map/ppermute | solution.py:118
  13.0 47.1 %collective-permute-start.4 = (bf16[9,128,128]{2,1,0:T(8,128)(2,1)S(1)}, bf16[9,128,128]{2,1,0:T(8,128)(2,1)S(1)}, u32[]{:S(2)}, u32[]{:S(2)}) collective-permute-start(bf16[9,128,128]{2,1,0:T(8,128)(2,1)S(1)} %get-tuple-element.84), channel_id=1, source_target_pairs={{0,5},{1,6},{2,7},{3,0},{4,1},{5,2},{6,3},{7,4},{8,13},{9,14},{10,... | collective-permute-start | bytes 884744 | tf_op jit(solution)/shard_map/ppermute | solution.py:118
  16.0 46.2 %collective-permute-start.5 = (bf16[9,128,128]{2,1,0:T(8,128)(2,1)S(1)}, bf16[9,128,128]{2,1,0:T(8,128)(2,1)S(1)}, u32[]{:S(2)}, u32[]{:S(2)}) collective-permute-start(bf16[9,128,128]{2,1,0:T(8,128)(2,1)S(1)} %get-tuple-element.83), channel_id=1, source_target_pairs={{0,6},{1,7},{2,0},{3,1},{4,2},{5,3},{6,4},{7,5},{8,14},{9,15},{10,... | collective-permute-start | bytes 884744 | tf_op jit(solution)/shard_map/ppermute | solution.py:118
  22.3 41.1 %collective-permute-start.6 = (bf16[9,128,128]{2,1,0:T(8,128)(2,1)S(1)}, bf16[9,128,128]{2,1,0:T(8,128)(2,1)S(1)}, u32[]{:S(2)}, u32[]{:S(2)}) collective-permute-start(bf16[9,128,128]{2,1,0:T(8,128)(2,1)S(1)} %get-tuple-element.82), channel_id=1, source_target_pairs={{0,7},{1,0},{2,1},{3,2},{4,3},{5,4},{6,5},{7,6},{8,15},{9,8},{10,9... | collective-permute-start | bytes 884744 | tf_op jit(solution)/shard_map/ppermute | solution.py:118
  65.9 2.4 %copy-start = (bf16[4,1024,128]{2,1,0:T(8,128)(2,1)}, bf16[4,1024,128]{2,1,0:T(8,128)(2,1)S(1)}, u32[]{:S(2)}) copy-start(bf16[4,1024,128]{2,1,0:T(8,128)(2,1)S(1)} %get-tuple-element.81) | copy-start | bytes 3145732
  76.9 2.5 %copy-start.10 = (bf16[4,8,128,128]{3,2,1,0:T(8,128)(2,1)}, bf16[4,8,128,128]{3,2,1,0:T(8,128)(2,1)S(1)}, u32[]{:S(2)}) copy-start(bf16[4,8,128,128]{3,2,1,0:T(8,128)(2,1)S(1)} %add_convert_fusion.3) | copy-start | bytes 3145732
  76.9 4.7 %collective-permute-start.7 = (bf16[4,8,128,128]{3,2,1,0:T(8,128)(2,1)S(1)}, bf16[4,8,128,128]{3,2,1,0:T(8,128)(2,1)S(1)}, u32[]{:S(2)}, u32[]{:S(2)}) collective-permute-start(bf16[4,8,128,128]{3,2,1,0:T(8,128)(2,1)S(1)} %add_convert_fusion.3), channel_id=1, source_target_pairs={{24,16},{25,17},{26,18},{27,19},{28,20},{29,21},{30,22},{31,23}} | collective-permute-start | bytes 3145736 | tf_op jit(solution)/shard_map/ppermute | solution.py:166
  84.3 13.2 %collective-permute-start.8 = (bf16[4,8,128,128]{3,2,1,0:T(8,128)(2,1)}, bf16[4,8,128,128]{3,2,1,0:T(8,128)(2,1)}, u32[]{:S(2)}, u32[]{:S(2)}) collective-permute-start(bf16[4,8,128,128]{3,2,1,0:T(8,128)(2,1)} %add_convert_fusion.2), channel_id=1, source_target_pairs={{16,8},{17,9},{18,10},{19,11},{20,12},{21,13},{22,14},{23,15}} | collective-permute-start | bytes 3145736 | tf_op jit(solution)/shard_map/ppermute | solution.py:166
  91.3 15.4 %collective-permute-start.10 = (bf16[4,128,128]{2,1,0:T(8,128)(2,1)}, bf16[4,128,128]{2,1,0:T(8,128)(2,1)}, u32[]{:S(2)}, u32[]{:S(2)}) collective-permute-start(bf16[4,128,128]{2,1,0:T(8,128)(2,1)} %bitcast.102), channel_id=1, source_target_pairs={{0,1},{1,2},{2,3},{3,4},{4,5},{5,6},{6,7},{7,0},{8,9},{9,10},{10,1... | collective-permute-start | bytes 393224 | tf_op jit(solution)/shard_map/ppermute | solution.py:118
  92.0 18.0 %collective-permute-start.11 = (bf16[4,128,128]{2,1,0:T(8,128)(2,1)}, bf16[4,128,128]{2,1,0:T(8,128)(2,1)}, u32[]{:S(2)}, u32[]{:S(2)}) collective-permute-start(bf16[4,128,128]{2,1,0:T(8,128)(2,1)} %bitcast.101), channel_id=1, source_target_pairs={{0,2},{1,3},{2,4},{3,5},{4,6},{5,7},{6,0},{7,1},{8,10},{9,11},{10,... | collective-permute-start | bytes 393224 | tf_op jit(solution)/shard_map/ppermute | solution.py:118
  92.7 20.9 %collective-permute-start.12 = (bf16[4,128,128]{2,1,0:T(8,128)(2,1)}, bf16[4,128,128]{2,1,0:T(8,128)(2,1)}, u32[]{:S(2)}, u32[]{:S(2)}) collective-permute-start(bf16[4,128,128]{2,1,0:T(8,128)(2,1)} %bitcast.100), channel_id=1, source_target_pairs={{0,3},{1,4},{2,5},{3,6},{4,7},{5,0},{6,1},{7,2},{8,11},{9,12},{10,... | collective-permute-start | bytes 393224 | tf_op jit(solution)/shard_map/ppermute | solution.py:118
  97.4 19.2 %collective-permute-start.13 = (bf16[4,128,128]{2,1,0:T(8,128)(2,1)}, bf16[4,128,128]{2,1,0:T(8,128)(2,1)}, u32[]{:S(2)}, u32[]{:S(2)}) collective-permute-start(bf16[4,128,128]{2,1,0:T(8,128)(2,1)} %bitcast.99), channel_id=1, source_target_pairs={{0,4},{1,5},{2,6},{3,7},{4,0},{5,1},{6,2},{7,3},{8,12},{9,13},{10,... | collective-permute-start | bytes 393224 | tf_op jit(solution)/shard_map/ppermute | solution.py:118
  102.6 21.0 %collective-permute-start.9 = (bf16[4,8,128,128]{3,2,1,0:T(8,128)(2,1)}, bf16[4,8,128,128]{3,2,1,0:T(8,128)(2,1)}, u32[]{:S(2)}, u32[]{:S(2)}) collective-permute-start(bf16[4,8,128,128]{3,2,1,0:T(8,128)(2,1)} %add_convert_fusion.1), channel_id=1, source_target_pairs={{8,0},{9,1},{10,2},{11,3},{12,4},{13,5},{14,6},{15,7}} | collective-permute-start | bytes 3145736 | tf_op jit(solution)/shard_map/ppermute | solution.py:166
  106.8 11.5 %collective-permute-start.14 = (bf16[4,128,128]{2,1,0:T(8,128)(2,1)}, bf16[4,128,128]{2,1,0:T(8,128)(2,1)S(1)}, u32[]{:S(2)}, u32[]{:S(2)}) collective-permute-start(bf16[4,128,128]{2,1,0:T(8,128)(2,1)} %bitcast.132), channel_id=1, source_target_pairs={{0,5},{1,6},{2,7},{3,0},{4,1},{5,2},{6,3},{7,4},{8,13},{9,14},{10,... | collective-permute-start | bytes 393224 | tf_op jit(solution)/shard_map/ppermute | solution.py:118
  110.0 8.9 %collective-permute-start.15 = (bf16[4,128,128]{2,1,0:T(8,128)(2,1)S(1)}, bf16[4,128,128]{2,1,0:T(8,128)(2,1)S(1)}, u32[]{:S(2)}, u32[]{:S(2)}) collective-permute-start(bf16[4,128,128]{2,1,0:T(8,128)(2,1)S(1)} %bitcast.131), channel_id=1, source_target_pairs={{0,6},{1,7},{2,0},{3,1},{4,2},{5,3},{6,4},{7,5},{8,14},{9,15},{10,... | collective-permute-start | bytes 393224 | tf_op jit(solution)/shard_map/ppermute | solution.py:118
  113.6 8.4 %collective-permute-start.16 = (bf16[4,128,128]{2,1,0:T(8,128)(2,1)S(1)}, bf16[4,128,128]{2,1,0:T(8,128)(2,1)S(1)}, u32[]{:S(2)}, u32[]{:S(2)}) collective-permute-start(bf16[4,128,128]{2,1,0:T(8,128)(2,1)S(1)} %bitcast.130), channel_id=1, source_target_pairs={{0,7},{1,0},{2,1},{3,2},{4,3},{5,4},{6,5},{7,6},{8,15},{9,8},{10,9... | collective-permute-start | bytes 393224 | tf_op jit(solution)/shard_map/ppermute | solution.py:118
  129.8 2.5 %copy-start.9 = (f32[4,8,128,256]{3,2,1,0:T(8,128)S(1)}, f32[4,8,128,256]{3,2,1,0:T(8,128)}, u32[]{:S(2)}) copy-start(f32[4,8,128,256]{3,2,1,0:T(8,128)} %copy-done.8) | copy-start | bytes 12582916
  132.3 2.6 %copy-start.5 = (bf16[4,8,128,128]{3,2,1,0:T(8,128)(2,1)S(1)}, bf16[4,8,128,128]{3,2,1,0:T(8,128)(2,1)}, u32[]{:S(2)}) copy-start(bf16[4,8,128,128]{3,2,1,0:T(8,128)(2,1)} %copy-done.4) | copy-start | bytes 3145732
  132.3 2.6 %copy-start.7 = (bf16[4,8,128,128]{3,2,1,0:T(8,128)(2,1)S(1)}, bf16[4,8,128,128]{3,2,1,0:T(8,128)(2,1)}, u32[]{:S(2)}) copy-start(bf16[4,8,128,128]{3,2,1,0:T(8,128)(2,1)} %copy-done.6) | copy-start | bytes 3145732
  139.9 8.0 %collective-permute-start.17 = (bf16[10,128,128]{2,1,0:T(8,128)(2,1)}, bf16[10,128,128]{2,1,0:T(8,128)(2,1)}, u32[]{:S(2)}, u32[]{:S(2)}) collective-permute-start(bf16[10,128,128]{2,1,0:T(8,128)(2,1)} %get-tuple-element.78), channel_id=1, source_target_pairs={{0,1},{1,2},{2,3},{3,4},{4,5},{5,6},{6,7},{7,0},{8,9},{9,10},{10,1... | collective-permute-start | bytes 983048 | tf_op jit(solution)/shard_map/ppermute | solution.py:118
  139.9 13.9 %collective-permute-start.18 = (bf16[10,128,128]{2,1,0:T(8,128)(2,1)}, bf16[10,128,128]{2,1,0:T(8,128)(2,1)}, u32[]{:S(2)}, u32[]{:S(2)}) collective-permute-start(bf16[10,128,128]{2,1,0:T(8,128)(2,1)} %get-tuple-element.77), channel_id=1, source_target_pairs={{0,2},{1,3},{2,4},{3,5},{4,6},{5,7},{6,0},{7,1},{8,10},{9,11},{10,... | collective-permute-start | bytes 983048 | tf_op jit(solution)/shard_map/ppermute | solution.py:118
  139.9 47.9 %collective-permute-start.19 = (bf16[10,128,128]{2,1,0:T(8,128)(2,1)}, bf16[10,128,128]{2,1,0:T(8,128)(2,1)}, u32[]{:S(2)}, u32[]{:S(2)}) collective-permute-start(bf16[10,128,128]{2,1,0:T(8,128)(2,1)} %get-tuple-element.76), channel_id=1, source_target_pairs={{0,3},{1,4},{2,5},{3,6},{4,7},{5,0},{6,1},{7,2},{8,11},{9,12},{10,... | collective-permute-start | bytes 983048 | tf_op jit(solution)/shard_map/ppermute | solution.py:118
  144.3 50.5 %collective-permute-start.20 = (bf16[10,128,128]{2,1,0:T(8,128)(2,1)}, bf16[10,128,128]{2,1,0:T(8,128)(2,1)S(1)}, u32[]{:S(2)}, u32[]{:S(2)}) collective-permute-start(bf16[10,128,128]{2,1,0:T(8,128)(2,1)} %get-tuple-element.75), channel_id=1, source_target_pairs={{0,4},{1,5},{2,6},{3,7},{4,0},{5,1},{6,2},{7,3},{8,12},{9,13},{10,... | collective-permute-start | bytes 983048 | tf_op jit(solution)/shard_map/ppermute | solution.py:118
  144.3 50.6 %collective-permute-start.21 = (bf16[10,128,128]{2,1,0:T(8,128)(2,1)}, bf16[10,128,128]{2,1,0:T(8,128)(2,1)S(1)}, u32[]{:S(2)}, u32[]{:S(2)}) collective-permute-start(bf16[10,128,128]{2,1,0:T(8,128)(2,1)} %get-tuple-element.74), channel_id=1, source_target_pairs={{0,5},{1,6},{2,7},{3,0},{4,1},{5,2},{6,3},{7,4},{8,13},{9,14},{10,... | collective-permute-start | bytes 983048 | tf_op jit(solution)/shard_map/ppermute | solution.py:118
  147.9 52.8 %collective-permute-start.22 = (bf16[10,128,128]{2,1,0:T(8,128)(2,1)S(1)}, bf16[10,128,128]{2,1,0:T(8,128)(2,1)S(1)}, u32[]{:S(2)}, u32[]{:S(2)}) collective-permute-start(bf16[10,128,128]{2,1,0:T(8,128)(2,1)S(1)} %get-tuple-element.73), channel_id=1, source_target_pairs={{0,6},{1,7},{2,0},{3,1},{4,2},{5,3},{6,4},{7,5},{8,14},{9,15},{10,... | collective-permute-start | bytes 983048 | tf_op jit(solution)/shard_map/ppermute | solution.py:118
  153.8 48.1 %collective-permute-start.23 = (bf16[10,128,128]{2,1,0:T(8,128)(2,1)S(1)}, bf16[10,128,128]{2,1,0:T(8,128)(2,1)S(1)}, u32[]{:S(2)}, u32[]{:S(2)}) collective-permute-start(bf16[10,128,128]{2,1,0:T(8,128)(2,1)S(1)} %get-tuple-element.72), channel_id=1, source_target_pairs={{0,7},{1,0},{2,1},{3,2},{4,3},{5,4},{6,5},{7,6},{8,15},{9,8},{10,9... | collective-permute-start | bytes 983048 | tf_op jit(solution)/shard_map/ppermute | solution.py:118
  203.1 2.0 copy-start.12
  (9 other events, 11.2 us)

commit v8 on v5

--- a/solution.py
+++ b/solution.py
@@ -130,12 +130,11 @@
     def head_major(rows):
         return jnp.transpose(rows.reshape(tok_rows, head_count, DH), (1, 0, 2))
 
-    stacked = jnp.stack([head_major(queries[0]), head_major(cotangent)])
+    stacked = jnp.stack([head_major(queries[0]), head_major(cotangent), head_major(inputs[0])])
     stacked_heads = transpose_seq(stacked, 1, 2)
     query_blocks = to_blocks(stacked_heads[0])
     cot_blocks = to_blocks(stacked_heads[1])
-    input_heads = transpose_seq(head_major(inputs[0]), 0, 1)
-    values_both = key_pair(to_blocks(input_heads))
+    values_both = key_pair(to_blocks(stacked_heads[2]))
     kv_pick = (jnp.arange(seq_ways) * local_heads) // group_size
     key_rows = jnp.transpose(key_heads[0].reshape(tok_rows, kv_count, DH), (1, 0, 2))[kv_pick]
     key_flat = lax.all_to_all(key_rows, "seq", split_axis=0, concat_axis=1, tiled=True)

time: 195 us -> 218 us (1.12)
  the two profiles are of different devices: /device:TPU:15 before, /device:TPU:24 now
where the time goes in v8:
time: 218 us; the launch traced here: 217 us
  starting transfers between devices  88.9 us (41%)
  waiting for transfers between devices  64.9 us (30%)
  local copies, waits for them, and re-layouts  40.8 us (19%)
  other arithmetic  11.9 us (5%)
  matrix products  8.87 us (4%)
    ppermute x14, starting transfers between devices, transpose_seq(): lax.ppermute(chunk, 'seq', [(s, (s + shift) % seq_ways) for s in range(se...  75 us
    ppermute x14, waiting for transfers between devices, transpose_seq(): lax.ppermute(chunk, 'seq', [(s, (s + shift) % seq_ways) for s in range(se...  45.7 us
    ppermute x3, waiting for transfers between devices, on_device(): grad_in = lax.ppermute(new_grad, 'pipe', [(sender, sender - 1)])  19.2 us
    dynamic_update_slice x15, local copies, waits for them, and re-layouts, transpose_seq(): lax.dynamic_update_slice_in_dim(result, chunk, source * concat_size, axis...  13.3 us
    unnamed x50, local copies, waits for them, and re-layouts  10.6 us
    all_to_all x1, starting transfers between devices, on_device(): lax.all_to_all(key_rows, 'seq', split_axis=0, concat_axis=1, tiled=True)  5.85 us
    all_to_all x1, starting transfers between devices, on_device(): lax.all_to_all(key_part[:, None, :], 'seq', split_axis=0, concat_axis=1,...  5.11 us
  transfers between devices with their start and end apart: 19, of which 6 were waited for; matrix products, arithmetic and copies ran while one was open for 11% of the time, Pallas kernels for 0%

profile of v8, /device:TPU:24, one launch (start us, length us, event | category | flops | bytes accessed | tf_op | source)
XLA Modules:
  0.0 216.7 jit_solution(7071365649713611093)
XLA Ops:
  0.8 1.6 copy.134
  3.9 2.0 copy_bitcast_fusion
  6.3 2.2 %broadcast_in_dim.43 = bf16[3,4,1024,128]{3,2,1,0:T(8,128)(2,1)} broadcast(bf16[]{:T(256)} %constant.260.clone.1), dimensions={} | broadcast | bytes 3145730 | tf_op jit(solution)/shard_map/broadcast_in_dim | solution.py:113
  8.5 1.5 constant_dynamic-slice_fusion
  10.0 1.5 collective-permute-start
  11.8 2.5 %collective-permute-start.2 = (bf16[3,4,128,128]{3,2,1,0:T(8,128)(2,1)S(1)}, bf16[3,4,128,128]{3,2,1,0:T(8,128)(2,1)}, u32[]{:S(2)}, u32[]{:S(2)}) collective-permute-start(bf16[3,4,128,128]{3,2,1,0:T(8,128)(2,1)S(1)} %get-tuple-element.75), channel_id=1, source_target_pairs={{0,3},{1,4},{2,5},{3,6},{4,7},{5,0},{6,1},{7,2},{8,11},{9,12},{10,... | collective-permute-start | bytes 1179656 | tf_op jit(solution)/shard_map/ppermute | solution.py:118
  14.5 2.8 %collective-permute-start.4 = (bf16[3,4,128,128]{3,2,1,0:T(8,128)(2,1)S(1)}, bf16[3,4,128,128]{3,2,1,0:T(8,128)(2,1)}, u32[]{:S(2)}, u32[]{:S(2)}) collective-permute-start(bf16[3,4,128,128]{3,2,1,0:T(8,128)(2,1)S(1)} %get-tuple-element.73), channel_id=1, source_target_pairs={{0,5},{1,6},{2,7},{3,0},{4,1},{5,2},{6,3},{7,4},{8,13},{9,14},{10,... | collective-permute-start | bytes 1179656 | tf_op jit(solution)/shard_map/ppermute | solution.py:118
  18.9 5.8 %all-to-all-start = ((bf16[8,128,128]{2,1,0:T(8,128)(2,1)}), bf16[8,128,128]{2,1,0:T(8,128)(2,1)S(1)}, u32[]{:S(2)}, u32[]{:S(2)}) async-start(bf16[8,128,128]{2,1,0:T(8,128)(2,1)} %gather_fusion), calls=%async_computation | async-start | bytes 524288 | tf_op jit(solution)/shard_map/all_to_all | solution.py:140
  26.3 1.8 constant_dynamic-update-slice_fusion.6
  28.2 32.1 %collective-permute-start.6 = (bf16[3,4,128,128]{3,2,1,0:T(8,128)(2,1)S(1)}, bf16[3,4,128,128]{3,2,1,0:T(8,128)(2,1)S(1)}, u32[]{:S(2)}, u32[]{:S(2)}) collective-permute-start(bf16[3,4,128,128]{3,2,1,0:T(8,128)(2,1)S(1)} %get-tuple-element.71), channel_id=1, source_target_pairs={{0,7},{1,0},{2,1},{3,2},{4,3},{5,4},{6,5},{7,6},{8,15},{9,8},{10,9... | collective-permute-start | bytes 1179656 | tf_op jit(solution)/shard_map/ppermute | solution.py:118
  60.2 1.8 constant_dynamic-update-slice_fusion.5
  62.1 14.2 %collective-permute-done.2 = bf16[3,4,128,128]{3,2,1,0:T(8,128)(2,1)} collective-permute-done((bf16[3,4,128,128]{3,2,1,0:T(8,128)(2,1)S(1)}, bf16[3,4,128,128]{3,2,1,0:T(8,128)(2,1)}, u32[]{:S(2)}, u32[]{:S(2)}) %collective-permute-start.2) | collective-permute-done | bytes 393248 | tf_op jit(solution)/shard_map/ppermute | solution.py:118
  76.3 1.9 constant_dynamic-update-slice_fusion.4
  78.1 1.8 constant_dynamic-update-slice_fusion.3
  80.0 1.8 constant_dynamic-update-slice_fusion.2
  83.5 3.0 %fusion.39 = (bf16[1,4,1024,128]{3,2,1,0:T(8,128)(2,1)}, bf16[1,4,1024,128]{3,2,1,0:T(8,128)(2,1)S(1)}, bf16[1,4,1024,128]{3,2,1,0:T(8,128)(2,1)S(1)}) fusion(bf16[3,4,1024,128]{3,2,1,0:T(8,128)(2,1)} %constant_dynamic-update-slice_fusion), kind=kLoop, calls=%fused_computation.125 | loop fusion | bytes 6291456 | tf_op jit(solution)/shard_map/slice | solution.py:137
  89.0 2.2 %fusion.41 = (f32[4,8,128]{2,1,0:T(8,128)S(1)}, f32[4,8,128,256]{3,2,1,0:T(8,128)S(1)}) fusion(f32[4,8,128,256]{3,2,1,0:T(8,128)S(1)} %fusion.3, pred[8,128,256]{2,1,0:T(8,128)(4,1)S(1)} %copy-done.20), kind=kOutput, calls=%fused_computation.127 | output fusion | flops 6291711 | bytes 8667136 | tf_op jit(solution)/shard_map/sub | solution.py:53
  101.4 1.5 collective-permute-start.9
  103.8 19.2 %collective-permute-done.9 = bf16[4,8,128,128]{3,2,1,0:T(8,128)(2,1)} collective-permute-done((bf16[4,8,128,128]{3,2,1,0:T(8,128)(2,1)}, bf16[4,8,128,128]{3,2,1,0:T(8,128)(2,1)}, u32[]{:S(2)}, u32[]{:S(2)}) %collective-permute-start.9) | collective-permute-done | bytes 1048608 | tf_op jit(solution)/shard_map/ppermute | solution.py:158
  123.0 2.0 fusion.45
  127.4 2.3 %fusion.9 = (bf16[4,8,128,128]{3,2,1,0:T(8,128)(2,1)S(1)}, bf16[4,8,128,128]{3,2,1,0:T(8,128)(2,1)S(1)}) fusion(f32[4,8,128,128]{3,2,1,0:T(8,128)S(1)} %fusion.27, bf16[4,8,128,128]{3,2,1,0:T(8,128)(2,1)} %collective-permute-done.9, bf16[4,8,128,128]{3,2,1,0:T(8,128)(2,1)} %add_convert_fusion.1, bf16[4,8,128,128]{3,2,1,0:T(8,128)(2,1)S(1)} %copy-done.17, ...), kind=kLoop, calls=%fused_computation.50 | loop fusion | flops 4718592 | bytes 11534339 | tf_op jit(solution)/shard_map/jit(_where)/select_n | solution.py:163
  130.7 1.4 copy-done.13
  132.1 1.5 multiply_convert_fusion
  137.4 7.2 %collective-permute-start.10 = (bf16[2,4,128,128]{3,2,1,0:T(8,128)(2,1)S(1)}, bf16[2,4,128,128]{3,2,1,0:T(8,128)(2,1)S(1)}, u32[]{:S(2)}, u32[]{:S(2)}) collective-permute-start(bf16[2,4,128,128]{3,2,1,0:T(8,128)(2,1)S(1)} %get-tuple-element.83), channel_id=1, source_target_pairs={{0,1},{1,2},{2,3},{3,4},{4,5},{5,6},{6,7},{7,0},{8,9},{9,10},{10,1... | collective-permute-start | bytes 786440 | tf_op jit(solution)/shard_map/ppermute | solution.py:118
  144.6 5.1 %all-to-all-start.1 = ((f32[1024,1,128]{2,1,0:T(1,128)}), f32[1024,1,128]{2,1,0:T(1,128)}, u32[]{:S(2)}, u32[]{:S(2)}) async-start(f32[1024,1,128]{2,1,0:T(1,128)} %bitcast.23), calls=%async_computation.1 | async-start | bytes 1048576 | tf_op jit(solution)/shard_map/all_to_all | solution.py:185
  149.7 1.5 collective-permute-start.14
  151.2 2.4 %collective-permute-start.11 = (bf16[2,4,128,128]{3,2,1,0:T(8,128)(2,1)S(1)}, bf16[2,4,128,128]{3,2,1,0:T(8,128)(2,1)S(1)}, u32[]{:S(2)}, u32[]{:S(2)}) collective-permute-start(bf16[2,4,128,128]{3,2,1,0:T(8,128)(2,1)S(1)} %get-tuple-element.84), channel_id=1, source_target_pairs={{0,2},{1,3},{2,4},{3,5},{4,6},{5,7},{6,0},{7,1},{8,10},{9,11},{10,... | collective-permute-start | bytes 786440 | tf_op jit(solution)/shard_map/ppermute | solution.py:118
  155.3 1.9 collective-permute-start.15
  157.4 13.3 %collective-permute-done.11 = bf16[2,4,128,128]{3,2,1,0:T(8,128)(2,1)S(1)} collective-permute-done((bf16[2,4,128,128]{3,2,1,0:T(8,128)(2,1)S(1)}, bf16[2,4,128,128]{3,2,1,0:T(8,128)(2,1)S(1)}, u32[]{:S(2)}, u32[]{:S(2)}) %collective-permute-start.11) | collective-permute-done | bytes 262176 | tf_op jit(solution)/shard_map/ppermute | solution.py:118
  170.7 21.1 %collective-permute-start.16 = (bf16[2,4,128,128]{3,2,1,0:T(8,128)(2,1)S(1)}, bf16[2,4,128,128]{3,2,1,0:T(8,128)(2,1)S(1)}, u32[]{:S(2)}, u32[]{:S(2)}) collective-permute-start(bf16[2,4,128,128]{3,2,1,0:T(8,128)(2,1)S(1)} %get-tuple-element.81), channel_id=1, source_target_pairs={{0,7},{1,0},{2,1},{3,2},{4,3},{5,4},{6,5},{7,6},{8,15},{9,8},{10,9... | collective-permute-start | bytes 786440 | tf_op jit(solution)/shard_map/ppermute | solution.py:118
  192.1 4.8 %collective-permute-done.12 = bf16[2,4,128,128]{3,2,1,0:T(8,128)(2,1)S(1)} collective-permute-done((bf16[2,4,128,128]{3,2,1,0:T(8,128)(2,1)S(1)}, bf16[2,4,128,128]{3,2,1,0:T(8,128)(2,1)S(1)}, u32[]{:S(2)}, u32[]{:S(2)}) %collective-permute-start.12) | collective-permute-done | bytes 262176 | tf_op jit(solution)/shard_map/ppermute | solution.py:118
  197.2 13.4 %collective-permute-done.13 = bf16[2,4,128,128]{3,2,1,0:T(8,128)(2,1)S(1)} collective-permute-done((bf16[2,4,128,128]{3,2,1,0:T(8,128)(2,1)S(1)}, bf16[2,4,128,128]{3,2,1,0:T(8,128)(2,1)S(1)}, u32[]{:S(2)}, u32[]{:S(2)}) %collective-permute-start.13) | collective-permute-done | bytes 262176 | tf_op jit(solution)/shard_map/ppermute | solution.py:118
  (132 shorter events, 36.3 us)
Async XLA Ops:
  0.6 3.0 %copy-start = (bf16[128,4096]{1,0:T(8,128)(2,1)S(1)}, bf16[128,4096]{1,0:T(8,128)(2,1)}, u32[]{:S(2)}) copy-start(bf16[128,4096]{1,0:T(8,128)(2,1)} %param.18) | copy-start | bytes 3145732
  0.6 1.7 copy-start.19
  8.5 8.8 %copy-start.21 = (bf16[1,128,512]{2,1,0:T(8,128)(2,1)S(1)}, bf16[1,128,512]{2,1,0:T(8,128)(2,1)}, u32[]{:S(2)}) copy-start(bf16[1,128,512]{2,1,0:T(8,128)(2,1)} %param.16) | copy-start | bytes 393220
  8.5 16.2 %copy-start.22 = (s32[8]{0:T(128)S(1)}, s32[8]{0:T(128)}, u32[]{:S(2)}) copy-start(s32[8]{0:T(128)} %param.19) | copy-start | bytes 100
  10.0 15.8 %collective-permute-start = (bf16[3,4,128,128]{3,2,1,0:T(8,128)(2,1)S(1)}, bf16[3,4,128,128]{3,2,1,0:T(8,128)(2,1)}, u32[]{:S(2)}, u32[]{:S(2)}) collective-permute-start(bf16[3,4,128,128]{3,2,1,0:T(8,128)(2,1)S(1)} %get-tuple-element.77), channel_id=1, source_target_pairs={{0,1},{1,2},{2,3},{3,4},{4,5},{5,6},{6,7},{7,0},{8,9},{9,10},{10,1... | collective-permute-start | bytes 1179656 | tf_op jit(solution)/shard_map/ppermute | solution.py:118
  11.6 16.6 %collective-permute-start.1 = (bf16[3,4,128,128]{3,2,1,0:T(8,128)(2,1)S(1)}, bf16[3,4,128,128]{3,2,1,0:T(8,128)(2,1)}, u32[]{:S(2)}, u32[]{:S(2)}) collective-permute-start(bf16[3,4,128,128]{3,2,1,0:T(8,128)(2,1)S(1)} %get-tuple-element.76), channel_id=1, source_target_pairs={{0,2},{1,3},{2,4},{3,5},{4,6},{5,7},{6,0},{7,1},{8,10},{9,11},{10,... | collective-permute-start | bytes 1179656 | tf_op jit(solution)/shard_map/ppermute | solution.py:118
  11.8 64.5 %collective-permute-start.2 = (bf16[3,4,128,128]{3,2,1,0:T(8,128)(2,1)S(1)}, bf16[3,4,128,128]{3,2,1,0:T(8,128)(2,1)}, u32[]{:S(2)}, u32[]{:S(2)}) collective-permute-start(bf16[3,4,128,128]{3,2,1,0:T(8,128)(2,1)S(1)} %get-tuple-element.75), channel_id=1, source_target_pairs={{0,3},{1,4},{2,5},{3,6},{4,7},{5,0},{6,1},{7,2},{8,11},{9,12},{10,... | collective-permute-start | bytes 1179656 | tf_op jit(solution)/shard_map/ppermute | solution.py:118
  14.3 63.9 %collective-permute-start.3 = (bf16[3,4,128,128]{3,2,1,0:T(8,128)(2,1)S(1)}, bf16[3,4,128,128]{3,2,1,0:T(8,128)(2,1)}, u32[]{:S(2)}, u32[]{:S(2)}) collective-permute-start(bf16[3,4,128,128]{3,2,1,0:T(8,128)(2,1)S(1)} %get-tuple-element.74), channel_id=1, source_target_pairs={{0,4},{1,5},{2,6},{3,7},{4,0},{5,1},{6,2},{7,3},{8,12},{9,13},{10,... | collective-permute-start | bytes 1179656 | tf_op jit(solution)/shard_map/ppermute | solution.py:118
  14.5 65.5 %collective-permute-start.4 = (bf16[3,4,128,128]{3,2,1,0:T(8,128)(2,1)S(1)}, bf16[3,4,128,128]{3,2,1,0:T(8,128)(2,1)}, u32[]{:S(2)}, u32[]{:S(2)}) collective-permute-start(bf16[3,4,128,128]{3,2,1,0:T(8,128)(2,1)S(1)} %get-tuple-element.73), channel_id=1, source_target_pairs={{0,5},{1,6},{2,7},{3,0},{4,1},{5,2},{6,3},{7,4},{8,13},{9,14},{10,... | collective-permute-start | bytes 1179656 | tf_op jit(solution)/shard_map/ppermute | solution.py:118
  18.9 67.8 %all-to-all-start = ((bf16[8,128,128]{2,1,0:T(8,128)(2,1)}), bf16[8,128,128]{2,1,0:T(8,128)(2,1)S(1)}, u32[]{:S(2)}, u32[]{:S(2)}) async-start(bf16[8,128,128]{2,1,0:T(8,128)(2,1)} %gather_fusion), calls=%async_computation | async-start | bytes 524288 | tf_op jit(solution)/shard_map/all_to_all | solution.py:140
  25.8 56.0 %collective-permute-start.5 = (bf16[3,4,128,128]{3,2,1,0:T(8,128)(2,1)S(1)}, bf16[3,4,128,128]{3,2,1,0:T(8,128)(2,1)S(1)}, u32[]{:S(2)}, u32[]{:S(2)}) collective-permute-start(bf16[3,4,128,128]{3,2,1,0:T(8,128)(2,1)S(1)} %get-tuple-element.72), channel_id=1, source_target_pairs={{0,6},{1,7},{2,0},{3,1},{4,2},{5,3},{6,4},{7,5},{8,14},{9,15},{10,... | collective-permute-start | bytes 1179656 | tf_op jit(solution)/shard_map/ppermute | solution.py:118
  28.2 54.5 %collective-permute-start.6 = (bf16[3,4,128,128]{3,2,1,0:T(8,128)(2,1)S(1)}, bf16[3,4,128,128]{3,2,1,0:T(8,128)(2,1)S(1)}, u32[]{:S(2)}, u32[]{:S(2)}) collective-permute-start(bf16[3,4,128,128]{3,2,1,0:T(8,128)(2,1)S(1)} %get-tuple-element.71), channel_id=1, source_target_pairs={{0,7},{1,0},{2,1},{3,2},{4,3},{5,4},{6,5},{7,6},{8,15},{9,8},{10,9... | collective-permute-start | bytes 1179656 | tf_op jit(solution)/shard_map/ppermute | solution.py:118
  86.6 2.1 copy-start.2
  91.2 1.9 copy-start.12
  94.9 1.1 collective-permute-start.7
  97.7 1.0 collective-permute-start.8
  101.4 21.6 %collective-permute-start.9 = (bf16[4,8,128,128]{3,2,1,0:T(8,128)(2,1)}, bf16[4,8,128,128]{3,2,1,0:T(8,128)(2,1)}, u32[]{:S(2)}, u32[]{:S(2)}) collective-permute-start(bf16[4,8,128,128]{3,2,1,0:T(8,128)(2,1)} %add_convert_fusion.1), channel_id=1, source_target_pairs={{8,0},{9,1},{10,2},{11,3},{12,4},{13,5},{14,6},{15,7}} | collective-permute-start | bytes 3145736 | tf_op jit(solution)/shard_map/ppermute | solution.py:158
  125.2 1.5 copy-start.7
  125.2 1.8 copy-start.15
  125.2 2.2 copy-start.17
  127.4 2.5 %copy-start.18 = (bf16[1,4,1024,128]{3,2,1,0:T(8,128)(2,1)S(1)}, bf16[1,4,1024,128]{3,2,1,0:T(8,128)(2,1)}, u32[]{:S(2)}) copy-start(bf16[1,4,1024,128]{3,2,1,0:T(8,128)(2,1)} %get-tuple-element.68) | copy-start | bytes 3145732
  129.9 2.2 %copy-start.13 = (f32[4,8,128,256]{3,2,1,0:T(8,128)S(1)}, f32[4,8,128,256]{3,2,1,0:T(8,128)}, u32[]{:S(2)}) copy-start(f32[4,8,128,256]{3,2,1,0:T(8,128)} %copy-done.12) | copy-start | bytes 12582916
  132.1 1.5 copy-start.3
  137.4 17.9 %collective-permute-start.10 = (bf16[2,4,128,128]{3,2,1,0:T(8,128)(2,1)S(1)}, bf16[2,4,128,128]{3,2,1,0:T(8,128)(2,1)S(1)}, u32[]{:S(2)}, u32[]{:S(2)}) collective-permute-start(bf16[2,4,128,128]{3,2,1,0:T(8,128)(2,1)S(1)} %get-tuple-element.83), channel_id=1, source_target_pairs={{0,1},{1,2},{2,3},{3,4},{4,5},{5,6},{6,7},{7,0},{8,9},{9,10},{10,1... | collective-permute-start | bytes 786440 | tf_op jit(solution)/shard_map/ppermute | solution.py:118
  144.6 70.1 %all-to-all-start.1 = ((f32[1024,1,128]{2,1,0:T(1,128)}), f32[1024,1,128]{2,1,0:T(1,128)}, u32[]{:S(2)}, u32[]{:S(2)}) async-start(f32[1024,1,128]{2,1,0:T(1,128)} %bitcast.23), calls=%async_computation.1 | async-start | bytes 1048576 | tf_op jit(solution)/shard_map/all_to_all | solution.py:185
  149.7 61.1 %collective-permute-start.14 = (bf16[2,4,128,128]{3,2,1,0:T(8,128)(2,1)S(1)}, bf16[2,4,128,128]{3,2,1,0:T(8,128)(2,1)S(1)}, u32[]{:S(2)}, u32[]{:S(2)}) collective-permute-start(bf16[2,4,128,128]{3,2,1,0:T(8,128)(2,1)S(1)} %get-tuple-element.88), channel_id=1, source_target_pairs={{0,5},{1,6},{2,7},{3,0},{4,1},{5,2},{6,3},{7,4},{8,13},{9,14},{10,... | collective-permute-start | bytes 786440 | tf_op jit(solution)/shard_map/ppermute | solution.py:118
  151.2 19.5 %collective-permute-start.11 = (bf16[2,4,128,128]{3,2,1,0:T(8,128)(2,1)S(1)}, bf16[2,4,128,128]{3,2,1,0:T(8,128)(2,1)S(1)}, u32[]{:S(2)}, u32[]{:S(2)}) collective-permute-start(bf16[2,4,128,128]{3,2,1,0:T(8,128)(2,1)S(1)} %get-tuple-element.84), channel_id=1, source_target_pairs={{0,2},{1,3},{2,4},{3,5},{4,6},{5,7},{6,0},{7,1},{8,10},{9,11},{10,... | collective-permute-start | bytes 786440 | tf_op jit(solution)/shard_map/ppermute | solution.py:118
  153.6 43.3 %collective-permute-start.12 = (bf16[2,4,128,128]{3,2,1,0:T(8,128)(2,1)S(1)}, bf16[2,4,128,128]{3,2,1,0:T(8,128)(2,1)S(1)}, u32[]{:S(2)}, u32[]{:S(2)}) collective-permute-start(bf16[2,4,128,128]{3,2,1,0:T(8,128)(2,1)S(1)} %get-tuple-element.85), channel_id=1, source_target_pairs={{0,3},{1,4},{2,5},{3,6},{4,7},{5,0},{6,1},{7,2},{8,11},{9,12},{10,... | collective-permute-start | bytes 786440 | tf_op jit(solution)/shard_map/ppermute | solution.py:118
  154.5 56.1 %collective-permute-start.13 = (bf16[2,4,128,128]{3,2,1,0:T(8,128)(2,1)S(1)}, bf16[2,4,128,128]{3,2,1,0:T(8,128)(2,1)S(1)}, u32[]{:S(2)}, u32[]{:S(2)}) collective-permute-start(bf16[2,4,128,128]{3,2,1,0:T(8,128)(2,1)S(1)} %get-tuple-element.86), channel_id=1, source_target_pairs={{0,4},{1,5},{2,6},{3,7},{4,0},{5,1},{6,2},{7,3},{8,12},{9,13},{10,... | collective-permute-start | bytes 786440 | tf_op jit(solution)/shard_map/ppermute | solution.py:118
  155.3 55.9 %collective-permute-start.15 = (bf16[2,4,128,128]{3,2,1,0:T(8,128)(2,1)S(1)}, bf16[2,4,128,128]{3,2,1,0:T(8,128)(2,1)S(1)}, u32[]{:S(2)}, u32[]{:S(2)}) collective-permute-start(bf16[2,4,128,128]{3,2,1,0:T(8,128)(2,1)S(1)} %get-tuple-element.87), channel_id=1, source_target_pairs={{0,6},{1,7},{2,0},{3,1},{4,2},{5,3},{6,4},{7,5},{8,14},{9,15},{10,... | collective-permute-start | bytes 786440 | tf_op jit(solution)/shard_map/ppermute | solution.py:118
  170.7 40.8 %collective-permute-start.16 = (bf16[2,4,128,128]{3,2,1,0:T(8,128)(2,1)S(1)}, bf16[2,4,128,128]{3,2,1,0:T(8,128)(2,1)S(1)}, u32[]{:S(2)}, u32[]{:S(2)}) collective-permute-start(bf16[2,4,128,128]{3,2,1,0:T(8,128)(2,1)S(1)} %get-tuple-element.81), channel_id=1, source_target_pairs={{0,7},{1,0},{2,1},{3,2},{4,3},{5,4},{6,5},{7,6},{8,15},{9,8},{10,9... | collective-permute-start | bytes 786440 | tf_op jit(solution)/shard_map/ppermute | solution.py:118
  212.2 4.5 %copy-start.1 = (bf16[128,4096]{1,0:T(8,128)(2,1)S(1)}, bf16[128,4096]{1,0:T(8,128)(2,1)}, u32[]{:S(2)}) copy-start(bf16[128,4096]{1,0:T(8,128)(2,1)} %param.18) | copy-start | bytes 3145732
  (10 other events, 11.9 us)

commit v9 on v8

--- a/solution.py
+++ b/solution.py
@@ -130,14 +130,22 @@
     def head_major(rows):
         return jnp.transpose(rows.reshape(tok_rows, head_count, DH), (1, 0, 2))
 
-    stacked = jnp.stack([head_major(queries[0]), head_major(cotangent), head_major(inputs[0])])
-    stacked_heads = transpose_seq(stacked, 1, 2)
-    query_blocks = to_blocks(stacked_heads[0])
-    cot_blocks = to_blocks(stacked_heads[1])
-    values_both = key_pair(to_blocks(stacked_heads[2]))
     kv_pick = (jnp.arange(seq_ways) * local_heads) // group_size
     key_rows = jnp.transpose(key_heads[0].reshape(tok_rows, kv_count, DH), (1, 0, 2))[kv_pick]
-    key_flat = lax.all_to_all(key_rows, "seq", split_axis=0, concat_axis=1, tiled=True)
+    per_target = jnp.concatenate(
+        [
+            head_major(queries[0]).reshape(seq_ways, local_heads, tok_rows, DH),
+            head_major(cotangent).reshape(seq_ways, local_heads, tok_rows, DH),
+            key_rows.reshape(seq_ways, 1, tok_rows, DH),
+        ],
+        axis=1,
+    ).reshape(seq_ways * (2 * local_heads + 1), tok_rows, DH)
+    stacked_heads = transpose_seq(per_target, 0, 1)
+    query_blocks = to_blocks(stacked_heads[:local_heads])
+    cot_blocks = to_blocks(stacked_heads[local_heads : 2 * local_heads])
+    key_flat = stacked_heads[2 * local_heads :]
+    input_heads = transpose_seq(head_major(inputs[0]), 0, 1)
+    values_both = key_pair(to_blocks(input_heads))
     key_blocks = jnp.broadcast_to(
         key_flat.reshape(1, block_count, BLK, DH), (local_heads, block_count, BLK, DH)
     )

time: 218 us -> 208 us (0.954)
  the two profiles are of different devices: /device:TPU:24 before, /device:TPU:15 now
where the time goes in v9:
time: 208 us; the launch traced here: 204 us
  waiting for transfers between devices  74.2 us (36%)
  starting transfers between devices  53.8 us (26%)
  local copies, waits for them, and re-layouts  49.4 us (24%)
  other arithmetic  13 us (6%)
  matrix products  12.4 us (6%)
    ppermute x21, waiting for transfers between devices, transpose_seq(): lax.ppermute(chunk, 'seq', [(s, (s + shift) % seq_ways) for s in range(se...  72 us
    ppermute x21, starting transfers between devices, transpose_seq(): lax.ppermute(chunk, 'seq', [(s, (s + shift) % seq_ways) for s in range(se...  43 us
    dynamic_update_slice x23, local copies, waits for them, and re-layouts, transpose_seq(): lax.dynamic_update_slice_in_dim(result, chunk, source * concat_size, axis...  17 us
    unnamed x44, local copies, waits for them, and re-layouts  14.1 us
    ppermute x3, starting transfers between devices, on_device(): grad_in = lax.ppermute(new_grad, 'pipe', [(sender, sender - 1)])  5.82 us
    dot_general x4, matrix products, value_grad(): jnp.einsum('hbij,hbid->hbjd', probs_low, grad_blocks, preferred_element_t...  5.47 us
    all_to_all x1, starting transfers between devices, on_device(): lax.all_to_all(key_part[:, None, :], 'seq', split_axis=0, concat_axis=1,...  4.99 us
    convert_element_type x3, other arithmetic, value_grad(): (grad_blocks.astype(jnp.float32) + fold_value(key_terms, block_len, group...  4.16 us
  transfers between devices with their start and end apart: 25, of which 12 were waited for; matrix products, arithmetic and copies ran while one was open for 18% of the time, Pallas kernels for 0%

profile of v9, /device:TPU:15, one launch (start us, length us, event | category | flops | bytes accessed | tf_op | source)
XLA Modules:
  0.0 204.3 jit_solution(642126982595701760)
XLA Ops:
  4.9 1.8 broadcast_in_dim.48
  17.2 5.2 %collective-permute-done.1 = bf16[9,128,128]{2,1,0:T(8,128)(2,1)S(1)} collective-permute-done((bf16[9,128,128]{2,1,0:T(8,128)(2,1)S(1)}, bf16[9,128,128]{2,1,0:T(8,128)(2,1)S(1)}, u32[]{:S(2)}, u32[]{:S(2)}) %collective-permute-start.1) | collective-permute-done | bytes 294944 | tf_op jit(solution)/shard_map/ppermute | solution.py:118
  23.1 29.9 %collective-permute-done.2 = bf16[9,128,128]{2,1,0:T(8,128)(2,1)S(1)} collective-permute-done((bf16[9,128,128]{2,1,0:T(8,128)(2,1)S(1)}, bf16[9,128,128]{2,1,0:T(8,128)(2,1)S(1)}, u32[]{:S(2)}, u32[]{:S(2)}) %collective-permute-start.2) | collective-permute-done | bytes 294944 | tf_op jit(solution)/shard_map/ppermute | solution.py:118
  53.8 5.5 %collective-permute-done.3 = bf16[9,128,128]{2,1,0:T(8,128)(2,1)S(1)} collective-permute-done((bf16[9,128,128]{2,1,0:T(8,128)(2,1)S(1)}, bf16[9,128,128]{2,1,0:T(8,128)(2,1)S(1)}, u32[]{:S(2)}, u32[]{:S(2)}) %collective-permute-start.3) | collective-permute-done | bytes 294944 | tf_op jit(solution)/shard_map/ppermute | solution.py:118
  64.3 1.7 fusion.40
  71.1 2.2 %fusion.42 = (f32[4,8,128]{2,1,0:T(8,128)S(1)}, f32[4,8,128,256]{3,2,1,0:T(8,128)S(1)}) fusion(f32[4,8,128,256]{3,2,1,0:T(8,128)S(1)} %fusion.3, pred[8,128,256]{2,1,0:T(8,128)(4,1)S(1)} %copy-done.13), kind=kOutput, calls=%fused_computation.148 | output fusion | flops 6291711 | bytes 8667136 | tf_op jit(solution)/shard_map/sub | solution.py:53
  76.9 2.5 %collective-permute-start.7 = (bf16[4,8,128,128]{3,2,1,0:T(8,128)(2,1)S(1)}, bf16[4,8,128,128]{3,2,1,0:T(8,128)(2,1)S(1)}, u32[]{:S(2)}, u32[]{:S(2)}) collective-permute-start(bf16[4,8,128,128]{3,2,1,0:T(8,128)(2,1)S(1)} %add_convert_fusion.3), channel_id=1, source_target_pairs={{24,16},{25,17},{26,18},{27,19},{28,20},{29,21},{30,22},{31,23}} | collective-permute-start | bytes 3145736 | tf_op jit(solution)/shard_map/ppermute | solution.py:166
  79.4 2.2 %collective-permute-done.7 = bf16[4,8,128,128]{3,2,1,0:T(8,128)(2,1)S(1)} collective-permute-done((bf16[4,8,128,128]{3,2,1,0:T(8,128)(2,1)S(1)}, bf16[4,8,128,128]{3,2,1,0:T(8,128)(2,1)S(1)}, u32[]{:S(2)}, u32[]{:S(2)}) %collective-permute-start.7) | collective-permute-done | bytes 1048608 | tf_op jit(solution)/shard_map/ppermute | solution.py:166
  84.3 1.7 collective-permute-start.8
  86.0 2.4 %copy.191 = bf16[16,8,32,128]{3,2,1,0:T(8,128)(2,1)} copy(bf16[16,8,32,128]{3,1,2,0:T(8,128)(2,1)} %bitcast.117) | data formatting | bytes 2097152
  88.4 2.3 %constant_dynamic-slice_fusion = (bf16[128,4,128]{2,1,0:T(4,128)(2,1)S(1)}, bf16[128,4,128]{2,1,0:T(4,128)(2,1)S(1)}, bf16[128,4,128]{2,1,0:T(4,128)(2,1)S(1)}, ...) fusion(bf16[128,32,128]{2,1,0:T(8,128)(2,1)} %bitcast.106, ...), kind=kLoop, calls=%fused_computation.101 | loop fusion | bytes 2097184 | tf_op jit(solution)/shard_map/dynamic-slice.43
  92.7 4.1 %collective-permute-start.12 = (bf16[4,128,128]{2,1,0:T(8,128)(2,1)}, bf16[4,128,128]{2,1,0:T(8,128)(2,1)}, u32[]{:S(2)}, u32[]{:S(2)}) collective-permute-start(bf16[4,128,128]{2,1,0:T(8,128)(2,1)} %bitcast.93), channel_id=1, source_target_pairs={{0,3},{1,4},{2,5},{3,6},{4,7},{5,0},{6,1},{7,2},{8,11},{9,12},{10,... | collective-permute-start | bytes 393224 | tf_op jit(solution)/shard_map/ppermute | solution.py:118
  97.4 2.0 fusion.45
  100.0 2.6 %add_convert_fusion.1 = bf16[4,8,128,128]{3,2,1,0:T(8,128)(2,1)} fusion(f32[4,8,128,128]{3,2,1,0:T(8,128)S(1)} %fusion.28, bf16[4,8,128,128]{3,2,1,0:T(8,128)(2,1)} %collective-permute-done.8), kind=kLoop, calls=%fused_computation.38 | loop fusion | flops 1572864 | bytes 4194304 | tf_op jit(solution)/shard_map/convert_element_type | solution.py:61
  102.6 1.6 collective-permute-start.9
  106.8 1.7 collective-permute-start.14
  108.4 1.6 constant_dynamic-update-slice_fusion.6
  110.0 1.9 collective-permute-start.15
  112.0 1.6 constant_dynamic-update-slice_fusion.5
  115.0 1.6 constant_dynamic-update-slice_fusion.4
  119.6 2.4 %collective-permute-done.16 = bf16[4,128,128]{2,1,0:T(8,128)(2,1)S(1)} collective-permute-done((bf16[4,128,128]{2,1,0:T(8,128)(2,1)S(1)}, bf16[4,128,128]{2,1,0:T(8,128)(2,1)S(1)}, u32[]{:S(2)}, u32[]{:S(2)}) %collective-permute-start.16) | collective-permute-done | bytes 131104 | tf_op jit(solution)/shard_map/ppermute | solution.py:118
  123.6 2.0 fusion.46
  127.4 2.2 %fusion.9 = (bf16[4,8,128,128]{3,2,1,0:T(8,128)(2,1)S(1)}, bf16[4,8,128,128]{3,2,1,0:T(8,128)(2,1)S(1)}) fusion(f32[4,8,128,128]{3,2,1,0:T(8,128)S(1)} %fusion.27, bf16[4,8,128,128]{3,2,1,0:T(8,128)(2,1)} %collective-permute-done.9, bf16[4,8,128,128]{3,2,1,0:T(8,128)(2,1)} %add_convert_fusion.1, bf16[4,8,128,128]{3,2,1,0:T(8,128)(2,1)} %add_convert_fusion.2, ...), kind=kLoop, calls=%fused_computation.50 | loop fusion | flops 4718592 | bytes 11534339 | tf_op jit(solution)/shard_map/jit(_where)/select_n | solution.py:171
  129.8 2.2 %multiply_reduce_fusion = f32[4,8,128]{2,1,0:T(8,128)S(1)} fusion(bf16[4,8,128,128]{3,2,1,0:T(8,128)(2,1)S(1)} %get-tuple-element.89, bf16[4,8,128,256]{3,2,1,0:T(8,128)(2,1)S(1)} %fusion.8, bf16[4,8,128,128]{3,2,1,0:T(8,128)(2,1)} %bitcast.26, bf16[4,8,128,128]{3,2,1,0:T(8,128)(2,1)S(1)} %broadcast_in_dim.55), kind=kOutput, calls=%fused_computation.37 | convolution fusion | flops 274198528 | bytes 5259264 | tf_op jit(solution)/shard_map/hbij,hbjd->hbid/dot_general | solution.py:69
  132.3 2.5 %multiply_convert_fusion = bf16[4,8,128,256]{3,2,1,0:T(8,128)(2,1)S(1)} fusion(bf16[4,8,128,128]{3,2,1,0:T(8,128)(2,1)S(1)} %get-tuple-element.89, f32[4,8,128]{2,1,0:T(8,128)S(1)} %multiply_reduce_fusion, bf16[4,8,128,128]{3,2,1,0:T(8,128)(2,1)} %bitcast.26, bf16[4,8,128,128]{3,2,1,0:T(8,128)(2,1)S(1)} %broadcast_in_dim.55, ...), kind=kOutput, calls=%fused_computation.2 | convolution fusion | flops 276824064 | bytes 9469952 | tf_op jit(solution)/shard_map/hbid,hbjd->hbij/dot_general | solution.py:73
  138.8 5.0 %all-to-all-start = ((f32[1024,1,128]{2,1,0:T(1,128)}), f32[1024,1,128]{2,1,0:T(1,128)S(1)}, u32[]{:S(2)}, u32[]{:S(2)}) async-start(f32[1024,1,128]{2,1,0:T(1,128)} %bitcast.33), calls=%async_computation | async-start | bytes 1048576 | tf_op jit(solution)/shard_map/all_to_all | solution.py:193
  145.2 3.9 %collective-permute-start.19 = (bf16[2,4,128,128]{3,2,1,0:T(8,128)(2,1)S(1)}, bf16[2,4,128,128]{3,2,1,0:T(8,128)(2,1)S(1)}, u32[]{:S(2)}, u32[]{:S(2)}) collective-permute-start(bf16[2,4,128,128]{3,2,1,0:T(8,128)(2,1)S(1)} %get-tuple-element.84), channel_id=1, source_target_pairs={{0,3},{1,4},{2,5},{3,6},{4,7},{5,0},{6,1},{7,2},{8,11},{9,12},{10,... | collective-permute-start | bytes 786440 | tf_op jit(solution)/shard_map/ppermute | solution.py:118
  151.5 15.6 %collective-permute-done.18 = bf16[2,4,128,128]{3,2,1,0:T(8,128)(2,1)S(1)} collective-permute-done((bf16[2,4,128,128]{3,2,1,0:T(8,128)(2,1)S(1)}, bf16[2,4,128,128]{3,2,1,0:T(8,128)(2,1)S(1)}, u32[]{:S(2)}, u32[]{:S(2)}) %collective-permute-start.18) | collective-permute-done | bytes 262176 | tf_op jit(solution)/shard_map/ppermute | solution.py:118
  167.1 20.8 %collective-permute-start.23 = (bf16[2,4,128,128]{3,2,1,0:T(8,128)(2,1)S(1)}, bf16[2,4,128,128]{3,2,1,0:T(8,128)(2,1)S(1)}, u32[]{:S(2)}, u32[]{:S(2)}) collective-permute-start(bf16[2,4,128,128]{3,2,1,0:T(8,128)(2,1)S(1)} %get-tuple-element.80), channel_id=1, source_target_pairs={{0,7},{1,0},{2,1},{3,2},{4,3},{5,4},{6,5},{7,6},{8,15},{9,8},{10,9... | collective-permute-start | bytes 786440 | tf_op jit(solution)/shard_map/ppermute | solution.py:118
  188.5 4.4 %collective-permute-done.20 = bf16[2,4,128,128]{3,2,1,0:T(8,128)(2,1)S(1)} collective-permute-done((bf16[2,4,128,128]{3,2,1,0:T(8,128)(2,1)S(1)}, bf16[2,4,128,128]{3,2,1,0:T(8,128)(2,1)S(1)}, u32[]{:S(2)}, u32[]{:S(2)}) %collective-permute-start.20) | collective-permute-done | bytes 262176 | tf_op jit(solution)/shard_map/ppermute | solution.py:118
  193.6 3.6 %collective-permute-done.22 = bf16[2,4,128,128]{3,2,1,0:T(8,128)(2,1)S(1)} collective-permute-done((bf16[2,4,128,128]{3,2,1,0:T(8,128)(2,1)S(1)}, bf16[2,4,128,128]{3,2,1,0:T(8,128)(2,1)S(1)}, u32[]{:S(2)}, u32[]{:S(2)}) %collective-permute-start.22) | collective-permute-done | bytes 262176 | tf_op jit(solution)/shard_map/ppermute | solution.py:118
  197.4 2.7 %collective-permute-done.23 = bf16[2,4,128,128]{3,2,1,0:T(8,128)(2,1)S(1)} collective-permute-done((bf16[2,4,128,128]{3,2,1,0:T(8,128)(2,1)S(1)}, bf16[2,4,128,128]{3,2,1,0:T(8,128)(2,1)S(1)}, u32[]{:S(2)}, u32[]{:S(2)}) %collective-permute-start.23) | collective-permute-done | bytes 262176 | tf_op jit(solution)/shard_map/ppermute | solution.py:118
  (149 shorter events, 59.6 us)
Async XLA Ops:
  0.8 2.0 copy-start.12
  6.7 7.4 %copy-start.15 = (s32[8]{0:T(128)S(1)}, s32[8]{0:T(128)}, u32[]{:S(2)}) copy-start(s32[8]{0:T(128)} %param.19) | copy-start | bytes 100
  8.2 7.9 %collective-permute-start = (bf16[9,128,128]{2,1,0:T(8,128)(2,1)S(1)}, bf16[9,128,128]{2,1,0:T(8,128)(2,1)S(1)}, u32[]{:S(2)}, u32[]{:S(2)}) collective-permute-start(bf16[9,128,128]{2,1,0:T(8,128)(2,1)S(1)} %get-tuple-element.76), channel_id=1, source_target_pairs={{0,1},{1,2},{2,3},{3,4},{4,5},{5,6},{6,7},{7,0},{8,9},{9,10},{10,1... | collective-permute-start | bytes 884744 | tf_op jit(solution)/shard_map/ppermute | solution.py:118
  9.5 12.9 %collective-permute-start.1 = (bf16[9,128,128]{2,1,0:T(8,128)(2,1)S(1)}, bf16[9,128,128]{2,1,0:T(8,128)(2,1)S(1)}, u32[]{:S(2)}, u32[]{:S(2)}) collective-permute-start(bf16[9,128,128]{2,1,0:T(8,128)(2,1)S(1)} %get-tuple-element.75), channel_id=1, source_target_pairs={{0,2},{1,3},{2,4},{3,5},{4,6},{5,7},{6,0},{7,1},{8,10},{9,11},{10,... | collective-permute-start | bytes 884744 | tf_op jit(solution)/shard_map/ppermute | solution.py:118
  10.7 42.3 %collective-permute-start.2 = (bf16[9,128,128]{2,1,0:T(8,128)(2,1)S(1)}, bf16[9,128,128]{2,1,0:T(8,128)(2,1)S(1)}, u32[]{:S(2)}, u32[]{:S(2)}) collective-permute-start(bf16[9,128,128]{2,1,0:T(8,128)(2,1)S(1)} %get-tuple-element.74), channel_id=1, source_target_pairs={{0,3},{1,4},{2,5},{3,6},{4,7},{5,0},{6,1},{7,2},{8,11},{9,12},{10,... | collective-permute-start | bytes 884744 | tf_op jit(solution)/shard_map/ppermute | solution.py:118
  11.7 47.7 %collective-permute-start.3 = (bf16[9,128,128]{2,1,0:T(8,128)(2,1)S(1)}, bf16[9,128,128]{2,1,0:T(8,128)(2,1)S(1)}, u32[]{:S(2)}, u32[]{:S(2)}) collective-permute-start(bf16[9,128,128]{2,1,0:T(8,128)(2,1)S(1)} %get-tuple-element.73), channel_id=1, source_target_pairs={{0,4},{1,5},{2,6},{3,7},{4,0},{5,1},{6,2},{7,3},{8,12},{9,13},{10,... | collective-permute-start | bytes 884744 | tf_op jit(solution)/shard_map/ppermute | solution.py:118
  13.0 47.1 %collective-permute-start.4 = (bf16[9,128,128]{2,1,0:T(8,128)(2,1)S(1)}, bf16[9,128,128]{2,1,0:T(8,128)(2,1)S(1)}, u32[]{:S(2)}, u32[]{:S(2)}) collective-permute-start(bf16[9,128,128]{2,1,0:T(8,128)(2,1)S(1)} %get-tuple-element.72), channel_id=1, source_target_pairs={{0,5},{1,6},{2,7},{3,0},{4,1},{5,2},{6,3},{7,4},{8,13},{9,14},{10,... | collective-permute-start | bytes 884744 | tf_op jit(solution)/shard_map/ppermute | solution.py:118
  16.1 46.2 %collective-permute-start.5 = (bf16[9,128,128]{2,1,0:T(8,128)(2,1)S(1)}, bf16[9,128,128]{2,1,0:T(8,128)(2,1)S(1)}, u32[]{:S(2)}, u32[]{:S(2)}) collective-permute-start(bf16[9,128,128]{2,1,0:T(8,128)(2,1)S(1)} %get-tuple-element.71), channel_id=1, source_target_pairs={{0,6},{1,7},{2,0},{3,1},{4,2},{5,3},{6,4},{7,5},{8,14},{9,15},{10,... | collective-permute-start | bytes 884744 | tf_op jit(solution)/shard_map/ppermute | solution.py:118
  22.4 41.1 %collective-permute-start.6 = (bf16[9,128,128]{2,1,0:T(8,128)(2,1)S(1)}, bf16[9,128,128]{2,1,0:T(8,128)(2,1)S(1)}, u32[]{:S(2)}, u32[]{:S(2)}) collective-permute-start(bf16[9,128,128]{2,1,0:T(8,128)(2,1)S(1)} %get-tuple-element.70), channel_id=1, source_target_pairs={{0,7},{1,0},{2,1},{3,2},{4,3},{5,4},{6,5},{7,6},{8,15},{9,8},{10,9... | collective-permute-start | bytes 884744 | tf_op jit(solution)/shard_map/ppermute | solution.py:118
  66.0 2.4 %copy-start = (bf16[4,1024,128]{2,1,0:T(8,128)(2,1)}, bf16[4,1024,128]{2,1,0:T(8,128)(2,1)S(1)}, u32[]{:S(2)}) copy-start(bf16[4,1024,128]{2,1,0:T(8,128)(2,1)S(1)} %get-tuple-element.69) | copy-start | bytes 3145732
  73.3 1.9 copy-start.8
  76.9 2.5 %copy-start.10 = (bf16[4,8,128,128]{3,2,1,0:T(8,128)(2,1)}, bf16[4,8,128,128]{3,2,1,0:T(8,128)(2,1)S(1)}, u32[]{:S(2)}) copy-start(bf16[4,8,128,128]{3,2,1,0:T(8,128)(2,1)S(1)} %add_convert_fusion.3) | copy-start | bytes 3145732
  76.9 4.7 %collective-permute-start.7 = (bf16[4,8,128,128]{3,2,1,0:T(8,128)(2,1)S(1)}, bf16[4,8,128,128]{3,2,1,0:T(8,128)(2,1)S(1)}, u32[]{:S(2)}, u32[]{:S(2)}) collective-permute-start(bf16[4,8,128,128]{3,2,1,0:T(8,128)(2,1)S(1)} %add_convert_fusion.3), channel_id=1, source_target_pairs={{24,16},{25,17},{26,18},{27,19},{28,20},{29,21},{30,22},{31,23}} | collective-permute-start | bytes 3145736 | tf_op jit(solution)/shard_map/ppermute | solution.py:166
  84.3 13.2 %collective-permute-start.8 = (bf16[4,8,128,128]{3,2,1,0:T(8,128)(2,1)}, bf16[4,8,128,128]{3,2,1,0:T(8,128)(2,1)}, u32[]{:S(2)}, u32[]{:S(2)}) collective-permute-start(bf16[4,8,128,128]{3,2,1,0:T(8,128)(2,1)} %add_convert_fusion.2), channel_id=1, source_target_pairs={{16,8},{17,9},{18,10},{19,11},{20,12},{21,13},{22,14},{23,15}} | collective-permute-start | bytes 3145736 | tf_op jit(solution)/shard_map/ppermute | solution.py:166
  91.3 15.4 %collective-permute-start.10 = (bf16[4,128,128]{2,1,0:T(8,128)(2,1)}, bf16[4,128,128]{2,1,0:T(8,128)(2,1)}, u32[]{:S(2)}, u32[]{:S(2)}) collective-permute-start(bf16[4,128,128]{2,1,0:T(8,128)(2,1)} %bitcast.95), channel_id=1, source_target_pairs={{0,1},{1,2},{2,3},{3,4},{4,5},{5,6},{6,7},{7,0},{8,9},{9,10},{10,1... | collective-permute-start | bytes 393224 | tf_op jit(solution)/shard_map/ppermute | solution.py:118
  92.0 18.0 %collective-permute-start.11 = (bf16[4,128,128]{2,1,0:T(8,128)(2,1)}, bf16[4,128,128]{2,1,0:T(8,128)(2,1)}, u32[]{:S(2)}, u32[]{:S(2)}) collective-permute-start(bf16[4,128,128]{2,1,0:T(8,128)(2,1)} %bitcast.94), channel_id=1, source_target_pairs={{0,2},{1,3},{2,4},{3,5},{4,6},{5,7},{6,0},{7,1},{8,10},{9,11},{10,... | collective-permute-start | bytes 393224 | tf_op jit(solution)/shard_map/ppermute | solution.py:118
  92.7 20.8 %collective-permute-start.12 = (bf16[4,128,128]{2,1,0:T(8,128)(2,1)}, bf16[4,128,128]{2,1,0:T(8,128)(2,1)}, u32[]{:S(2)}, u32[]{:S(2)}) collective-permute-start(bf16[4,128,128]{2,1,0:T(8,128)(2,1)} %bitcast.93), channel_id=1, source_target_pairs={{0,3},{1,4},{2,5},{3,6},{4,7},{5,0},{6,1},{7,2},{8,11},{9,12},{10,... | collective-permute-start | bytes 393224 | tf_op jit(solution)/shard_map/ppermute | solution.py:118
  97.4 19.2 %collective-permute-start.13 = (bf16[4,128,128]{2,1,0:T(8,128)(2,1)}, bf16[4,128,128]{2,1,0:T(8,128)(2,1)}, u32[]{:S(2)}, u32[]{:S(2)}) collective-permute-start(bf16[4,128,128]{2,1,0:T(8,128)(2,1)} %bitcast.92), channel_id=1, source_target_pairs={{0,4},{1,5},{2,6},{3,7},{4,0},{5,1},{6,2},{7,3},{8,12},{9,13},{10,... | collective-permute-start | bytes 393224 | tf_op jit(solution)/shard_map/ppermute | solution.py:118
  102.6 21.0 %collective-permute-start.9 = (bf16[4,8,128,128]{3,2,1,0:T(8,128)(2,1)}, bf16[4,8,128,128]{3,2,1,0:T(8,128)(2,1)}, u32[]{:S(2)}, u32[]{:S(2)}) collective-permute-start(bf16[4,8,128,128]{3,2,1,0:T(8,128)(2,1)} %add_convert_fusion.1), channel_id=1, source_target_pairs={{8,0},{9,1},{10,2},{11,3},{12,4},{13,5},{14,6},{15,7}} | collective-permute-start | bytes 3145736 | tf_op jit(solution)/shard_map/ppermute | solution.py:166
  106.8 11.4 %collective-permute-start.14 = (bf16[4,128,128]{2,1,0:T(8,128)(2,1)}, bf16[4,128,128]{2,1,0:T(8,128)(2,1)S(1)}, u32[]{:S(2)}, u32[]{:S(2)}) collective-permute-start(bf16[4,128,128]{2,1,0:T(8,128)(2,1)} %bitcast.122), channel_id=1, source_target_pairs={{0,5},{1,6},{2,7},{3,0},{4,1},{5,2},{6,3},{7,4},{8,13},{9,14},{10,... | collective-permute-start | bytes 393224 | tf_op jit(solution)/shard_map/ppermute | solution.py:118
  110.0 8.9 %collective-permute-start.15 = (bf16[4,128,128]{2,1,0:T(8,128)(2,1)S(1)}, bf16[4,128,128]{2,1,0:T(8,128)(2,1)S(1)}, u32[]{:S(2)}, u32[]{:S(2)}) collective-permute-start(bf16[4,128,128]{2,1,0:T(8,128)(2,1)S(1)} %bitcast.121), channel_id=1, source_target_pairs={{0,6},{1,7},{2,0},{3,1},{4,2},{5,3},{6,4},{7,5},{8,14},{9,15},{10,... | collective-permute-start | bytes 393224 | tf_op jit(solution)/shard_map/ppermute | solution.py:118
  113.5 8.4 %collective-permute-start.16 = (bf16[4,128,128]{2,1,0:T(8,128)(2,1)S(1)}, bf16[4,128,128]{2,1,0:T(8,128)(2,1)S(1)}, u32[]{:S(2)}, u32[]{:S(2)}) collective-permute-start(bf16[4,128,128]{2,1,0:T(8,128)(2,1)S(1)} %bitcast.120), channel_id=1, source_target_pairs={{0,7},{1,0},{2,1},{3,2},{4,3},{5,4},{6,5},{7,6},{8,15},{9,8},{10,9... | collective-permute-start | bytes 393224 | tf_op jit(solution)/shard_map/ppermute | solution.py:118
  129.8 2.5 %copy-start.9 = (f32[4,8,128,256]{3,2,1,0:T(8,128)S(1)}, f32[4,8,128,256]{3,2,1,0:T(8,128)}, u32[]{:S(2)}) copy-start(f32[4,8,128,256]{3,2,1,0:T(8,128)} %copy-done.8) | copy-start | bytes 12582916
  132.3 2.6 %copy-start.1 = (bf16[4,1024,128]{2,1,0:T(8,128)(2,1)S(1)}, bf16[4,1024,128]{2,1,0:T(8,128)(2,1)}, u32[]{:S(2)}) copy-start(bf16[4,1024,128]{2,1,0:T(8,128)(2,1)} %copy-done) | copy-start | bytes 3145732
  138.6 11.1 %collective-permute-start.17 = (bf16[2,4,128,128]{3,2,1,0:T(8,128)(2,1)S(1)}, bf16[2,4,128,128]{3,2,1,0:T(8,128)(2,1)S(1)}, u32[]{:S(2)}, u32[]{:S(2)}) collective-permute-start(bf16[2,4,128,128]{3,2,1,0:T(8,128)(2,1)S(1)} %get-tuple-element.82), channel_id=1, source_target_pairs={{0,1},{1,2},{2,3},{3,4},{4,5},{5,6},{6,7},{7,0},{8,9},{9,10},{10,1... | collective-permute-start | bytes 786440 | tf_op jit(solution)/shard_map/ppermute | solution.py:118
  138.8 64.6 %all-to-all-start = ((f32[1024,1,128]{2,1,0:T(1,128)}), f32[1024,1,128]{2,1,0:T(1,128)S(1)}, u32[]{:S(2)}, u32[]{:S(2)}) async-start(f32[1024,1,128]{2,1,0:T(1,128)} %bitcast.33), calls=%async_computation | async-start | bytes 1048576 | tf_op jit(solution)/shard_map/all_to_all | solution.py:193
  143.8 49.5 %collective-permute-start.21 = (bf16[2,4,128,128]{3,2,1,0:T(8,128)(2,1)S(1)}, bf16[2,4,128,128]{3,2,1,0:T(8,128)(2,1)S(1)}, u32[]{:S(2)}, u32[]{:S(2)}) collective-permute-start(bf16[2,4,128,128]{3,2,1,0:T(8,128)(2,1)S(1)} %get-tuple-element.87), channel_id=1, source_target_pairs={{0,5},{1,6},{2,7},{3,0},{4,1},{5,2},{6,3},{7,4},{8,13},{9,14},{10,... | collective-permute-start | bytes 786440 | tf_op jit(solution)/shard_map/ppermute | solution.py:118
  143.9 23.2 %collective-permute-start.18 = (bf16[2,4,128,128]{3,2,1,0:T(8,128)(2,1)S(1)}, bf16[2,4,128,128]{3,2,1,0:T(8,128)(2,1)S(1)}, u32[]{:S(2)}, u32[]{:S(2)}) collective-permute-start(bf16[2,4,128,128]{3,2,1,0:T(8,128)(2,1)S(1)} %get-tuple-element.83), channel_id=1, source_target_pairs={{0,2},{1,3},{2,4},{3,5},{4,6},{5,7},{6,0},{7,1},{8,10},{9,11},{10,... | collective-permute-start | bytes 786440 | tf_op jit(solution)/shard_map/ppermute | solution.py:118
  145.2 43.0 %collective-permute-start.19 = (bf16[2,4,128,128]{3,2,1,0:T(8,128)(2,1)S(1)}, bf16[2,4,128,128]{3,2,1,0:T(8,128)(2,1)S(1)}, u32[]{:S(2)}, u32[]{:S(2)}) collective-permute-start(bf16[2,4,128,128]{3,2,1,0:T(8,128)(2,1)S(1)} %get-tuple-element.84), channel_id=1, source_target_pairs={{0,3},{1,4},{2,5},{3,6},{4,7},{5,0},{6,1},{7,2},{8,11},{9,12},{10,... | collective-permute-start | bytes 786440 | tf_op jit(solution)/shard_map/ppermute | solution.py:118
  149.1 43.8 %collective-permute-start.20 = (bf16[2,4,128,128]{3,2,1,0:T(8,128)(2,1)S(1)}, bf16[2,4,128,128]{3,2,1,0:T(8,128)(2,1)S(1)}, u32[]{:S(2)}, u32[]{:S(2)}) collective-permute-start(bf16[2,4,128,128]{3,2,1,0:T(8,128)(2,1)S(1)} %get-tuple-element.85), channel_id=1, source_target_pairs={{0,4},{1,5},{2,6},{3,7},{4,0},{5,1},{6,2},{7,3},{8,12},{9,13},{10,... | collective-permute-start | bytes 786440 | tf_op jit(solution)/shard_map/ppermute | solution.py:118
  149.7 47.4 %collective-permute-start.22 = (bf16[2,4,128,128]{3,2,1,0:T(8,128)(2,1)S(1)}, bf16[2,4,128,128]{3,2,1,0:T(8,128)(2,1)S(1)}, u32[]{:S(2)}, u32[]{:S(2)}) collective-permute-start(bf16[2,4,128,128]{3,2,1,0:T(8,128)(2,1)S(1)} %get-tuple-element.86), channel_id=1, source_target_pairs={{0,6},{1,7},{2,0},{3,1},{4,2},{5,3},{6,4},{7,5},{8,14},{9,15},{10,... | collective-permute-start | bytes 786440 | tf_op jit(solution)/shard_map/ppermute | solution.py:118
  167.1 33.0 %collective-permute-start.23 = (bf16[2,4,128,128]{3,2,1,0:T(8,128)(2,1)S(1)}, bf16[2,4,128,128]{3,2,1,0:T(8,128)(2,1)S(1)}, u32[]{:S(2)}, u32[]{:S(2)}) collective-permute-start(bf16[2,4,128,128]{3,2,1,0:T(8,128)(2,1)S(1)} %get-tuple-element.80), channel_id=1, source_target_pairs={{0,7},{1,0},{2,1},{3,2},{4,3},{5,4},{6,5},{7,6},{8,15},{9,8},{10,9... | collective-permute-start | bytes 786440 | tf_op jit(solution)/shard_map/ppermute | solution.py:118
  (9 other events, 10.7 us)

commit v10 on v5

--- a/solution.py
+++ b/solution.py
@@ -102,7 +102,7 @@
 
     seq_index = lax.axis_index("seq")
 
-    def transpose_seq(value, split_axis, concat_axis):
+    def transpose_seq(value, split_axis, concat_axis, section=None):
         if seq_ways > 8:
             return lax.all_to_all(value, "seq", split_axis, concat_axis, tiled=True)
         split_size = value.shape[split_axis] // seq_ways
@@ -114,9 +114,16 @@
         for shift in range(seq_ways):
             target = (seq_index + shift) % seq_ways
             chunk = lax.dynamic_slice_in_dim(value, target * split_size, split_size, axis=split_axis)
-            if shift > 0:
+            if shift > 0 and section is None:
                 chunk = lax.ppermute(
                     chunk, "seq", [(s, (s + shift) % seq_ways) for s in range(seq_ways)]
+                )
+            elif shift > 0:
+                base = section * seq_ways
+                chunk = lax.ppermute(
+                    chunk,
+                    ("pipe", "seq"),
+                    [(base + s, base + (s + shift) % seq_ways) for s in range(seq_ways)],
                 )
             source = (seq_index + seq_ways - shift) % seq_ways
             result = lax.dynamic_update_slice_in_dim(
@@ -130,11 +137,14 @@
     def head_major(rows):
         return jnp.transpose(rows.reshape(tok_rows, head_count, DH), (1, 0, 2))
 
-    stacked = jnp.stack([head_major(queries[0]), head_major(cotangent)])
+    is_last = section_index == last_section
+    second = jnp.where(is_last, head_major(cotangent), head_major(inputs[0]))
+    stacked = jnp.stack([head_major(queries[0]), second])
     stacked_heads = transpose_seq(stacked, 1, 2)
     query_blocks = to_blocks(stacked_heads[0])
     cot_blocks = to_blocks(stacked_heads[1])
-    input_heads = transpose_seq(head_major(inputs[0]), 0, 1)
+    last_inputs = transpose_seq(head_major(inputs[0]), 0, 1, section=last_section)
+    input_heads = jnp.where(is_last, last_inputs, stacked_heads[1])
     values_both = key_pair(to_blocks(input_heads))
     kv_pick = (jnp.arange(seq_ways) * local_heads) // group_size
     key_rows = jnp.transpose(key_heads[0].reshape(tok_rows, kv_count, DH), (1, 0, 2))[kv_pick]

time: 195 us -> 191 us (0.979)
  local copies, waits for them, and re-layouts: 44.9 us -> 37 us
  other arithmetic: 13 us -> 17.3 us
  waiting for transfers between devices: 66 us -> 68.7 us
  matrix products: 11.2 us -> 8.83 us
    ppermute x21 -> x14, starting transfers between devices: 38.6 us -> 18.6 us  [transpose_seq(): lax.ppermute(chunk, 'seq', [(s, (s + shift) % seq_ways) for s in range(se...]
    ppermute x0 -> x7, starting transfers between devices: none -> 19.6 us  [transpose_seq(): lax.ppermute(chunk, ('pipe', 'seq'), [(base + s, base + (s + shift) % seq...]
    dynamic_update_slice x23, local copies, waits for them, and re-layouts: 19.8 us -> 14.5 us  [transpose_seq(): lax.dynamic_update_slice_in_dim(result, chunk, source * concat_size, axis...]
    another operation x2 -> x3, other arithmetic: 1.37 us -> 4.59 us  [the longest x2 3 us: on_device(): stacked = jnp.stack([head_major(queries[0]), second])]
    ppermute x21 -> x14, waiting for transfers between devices: 63.8 us -> 66.5 us  [transpose_seq(): lax.ppermute(chunk, 'seq', [(s, (s + shift) % seq_ways) for s in range(se...]
    unnamed x57 -> x48, local copies, waits for them, and re-layouts: 11.5 us -> 10.7 us
  transfers between devices with their start and end apart: 26 -> 26, of which waited for: 12 -> 9; matrix products, arithmetic and copies ran while one was open for 19% -> 16% of each run, Pallas kernels for 0% -> 0%
where the time goes in v10:
time: 191 us; the launch traced here: 189 us
  waiting for transfers between devices  68.7 us (36%)
  starting transfers between devices  55.5 us (29%)
  local copies, waits for them, and re-layouts  37 us (19%)
  other arithmetic  17.3 us (9%)
  matrix products  8.83 us (5%)
    ppermute x14, waiting for transfers between devices, transpose_seq(): lax.ppermute(chunk, 'seq', [(s, (s + shift) % seq_ways) for s in range(se...  66.5 us
    ppermute x7, starting transfers between devices, transpose_seq(): lax.ppermute(chunk, ('pipe', 'seq'), [(base + s, base + (s + shift) % seq...  19.6 us
    ppermute x14, starting transfers between devices, transpose_seq(): lax.ppermute(chunk, 'seq', [(s, (s + shift) % seq_ways) for s in range(se...  18.6 us
    dynamic_update_slice x23, local copies, waits for them, and re-layouts, transpose_seq(): lax.dynamic_update_slice_in_dim(result, chunk, source * concat_size, axis...  14.5 us
    unnamed x48, local copies, waits for them, and re-layouts  10.7 us
    all_to_all x1, starting transfers between devices, on_device(): lax.all_to_all(key_part[:, None, :], 'seq', split_axis=0, concat_axis=1,...  6.62 us
    all_to_all x1, starting transfers between devices, on_device(): lax.all_to_all(key_rows, 'seq', split_axis=0, concat_axis=1, tiled=True)  5.69 us
    ppermute x3, starting transfers between devices, on_device(): grad_in = lax.ppermute(new_grad, 'pipe', [(sender, sender - 1)])  5.02 us
  transfers between devices with their start and end apart: 26, of which 9 were waited for; matrix products, arithmetic and copies ran while one was open for 16% of the time, Pallas kernels for 0%

profile of v10, /device:TPU:15, one launch (start us, length us, event | category | flops | bytes accessed | tf_op | source)
XLA Modules:
  0.0 188.8 jit_solution(16549316691827588218)
XLA Ops:
  0.7 1.6 copy.183
  4.0 1.6 fusion.51
  11.3 2.0 %fusion.34 = (bf16[2,4,128,128]{3,2,1,0:T(8,128)(2,1)}, bf16[2,4,128,128]{3,2,1,0:T(8,128)(2,1)}, bf16[2,4,128,128]{3,2,1,0:T(8,128)(2,1)}) fusion(s32[]{:T(128)S(6)} %select_n.317, bf16[1,32,128,128]{3,2,1,0:T(8,128)(2,1)} %bitcast.98, bf16[1,32,128,128]{3,2,1,0:T(8,128)(2,1)S(1)} %get-tuple-element.98, s32[]{:T(128)S(6)} %select_n.313, s32[]{:T(128)S(6)} %select_n.315), kind=kLoop, calls=%fused_computation.96 | loop fusion | flops 393216 | bytes 2883596 | tf_op jit(solution)/shard_map/stack | solution.py:142
  17.2 5.7 %all-to-all-start = ((bf16[8,128,128]{2,1,0:T(8,128)(2,1)}), bf16[8,128,128]{2,1,0:T(8,128)(2,1)S(1)}, u32[]{:S(2)}, u32[]{:S(2)}) async-start(bf16[8,128,128]{2,1,0:T(8,128)(2,1)} %gather_fusion), calls=%async_computation | async-start | bytes 524288 | tf_op jit(solution)/shard_map/all_to_all | solution.py:151
  26.5 24.4 %collective-permute-done.2 = bf16[2,4,128,128]{3,2,1,0:T(8,128)(2,1)} collective-permute-done((bf16[2,4,128,128]{3,2,1,0:T(8,128)(2,1)}, bf16[2,4,128,128]{3,2,1,0:T(8,128)(2,1)}, u32[]{:S(2)}, u32[]{:S(2)}) %collective-permute-start.2) | collective-permute-done | bytes 262176 | tf_op jit(solution)/shard_map/ppermute | solution.py:118
  51.9 4.6 %collective-permute-done.3 = bf16[2,4,128,128]{3,2,1,0:T(8,128)(2,1)S(1)} collective-permute-done((bf16[2,4,128,128]{3,2,1,0:T(8,128)(2,1)}, bf16[2,4,128,128]{3,2,1,0:T(8,128)(2,1)S(1)}, u32[]{:S(2)}, u32[]{:S(2)}) %collective-permute-start.3) | collective-permute-done | bytes 262176 | tf_op jit(solution)/shard_map/ppermute | solution.py:118
  56.6 5.6 %collective-permute-done.5 = bf16[2,4,128,128]{3,2,1,0:T(8,128)(2,1)S(1)} collective-permute-done((bf16[2,4,128,128]{3,2,1,0:T(8,128)(2,1)}, bf16[2,4,128,128]{3,2,1,0:T(8,128)(2,1)S(1)}, u32[]{:S(2)}, u32[]{:S(2)}) %collective-permute-start.5) | collective-permute-done | bytes 262176 | tf_op jit(solution)/shard_map/ppermute | solution.py:118
  68.2 2.2 %fusion.52 = (f32[4,8,128]{2,1,0:T(8,128)S(1)}, f32[4,8,128,256]{3,2,1,0:T(8,128)S(1)}) fusion(f32[4,8,128,256]{3,2,1,0:T(8,128)S(1)} %fusion.3, pred[8,128,256]{2,1,0:T(8,128)(4,1)S(1)} %copy-done.19), kind=kOutput, calls=%fused_computation.160 | output fusion | flops 6291711 | bytes 8667136 | tf_op jit(solution)/shard_map/sub | solution.py:53
  74.1 2.5 %collective-permute-start.7 = (bf16[4,8,128,128]{3,2,1,0:T(8,128)(2,1)S(1)}, bf16[4,8,128,128]{3,2,1,0:T(8,128)(2,1)S(1)}, u32[]{:S(2)}, u32[]{:S(2)}) collective-permute-start(bf16[4,8,128,128]{3,2,1,0:T(8,128)(2,1)S(1)} %add_convert_fusion.3), channel_id=1, source_target_pairs={{24,16},{25,17},{26,18},{27,19},{28,20},{29,21},{30,22},{31,23}} | collective-permute-start | bytes 3145736 | tf_op jit(solution)/shard_map/ppermute | solution.py:169
  76.6 2.2 %collective-permute-done.7 = bf16[4,8,128,128]{3,2,1,0:T(8,128)(2,1)S(1)} collective-permute-done((bf16[4,8,128,128]{3,2,1,0:T(8,128)(2,1)S(1)}, bf16[4,8,128,128]{3,2,1,0:T(8,128)(2,1)S(1)}, u32[]{:S(2)}, u32[]{:S(2)}) %collective-permute-start.7) | collective-permute-done | bytes 1048608 | tf_op jit(solution)/shard_map/ppermute | solution.py:169
  81.5 1.6 collective-permute-start.8
  83.9 1.9 %collective-permute-start.10 = (bf16[4,128,128]{2,1,0:T(8,128)(2,1)}, bf16[4,128,128]{2,1,0:T(8,128)(2,1)}, u32[]{:S(2)}, u32[]{:S(2)}) collective-permute-start(bf16[4,128,128]{2,1,0:T(8,128)(2,1)} %get-tuple-element.96), channel_id=1, source_target_pairs={{24,25},{25,26},{26,27},{27,28},{28,29},{29,30},{30,31},{31,24}} | collective-permute-start | bytes 393224 | tf_op jit(solution)/shard_map/ppermute | solution.py:123
  85.9 1.9 %collective-permute-start.11 = (bf16[4,128,128]{2,1,0:T(8,128)(2,1)}, bf16[4,128,128]{2,1,0:T(8,128)(2,1)}, u32[]{:S(2)}, u32[]{:S(2)}) collective-permute-start(bf16[4,128,128]{2,1,0:T(8,128)(2,1)} %get-tuple-element.95), channel_id=1, source_target_pairs={{24,26},{25,27},{26,28},{27,29},{28,30},{29,31},{30,24},{31,25}} | collective-permute-start | bytes 393224 | tf_op jit(solution)/shard_map/ppermute | solution.py:123
  87.8 3.1 %collective-permute-start.12 = (bf16[4,128,128]{2,1,0:T(8,128)(2,1)}, bf16[4,128,128]{2,1,0:T(8,128)(2,1)}, u32[]{:S(2)}, u32[]{:S(2)}) collective-permute-start(bf16[4,128,128]{2,1,0:T(8,128)(2,1)} %get-tuple-element.94), channel_id=1, source_target_pairs={{24,27},{25,28},{26,29},{27,30},{28,31},{29,24},{30,25},{31,26}} | collective-permute-start | bytes 393224 | tf_op jit(solution)/shard_map/ppermute | solution.py:123
  90.9 4.2 %collective-permute-start.13 = (bf16[4,128,128]{2,1,0:T(8,128)(2,1)}, bf16[4,128,128]{2,1,0:T(8,128)(2,1)}, u32[]{:S(2)}, u32[]{:S(2)}) collective-permute-start(bf16[4,128,128]{2,1,0:T(8,128)(2,1)} %get-tuple-element.93), channel_id=1, source_target_pairs={{24,28},{25,29},{26,30},{27,31},{28,24},{29,25},{30,26},{31,27}} | collective-permute-start | bytes 393224 | tf_op jit(solution)/shard_map/ppermute | solution.py:123
  97.0 1.9 %collective-permute-start.14 = (bf16[4,128,128]{2,1,0:T(8,128)(2,1)S(1)}, bf16[4,128,128]{2,1,0:T(8,128)(2,1)S(1)}, u32[]{:S(2)}, u32[]{:S(2)}) collective-permute-start(bf16[4,128,128]{2,1,0:T(8,128)(2,1)S(1)} %get-tuple-element.92), channel_id=1, source_target_pairs={{24,29},{25,30},{26,31},{27,24},{28,25},{29,26},{30,27},{31,28}} | collective-permute-start | bytes 393224 | tf_op jit(solution)/shard_map/ppermute | solution.py:123
  98.9 1.6 constant_dynamic-update-slice_fusion.6
  100.5 4.0 %collective-permute-start.15 = (bf16[4,128,128]{2,1,0:T(8,128)(2,1)S(1)}, bf16[4,128,128]{2,1,0:T(8,128)(2,1)S(1)}, u32[]{:S(2)}, u32[]{:S(2)}) collective-permute-start(bf16[4,128,128]{2,1,0:T(8,128)(2,1)S(1)} %get-tuple-element.91), channel_id=1, source_target_pairs={{24,30},{25,31},{26,24},{27,25},{28,26},{29,27},{30,28},{31,29}} | collective-permute-start | bytes 393224 | tf_op jit(solution)/shard_map/ppermute | solution.py:123
  104.4 1.6 constant_dynamic-update-slice_fusion.5
  106.0 2.5 %collective-permute-start.16 = (bf16[4,128,128]{2,1,0:T(8,128)(2,1)S(1)}, bf16[4,128,128]{2,1,0:T(8,128)(2,1)S(1)}, u32[]{:S(2)}, u32[]{:S(2)}) collective-permute-start(bf16[4,128,128]{2,1,0:T(8,128)(2,1)S(1)} %get-tuple-element.90), channel_id=1, source_target_pairs={{24,31},{25,24},{26,25},{27,26},{28,27},{29,28},{30,29},{31,30}} | collective-permute-start | bytes 393224 | tf_op jit(solution)/shard_map/ppermute | solution.py:123
  108.6 2.0 %fusion.55 = f32[4,8,256,128]{3,2,1,0:T(8,128)S(1)} fusion(bf16[4,8,128,256]{3,2,1,0:T(8,128)(2,1)S(1)} %fusion.8, bf16[4,8,128,128]{3,2,1,0:T(8,128)(2,1)} %collective-permute-done.8), kind=kOutput, calls=%fused_computation.163 | convolution fusion | flops 268435456 | bytes 7340032 | tf_op jit(solution)/shard_map/hbij,hbid->hbjd/dot_general | solution.py:58
  111.1 1.7 add_convert_fusion.1
  113.8 1.6 constant_dynamic-update-slice_fusion.4
  115.4 1.6 constant_dynamic-update-slice_fusion.3
  126.0 1.5 multiply_convert_fusion
  131.3 1.8 collective-permute-start.17
  133.2 6.6 %all-to-all-start.1 = ((f32[1024,1,128]{2,1,0:T(1,128)}), f32[1024,1,128]{2,1,0:T(1,128)}, u32[]{:S(2)}, u32[]{:S(2)}) async-start(f32[1024,1,128]{2,1,0:T(1,128)} %bitcast.30), calls=%async_computation.1 | async-start | bytes 1048576 | tf_op jit(solution)/shard_map/all_to_all | solution.py:196
  141.3 3.9 %collective-permute-start.19 = (bf16[2,4,128,128]{3,2,1,0:T(8,128)(2,1)S(1)}, bf16[2,4,128,128]{3,2,1,0:T(8,128)(2,1)S(1)}, u32[]{:S(2)}, u32[]{:S(2)}) collective-permute-start(bf16[2,4,128,128]{3,2,1,0:T(8,128)(2,1)S(1)} %get-tuple-element.74), channel_id=1, source_target_pairs={{0,3},{1,4},{2,5},{3,6},{4,7},{5,0},{6,1},{7,2},{8,11},{9,12},{10,... | collective-permute-start | bytes 786440 | tf_op jit(solution)/shard_map/ppermute | solution.py:118
  147.6 25.5 %collective-permute-done.18 = bf16[2,4,128,128]{3,2,1,0:T(8,128)(2,1)S(1)} collective-permute-done((bf16[2,4,128,128]{3,2,1,0:T(8,128)(2,1)S(1)}, bf16[2,4,128,128]{3,2,1,0:T(8,128)(2,1)S(1)}, u32[]{:S(2)}, u32[]{:S(2)}) %collective-permute-start.18) | collective-permute-done | bytes 262176 | tf_op jit(solution)/shard_map/ppermute | solution.py:118
  173.1 3.6 %collective-permute-start.23 = (bf16[2,4,128,128]{3,2,1,0:T(8,128)(2,1)S(1)}, bf16[2,4,128,128]{3,2,1,0:T(8,128)(2,1)S(1)}, u32[]{:S(2)}, u32[]{:S(2)}) collective-permute-start(bf16[2,4,128,128]{3,2,1,0:T(8,128)(2,1)S(1)} %get-tuple-element.70), channel_id=1, source_target_pairs={{0,7},{1,0},{2,1},{3,2},{4,3},{5,4},{6,5},{7,6},{8,15},{9,8},{10,9... | collective-permute-start | bytes 786440 | tf_op jit(solution)/shard_map/ppermute | solution.py:118
  177.3 1.8 collective-permute-done.20
  181.3 2.2 %collective-permute-done.23 = bf16[2,4,128,128]{3,2,1,0:T(8,128)(2,1)S(1)} collective-permute-done((bf16[2,4,128,128]{3,2,1,0:T(8,128)(2,1)S(1)}, bf16[2,4,128,128]{3,2,1,0:T(8,128)(2,1)S(1)}, u32[]{:S(2)}, u32[]{:S(2)}) %collective-permute-start.23) | collective-permute-done | bytes 262176 | tf_op jit(solution)/shard_map/ppermute | solution.py:118
  (155 shorter events, 56.8 us)
Async XLA Ops:
  0.6 3.4 %copy-start = (bf16[128,4096]{1,0:T(8,128)(2,1)S(1)}, bf16[128,4096]{1,0:T(8,128)(2,1)}, u32[]{:S(2)}) copy-start(bf16[128,4096]{1,0:T(8,128)(2,1)} %param.18) | copy-start | bytes 3145732
  7.8 7.9 %copy-start.20 = (bf16[1,128,512]{2,1,0:T(8,128)(2,1)S(1)}, bf16[1,128,512]{2,1,0:T(8,128)(2,1)}, u32[]{:S(2)}) copy-start(bf16[1,128,512]{2,1,0:T(8,128)(2,1)} %param.16) | copy-start | bytes 393220
  7.8 16.2 %collective-permute-start = (bf16[2,4,128,128]{3,2,1,0:T(8,128)(2,1)}, bf16[2,4,128,128]{3,2,1,0:T(8,128)(2,1)}, u32[]{:S(2)}, u32[]{:S(2)}) collective-permute-start(bf16[2,4,128,128]{3,2,1,0:T(8,128)(2,1)} %get-tuple-element.82), channel_id=1, source_target_pairs={{0,1},{1,2},{2,3},{3,4},{4,5},{5,6},{6,7},{7,0},{8,9},{9,10},{10,1... | collective-permute-start | bytes 786440 | tf_op jit(solution)/shard_map/ppermute | solution.py:118
  9.1 16.2 %collective-permute-start.1 = (bf16[2,4,128,128]{3,2,1,0:T(8,128)(2,1)}, bf16[2,4,128,128]{3,2,1,0:T(8,128)(2,1)}, u32[]{:S(2)}, u32[]{:S(2)}) collective-permute-start(bf16[2,4,128,128]{3,2,1,0:T(8,128)(2,1)} %get-tuple-element.83), channel_id=1, source_target_pairs={{0,2},{1,3},{2,4},{3,5},{4,6},{5,7},{6,0},{7,1},{8,10},{9,11},{10,... | collective-permute-start | bytes 786440 | tf_op jit(solution)/shard_map/ppermute | solution.py:118
  10.4 40.5 %collective-permute-start.2 = (bf16[2,4,128,128]{3,2,1,0:T(8,128)(2,1)}, bf16[2,4,128,128]{3,2,1,0:T(8,128)(2,1)}, u32[]{:S(2)}, u32[]{:S(2)}) collective-permute-start(bf16[2,4,128,128]{3,2,1,0:T(8,128)(2,1)} %get-tuple-element.84), channel_id=1, source_target_pairs={{0,3},{1,4},{2,5},{3,6},{4,7},{5,0},{6,1},{7,2},{8,11},{9,12},{10,... | collective-permute-start | bytes 786440 | tf_op jit(solution)/shard_map/ppermute | solution.py:118
  11.3 11.6 %copy-start.21 = (s32[8]{0:T(128)S(1)}, s32[8]{0:T(128)}, u32[]{:S(2)}) copy-start(s32[8]{0:T(128)} %param.19) | copy-start | bytes 100
  13.3 43.2 %collective-permute-start.3 = (bf16[2,4,128,128]{3,2,1,0:T(8,128)(2,1)}, bf16[2,4,128,128]{3,2,1,0:T(8,128)(2,1)S(1)}, u32[]{:S(2)}, u32[]{:S(2)}) collective-permute-start(bf16[2,4,128,128]{3,2,1,0:T(8,128)(2,1)} %get-tuple-element.86), channel_id=1, source_target_pairs={{0,4},{1,5},{2,6},{3,7},{4,0},{5,1},{6,2},{7,3},{8,12},{9,13},{10,... | collective-permute-start | bytes 786440 | tf_op jit(solution)/shard_map/ppermute | solution.py:118
  14.7 41.9 %collective-permute-start.4 = (bf16[2,4,128,128]{3,2,1,0:T(8,128)(2,1)}, bf16[2,4,128,128]{3,2,1,0:T(8,128)(2,1)S(1)}, u32[]{:S(2)}, u32[]{:S(2)}) collective-permute-start(bf16[2,4,128,128]{3,2,1,0:T(8,128)(2,1)} %get-tuple-element.87), channel_id=1, source_target_pairs={{0,5},{1,6},{2,7},{3,0},{4,1},{5,2},{6,3},{7,4},{8,13},{9,14},{10,... | collective-permute-start | bytes 786440 | tf_op jit(solution)/shard_map/ppermute | solution.py:118
  17.2 47.7 %all-to-all-start = ((bf16[8,128,128]{2,1,0:T(8,128)(2,1)}), bf16[8,128,128]{2,1,0:T(8,128)(2,1)S(1)}, u32[]{:S(2)}, u32[]{:S(2)}) async-start(bf16[8,128,128]{2,1,0:T(8,128)(2,1)} %gather_fusion), calls=%async_computation | async-start | bytes 524288 | tf_op jit(solution)/shard_map/all_to_all | solution.py:151
  24.0 38.1 %collective-permute-start.5 = (bf16[2,4,128,128]{3,2,1,0:T(8,128)(2,1)}, bf16[2,4,128,128]{3,2,1,0:T(8,128)(2,1)S(1)}, u32[]{:S(2)}, u32[]{:S(2)}) collective-permute-start(bf16[2,4,128,128]{3,2,1,0:T(8,128)(2,1)} %get-tuple-element.85), channel_id=1, source_target_pairs={{0,6},{1,7},{2,0},{3,1},{4,2},{5,3},{6,4},{7,5},{8,14},{9,15},{10,... | collective-permute-start | bytes 786440 | tf_op jit(solution)/shard_map/ppermute | solution.py:118
  25.3 37.9 %collective-permute-start.6 = (bf16[2,4,128,128]{3,2,1,0:T(8,128)(2,1)}, bf16[2,4,128,128]{3,2,1,0:T(8,128)(2,1)S(1)}, u32[]{:S(2)}, u32[]{:S(2)}) collective-permute-start(bf16[2,4,128,128]{3,2,1,0:T(8,128)(2,1)} %get-tuple-element.80), channel_id=1, source_target_pairs={{0,7},{1,0},{2,1},{3,2},{4,3},{5,4},{6,5},{7,6},{8,15},{9,8},{10,9... | collective-permute-start | bytes 786440 | tf_op jit(solution)/shard_map/ppermute | solution.py:118
  74.1 4.7 %collective-permute-start.7 = (bf16[4,8,128,128]{3,2,1,0:T(8,128)(2,1)S(1)}, bf16[4,8,128,128]{3,2,1,0:T(8,128)(2,1)S(1)}, u32[]{:S(2)}, u32[]{:S(2)}) collective-permute-start(bf16[4,8,128,128]{3,2,1,0:T(8,128)(2,1)S(1)} %add_convert_fusion.3), channel_id=1, source_target_pairs={{24,16},{25,17},{26,18},{27,19},{28,20},{29,21},{30,22},{31,23}} | collective-permute-start | bytes 3145736 | tf_op jit(solution)/shard_map/ppermute | solution.py:169
  80.1 3.0 %copy-start.9 = (bf16[128,32,128]{2,0,1:T(8,128)(2,1)S(1)}, bf16[128,32,128]{2,0,1:T(8,128)(2,1)}, u32[]{:S(2)}) copy-start(bf16[128,32,128]{2,0,1:T(8,128)(2,1)} %get-tuple-element.97) | copy-start | bytes 3145732
  81.5 24.6 %collective-permute-start.8 = (bf16[4,8,128,128]{3,2,1,0:T(8,128)(2,1)}, bf16[4,8,128,128]{3,2,1,0:T(8,128)(2,1)}, u32[]{:S(2)}, u32[]{:S(2)}) collective-permute-start(bf16[4,8,128,128]{3,2,1,0:T(8,128)(2,1)} %add_convert_fusion.2), channel_id=1, source_target_pairs={{16,8},{17,9},{18,10},{19,11},{20,12},{21,13},{22,14},{23,15}} | collective-permute-start | bytes 3145736 | tf_op jit(solution)/shard_map/ppermute | solution.py:169
  83.9 13.0 %collective-permute-start.10 = (bf16[4,128,128]{2,1,0:T(8,128)(2,1)}, bf16[4,128,128]{2,1,0:T(8,128)(2,1)}, u32[]{:S(2)}, u32[]{:S(2)}) collective-permute-start(bf16[4,128,128]{2,1,0:T(8,128)(2,1)} %get-tuple-element.96), channel_id=1, source_target_pairs={{24,25},{25,26},{26,27},{27,28},{28,29},{29,30},{30,31},{31,24}} | collective-permute-start | bytes 393224 | tf_op jit(solution)/shard_map/ppermute | solution.py:123
  85.9 14.6 %collective-permute-start.11 = (bf16[4,128,128]{2,1,0:T(8,128)(2,1)}, bf16[4,128,128]{2,1,0:T(8,128)(2,1)}, u32[]{:S(2)}, u32[]{:S(2)}) collective-permute-start(bf16[4,128,128]{2,1,0:T(8,128)(2,1)} %get-tuple-element.95), channel_id=1, source_target_pairs={{24,26},{25,27},{26,28},{27,29},{28,30},{29,31},{30,24},{31,25}} | collective-permute-start | bytes 393224 | tf_op jit(solution)/shard_map/ppermute | solution.py:123
  87.8 25.0 %collective-permute-start.12 = (bf16[4,128,128]{2,1,0:T(8,128)(2,1)}, bf16[4,128,128]{2,1,0:T(8,128)(2,1)}, u32[]{:S(2)}, u32[]{:S(2)}) collective-permute-start(bf16[4,128,128]{2,1,0:T(8,128)(2,1)} %get-tuple-element.94), channel_id=1, source_target_pairs={{24,27},{25,28},{26,29},{27,30},{28,31},{29,24},{30,25},{31,26}} | collective-permute-start | bytes 393224 | tf_op jit(solution)/shard_map/ppermute | solution.py:123
  90.9 24.4 %collective-permute-start.13 = (bf16[4,128,128]{2,1,0:T(8,128)(2,1)}, bf16[4,128,128]{2,1,0:T(8,128)(2,1)}, u32[]{:S(2)}, u32[]{:S(2)}) collective-permute-start(bf16[4,128,128]{2,1,0:T(8,128)(2,1)} %get-tuple-element.93), channel_id=1, source_target_pairs={{24,28},{25,29},{26,30},{27,31},{28,24},{29,25},{30,26},{31,27}} | collective-permute-start | bytes 393224 | tf_op jit(solution)/shard_map/ppermute | solution.py:123
  97.0 20.0 %collective-permute-start.14 = (bf16[4,128,128]{2,1,0:T(8,128)(2,1)S(1)}, bf16[4,128,128]{2,1,0:T(8,128)(2,1)S(1)}, u32[]{:S(2)}, u32[]{:S(2)}) collective-permute-start(bf16[4,128,128]{2,1,0:T(8,128)(2,1)S(1)} %get-tuple-element.92), channel_id=1, source_target_pairs={{24,29},{25,30},{26,31},{27,24},{28,25},{29,26},{30,27},{31,28}} | collective-permute-start | bytes 393224 | tf_op jit(solution)/shard_map/ppermute | solution.py:123
  100.5 17.2 %collective-permute-start.15 = (bf16[4,128,128]{2,1,0:T(8,128)(2,1)S(1)}, bf16[4,128,128]{2,1,0:T(8,128)(2,1)S(1)}, u32[]{:S(2)}, u32[]{:S(2)}) collective-permute-start(bf16[4,128,128]{2,1,0:T(8,128)(2,1)S(1)} %get-tuple-element.91), channel_id=1, source_target_pairs={{24,30},{25,31},{26,24},{27,25},{28,26},{29,27},{30,28},{31,29}} | collective-permute-start | bytes 393224 | tf_op jit(solution)/shard_map/ppermute | solution.py:123
  106.0 12.3 %collective-permute-start.16 = (bf16[4,128,128]{2,1,0:T(8,128)(2,1)S(1)}, bf16[4,128,128]{2,1,0:T(8,128)(2,1)S(1)}, u32[]{:S(2)}, u32[]{:S(2)}) collective-permute-start(bf16[4,128,128]{2,1,0:T(8,128)(2,1)S(1)} %get-tuple-element.90), channel_id=1, source_target_pairs={{24,31},{25,24},{26,25},{27,26},{28,27},{29,28},{30,29},{31,30}} | collective-permute-start | bytes 393224 | tf_op jit(solution)/shard_map/ppermute | solution.py:123
  111.1 7.9 %copy-start.3 = (bf16[2,4,1024,128]{3,2,1,0:T(8,128)(2,1)S(1)}, bf16[2,4,1024,128]{3,2,1,0:T(8,128)(2,1)}, u32[]{:S(2)}) copy-start(bf16[2,4,1024,128]{3,2,1,0:T(8,128)(2,1)} %copy-done.2) | copy-start | bytes 6291460
  112.8 7.5 %collective-permute-start.9 = (bf16[4,8,128,128]{3,2,1,0:T(8,128)(2,1)S(1)}, bf16[4,8,128,128]{3,2,1,0:T(8,128)(2,1)S(1)}, u32[]{:S(2)}, u32[]{:S(2)}) collective-permute-start(bf16[4,8,128,128]{3,2,1,0:T(8,128)(2,1)S(1)} %add_convert_fusion.1), channel_id=1, source_target_pairs={{8,0},{9,1},{10,2},{11,3},{12,4},{13,5},{14,6},{15,7}} | collective-permute-start | bytes 3145736 | tf_op jit(solution)/shard_map/ppermute | solution.py:169
  131.3 14.4 %collective-permute-start.17 = (bf16[2,4,128,128]{3,2,1,0:T(8,128)(2,1)S(1)}, bf16[2,4,128,128]{3,2,1,0:T(8,128)(2,1)S(1)}, u32[]{:S(2)}, u32[]{:S(2)}) collective-permute-start(bf16[2,4,128,128]{3,2,1,0:T(8,128)(2,1)S(1)} %get-tuple-element.72), channel_id=1, source_target_pairs={{0,1},{1,2},{2,3},{3,4},{4,5},{5,6},{6,7},{7,0},{8,9},{9,10},{10,1... | collective-permute-start | bytes 786440 | tf_op jit(solution)/shard_map/ppermute | solution.py:118
  133.2 53.6 %all-to-all-start.1 = ((f32[1024,1,128]{2,1,0:T(1,128)}), f32[1024,1,128]{2,1,0:T(1,128)}, u32[]{:S(2)}, u32[]{:S(2)}) async-start(f32[1024,1,128]{2,1,0:T(1,128)} %bitcast.30), calls=%async_computation.1 | async-start | bytes 1048576 | tf_op jit(solution)/shard_map/all_to_all | solution.py:196
  139.8 39.6 %collective-permute-start.21 = (bf16[2,4,128,128]{3,2,1,0:T(8,128)(2,1)S(1)}, bf16[2,4,128,128]{3,2,1,0:T(8,128)(2,1)S(1)}, u32[]{:S(2)}, u32[]{:S(2)}) collective-permute-start(bf16[2,4,128,128]{3,2,1,0:T(8,128)(2,1)S(1)} %get-tuple-element.77), channel_id=1, source_target_pairs={{0,5},{1,6},{2,7},{3,0},{4,1},{5,2},{6,3},{7,4},{8,13},{9,14},{10,... | collective-permute-start | bytes 786440 | tf_op jit(solution)/shard_map/ppermute | solution.py:118
  139.9 33.2 %collective-permute-start.18 = (bf16[2,4,128,128]{3,2,1,0:T(8,128)(2,1)S(1)}, bf16[2,4,128,128]{3,2,1,0:T(8,128)(2,1)S(1)}, u32[]{:S(2)}, u32[]{:S(2)}) collective-permute-start(bf16[2,4,128,128]{3,2,1,0:T(8,128)(2,1)S(1)} %get-tuple-element.73), channel_id=1, source_target_pairs={{0,2},{1,3},{2,4},{3,5},{4,6},{5,7},{6,0},{7,1},{8,10},{9,11},{10,... | collective-permute-start | bytes 786440 | tf_op jit(solution)/shard_map/ppermute | solution.py:118
  141.3 35.7 %collective-permute-start.19 = (bf16[2,4,128,128]{3,2,1,0:T(8,128)(2,1)S(1)}, bf16[2,4,128,128]{3,2,1,0:T(8,128)(2,1)S(1)}, u32[]{:S(2)}, u32[]{:S(2)}) collective-permute-start(bf16[2,4,128,128]{3,2,1,0:T(8,128)(2,1)S(1)} %get-tuple-element.74), channel_id=1, source_target_pairs={{0,3},{1,4},{2,5},{3,6},{4,7},{5,0},{6,1},{7,2},{8,11},{9,12},{10,... | collective-permute-start | bytes 786440 | tf_op jit(solution)/shard_map/ppermute | solution.py:118
  145.2 33.9 %collective-permute-start.20 = (bf16[2,4,128,128]{3,2,1,0:T(8,128)(2,1)S(1)}, bf16[2,4,128,128]{3,2,1,0:T(8,128)(2,1)S(1)}, u32[]{:S(2)}, u32[]{:S(2)}) collective-permute-start(bf16[2,4,128,128]{3,2,1,0:T(8,128)(2,1)S(1)} %get-tuple-element.75), channel_id=1, source_target_pairs={{0,4},{1,5},{2,6},{3,7},{4,0},{5,1},{6,2},{7,3},{8,12},{9,13},{10,... | collective-permute-start | bytes 786440 | tf_op jit(solution)/shard_map/ppermute | solution.py:118
  145.8 35.3 %collective-permute-start.22 = (bf16[2,4,128,128]{3,2,1,0:T(8,128)(2,1)S(1)}, bf16[2,4,128,128]{3,2,1,0:T(8,128)(2,1)S(1)}, u32[]{:S(2)}, u32[]{:S(2)}) collective-permute-start(bf16[2,4,128,128]{3,2,1,0:T(8,128)(2,1)S(1)} %get-tuple-element.76), channel_id=1, source_target_pairs={{0,6},{1,7},{2,0},{3,1},{4,2},{5,3},{6,4},{7,5},{8,14},{9,15},{10,... | collective-permute-start | bytes 786440 | tf_op jit(solution)/shard_map/ppermute | solution.py:118
  173.1 10.5 %collective-permute-start.23 = (bf16[2,4,128,128]{3,2,1,0:T(8,128)(2,1)S(1)}, bf16[2,4,128,128]{3,2,1,0:T(8,128)(2,1)S(1)}, u32[]{:S(2)}, u32[]{:S(2)}) collective-permute-start(bf16[2,4,128,128]{3,2,1,0:T(8,128)(2,1)S(1)} %get-tuple-element.70), channel_id=1, source_target_pairs={{0,7},{1,0},{2,1},{3,2},{4,3},{5,4},{6,5},{7,6},{8,15},{9,8},{10,9... | collective-permute-start | bytes 786440 | tf_op jit(solution)/shard_map/ppermute | solution.py:118
  184.2 4.5 %copy-start.1 = (bf16[128,4096]{1,0:T(8,128)(2,1)S(1)}, bf16[128,4096]{1,0:T(8,128)(2,1)}, u32[]{:S(2)}) copy-start(bf16[128,4096]{1,0:T(8,128)(2,1)} %param.18) | copy-start | bytes 3145732
  (16 other events, 25.0 us)

commit v11 on v10

--- a/solution.py
+++ b/solution.py
@@ -110,7 +110,7 @@
         out_shape = list(value.shape)
         out_shape[split_axis] = split_size
         out_shape[concat_axis] = concat_size * seq_ways
-        result = jnp.zeros(out_shape, value.dtype)
+        received = []
         for shift in range(seq_ways):
             target = (seq_index + shift) % seq_ways
             chunk = lax.dynamic_slice_in_dim(value, target * split_size, split_size, axis=split_axis)
@@ -125,11 +125,25 @@
                     ("pipe", "seq"),
                     [(base + s, base + (s + shift) % seq_ways) for s in range(seq_ways)],
                 )
-            source = (seq_index + seq_ways - shift) % seq_ways
-            result = lax.dynamic_update_slice_in_dim(
-                result, chunk, source * concat_size, axis=concat_axis
-            )
-        return result
+            received.append(chunk)
+
+        def assemble(chunks):
+            result = jnp.zeros(out_shape, value.dtype)
+            for shift, chunk in enumerate(chunks):
+                source = (seq_index + seq_ways - shift) % seq_ways
+                result = lax.dynamic_update_slice_in_dim(
+                    result, chunk, source * concat_size, axis=concat_axis
+                )
+            return result
+
+        if section is None:
+            return assemble(received)
+        return lax.cond(
+            section_index == section,
+            assemble,
+            lambda chunks: jnp.zeros(out_shape, value.dtype),
+            received,
+        )
 
     def to_blocks(head_rows):
         return head_rows.reshape(local_heads, block_count, BLK, DH)

time: 191 us -> 198 us (1.037)
  local copies, waits for them, and re-layouts: 37 us -> 45.4 us
  starting transfers between devices: 55.5 us -> 52.2 us
  waiting for transfers between devices: 68.7 us -> 70.7 us
    ppermute x0 -> x7, local copies, waits for them, and re-layouts: none -> 6.88 us  [transpose_seq(): lax.ppermute(chunk, 'seq', [(s, (s + shift) % seq_ways) for s in range(se...]
    dynamic_update_slice x23 -> x24, local copies, waits for them, and re-layouts: 14.5 us -> 8.29 us  [assemble(): lax.dynamic_update_slice_in_dim(result, chunk, source * concat_size, axis...]
    another operation x1 -> x9, local copies, waits for them, and re-layouts: 1.38 us -> 7.53 us  [head_major(): return jnp.transpose(rows.reshape(tok_rows, head_count, DH), (1, 0, 2))]
    ppermute x7, waiting for transfers between devices: 0.02 us -> 4.2 us  [transpose_seq(): lax.ppermute(chunk, ('pipe', 'seq'), [(base + s, base + (s + shift) % seq...]
    ppermute x14, starting transfers between devices: 18.6 us -> 15.6 us  [transpose_seq(): lax.ppermute(chunk, 'seq', [(s, (s + shift) % seq_ways) for s in range(se...]
    unnamed x48 -> x57, local copies, waits for them, and re-layouts: 10.7 us -> 13.2 us
    ppermute x14, waiting for transfers between devices: 66.5 us -> 64.3 us  [transpose_seq(): lax.ppermute(chunk, 'seq', [(s, (s + shift) % seq_ways) for s in range(se...]
  transfers between devices with their start and end apart: 26 -> 26, of which waited for: 9 -> 11; matrix products, arithmetic and copies ran while one was open for 16% -> 17% of each run, Pallas kernels for 0% -> 0%
where the time goes in v11:
time: 198 us; the launch traced here: 195 us
  waiting for transfers between devices  70.7 us (36%)
  starting transfers between devices  52.2 us (26%)
  local copies, waits for them, and re-layouts  45.4 us (23%)
  other arithmetic  16.1 us (8%)
  matrix products  8.82 us (4%)
    ppermute x14, waiting for transfers between devices, transpose_seq(): lax.ppermute(chunk, 'seq', [(s, (s + shift) % seq_ways) for s in range(se...  64.3 us
    ppermute x7, starting transfers between devices, transpose_seq(): lax.ppermute(chunk, ('pipe', 'seq'), [(base + s, base + (s + shift) % seq...  19.5 us
    ppermute x14, starting transfers between devices, transpose_seq(): lax.ppermute(chunk, 'seq', [(s, (s + shift) % seq_ways) for s in range(se...  15.6 us
    unnamed x57, local copies, waits for them, and re-layouts  13.2 us
    dynamic_update_slice x24, local copies, waits for them, and re-layouts, assemble(): lax.dynamic_update_slice_in_dim(result, chunk, source * concat_size, axis...  8.29 us
    another operation x9, local copies, waits for them, and re-layouts  7.53 us
    ppermute x7, local copies, waits for them, and re-layouts, transpose_seq(): lax.ppermute(chunk, 'seq', [(s, (s + shift) % seq_ways) for s in range(se...  6.88 us
    all_to_all x1, starting transfers between devices, on_device(): lax.all_to_all(key_part[:, None, :], 'seq', split_axis=0, concat_axis=1,...  6.35 us
  transfers between devices with their start and end apart: 26, of which 11 were waited for; matrix products, arithmetic and copies ran while one was open for 17% of the time, Pallas kernels for 0%

profile of v11, /device:TPU:15, one launch (start us, length us, event | category | flops | bytes accessed | tf_op | source)
XLA Modules:
  0.0 194.9 jit_solution(7472310856789674252)
XLA Ops:
  0.7 1.7 copy.167
  15.2 5.8 %all-to-all-start = ((bf16[8,128,128]{2,1,0:T(8,128)(2,1)}), bf16[8,128,128]{2,1,0:T(8,128)(2,1)S(1)}, u32[]{:S(2)}, u32[]{:S(2)}) async-start(bf16[8,128,128]{2,1,0:T(8,128)(2,1)} %gather_fusion), calls=%async_computation | async-start | bytes 524288 | tf_op jit(solution)/shard_map/all_to_all | solution.py:165
  25.6 25.5 %collective-permute-done.2 = bf16[2,4,128,128]{2,3,1,0:T(8,128)(2,1)} collective-permute-done((bf16[2,4,128,128]{2,3,1,0:T(8,128)(2,1)}, bf16[2,4,128,128]{2,3,1,0:T(8,128)(2,1)}, u32[]{:S(2)}, u32[]{:S(2)}) %collective-permute-start.2) | collective-permute-done | bytes 262176 | tf_op jit(solution)/shard_map/ppermute | solution.py:118
  52.3 4.5 %collective-permute-done.3 = bf16[2,4,128,128]{2,3,1,0:T(8,128)(2,1)} collective-permute-done((bf16[2,4,128,128]{2,3,1,0:T(8,128)(2,1)}, bf16[2,4,128,128]{2,3,1,0:T(8,128)(2,1)}, u32[]{:S(2)}, u32[]{:S(2)}) %collective-permute-start.3) | collective-permute-done | bytes 262176 | tf_op jit(solution)/shard_map/ppermute | solution.py:118
  58.2 3.1 %collective-permute-done.5 = bf16[2,4,128,128]{2,3,1,0:T(8,128)(2,1)} collective-permute-done((bf16[2,4,128,128]{2,3,1,0:T(8,128)(2,1)S(1)}, bf16[2,4,128,128]{2,3,1,0:T(8,128)(2,1)}, u32[]{:S(2)}, u32[]{:S(2)}) %collective-permute-start.5) | collective-permute-done | bytes 262176 | tf_op jit(solution)/shard_map/ppermute | solution.py:118
  68.8 2.2 %fusion.49 = (f32[4,8,128]{2,1,0:T(8,128)S(1)}, f32[4,8,128,256]{3,2,1,0:T(8,128)S(1)}) fusion(f32[4,8,128,256]{3,2,1,0:T(8,128)S(1)} %fusion.3, pred[8,128,256]{2,1,0:T(8,128)(4,1)S(1)} %copy-done.22), kind=kOutput, calls=%fused_computation.158 | output fusion | flops 6291711 | bytes 8667136 | tf_op jit(solution)/shard_map/sub | solution.py:53
  74.7 2.4 %collective-permute-start.7 = (bf16[4,8,128,128]{3,2,1,0:T(8,128)(2,1)S(1)}, bf16[4,8,128,128]{3,2,1,0:T(8,128)(2,1)S(1)}, u32[]{:S(2)}, u32[]{:S(2)}) collective-permute-start(bf16[4,8,128,128]{3,2,1,0:T(8,128)(2,1)S(1)} %add_convert_fusion.3), channel_id=1, source_target_pairs={{24,16},{25,17},{26,18},{27,19},{28,20},{29,21},{30,22},{31,23}} | collective-permute-start | bytes 3145736 | tf_op jit(solution)/shard_map/ppermute | solution.py:183
  77.1 2.2 %collective-permute-done.7 = bf16[4,8,128,128]{3,2,1,0:T(8,128)(2,1)S(1)} collective-permute-done((bf16[4,8,128,128]{3,2,1,0:T(8,128)(2,1)S(1)}, bf16[4,8,128,128]{3,2,1,0:T(8,128)(2,1)S(1)}, u32[]{:S(2)}, u32[]{:S(2)}) %collective-permute-start.7) | collective-permute-done | bytes 1048608 | tf_op jit(solution)/shard_map/ppermute | solution.py:183
  84.7 1.6 collective-permute-start.9
  87.1 1.9 collective-permute-start.10
  89.0 1.9 collective-permute-start.11
  91.0 3.1 %collective-permute-start.12 = (bf16[4,128,128]{1,2,0:T(8,128)(2,1)S(1)}, bf16[4,128,128]{1,2,0:T(8,128)(2,1)S(1)}, u32[]{:S(2)}, u32[]{:S(2)}) collective-permute-start(bf16[4,128,128]{1,2,0:T(8,128)(2,1)S(1)} %get-tuple-element.169), channel_id=1, source_target_pairs={{24,27},{25,28},{26,29},{27,30},{28,31},{29,24},{30,25},{31,26}} | collective-permute-start | bytes 393224 | tf_op jit(solution)/shard_map/ppermute | solution.py:123
  94.0 4.3 %collective-permute-start.13 = (bf16[4,128,128]{1,2,0:T(8,128)(2,1)}, bf16[4,128,128]{1,2,0:T(8,128)(2,1)}, u32[]{:S(2)}, u32[]{:S(2)}) collective-permute-start(bf16[4,128,128]{1,2,0:T(8,128)(2,1)} %get-tuple-element.168), channel_id=1, source_target_pairs={{24,28},{25,29},{26,30},{27,31},{28,24},{29,25},{30,26},{31,27}} | collective-permute-start | bytes 393224 | tf_op jit(solution)/shard_map/ppermute | solution.py:123
  98.3 1.9 collective-permute-start.14
  100.3 4.0 %collective-permute-start.15 = (bf16[4,128,128]{1,2,0:T(8,128)(2,1)S(1)}, bf16[4,128,128]{1,2,0:T(8,128)(2,1)}, u32[]{:S(2)}, u32[]{:S(2)}) collective-permute-start(bf16[4,128,128]{1,2,0:T(8,128)(2,1)S(1)} %get-tuple-element.166), channel_id=1, source_target_pairs={{24,30},{25,31},{26,24},{27,25},{28,26},{29,27},{30,28},{31,29}} | collective-permute-start | bytes 393224 | tf_op jit(solution)/shard_map/ppermute | solution.py:123
  105.0 2.5 %collective-permute-start.16 = (bf16[4,128,128]{1,2,0:T(8,128)(2,1)S(1)}, bf16[4,128,128]{1,2,0:T(8,128)(2,1)}, u32[]{:S(2)}, u32[]{:S(2)}) collective-permute-start(bf16[4,128,128]{1,2,0:T(8,128)(2,1)S(1)} %get-tuple-element.165), channel_id=1, source_target_pairs={{24,31},{25,24},{26,25},{27,26},{28,27},{29,28},{30,29},{31,30}} | collective-permute-start | bytes 393224 | tf_op jit(solution)/shard_map/ppermute | solution.py:123
  107.5 4.2 %collective-permute-done.16 = bf16[4,128,128]{1,2,0:T(8,128)(2,1)} collective-permute-done((bf16[4,128,128]{1,2,0:T(8,128)(2,1)S(1)}, bf16[4,128,128]{1,2,0:T(8,128)(2,1)}, u32[]{:S(2)}, u32[]{:S(2)}) %collective-permute-start.16) | collective-permute-done | bytes 131104 | tf_op jit(solution)/shard_map/ppermute | solution.py:123
  111.7 13.2 %conditional.1 = (bf16[4,1024,128]{2,1,0:T(8,128)(2,1)}) conditional(s32[]{:T(128)} %convert_element_type.84, () %tuple.34, (s32[]{:T(128)}, bf16[4,128,128]{1,2,0:T(8,128)(2,1)S(1)}, bf16[4,128,128]{1,2,0:T(8,128)(2,1)}, bf16[4,128,128]{1,2,0:T(8,128)(2,1)}, bf16[4,128,128]{1,2,0:T(8,128)(2,1)}, /*index=5*/bf16[4,128,128]{1,2,0:T(8,128)(2,1)}, ...), branch_computations={%region_5.6_spmd, %region_6.7_spmd} | conditional | flops 128 | bytes 5768574 | solution.py:141
  124.9 1.7 bitcast_select_fusion
  126.5 2.0 %fusion.53 = f32[4,8,256,128]{3,2,1,0:T(8,128)S(1)} fusion(bf16[4,8,128,256]{3,2,1,0:T(8,128)(2,1)S(1)} %fusion.8, bf16[4,8,128,128]{3,2,1,0:T(8,128)(2,1)} %collective-permute-done.9), kind=kOutput, calls=%fused_computation.162 | convolution fusion | flops 268435456 | bytes 7340032 | tf_op jit(solution)/shard_map/hbij,hbid->hbjd/dot_general | solution.py:58
  130.9 2.2 %fusion.9 = (bf16[4,8,128,128]{3,2,1,0:T(8,128)(2,1)S(1)}, bf16[4,8,128,128]{3,2,1,0:T(8,128)(2,1)S(1)}) fusion(f32[4,8,128,128]{3,2,1,0:T(8,128)S(1)} %fusion.35, bf16[4,8,128,128]{3,2,1,0:T(8,128)(2,1)} %collective-permute-done.9, bf16[4,8,128,128]{3,2,1,0:T(8,128)(2,1)} %add_convert_fusion.1, bf16[4,8,128,128]{3,2,1,0:T(8,128)(2,1)S(1)} %copy-done.18, ...), kind=kLoop, calls=%fused_computation.73 | loop fusion | flops 4718592 | bytes 11534339 | tf_op jit(solution)/shard_map/jit(_where)/select_n | solution.py:188
  134.2 1.4 copy-done.14
  135.5 1.5 multiply_convert_fusion
  142.2 6.4 %all-to-all-start.1 = ((f32[1024,1,128]{2,1,0:T(1,128)}), f32[1024,1,128]{2,1,0:T(1,128)S(1)}, u32[]{:S(2)}, u32[]{:S(2)}) async-start(f32[1024,1,128]{2,1,0:T(1,128)} %bitcast.33), calls=%async_computation.1 | async-start | bytes 1048576 | tf_op jit(solution)/shard_map/all_to_all | solution.py:210
  148.5 1.4 collective-permute-start.18
  150.0 3.9 %collective-permute-start.19 = (bf16[2,4,128,128]{3,2,1,0:T(8,128)(2,1)S(1)}, bf16[2,4,128,128]{3,2,1,0:T(8,128)(2,1)S(1)}, u32[]{:S(2)}, u32[]{:S(2)}) collective-permute-start(bf16[2,4,128,128]{3,2,1,0:T(8,128)(2,1)S(1)} %get-tuple-element.149), channel_id=1, source_target_pairs={{0,3},{1,4},{2,5},{3,6},{4,7},{5,0},{6,1},{7,2},{8,11},{9,12},{10,... | collective-permute-start | bytes 786440 | tf_op jit(solution)/shard_map/ppermute | solution.py:118
  154.4 7.9 %collective-permute-done.17 = bf16[2,4,128,128]{3,2,1,0:T(8,128)(2,1)S(1)} collective-permute-done((bf16[2,4,128,128]{3,2,1,0:T(8,128)(2,1)S(1)}, bf16[2,4,128,128]{3,2,1,0:T(8,128)(2,1)S(1)}, u32[]{:S(2)}, u32[]{:S(2)}) %collective-permute-start.17) | collective-permute-done | bytes 262176 | tf_op jit(solution)/shard_map/ppermute | solution.py:118
  162.6 18.0 %collective-permute-done.18 = bf16[2,4,128,128]{3,2,1,0:T(8,128)(2,1)S(1)} collective-permute-done((bf16[2,4,128,128]{3,2,1,0:T(8,128)(2,1)}, bf16[2,4,128,128]{3,2,1,0:T(8,128)(2,1)S(1)}, u32[]{:S(2)}, u32[]{:S(2)}) %collective-permute-start.18) | collective-permute-done | bytes 262176 | tf_op jit(solution)/shard_map/ppermute | solution.py:118
  180.7 3.4 %collective-permute-start.23 = (bf16[2,4,128,128]{3,2,1,0:T(8,128)(2,1)S(1)}, bf16[2,4,128,128]{3,2,1,0:T(8,128)(2,1)S(1)}, u32[]{:S(2)}, u32[]{:S(2)}) collective-permute-start(bf16[2,4,128,128]{3,2,1,0:T(8,128)(2,1)S(1)} %get-tuple-element.145), channel_id=1, source_target_pairs={{0,7},{1,0},{2,1},{3,2},{4,3},{5,4},{6,5},{7,6},{8,15},{9,8},{10,9... | collective-permute-start | bytes 786440 | tf_op jit(solution)/shard_map/ppermute | solution.py:118
  184.7 1.5 collective-permute-done.20
  186.8 1.4 collective-permute-done.22
  188.5 2.3 %collective-permute-done.23 = bf16[2,4,128,128]{3,2,1,0:T(8,128)(2,1)S(1)} collective-permute-done((bf16[2,4,128,128]{3,2,1,0:T(8,128)(2,1)S(1)}, bf16[2,4,128,128]{3,2,1,0:T(8,128)(2,1)S(1)}, u32[]{:S(2)}, u32[]{:S(2)}) %collective-permute-start.23) | collective-permute-done | bytes 262176 | tf_op jit(solution)/shard_map/ppermute | solution.py:118
  (183 shorter events, 65.5 us)
Async XLA Ops:
  0.7 3.1 %copy-start.20 = (bf16[1,128,4096]{2,1,0:T(8,128)(2,1)S(1)}, bf16[1,128,4096]{2,1,0:T(8,128)(2,1)}, u32[]{:S(2)}) copy-start(bf16[1,128,4096]{2,1,0:T(8,128)(2,1)} %param.17) | copy-start | bytes 3145732
  7.0 6.7 %copy-start.23 = (bf16[1,128,512]{2,1,0:T(8,128)(2,1)S(1)}, bf16[1,128,512]{2,1,0:T(8,128)(2,1)}, u32[]{:S(2)}) copy-start(bf16[1,128,512]{2,1,0:T(8,128)(2,1)} %param.18) | copy-start | bytes 393220
  7.0 15.8 %collective-permute-start = (bf16[2,4,128,128]{2,3,1,0:T(8,128)(2,1)}, bf16[2,4,128,128]{2,3,1,0:T(8,128)(2,1)}, u32[]{:S(2)}, u32[]{:S(2)}) collective-permute-start(bf16[2,4,128,128]{2,3,1,0:T(8,128)(2,1)} %get-tuple-element.157), channel_id=1, source_target_pairs={{0,1},{1,2},{2,3},{3,4},{4,5},{5,6},{6,7},{7,0},{8,9},{9,10},{10,1... | collective-permute-start | bytes 786440 | tf_op jit(solution)/shard_map/ppermute | solution.py:118
  8.2 16.0 %collective-permute-start.1 = (bf16[2,4,128,128]{2,3,1,0:T(8,128)(2,1)}, bf16[2,4,128,128]{2,3,1,0:T(8,128)(2,1)}, u32[]{:S(2)}, u32[]{:S(2)}) collective-permute-start(bf16[2,4,128,128]{2,3,1,0:T(8,128)(2,1)} %get-tuple-element.158), channel_id=1, source_target_pairs={{0,2},{1,3},{2,4},{3,5},{4,6},{5,7},{6,0},{7,1},{8,10},{9,11},{10,... | collective-permute-start | bytes 786440 | tf_op jit(solution)/shard_map/ppermute | solution.py:118
  9.5 41.7 %collective-permute-start.2 = (bf16[2,4,128,128]{2,3,1,0:T(8,128)(2,1)}, bf16[2,4,128,128]{2,3,1,0:T(8,128)(2,1)}, u32[]{:S(2)}, u32[]{:S(2)}) collective-permute-start(bf16[2,4,128,128]{2,3,1,0:T(8,128)(2,1)} %get-tuple-element.159), channel_id=1, source_target_pairs={{0,3},{1,4},{2,5},{3,6},{4,7},{5,0},{6,1},{7,2},{8,11},{9,12},{10,... | collective-permute-start | bytes 786440 | tf_op jit(solution)/shard_map/ppermute | solution.py:118
  10.5 46.3 %collective-permute-start.3 = (bf16[2,4,128,128]{2,3,1,0:T(8,128)(2,1)}, bf16[2,4,128,128]{2,3,1,0:T(8,128)(2,1)}, u32[]{:S(2)}, u32[]{:S(2)}) collective-permute-start(bf16[2,4,128,128]{2,3,1,0:T(8,128)(2,1)} %get-tuple-element.160), channel_id=1, source_target_pairs={{0,4},{1,5},{2,6},{3,7},{4,0},{5,1},{6,2},{7,3},{8,12},{9,13},{10,... | collective-permute-start | bytes 786440 | tf_op jit(solution)/shard_map/ppermute | solution.py:118
  11.8 9.5 %copy-start.26 = (s32[8]{0:T(128)S(1)}, s32[8]{0:T(128)}, u32[]{:S(2)}) copy-start(s32[8]{0:T(128)} %param.21) | copy-start | bytes 100
  12.7 45.3 %collective-permute-start.4 = (bf16[2,4,128,128]{2,3,1,0:T(8,128)(2,1)}, bf16[2,4,128,128]{2,3,1,0:T(8,128)(2,1)S(1)}, u32[]{:S(2)}, u32[]{:S(2)}) collective-permute-start(bf16[2,4,128,128]{2,3,1,0:T(8,128)(2,1)} %get-tuple-element.162), channel_id=1, source_target_pairs={{0,5},{1,6},{2,7},{3,0},{4,1},{5,2},{6,3},{7,4},{8,13},{9,14},{10,... | collective-permute-start | bytes 786440 | tf_op jit(solution)/shard_map/ppermute | solution.py:118
  15.2 7.5 %copy-start.21 = (bf16[2,4,128,128]{2,3,1,0:T(8,128)(2,1)S(1)}, bf16[2,4,128,128]{2,3,1,0:T(8,128)(2,1)}, u32[]{:S(2)}) copy-start(bf16[2,4,128,128]{2,3,1,0:T(8,128)(2,1)} %get-tuple-element.161) | copy-start | bytes 786436
  15.2 50.3 %all-to-all-start = ((bf16[8,128,128]{2,1,0:T(8,128)(2,1)}), bf16[8,128,128]{2,1,0:T(8,128)(2,1)S(1)}, u32[]{:S(2)}, u32[]{:S(2)}) async-start(bf16[8,128,128]{2,1,0:T(8,128)(2,1)} %gather_fusion), calls=%async_computation | async-start | bytes 524288 | tf_op jit(solution)/shard_map/all_to_all | solution.py:165
  22.8 38.5 %collective-permute-start.5 = (bf16[2,4,128,128]{2,3,1,0:T(8,128)(2,1)S(1)}, bf16[2,4,128,128]{2,3,1,0:T(8,128)(2,1)}, u32[]{:S(2)}, u32[]{:S(2)}) collective-permute-start(bf16[2,4,128,128]{2,3,1,0:T(8,128)(2,1)S(1)} %copy-done.21), channel_id=1, source_target_pairs={{0,6},{1,7},{2,0},{3,1},{4,2},{5,3},{6,4},{7,5},{8,14},{9,15},{10,... | collective-permute-start | bytes 786440 | tf_op jit(solution)/shard_map/ppermute | solution.py:118
  24.2 38.4 %collective-permute-start.6 = (bf16[2,4,128,128]{2,3,1,0:T(8,128)(2,1)}, bf16[2,4,128,128]{2,3,1,0:T(8,128)(2,1)}, u32[]{:S(2)}, u32[]{:S(2)}) collective-permute-start(bf16[2,4,128,128]{2,3,1,0:T(8,128)(2,1)} %get-tuple-element.155), channel_id=1, source_target_pairs={{0,7},{1,0},{2,1},{3,2},{4,3},{5,4},{6,5},{7,6},{8,15},{9,8},{10,9... | collective-permute-start | bytes 786440 | tf_op jit(solution)/shard_map/ppermute | solution.py:118
  74.7 4.6 %collective-permute-start.7 = (bf16[4,8,128,128]{3,2,1,0:T(8,128)(2,1)S(1)}, bf16[4,8,128,128]{3,2,1,0:T(8,128)(2,1)S(1)}, u32[]{:S(2)}, u32[]{:S(2)}) collective-permute-start(bf16[4,8,128,128]{3,2,1,0:T(8,128)(2,1)S(1)} %add_convert_fusion.3), channel_id=1, source_target_pairs={{24,16},{25,17},{26,18},{27,19},{28,20},{29,21},{30,22},{31,23}} | collective-permute-start | bytes 3145736 | tf_op jit(solution)/shard_map/ppermute | solution.py:183
  81.0 1.0 collective-permute-start.8
  83.4 2.9 %copy-start.8 = (bf16[1,128,4096]{1,2,0:T(8,128)(2,1)S(1)}, bf16[1,128,4096]{1,2,0:T(8,128)(2,1)}, u32[]{:S(2)}) copy-start(bf16[1,128,4096]{1,2,0:T(8,128)(2,1)} %copy-done.7) | copy-start | bytes 3145732
  84.7 41.8 %collective-permute-start.9 = (bf16[4,8,128,128]{3,2,1,0:T(8,128)(2,1)}, bf16[4,8,128,128]{3,2,1,0:T(8,128)(2,1)}, u32[]{:S(2)}, u32[]{:S(2)}) collective-permute-start(bf16[4,8,128,128]{3,2,1,0:T(8,128)(2,1)} %add_convert_fusion.1), channel_id=1, source_target_pairs={{8,0},{9,1},{10,2},{11,3},{12,4},{13,5},{14,6},{15,7}} | collective-permute-start | bytes 3145736 | tf_op jit(solution)/shard_map/ppermute | solution.py:183
  87.1 11.2 %collective-permute-start.10 = (bf16[4,128,128]{1,2,0:T(8,128)(2,1)S(1)}, bf16[4,128,128]{1,2,0:T(8,128)(2,1)}, u32[]{:S(2)}, u32[]{:S(2)}) collective-permute-start(bf16[4,128,128]{1,2,0:T(8,128)(2,1)S(1)} %get-tuple-element.171), channel_id=1, source_target_pairs={{24,25},{25,26},{26,27},{27,28},{28,29},{29,30},{30,31},{31,24}} | collective-permute-start | bytes 393224 | tf_op jit(solution)/shard_map/ppermute | solution.py:123
  89.0 11.2 %collective-permute-start.11 = (bf16[4,128,128]{1,2,0:T(8,128)(2,1)S(1)}, bf16[4,128,128]{1,2,0:T(8,128)(2,1)}, u32[]{:S(2)}, u32[]{:S(2)}) collective-permute-start(bf16[4,128,128]{1,2,0:T(8,128)(2,1)S(1)} %get-tuple-element.170), channel_id=1, source_target_pairs={{24,26},{25,27},{26,28},{27,29},{28,30},{29,31},{30,24},{31,25}} | collective-permute-start | bytes 393224 | tf_op jit(solution)/shard_map/ppermute | solution.py:123
  91.0 13.3 %collective-permute-start.12 = (bf16[4,128,128]{1,2,0:T(8,128)(2,1)S(1)}, bf16[4,128,128]{1,2,0:T(8,128)(2,1)S(1)}, u32[]{:S(2)}, u32[]{:S(2)}) collective-permute-start(bf16[4,128,128]{1,2,0:T(8,128)(2,1)S(1)} %get-tuple-element.169), channel_id=1, source_target_pairs={{24,27},{25,28},{26,29},{27,30},{28,31},{29,24},{30,25},{31,26}} | collective-permute-start | bytes 393224 | tf_op jit(solution)/shard_map/ppermute | solution.py:123
  94.0 13.4 %collective-permute-start.13 = (bf16[4,128,128]{1,2,0:T(8,128)(2,1)}, bf16[4,128,128]{1,2,0:T(8,128)(2,1)}, u32[]{:S(2)}, u32[]{:S(2)}) collective-permute-start(bf16[4,128,128]{1,2,0:T(8,128)(2,1)} %get-tuple-element.168), channel_id=1, source_target_pairs={{24,28},{25,29},{26,30},{27,31},{28,24},{29,25},{30,26},{31,27}} | collective-permute-start | bytes 393224 | tf_op jit(solution)/shard_map/ppermute | solution.py:123
  98.3 9.1 %collective-permute-start.14 = (bf16[4,128,128]{1,2,0:T(8,128)(2,1)}, bf16[4,128,128]{1,2,0:T(8,128)(2,1)}, u32[]{:S(2)}, u32[]{:S(2)}) collective-permute-start(bf16[4,128,128]{1,2,0:T(8,128)(2,1)} %get-tuple-element.167), channel_id=1, source_target_pairs={{24,29},{25,30},{26,31},{27,24},{28,25},{29,26},{30,27},{31,28}} | collective-permute-start | bytes 393224 | tf_op jit(solution)/shard_map/ppermute | solution.py:123
  100.3 7.2 %collective-permute-start.15 = (bf16[4,128,128]{1,2,0:T(8,128)(2,1)S(1)}, bf16[4,128,128]{1,2,0:T(8,128)(2,1)}, u32[]{:S(2)}, u32[]{:S(2)}) collective-permute-start(bf16[4,128,128]{1,2,0:T(8,128)(2,1)S(1)} %get-tuple-element.166), channel_id=1, source_target_pairs={{24,30},{25,31},{26,24},{27,25},{28,26},{29,27},{30,28},{31,29}} | collective-permute-start | bytes 393224 | tf_op jit(solution)/shard_map/ppermute | solution.py:123
  105.0 6.7 %collective-permute-start.16 = (bf16[4,128,128]{1,2,0:T(8,128)(2,1)S(1)}, bf16[4,128,128]{1,2,0:T(8,128)(2,1)}, u32[]{:S(2)}, u32[]{:S(2)}) collective-permute-start(bf16[4,128,128]{1,2,0:T(8,128)(2,1)S(1)} %get-tuple-element.165), channel_id=1, source_target_pairs={{24,31},{25,24},{26,25},{27,26},{28,27},{29,28},{30,29},{31,30}} | collective-permute-start | bytes 393224 | tf_op jit(solution)/shard_map/ppermute | solution.py:123
  111.7 5.4 %copy-start.25 = (bf16[4,128,128]{1,2,0:T(8,128)(2,1)S(1)}, bf16[4,128,128]{1,2,0:T(8,128)(2,1)}, u32[]{:S(2)}) copy-start(bf16[4,128,128]{1,2,0:T(8,128)(2,1)} %get-tuple-element.133) | copy-start | bytes 393220 | tf_op jit(solution)/shard_map/cond
  141.6 20.8 %collective-permute-start.17 = (bf16[2,4,128,128]{3,2,1,0:T(8,128)(2,1)S(1)}, bf16[2,4,128,128]{3,2,1,0:T(8,128)(2,1)S(1)}, u32[]{:S(2)}, u32[]{:S(2)}) collective-permute-start(bf16[2,4,128,128]{3,2,1,0:T(8,128)(2,1)S(1)} %get-tuple-element.147), channel_id=1, source_target_pairs={{0,1},{1,2},{2,3},{3,4},{4,5},{5,6},{6,7},{7,0},{8,9},{9,10},{10,1... | collective-permute-start | bytes 786440 | tf_op jit(solution)/shard_map/ppermute | solution.py:118
  142.2 51.8 %all-to-all-start.1 = ((f32[1024,1,128]{2,1,0:T(1,128)}), f32[1024,1,128]{2,1,0:T(1,128)S(1)}, u32[]{:S(2)}, u32[]{:S(2)}) async-start(f32[1024,1,128]{2,1,0:T(1,128)} %bitcast.33), calls=%async_computation.1 | async-start | bytes 1048576 | tf_op jit(solution)/shard_map/all_to_all | solution.py:210
  148.5 38.0 %collective-permute-start.21 = (bf16[2,4,128,128]{3,2,1,0:T(8,128)(2,1)S(1)}, bf16[2,4,128,128]{3,2,1,0:T(8,128)(2,1)S(1)}, u32[]{:S(2)}, u32[]{:S(2)}) collective-permute-start(bf16[2,4,128,128]{3,2,1,0:T(8,128)(2,1)S(1)} %get-tuple-element.152), channel_id=1, source_target_pairs={{0,5},{1,6},{2,7},{3,0},{4,1},{5,2},{6,3},{7,4},{8,13},{9,14},{10,... | collective-permute-start | bytes 786440 | tf_op jit(solution)/shard_map/ppermute | solution.py:118
  148.5 32.1 %collective-permute-start.18 = (bf16[2,4,128,128]{3,2,1,0:T(8,128)(2,1)}, bf16[2,4,128,128]{3,2,1,0:T(8,128)(2,1)S(1)}, u32[]{:S(2)}, u32[]{:S(2)}) collective-permute-start(bf16[2,4,128,128]{3,2,1,0:T(8,128)(2,1)} %get-tuple-element.148), channel_id=1, source_target_pairs={{0,2},{1,3},{2,4},{3,5},{4,6},{5,7},{6,0},{7,1},{8,10},{9,11},{10,... | collective-permute-start | bytes 786440 | tf_op jit(solution)/shard_map/ppermute | solution.py:118
  150.0 34.4 %collective-permute-start.19 = (bf16[2,4,128,128]{3,2,1,0:T(8,128)(2,1)S(1)}, bf16[2,4,128,128]{3,2,1,0:T(8,128)(2,1)S(1)}, u32[]{:S(2)}, u32[]{:S(2)}) collective-permute-start(bf16[2,4,128,128]{3,2,1,0:T(8,128)(2,1)S(1)} %get-tuple-element.149), channel_id=1, source_target_pairs={{0,3},{1,4},{2,5},{3,6},{4,7},{5,0},{6,1},{7,2},{8,11},{9,12},{10,... | collective-permute-start | bytes 786440 | tf_op jit(solution)/shard_map/ppermute | solution.py:118
  153.9 32.3 %collective-permute-start.20 = (bf16[2,4,128,128]{3,2,1,0:T(8,128)(2,1)S(1)}, bf16[2,4,128,128]{3,2,1,0:T(8,128)(2,1)S(1)}, u32[]{:S(2)}, u32[]{:S(2)}) collective-permute-start(bf16[2,4,128,128]{3,2,1,0:T(8,128)(2,1)S(1)} %get-tuple-element.150), channel_id=1, source_target_pairs={{0,4},{1,5},{2,6},{3,7},{4,0},{5,1},{6,2},{7,3},{8,12},{9,13},{10,... | collective-permute-start | bytes 786440 | tf_op jit(solution)/shard_map/ppermute | solution.py:118
  162.3 25.8 %collective-permute-start.22 = (bf16[2,4,128,128]{3,2,1,0:T(8,128)(2,1)S(1)}, bf16[2,4,128,128]{3,2,1,0:T(8,128)(2,1)S(1)}, u32[]{:S(2)}, u32[]{:S(2)}) collective-permute-start(bf16[2,4,128,128]{3,2,1,0:T(8,128)(2,1)S(1)} %get-tuple-element.151), channel_id=1, source_target_pairs={{0,6},{1,7},{2,0},{3,1},{4,2},{5,3},{6,4},{7,5},{8,14},{9,15},{10,... | collective-permute-start | bytes 786440 | tf_op jit(solution)/shard_map/ppermute | solution.py:118
  180.7 10.0 %collective-permute-start.23 = (bf16[2,4,128,128]{3,2,1,0:T(8,128)(2,1)S(1)}, bf16[2,4,128,128]{3,2,1,0:T(8,128)(2,1)S(1)}, u32[]{:S(2)}, u32[]{:S(2)}) collective-permute-start(bf16[2,4,128,128]{3,2,1,0:T(8,128)(2,1)S(1)} %get-tuple-element.145), channel_id=1, source_target_pairs={{0,7},{1,0},{2,1},{3,2},{4,3},{5,4},{6,5},{7,6},{8,15},{9,8},{10,9... | collective-permute-start | bytes 786440 | tf_op jit(solution)/shard_map/ppermute | solution.py:118
  (21 other events, 33.0 us)

commit v12 on v10

--- a/solution.py
+++ b/solution.py
@@ -193,7 +193,7 @@
         key_part = grad_key.reshape(seq_len, DH)
     else:
         key_part = jnp.sum(grad_key.astype(jnp.float32), axis=0).reshape(seq_len, DH)
-    key_out = lax.all_to_all(key_part[:, None, :], "seq", split_axis=0, concat_axis=1, tiled=True)
+    key_out = transpose_seq(key_part[:, None, :], 0, 1)
     key_sum = jnp.sum(
         key_out.reshape(tok_rows, kv_count, seq_ways // kv_count, DH).astype(jnp.float32), axis=2
     )

time: 191 us -> 192 us (level)
  local copies, waits for them, and re-layouts: 37 us -> 42.1 us
  waiting for transfers between devices: 68.7 us -> 65 us
    ppermute x14 -> x21, starting transfers between devices: 18.6 us -> 26.6 us  [transpose_seq(): lax.ppermute(chunk, 'seq', [(s, (s + shift) % seq_ways) for s in range(se...]
    all_to_all x1 -> x0, starting transfers between devices: 6.62 us -> none  [on_device(): lax.all_to_all(key_part[:, None, :], 'seq', split_axis=0, concat_axis=1,...]
    ppermute x14 -> x21, waiting for transfers between devices: 66.5 us -> 62.8 us  [transpose_seq(): lax.ppermute(chunk, 'seq', [(s, (s + shift) % seq_ways) for s in range(se...]
    dynamic_update_slice x23 -> x30, local copies, waits for them, and re-layouts: 14.5 us -> 17.4 us  [transpose_seq(): lax.dynamic_update_slice_in_dim(result, chunk, source * concat_size, axis...]
    slice x3, local copies, waits for them, and re-layouts: 2.89 us -> 4.97 us  [on_device(): return (pair_rows[0][None], key_final[None], pair_rows[1][None])]
  transfers between devices with their start and end apart: 26 -> 32, of which waited for: 9 -> 11; matrix products, arithmetic and copies ran while one was open for 16% -> 17% of each run, Pallas kernels for 0% -> 0%
where the time goes in v12:
time: 192 us; the launch traced here: 191 us
  waiting for transfers between devices  65 us (34%)
  starting transfers between devices  56.8 us (30%)
  local copies, waits for them, and re-layouts  42.1 us (22%)
  other arithmetic  16.4 us (9%)
  matrix products  8.84 us (5%)
    ppermute x21, waiting for transfers between devices, transpose_seq(): lax.ppermute(chunk, 'seq', [(s, (s + shift) % seq_ways) for s in range(se...  62.8 us
    ppermute x21, starting transfers between devices, transpose_seq(): lax.ppermute(chunk, 'seq', [(s, (s + shift) % seq_ways) for s in range(se...  26.6 us
    ppermute x7, starting transfers between devices, transpose_seq(): lax.ppermute(chunk, ('pipe', 'seq'), [(base + s, base + (s + shift) % seq...  19.6 us
    dynamic_update_slice x30, local copies, waits for them, and re-layouts, transpose_seq(): lax.dynamic_update_slice_in_dim(result, chunk, source * concat_size, axis...  17.4 us
    unnamed x48, local copies, waits for them, and re-layouts  10.7 us
    all_to_all x1, starting transfers between devices, on_device(): lax.all_to_all(key_rows, 'seq', split_axis=0, concat_axis=1, tiled=True)  5.69 us
    ppermute x3, starting transfers between devices, on_device(): grad_in = lax.ppermute(new_grad, 'pipe', [(sender, sender - 1)])  5.01 us
    slice x3, local copies, waits for them, and re-layouts, on_device(): return (pair_rows[0][None], key_final[None], pair_rows[1][None])  4.97 us
  transfers between devices with their start and end apart: 32, of which 11 were waited for; matrix products, arithmetic and copies ran while one was open for 17% of the time, Pallas kernels for 0%

profile of v12, /device:TPU:15, one launch (start us, length us, event | category | flops | bytes accessed | tf_op | source)
XLA Modules:
  0.0 190.6 jit_solution(17687435842873692772)
XLA Ops:
  4.0 1.6 fusion.51
  11.3 2.0 %fusion.34 = (bf16[2,4,128,128]{3,2,1,0:T(8,128)(2,1)}, bf16[2,4,128,128]{3,2,1,0:T(8,128)(2,1)}, bf16[2,4,128,128]{3,2,1,0:T(8,128)(2,1)}) fusion(s32[]{:T(128)S(6)} %select_n.381, bf16[1,32,128,128]{3,2,1,0:T(8,128)(2,1)} %bitcast.95, bf16[1,32,128,128]{3,2,1,0:T(8,128)(2,1)S(1)} %get-tuple-element.98, s32[]{:T(128)S(6)} %select_n.377, s32[]{:T(128)S(6)} %select_n.379), kind=kLoop, calls=%fused_computation.97 | loop fusion | flops 393216 | bytes 2883596 | tf_op jit(solution)/shard_map/stack | solution.py:142
  17.2 5.7 %all-to-all-start = ((bf16[8,128,128]{2,1,0:T(8,128)(2,1)}), bf16[8,128,128]{2,1,0:T(8,128)(2,1)S(1)}, u32[]{:S(2)}, u32[]{:S(2)}) async-start(bf16[8,128,128]{2,1,0:T(8,128)(2,1)} %gather_fusion), calls=%async_computation | async-start | bytes 524288 | tf_op jit(solution)/shard_map/all_to_all | solution.py:151
  26.4 24.4 %collective-permute-done.2 = bf16[2,4,128,128]{3,2,1,0:T(8,128)(2,1)} collective-permute-done((bf16[2,4,128,128]{3,2,1,0:T(8,128)(2,1)}, bf16[2,4,128,128]{3,2,1,0:T(8,128)(2,1)}, u32[]{:S(2)}, u32[]{:S(2)}) %collective-permute-start.2) | collective-permute-done | bytes 262176 | tf_op jit(solution)/shard_map/ppermute | solution.py:118
  51.8 4.6 %collective-permute-done.3 = bf16[2,4,128,128]{3,2,1,0:T(8,128)(2,1)S(1)} collective-permute-done((bf16[2,4,128,128]{3,2,1,0:T(8,128)(2,1)}, bf16[2,4,128,128]{3,2,1,0:T(8,128)(2,1)S(1)}, u32[]{:S(2)}, u32[]{:S(2)}) %collective-permute-start.3) | collective-permute-done | bytes 262176 | tf_op jit(solution)/shard_map/ppermute | solution.py:118
  56.6 5.6 %collective-permute-done.5 = bf16[2,4,128,128]{3,2,1,0:T(8,128)(2,1)S(1)} collective-permute-done((bf16[2,4,128,128]{3,2,1,0:T(8,128)(2,1)}, bf16[2,4,128,128]{3,2,1,0:T(8,128)(2,1)S(1)}, u32[]{:S(2)}, u32[]{:S(2)}) %collective-permute-start.5) | collective-permute-done | bytes 262176 | tf_op jit(solution)/shard_map/ppermute | solution.py:118
  68.2 2.2 %fusion.52 = (f32[4,8,128]{2,1,0:T(8,128)S(1)}, f32[4,8,128,256]{3,2,1,0:T(8,128)S(1)}) fusion(f32[4,8,128,256]{3,2,1,0:T(8,128)S(1)} %fusion.3, pred[8,128,256]{2,1,0:T(8,128)(4,1)S(1)} %copy-done.19), kind=kOutput, calls=%fused_computation.176 | output fusion | flops 6291711 | bytes 8667136 | tf_op jit(solution)/shard_map/sub | solution.py:53
  74.1 2.5 %collective-permute-start.7 = (bf16[4,8,128,128]{3,2,1,0:T(8,128)(2,1)S(1)}, bf16[4,8,128,128]{3,2,1,0:T(8,128)(2,1)S(1)}, u32[]{:S(2)}, u32[]{:S(2)}) collective-permute-start(bf16[4,8,128,128]{3,2,1,0:T(8,128)(2,1)S(1)} %add_convert_fusion.3), channel_id=1, source_target_pairs={{24,16},{25,17},{26,18},{27,19},{28,20},{29,21},{30,22},{31,23}} | collective-permute-start | bytes 3145736 | tf_op jit(solution)/shard_map/ppermute | solution.py:169
  76.6 2.2 %collective-permute-done.7 = bf16[4,8,128,128]{3,2,1,0:T(8,128)(2,1)S(1)} collective-permute-done((bf16[4,8,128,128]{3,2,1,0:T(8,128)(2,1)S(1)}, bf16[4,8,128,128]{3,2,1,0:T(8,128)(2,1)S(1)}, u32[]{:S(2)}, u32[]{:S(2)}) %collective-permute-start.7) | collective-permute-done | bytes 1048608 | tf_op jit(solution)/shard_map/ppermute | solution.py:169
  81.5 1.6 collective-permute-start.8
  83.9 1.9 %collective-permute-start.10 = (bf16[4,128,128]{2,1,0:T(8,128)(2,1)}, bf16[4,128,128]{2,1,0:T(8,128)(2,1)}, u32[]{:S(2)}, u32[]{:S(2)}) collective-permute-start(bf16[4,128,128]{2,1,0:T(8,128)(2,1)} %get-tuple-element.96), channel_id=1, source_target_pairs={{24,25},{25,26},{26,27},{27,28},{28,29},{29,30},{30,31},{31,24}} | collective-permute-start | bytes 393224 | tf_op jit(solution)/shard_map/ppermute | solution.py:123
  85.8 1.9 %collective-permute-start.11 = (bf16[4,128,128]{2,1,0:T(8,128)(2,1)}, bf16[4,128,128]{2,1,0:T(8,128)(2,1)}, u32[]{:S(2)}, u32[]{:S(2)}) collective-permute-start(bf16[4,128,128]{2,1,0:T(8,128)(2,1)} %get-tuple-element.95), channel_id=1, source_target_pairs={{24,26},{25,27},{26,28},{27,29},{28,30},{29,31},{30,24},{31,25}} | collective-permute-start | bytes 393224 | tf_op jit(solution)/shard_map/ppermute | solution.py:123
  87.8 3.1 %collective-permute-start.12 = (bf16[4,128,128]{2,1,0:T(8,128)(2,1)}, bf16[4,128,128]{2,1,0:T(8,128)(2,1)}, u32[]{:S(2)}, u32[]{:S(2)}) collective-permute-start(bf16[4,128,128]{2,1,0:T(8,128)(2,1)} %get-tuple-element.94), channel_id=1, source_target_pairs={{24,27},{25,28},{26,29},{27,30},{28,31},{29,24},{30,25},{31,26}} | collective-permute-start | bytes 393224 | tf_op jit(solution)/shard_map/ppermute | solution.py:123
  90.9 4.2 %collective-permute-start.13 = (bf16[4,128,128]{2,1,0:T(8,128)(2,1)}, bf16[4,128,128]{2,1,0:T(8,128)(2,1)}, u32[]{:S(2)}, u32[]{:S(2)}) collective-permute-start(bf16[4,128,128]{2,1,0:T(8,128)(2,1)} %get-tuple-element.93), channel_id=1, source_target_pairs={{24,28},{25,29},{26,30},{27,31},{28,24},{29,25},{30,26},{31,27}} | collective-permute-start | bytes 393224 | tf_op jit(solution)/shard_map/ppermute | solution.py:123
  96.9 1.9 %collective-permute-start.14 = (bf16[4,128,128]{2,1,0:T(8,128)(2,1)S(1)}, bf16[4,128,128]{2,1,0:T(8,128)(2,1)S(1)}, u32[]{:S(2)}, u32[]{:S(2)}) collective-permute-start(bf16[4,128,128]{2,1,0:T(8,128)(2,1)S(1)} %get-tuple-element.92), channel_id=1, source_target_pairs={{24,29},{25,30},{26,31},{27,24},{28,25},{29,26},{30,27},{31,28}} | collective-permute-start | bytes 393224 | tf_op jit(solution)/shard_map/ppermute | solution.py:123
  98.8 1.6 constant_dynamic-update-slice_fusion.12
  100.4 4.0 %collective-permute-start.15 = (bf16[4,128,128]{2,1,0:T(8,128)(2,1)S(1)}, bf16[4,128,128]{2,1,0:T(8,128)(2,1)S(1)}, u32[]{:S(2)}, u32[]{:S(2)}) collective-permute-start(bf16[4,128,128]{2,1,0:T(8,128)(2,1)S(1)} %get-tuple-element.91), channel_id=1, source_target_pairs={{24,30},{25,31},{26,24},{27,25},{28,26},{29,27},{30,28},{31,29}} | collective-permute-start | bytes 393224 | tf_op jit(solution)/shard_map/ppermute | solution.py:123
  104.4 1.6 constant_dynamic-update-slice_fusion.11
  106.0 2.5 %collective-permute-start.16 = (bf16[4,128,128]{2,1,0:T(8,128)(2,1)S(1)}, bf16[4,128,128]{2,1,0:T(8,128)(2,1)S(1)}, u32[]{:S(2)}, u32[]{:S(2)}) collective-permute-start(bf16[4,128,128]{2,1,0:T(8,128)(2,1)S(1)} %get-tuple-element.90), channel_id=1, source_target_pairs={{24,31},{25,24},{26,25},{27,26},{28,27},{29,28},{30,29},{31,30}} | collective-permute-start | bytes 393224 | tf_op jit(solution)/shard_map/ppermute | solution.py:123
  108.5 2.0 %fusion.55 = f32[4,8,256,128]{3,2,1,0:T(8,128)S(1)} fusion(bf16[4,8,128,256]{3,2,1,0:T(8,128)(2,1)S(1)} %fusion.8, bf16[4,8,128,128]{3,2,1,0:T(8,128)(2,1)} %collective-permute-done.8), kind=kOutput, calls=%fused_computation.179 | convolution fusion | flops 268435456 | bytes 7340032 | tf_op jit(solution)/shard_map/hbij,hbid->hbjd/dot_general | solution.py:58
  111.1 1.7 add_convert_fusion.1
  130.5 1.8 collective-permute-start.24
  132.8 3.0 %collective-permute-start.26 = (f32[128,1,128]{2,0,1:T(8,128)S(1)}, f32[128,1,128]{2,0,1:T(8,128)S(1)}, u32[]{:S(2)}, u32[]{:S(2)}) collective-permute-start(f32[128,1,128]{2,0,1:T(8,128)S(1)} %get-tuple-element.103), channel_id=1, source_target_pairs={{0,3},{1,4},{2,5},{3,6},{4,7},{5,0},{6,1},{7,2},{8,11},{9,12},{10,... | collective-permute-start | bytes 196616 | tf_op jit(solution)/shard_map/ppermute | solution.py:118
  135.8 2.1 %collective-permute-start.28 = (f32[128,1,128]{2,0,1:T(8,128)S(1)}, f32[128,1,128]{2,0,1:T(8,128)S(1)}, u32[]{:S(2)}, u32[]{:S(2)}) collective-permute-start(f32[128,1,128]{2,0,1:T(8,128)S(1)} %get-tuple-element.101), channel_id=1, source_target_pairs={{0,5},{1,6},{2,7},{3,0},{4,1},{5,2},{6,3},{7,4},{8,13},{9,14},{10,... | collective-permute-start | bytes 196616 | tf_op jit(solution)/shard_map/ppermute | solution.py:118
  139.6 2.4 %collective-permute-start.29 = (f32[128,1,128]{2,0,1:T(8,128)S(1)}, f32[128,1,128]{2,0,1:T(8,128)S(1)}, u32[]{:S(2)}, u32[]{:S(2)}) collective-permute-start(f32[128,1,128]{2,0,1:T(8,128)S(1)} %get-tuple-element.100), channel_id=1, source_target_pairs={{0,6},{1,7},{2,0},{3,1},{4,2},{5,3},{6,4},{7,5},{8,14},{9,15},{10,... | collective-permute-start | bytes 196616 | tf_op jit(solution)/shard_map/ppermute | solution.py:118
  142.1 5.0 %collective-permute-start.21 = (bf16[2,4,128,128]{3,2,1,0:T(8,128)(2,1)S(1)}, bf16[2,4,128,128]{3,2,1,0:T(8,128)(2,1)S(1)}, u32[]{:S(2)}, u32[]{:S(2)}) collective-permute-start(bf16[2,4,128,128]{3,2,1,0:T(8,128)(2,1)S(1)} %get-tuple-element.77), channel_id=1, source_target_pairs={{0,5},{1,6},{2,7},{3,0},{4,1},{5,2},{6,3},{7,4},{8,13},{9,14},{10,... | collective-permute-start | bytes 786440 | tf_op jit(solution)/shard_map/ppermute | solution.py:118
  147.3 3.8 %collective-permute-start.18 = (bf16[2,4,128,128]{3,2,1,0:T(8,128)(2,1)}, bf16[2,4,128,128]{3,2,1,0:T(8,128)(2,1)}, u32[]{:S(2)}, u32[]{:S(2)}) collective-permute-start(bf16[2,4,128,128]{3,2,1,0:T(8,128)(2,1)} %get-tuple-element.73), channel_id=1, source_target_pairs={{0,2},{1,3},{2,4},{3,5},{4,6},{5,7},{6,0},{7,1},{8,10},{9,11},{10,... | collective-permute-start | bytes 786440 | tf_op jit(solution)/shard_map/ppermute | solution.py:118
  151.1 4.7 %collective-permute-done.29 = f32[128,1,128]{2,0,1:T(8,128)S(1)} collective-permute-done((f32[128,1,128]{2,0,1:T(8,128)S(1)}, f32[128,1,128]{2,0,1:T(8,128)S(1)}, u32[]{:S(2)}, u32[]{:S(2)}) %collective-permute-start.29) | collective-permute-done | bytes 65568 | tf_op jit(solution)/shard_map/ppermute | solution.py:118
  158.7 3.6 %collective-permute-done.17 = bf16[2,4,128,128]{3,2,1,0:T(8,128)(2,1)S(1)} collective-permute-done((bf16[2,4,128,128]{3,2,1,0:T(8,128)(2,1)}, bf16[2,4,128,128]{3,2,1,0:T(8,128)(2,1)S(1)}, u32[]{:S(2)}, u32[]{:S(2)}) %collective-permute-start.17) | collective-permute-done | bytes 262176 | tf_op jit(solution)/shard_map/ppermute | solution.py:118
  162.6 14.4 %collective-permute-done.18 = bf16[2,4,128,128]{3,2,1,0:T(8,128)(2,1)} collective-permute-done((bf16[2,4,128,128]{3,2,1,0:T(8,128)(2,1)}, bf16[2,4,128,128]{3,2,1,0:T(8,128)(2,1)}, u32[]{:S(2)}, u32[]{:S(2)}) %collective-permute-start.18) | collective-permute-done | bytes 262176 | tf_op jit(solution)/shard_map/ppermute | solution.py:118
  178.2 2.4 %collective-permute-done.19 = bf16[2,4,128,128]{3,2,1,0:T(8,128)(2,1)} collective-permute-done((bf16[2,4,128,128]{3,2,1,0:T(8,128)(2,1)}, bf16[2,4,128,128]{3,2,1,0:T(8,128)(2,1)}, u32[]{:S(2)}, u32[]{:S(2)}) %collective-permute-start.19) | collective-permute-done | bytes 262176 | tf_op jit(solution)/shard_map/ppermute | solution.py:118
  187.0 2.4 %slice.225 = bf16[1,128,4096]{2,1,0:T(8,128)(2,1)} reshape(bf16[1,128,32,128]{3,2,1,0:T(8,128)(2,1)} %get-tuple-element.69) | data formatting | bytes 2097152 | tf_op jit(solution)/shard_map/slice | solution.py:201
  (176 shorter events, 64.7 us)
Async XLA Ops:
  7.8 16.2 %collective-permute-start = (bf16[2,4,128,128]{3,2,1,0:T(8,128)(2,1)}, bf16[2,4,128,128]{3,2,1,0:T(8,128)(2,1)}, u32[]{:S(2)}, u32[]{:S(2)}) collective-permute-start(bf16[2,4,128,128]{3,2,1,0:T(8,128)(2,1)} %get-tuple-element.82), channel_id=1, source_target_pairs={{0,1},{1,2},{2,3},{3,4},{4,5},{5,6},{6,7},{7,0},{8,9},{9,10},{10,1... | collective-permute-start | bytes 786440 | tf_op jit(solution)/shard_map/ppermute | solution.py:118
  9.1 16.2 %collective-permute-start.1 = (bf16[2,4,128,128]{3,2,1,0:T(8,128)(2,1)}, bf16[2,4,128,128]{3,2,1,0:T(8,128)(2,1)}, u32[]{:S(2)}, u32[]{:S(2)}) collective-permute-start(bf16[2,4,128,128]{3,2,1,0:T(8,128)(2,1)} %get-tuple-element.83), channel_id=1, source_target_pairs={{0,2},{1,3},{2,4},{3,5},{4,6},{5,7},{6,0},{7,1},{8,10},{9,11},{10,... | collective-permute-start | bytes 786440 | tf_op jit(solution)/shard_map/ppermute | solution.py:118
  10.3 40.5 %collective-permute-start.2 = (bf16[2,4,128,128]{3,2,1,0:T(8,128)(2,1)}, bf16[2,4,128,128]{3,2,1,0:T(8,128)(2,1)}, u32[]{:S(2)}, u32[]{:S(2)}) collective-permute-start(bf16[2,4,128,128]{3,2,1,0:T(8,128)(2,1)} %get-tuple-element.84), channel_id=1, source_target_pairs={{0,3},{1,4},{2,5},{3,6},{4,7},{5,0},{6,1},{7,2},{8,11},{9,12},{10,... | collective-permute-start | bytes 786440 | tf_op jit(solution)/shard_map/ppermute | solution.py:118
  13.3 43.2 %collective-permute-start.3 = (bf16[2,4,128,128]{3,2,1,0:T(8,128)(2,1)}, bf16[2,4,128,128]{3,2,1,0:T(8,128)(2,1)S(1)}, u32[]{:S(2)}, u32[]{:S(2)}) collective-permute-start(bf16[2,4,128,128]{3,2,1,0:T(8,128)(2,1)} %get-tuple-element.86), channel_id=1, source_target_pairs={{0,4},{1,5},{2,6},{3,7},{4,0},{5,1},{6,2},{7,3},{8,12},{9,13},{10,... | collective-permute-start | bytes 786440 | tf_op jit(solution)/shard_map/ppermute | solution.py:118
  14.6 41.9 %collective-permute-start.4 = (bf16[2,4,128,128]{3,2,1,0:T(8,128)(2,1)}, bf16[2,4,128,128]{3,2,1,0:T(8,128)(2,1)S(1)}, u32[]{:S(2)}, u32[]{:S(2)}) collective-permute-start(bf16[2,4,128,128]{3,2,1,0:T(8,128)(2,1)} %get-tuple-element.87), channel_id=1, source_target_pairs={{0,5},{1,6},{2,7},{3,0},{4,1},{5,2},{6,3},{7,4},{8,13},{9,14},{10,... | collective-permute-start | bytes 786440 | tf_op jit(solution)/shard_map/ppermute | solution.py:118
  17.2 47.8 %all-to-all-start = ((bf16[8,128,128]{2,1,0:T(8,128)(2,1)}), bf16[8,128,128]{2,1,0:T(8,128)(2,1)S(1)}, u32[]{:S(2)}, u32[]{:S(2)}) async-start(bf16[8,128,128]{2,1,0:T(8,128)(2,1)} %gather_fusion), calls=%async_computation | async-start | bytes 524288 | tf_op jit(solution)/shard_map/all_to_all | solution.py:151
  24.0 38.1 %collective-permute-start.5 = (bf16[2,4,128,128]{3,2,1,0:T(8,128)(2,1)}, bf16[2,4,128,128]{3,2,1,0:T(8,128)(2,1)S(1)}, u32[]{:S(2)}, u32[]{:S(2)}) collective-permute-start(bf16[2,4,128,128]{3,2,1,0:T(8,128)(2,1)} %get-tuple-element.85), channel_id=1, source_target_pairs={{0,6},{1,7},{2,0},{3,1},{4,2},{5,3},{6,4},{7,5},{8,14},{9,15},{10,... | collective-permute-start | bytes 786440 | tf_op jit(solution)/shard_map/ppermute | solution.py:118
  25.3 38.0 %collective-permute-start.6 = (bf16[2,4,128,128]{3,2,1,0:T(8,128)(2,1)}, bf16[2,4,128,128]{3,2,1,0:T(8,128)(2,1)S(1)}, u32[]{:S(2)}, u32[]{:S(2)}) collective-permute-start(bf16[2,4,128,128]{3,2,1,0:T(8,128)(2,1)} %get-tuple-element.80), channel_id=1, source_target_pairs={{0,7},{1,0},{2,1},{3,2},{4,3},{5,4},{6,5},{7,6},{8,15},{9,8},{10,9... | collective-permute-start | bytes 786440 | tf_op jit(solution)/shard_map/ppermute | solution.py:118
  74.1 4.7 %collective-permute-start.7 = (bf16[4,8,128,128]{3,2,1,0:T(8,128)(2,1)S(1)}, bf16[4,8,128,128]{3,2,1,0:T(8,128)(2,1)S(1)}, u32[]{:S(2)}, u32[]{:S(2)}) collective-permute-start(bf16[4,8,128,128]{3,2,1,0:T(8,128)(2,1)S(1)} %add_convert_fusion.3), channel_id=1, source_target_pairs={{24,16},{25,17},{26,18},{27,19},{28,20},{29,21},{30,22},{31,23}} | collective-permute-start | bytes 3145736 | tf_op jit(solution)/shard_map/ppermute | solution.py:169
  81.5 24.5 %collective-permute-start.8 = (bf16[4,8,128,128]{3,2,1,0:T(8,128)(2,1)}, bf16[4,8,128,128]{3,2,1,0:T(8,128)(2,1)}, u32[]{:S(2)}, u32[]{:S(2)}) collective-permute-start(bf16[4,8,128,128]{3,2,1,0:T(8,128)(2,1)} %add_convert_fusion.2), channel_id=1, source_target_pairs={{16,8},{17,9},{18,10},{19,11},{20,12},{21,13},{22,14},{23,15}} | collective-permute-start | bytes 3145736 | tf_op jit(solution)/shard_map/ppermute | solution.py:169
  83.9 13.0 %collective-permute-start.10 = (bf16[4,128,128]{2,1,0:T(8,128)(2,1)}, bf16[4,128,128]{2,1,0:T(8,128)(2,1)}, u32[]{:S(2)}, u32[]{:S(2)}) collective-permute-start(bf16[4,128,128]{2,1,0:T(8,128)(2,1)} %get-tuple-element.96), channel_id=1, source_target_pairs={{24,25},{25,26},{26,27},{27,28},{28,29},{29,30},{30,31},{31,24}} | collective-permute-start | bytes 393224 | tf_op jit(solution)/shard_map/ppermute | solution.py:123
  85.8 14.6 %collective-permute-start.11 = (bf16[4,128,128]{2,1,0:T(8,128)(2,1)}, bf16[4,128,128]{2,1,0:T(8,128)(2,1)}, u32[]{:S(2)}, u32[]{:S(2)}) collective-permute-start(bf16[4,128,128]{2,1,0:T(8,128)(2,1)} %get-tuple-element.95), channel_id=1, source_target_pairs={{24,26},{25,27},{26,28},{27,29},{28,30},{29,31},{30,24},{31,25}} | collective-permute-start | bytes 393224 | tf_op jit(solution)/shard_map/ppermute | solution.py:123
  87.8 25.0 %collective-permute-start.12 = (bf16[4,128,128]{2,1,0:T(8,128)(2,1)}, bf16[4,128,128]{2,1,0:T(8,128)(2,1)}, u32[]{:S(2)}, u32[]{:S(2)}) collective-permute-start(bf16[4,128,128]{2,1,0:T(8,128)(2,1)} %get-tuple-element.94), channel_id=1, source_target_pairs={{24,27},{25,28},{26,29},{27,30},{28,31},{29,24},{30,25},{31,26}} | collective-permute-start | bytes 393224 | tf_op jit(solution)/shard_map/ppermute | solution.py:123
  90.9 24.4 %collective-permute-start.13 = (bf16[4,128,128]{2,1,0:T(8,128)(2,1)}, bf16[4,128,128]{2,1,0:T(8,128)(2,1)}, u32[]{:S(2)}, u32[]{:S(2)}) collective-permute-start(bf16[4,128,128]{2,1,0:T(8,128)(2,1)} %get-tuple-element.93), channel_id=1, source_target_pairs={{24,28},{25,29},{26,30},{27,31},{28,24},{29,25},{30,26},{31,27}} | collective-permute-start | bytes 393224 | tf_op jit(solution)/shard_map/ppermute | solution.py:123
  96.9 20.0 %collective-permute-start.14 = (bf16[4,128,128]{2,1,0:T(8,128)(2,1)S(1)}, bf16[4,128,128]{2,1,0:T(8,128)(2,1)S(1)}, u32[]{:S(2)}, u32[]{:S(2)}) collective-permute-start(bf16[4,128,128]{2,1,0:T(8,128)(2,1)S(1)} %get-tuple-element.92), channel_id=1, source_target_pairs={{24,29},{25,30},{26,31},{27,24},{28,25},{29,26},{30,27},{31,28}} | collective-permute-start | bytes 393224 | tf_op jit(solution)/shard_map/ppermute | solution.py:123
  100.4 17.2 %collective-permute-start.15 = (bf16[4,128,128]{2,1,0:T(8,128)(2,1)S(1)}, bf16[4,128,128]{2,1,0:T(8,128)(2,1)S(1)}, u32[]{:S(2)}, u32[]{:S(2)}) collective-permute-start(bf16[4,128,128]{2,1,0:T(8,128)(2,1)S(1)} %get-tuple-element.91), channel_id=1, source_target_pairs={{24,30},{25,31},{26,24},{27,25},{28,26},{29,27},{30,28},{31,29}} | collective-permute-start | bytes 393224 | tf_op jit(solution)/shard_map/ppermute | solution.py:123
  106.0 12.3 %collective-permute-start.16 = (bf16[4,128,128]{2,1,0:T(8,128)(2,1)S(1)}, bf16[4,128,128]{2,1,0:T(8,128)(2,1)S(1)}, u32[]{:S(2)}, u32[]{:S(2)}) collective-permute-start(bf16[4,128,128]{2,1,0:T(8,128)(2,1)S(1)} %get-tuple-element.90), channel_id=1, source_target_pairs={{24,31},{25,24},{26,25},{27,26},{28,27},{29,28},{30,29},{31,30}} | collective-permute-start | bytes 393224 | tf_op jit(solution)/shard_map/ppermute | solution.py:123
  112.8 7.5 %collective-permute-start.9 = (bf16[4,8,128,128]{3,2,1,0:T(8,128)(2,1)S(1)}, bf16[4,8,128,128]{3,2,1,0:T(8,128)(2,1)S(1)}, u32[]{:S(2)}, u32[]{:S(2)}) collective-permute-start(bf16[4,8,128,128]{3,2,1,0:T(8,128)(2,1)S(1)} %add_convert_fusion.1), channel_id=1, source_target_pairs={{8,0},{9,1},{10,2},{11,3},{12,4},{13,5},{14,6},{15,7}} | collective-permute-start | bytes 3145736 | tf_op jit(solution)/shard_map/ppermute | solution.py:169
  130.5 9.1 %collective-permute-start.24 = (f32[128,1,128]{2,0,1:T(8,128)S(1)}, f32[128,1,128]{2,0,1:T(8,128)S(1)}, u32[]{:S(2)}, u32[]{:S(2)}) collective-permute-start(f32[128,1,128]{2,0,1:T(8,128)S(1)} %get-tuple-element.105), channel_id=1, source_target_pairs={{0,1},{1,2},{2,3},{3,4},{4,5},{5,6},{6,7},{7,0},{8,9},{9,10},{10,1... | collective-permute-start | bytes 196616 | tf_op jit(solution)/shard_map/ppermute | solution.py:118
  132.3 9.8 %collective-permute-start.25 = (f32[128,1,128]{2,0,1:T(8,128)S(1)}, f32[128,1,128]{2,0,1:T(8,128)S(1)}, u32[]{:S(2)}, u32[]{:S(2)}) collective-permute-start(f32[128,1,128]{2,0,1:T(8,128)S(1)} %get-tuple-element.104), channel_id=1, source_target_pairs={{0,2},{1,3},{2,4},{3,5},{4,6},{5,7},{6,0},{7,1},{8,10},{9,11},{10,... | collective-permute-start | bytes 196616 | tf_op jit(solution)/shard_map/ppermute | solution.py:118
  132.8 9.3 %collective-permute-start.26 = (f32[128,1,128]{2,0,1:T(8,128)S(1)}, f32[128,1,128]{2,0,1:T(8,128)S(1)}, u32[]{:S(2)}, u32[]{:S(2)}) collective-permute-start(f32[128,1,128]{2,0,1:T(8,128)S(1)} %get-tuple-element.103), channel_id=1, source_target_pairs={{0,3},{1,4},{2,5},{3,6},{4,7},{5,0},{6,1},{7,2},{8,11},{9,12},{10,... | collective-permute-start | bytes 196616 | tf_op jit(solution)/shard_map/ppermute | solution.py:118
  135.8 11.4 %collective-permute-start.27 = (f32[128,1,128]{2,0,1:T(8,128)S(1)}, f32[128,1,128]{2,0,1:T(8,128)S(1)}, u32[]{:S(2)}, u32[]{:S(2)}) collective-permute-start(f32[128,1,128]{2,0,1:T(8,128)S(1)} %get-tuple-element.102), channel_id=1, source_target_pairs={{0,4},{1,5},{2,6},{3,7},{4,0},{5,1},{6,2},{7,3},{8,12},{9,13},{10,... | collective-permute-start | bytes 196616 | tf_op jit(solution)/shard_map/ppermute | solution.py:118
  135.8 11.5 %collective-permute-start.28 = (f32[128,1,128]{2,0,1:T(8,128)S(1)}, f32[128,1,128]{2,0,1:T(8,128)S(1)}, u32[]{:S(2)}, u32[]{:S(2)}) collective-permute-start(f32[128,1,128]{2,0,1:T(8,128)S(1)} %get-tuple-element.101), channel_id=1, source_target_pairs={{0,5},{1,6},{2,7},{3,0},{4,1},{5,2},{6,3},{7,4},{8,13},{9,14},{10,... | collective-permute-start | bytes 196616 | tf_op jit(solution)/shard_map/ppermute | solution.py:118
  139.6 16.2 %collective-permute-start.29 = (f32[128,1,128]{2,0,1:T(8,128)S(1)}, f32[128,1,128]{2,0,1:T(8,128)S(1)}, u32[]{:S(2)}, u32[]{:S(2)}) collective-permute-start(f32[128,1,128]{2,0,1:T(8,128)S(1)} %get-tuple-element.100), channel_id=1, source_target_pairs={{0,6},{1,7},{2,0},{3,1},{4,2},{5,3},{6,4},{7,5},{8,14},{9,15},{10,... | collective-permute-start | bytes 196616 | tf_op jit(solution)/shard_map/ppermute | solution.py:118
  142.1 14.6 %collective-permute-start.30 = (f32[128,1,128]{2,0,1:T(8,128)S(1)}, f32[128,1,128]{2,0,1:T(8,128)S(1)}, u32[]{:S(2)}, u32[]{:S(2)}) collective-permute-start(f32[128,1,128]{2,0,1:T(8,128)S(1)} %get-tuple-element.99), channel_id=1, source_target_pairs={{0,7},{1,0},{2,1},{3,2},{4,3},{5,4},{6,5},{7,6},{8,15},{9,8},{10,9... | collective-permute-start | bytes 196616 | tf_op jit(solution)/shard_map/ppermute | solution.py:118
  142.1 42.6 %collective-permute-start.21 = (bf16[2,4,128,128]{3,2,1,0:T(8,128)(2,1)S(1)}, bf16[2,4,128,128]{3,2,1,0:T(8,128)(2,1)S(1)}, u32[]{:S(2)}, u32[]{:S(2)}) collective-permute-start(bf16[2,4,128,128]{3,2,1,0:T(8,128)(2,1)S(1)} %get-tuple-element.77), channel_id=1, source_target_pairs={{0,5},{1,6},{2,7},{3,0},{4,1},{5,2},{6,3},{7,4},{8,13},{9,14},{10,... | collective-permute-start | bytes 786440 | tf_op jit(solution)/shard_map/ppermute | solution.py:118
  147.2 15.1 %collective-permute-start.17 = (bf16[2,4,128,128]{3,2,1,0:T(8,128)(2,1)}, bf16[2,4,128,128]{3,2,1,0:T(8,128)(2,1)S(1)}, u32[]{:S(2)}, u32[]{:S(2)}) collective-permute-start(bf16[2,4,128,128]{3,2,1,0:T(8,128)(2,1)} %get-tuple-element.72), channel_id=1, source_target_pairs={{0,1},{1,2},{2,3},{3,4},{4,5},{5,6},{6,7},{7,0},{8,9},{9,10},{10,1... | collective-permute-start | bytes 786440 | tf_op jit(solution)/shard_map/ppermute | solution.py:118
  147.3 29.7 %collective-permute-start.18 = (bf16[2,4,128,128]{3,2,1,0:T(8,128)(2,1)}, bf16[2,4,128,128]{3,2,1,0:T(8,128)(2,1)}, u32[]{:S(2)}, u32[]{:S(2)}) collective-permute-start(bf16[2,4,128,128]{3,2,1,0:T(8,128)(2,1)} %get-tuple-element.73), channel_id=1, source_target_pairs={{0,2},{1,3},{2,4},{3,5},{4,6},{5,7},{6,0},{7,1},{8,10},{9,11},{10,... | collective-permute-start | bytes 786440 | tf_op jit(solution)/shard_map/ppermute | solution.py:118
  155.9 24.8 %collective-permute-start.19 = (bf16[2,4,128,128]{3,2,1,0:T(8,128)(2,1)}, bf16[2,4,128,128]{3,2,1,0:T(8,128)(2,1)}, u32[]{:S(2)}, u32[]{:S(2)}) collective-permute-start(bf16[2,4,128,128]{3,2,1,0:T(8,128)(2,1)} %get-tuple-element.74), channel_id=1, source_target_pairs={{0,3},{1,4},{2,5},{3,6},{4,7},{5,0},{6,1},{7,2},{8,11},{9,12},{10,... | collective-permute-start | bytes 786440 | tf_op jit(solution)/shard_map/ppermute | solution.py:118
  156.7 26.8 %collective-permute-start.20 = (bf16[2,4,128,128]{3,2,1,0:T(8,128)(2,1)}, bf16[2,4,128,128]{3,2,1,0:T(8,128)(2,1)}, u32[]{:S(2)}, u32[]{:S(2)}) collective-permute-start(bf16[2,4,128,128]{3,2,1,0:T(8,128)(2,1)} %get-tuple-element.75), channel_id=1, source_target_pairs={{0,4},{1,5},{2,6},{3,7},{4,0},{5,1},{6,2},{7,3},{8,12},{9,13},{10,... | collective-permute-start | bytes 786440 | tf_op jit(solution)/shard_map/ppermute | solution.py:118
  162.3 22.7 %collective-permute-start.22 = (bf16[2,4,128,128]{3,2,1,0:T(8,128)(2,1)S(1)}, bf16[2,4,128,128]{3,2,1,0:T(8,128)(2,1)S(1)}, u32[]{:S(2)}, u32[]{:S(2)}) collective-permute-start(bf16[2,4,128,128]{3,2,1,0:T(8,128)(2,1)S(1)} %get-tuple-element.76), channel_id=1, source_target_pairs={{0,6},{1,7},{2,0},{3,1},{4,2},{5,3},{6,4},{7,5},{8,14},{9,15},{10,... | collective-permute-start | bytes 786440 | tf_op jit(solution)/shard_map/ppermute | solution.py:118
  177.0 8.4 %collective-permute-start.23 = (bf16[2,4,128,128]{3,2,1,0:T(8,128)(2,1)}, bf16[2,4,128,128]{3,2,1,0:T(8,128)(2,1)S(1)}, u32[]{:S(2)}, u32[]{:S(2)}) collective-permute-start(bf16[2,4,128,128]{3,2,1,0:T(8,128)(2,1)} %get-tuple-element.70), channel_id=1, source_target_pairs={{0,7},{1,0},{2,1},{3,2},{4,3},{5,4},{6,5},{7,6},{8,15},{9,8},{10,9... | collective-permute-start | bytes 786440 | tf_op jit(solution)/shard_map/ppermute | solution.py:118
  (22 other events, 62.2 us)

commit v13 on v10

--- a/solution.py
+++ b/solution.py
@@ -111,7 +111,11 @@
         out_shape[split_axis] = split_size
         out_shape[concat_axis] = concat_size * seq_ways
         result = jnp.zeros(out_shape, value.dtype)
-        for shift in range(seq_ways):
+        if seq_ways == 8:
+            shifts = (0, 1, 7, 3, 5, 2, 6, 4)
+        else:
+            shifts = tuple(range(seq_ways))
+        for shift in shifts:
             target = (seq_index + shift) % seq_ways
             chunk = lax.dynamic_slice_in_dim(value, target * split_size, split_size, axis=split_axis)
             if shift > 0 and section is None:

time: 191 us -> 195 us (1.021)
  the two profiles are of different devices: /device:TPU:15 before, /device:TPU:3 now
where the time goes in v13:
time: 195 us; the launch traced here: 194 us
  starting transfers between devices  77.2 us (40%)
  waiting for transfers between devices  52 us (27%)
  local copies, waits for them, and re-layouts  37 us (19%)
  other arithmetic  17.3 us (9%)
  matrix products  8.85 us (5%)
    ppermute x14, waiting for transfers between devices, transpose_seq(): lax.ppermute(chunk, 'seq', [(s, (s + shift) % seq_ways) for s in range(se...  49.8 us
    ppermute x14, starting transfers between devices, transpose_seq(): lax.ppermute(chunk, 'seq', [(s, (s + shift) % seq_ways) for s in range(se...  37.3 us
    ppermute x7, starting transfers between devices, transpose_seq(): lax.ppermute(chunk, ('pipe', 'seq'), [(base + s, base + (s + shift) % seq...  24 us
    dynamic_update_slice x23, local copies, waits for them, and re-layouts, transpose_seq(): lax.dynamic_update_slice_in_dim(result, chunk, source * concat_size, axis...  14.5 us
    unnamed x48, local copies, waits for them, and re-layouts  10.7 us
    ppermute x3, starting transfers between devices, on_device(): grad_in = lax.ppermute(new_grad, 'pipe', [(sender, sender - 1)])  5.89 us
    all_to_all x1, starting transfers between devices, on_device(): lax.all_to_all(key_part[:, None, :], 'seq', split_axis=0, concat_axis=1,...  5.43 us
    all_to_all x1, starting transfers between devices, on_device(): lax.all_to_all(key_rows, 'seq', split_axis=0, concat_axis=1, tiled=True)  4.54 us
  transfers between devices with their start and end apart: 26, of which 7 were waited for; matrix products, arithmetic and copies ran while one was open for 16% of the time, Pallas kernels for 0%

profile of v13, /device:TPU:3, one launch (start us, length us, event | category | flops | bytes accessed | tf_op | source)
XLA Modules:
  0.0 193.9 jit_solution(14387101371927525748)
XLA Ops:
  4.0 1.6 fusion.51
  9.1 3.0 %collective-permute-start.1 = (bf16[2,4,128,128]{3,2,1,0:T(8,128)(2,1)}, bf16[2,4,128,128]{3,2,1,0:T(8,128)(2,1)}, u32[]{:S(2)}, u32[]{:S(2)}) collective-permute-start(bf16[2,4,128,128]{3,2,1,0:T(8,128)(2,1)} %get-tuple-element.83), channel_id=1, source_target_pairs={{0,7},{1,0},{2,1},{3,2},{4,3},{5,4},{6,5},{7,6},{8,15},{9,8},{10,9... | collective-permute-start | bytes 786440 | tf_op jit(solution)/shard_map/ppermute | solution.py:122
  12.1 2.0 %fusion.34 = (bf16[2,4,128,128]{3,2,1,0:T(8,128)(2,1)}, bf16[2,4,128,128]{3,2,1,0:T(8,128)(2,1)}, bf16[2,4,128,128]{3,2,1,0:T(8,128)(2,1)}) fusion(s32[]{:T(128)S(6)} %select_n.316, bf16[1,32,128,128]{3,2,1,0:T(8,128)(2,1)} %bitcast.98, bf16[1,32,128,128]{3,2,1,0:T(8,128)(2,1)S(1)} %get-tuple-element.98, s32[]{:T(128)S(6)} %select_n.310, s32[]{:T(128)S(6)} %select_n.313), kind=kLoop, calls=%fused_computation.96 | loop fusion | flops 393216 | bytes 2883596 | tf_op jit(solution)/shard_map/stack | solution.py:146
  14.1 3.3 %collective-permute-start.3 = (bf16[2,4,128,128]{3,2,1,0:T(8,128)(2,1)}, bf16[2,4,128,128]{3,2,1,0:T(8,128)(2,1)S(1)}, u32[]{:S(2)}, u32[]{:S(2)}) collective-permute-start(bf16[2,4,128,128]{3,2,1,0:T(8,128)(2,1)} %get-tuple-element.86), channel_id=1, source_target_pairs={{0,5},{1,6},{2,7},{3,0},{4,1},{5,2},{6,3},{7,4},{8,13},{9,14},{10,... | collective-permute-start | bytes 786440 | tf_op jit(solution)/shard_map/ppermute | solution.py:122
  18.9 4.5 %all-to-all-start = ((bf16[8,128,128]{2,1,0:T(8,128)(2,1)}), bf16[8,128,128]{2,1,0:T(8,128)(2,1)S(1)}, u32[]{:S(2)}, u32[]{:S(2)}) async-start(bf16[8,128,128]{2,1,0:T(8,128)(2,1)} %gather_fusion), calls=%async_computation | async-start | bytes 524288 | tf_op jit(solution)/shard_map/all_to_all | solution.py:155
  24.6 2.8 %collective-permute-done = bf16[2,4,128,128]{3,2,1,0:T(8,128)(2,1)} collective-permute-done((bf16[2,4,128,128]{3,2,1,0:T(8,128)(2,1)}, bf16[2,4,128,128]{3,2,1,0:T(8,128)(2,1)}, u32[]{:S(2)}, u32[]{:S(2)}) %collective-permute-start) | collective-permute-done | bytes 262176 | tf_op jit(solution)/shard_map/ppermute | solution.py:122
  27.4 2.1 %collective-permute-start.5 = (bf16[2,4,128,128]{3,2,1,0:T(8,128)(2,1)}, bf16[2,4,128,128]{3,2,1,0:T(8,128)(2,1)S(1)}, u32[]{:S(2)}, u32[]{:S(2)}) collective-permute-start(bf16[2,4,128,128]{3,2,1,0:T(8,128)(2,1)} %get-tuple-element.85), channel_id=1, source_target_pairs={{0,6},{1,7},{2,0},{3,1},{4,2},{5,3},{6,4},{7,5},{8,14},{9,15},{10,... | collective-permute-start | bytes 786440 | tf_op jit(solution)/shard_map/ppermute | solution.py:122
  30.5 2.6 %collective-permute-done.1 = bf16[2,4,128,128]{3,2,1,0:T(8,128)(2,1)} collective-permute-done((bf16[2,4,128,128]{3,2,1,0:T(8,128)(2,1)}, bf16[2,4,128,128]{3,2,1,0:T(8,128)(2,1)}, u32[]{:S(2)}, u32[]{:S(2)}) %collective-permute-start.1) | collective-permute-done | bytes 262176 | tf_op jit(solution)/shard_map/ppermute | solution.py:122
  33.1 3.7 %collective-permute-start.6 = (bf16[2,4,128,128]{3,2,1,0:T(8,128)(2,1)}, bf16[2,4,128,128]{3,2,1,0:T(8,128)(2,1)S(1)}, u32[]{:S(2)}, u32[]{:S(2)}) collective-permute-start(bf16[2,4,128,128]{3,2,1,0:T(8,128)(2,1)} %get-tuple-element.80), channel_id=1, source_target_pairs={{0,4},{1,5},{2,6},{3,7},{4,0},{5,1},{6,2},{7,3},{8,12},{9,13},{10,... | collective-permute-start | bytes 786440 | tf_op jit(solution)/shard_map/ppermute | solution.py:122
  38.9 9.8 %collective-permute-done.5 = bf16[2,4,128,128]{3,2,1,0:T(8,128)(2,1)S(1)} collective-permute-done((bf16[2,4,128,128]{3,2,1,0:T(8,128)(2,1)}, bf16[2,4,128,128]{3,2,1,0:T(8,128)(2,1)S(1)}, u32[]{:S(2)}, u32[]{:S(2)}) %collective-permute-start.5) | collective-permute-done | bytes 262176 | tf_op jit(solution)/shard_map/ppermute | solution.py:122
  48.8 14.8 %collective-permute-done.6 = bf16[2,4,128,128]{3,2,1,0:T(8,128)(2,1)S(1)} collective-permute-done((bf16[2,4,128,128]{3,2,1,0:T(8,128)(2,1)}, bf16[2,4,128,128]{3,2,1,0:T(8,128)(2,1)S(1)}, u32[]{:S(2)}, u32[]{:S(2)}) %collective-permute-start.6) | collective-permute-done | bytes 262176 | tf_op jit(solution)/shard_map/ppermute | solution.py:122
  68.6 2.2 %fusion.52 = (f32[4,8,128]{2,1,0:T(8,128)S(1)}, f32[4,8,128,256]{3,2,1,0:T(8,128)S(1)}) fusion(f32[4,8,128,256]{3,2,1,0:T(8,128)S(1)} %fusion.3, pred[8,128,256]{2,1,0:T(8,128)(4,1)S(1)} %copy-done.19), kind=kOutput, calls=%fused_computation.160 | output fusion | flops 6291711 | bytes 8667136 | tf_op jit(solution)/shard_map/sub | solution.py:53
  74.5 3.3 %collective-permute-start.7 = (bf16[4,8,128,128]{3,2,1,0:T(8,128)(2,1)S(1)}, bf16[4,8,128,128]{3,2,1,0:T(8,128)(2,1)S(1)}, u32[]{:S(2)}, u32[]{:S(2)}) collective-permute-start(bf16[4,8,128,128]{3,2,1,0:T(8,128)(2,1)S(1)} %add_convert_fusion.3), channel_id=1, source_target_pairs={{24,16},{25,17},{26,18},{27,19},{28,20},{29,21},{30,22},{31,23}} | collective-permute-start | bytes 3145736 | tf_op jit(solution)/shard_map/ppermute | solution.py:173
  77.8 2.2 %collective-permute-done.7 = bf16[4,8,128,128]{3,2,1,0:T(8,128)(2,1)S(1)} collective-permute-done((bf16[4,8,128,128]{3,2,1,0:T(8,128)(2,1)S(1)}, bf16[4,8,128,128]{3,2,1,0:T(8,128)(2,1)S(1)}, u32[]{:S(2)}, u32[]{:S(2)}) %collective-permute-start.7) | collective-permute-done | bytes 1048608 | tf_op jit(solution)/shard_map/ppermute | solution.py:173
  82.7 1.6 collective-permute-start.8
  85.2 1.9 collective-permute-start.10
  87.1 6.1 %collective-permute-start.11 = (bf16[4,128,128]{2,1,0:T(8,128)(2,1)}, bf16[4,128,128]{2,1,0:T(8,128)(2,1)}, u32[]{:S(2)}, u32[]{:S(2)}) collective-permute-start(bf16[4,128,128]{2,1,0:T(8,128)(2,1)} %get-tuple-element.95), channel_id=1, source_target_pairs={{24,31},{25,24},{26,25},{27,26},{28,27},{29,28},{30,29},{31,30}} | collective-permute-start | bytes 393224 | tf_op jit(solution)/shard_map/ppermute | solution.py:127
  93.2 1.9 collective-permute-start.12
  95.1 5.2 %collective-permute-start.13 = (bf16[4,128,128]{2,1,0:T(8,128)(2,1)}, bf16[4,128,128]{2,1,0:T(8,128)(2,1)}, u32[]{:S(2)}, u32[]{:S(2)}) collective-permute-start(bf16[4,128,128]{2,1,0:T(8,128)(2,1)} %get-tuple-element.93), channel_id=1, source_target_pairs={{24,29},{25,30},{26,31},{27,24},{28,25},{29,26},{30,27},{31,28}} | collective-permute-start | bytes 393224 | tf_op jit(solution)/shard_map/ppermute | solution.py:127
  102.1 1.9 collective-permute-start.14
  104.0 1.6 constant_dynamic-update-slice_fusion.6
  105.6 5.1 %collective-permute-start.15 = (bf16[4,128,128]{2,1,0:T(8,128)(2,1)S(1)}, bf16[4,128,128]{2,1,0:T(8,128)(2,1)S(1)}, u32[]{:S(2)}, u32[]{:S(2)}) collective-permute-start(bf16[4,128,128]{2,1,0:T(8,128)(2,1)S(1)} %get-tuple-element.91), channel_id=1, source_target_pairs={{24,30},{25,31},{26,24},{27,25},{28,26},{29,27},{30,28},{31,29}} | collective-permute-start | bytes 393224 | tf_op jit(solution)/shard_map/ppermute | solution.py:127
  110.8 1.6 constant_dynamic-update-slice_fusion.5
  112.3 1.9 collective-permute-start.16
  114.3 2.0 %fusion.55 = f32[4,8,256,128]{3,2,1,0:T(8,128)S(1)} fusion(bf16[4,8,128,256]{3,2,1,0:T(8,128)(2,1)S(1)} %fusion.8, bf16[4,8,128,128]{3,2,1,0:T(8,128)(2,1)} %collective-permute-done.8), kind=kOutput, calls=%fused_computation.163 | convolution fusion | flops 268435456 | bytes 7340032 | tf_op jit(solution)/shard_map/hbij,hbid->hbjd/dot_general | solution.py:58
  116.8 1.7 add_convert_fusion.1
  137.2 5.4 %all-to-all-start.1 = ((f32[1024,1,128]{2,1,0:T(1,128)}), f32[1024,1,128]{2,1,0:T(1,128)}, u32[]{:S(2)}, u32[]{:S(2)}) async-start(f32[1024,1,128]{2,1,0:T(1,128)} %bitcast.30), calls=%async_computation.1 | async-start | bytes 1048576 | tf_op jit(solution)/shard_map/all_to_all | solution.py:200
  144.1 3.0 %collective-permute-start.18 = (bf16[2,4,128,128]{3,2,1,0:T(8,128)(2,1)S(1)}, bf16[2,4,128,128]{3,2,1,0:T(8,128)(2,1)S(1)}, u32[]{:S(2)}, u32[]{:S(2)}) collective-permute-start(bf16[2,4,128,128]{3,2,1,0:T(8,128)(2,1)S(1)} %get-tuple-element.73), channel_id=1, source_target_pairs={{0,7},{1,0},{2,1},{3,2},{4,3},{5,4},{6,5},{7,6},{8,15},{9,8},{10,9... | collective-permute-start | bytes 786440 | tf_op jit(solution)/shard_map/ppermute | solution.py:122
  147.1 3.3 %collective-permute-start.20 = (bf16[2,4,128,128]{3,2,1,0:T(8,128)(2,1)S(1)}, bf16[2,4,128,128]{3,2,1,0:T(8,128)(2,1)S(1)}, u32[]{:S(2)}, u32[]{:S(2)}) collective-permute-start(bf16[2,4,128,128]{3,2,1,0:T(8,128)(2,1)S(1)} %get-tuple-element.75), channel_id=1, source_target_pairs={{0,5},{1,6},{2,7},{3,0},{4,1},{5,2},{6,3},{7,4},{8,13},{9,14},{10,... | collective-permute-start | bytes 786440 | tf_op jit(solution)/shard_map/ppermute | solution.py:122
  152.4 8.6 %collective-permute-done.18 = bf16[2,4,128,128]{3,2,1,0:T(8,128)(2,1)S(1)} collective-permute-done((bf16[2,4,128,128]{3,2,1,0:T(8,128)(2,1)S(1)}, bf16[2,4,128,128]{3,2,1,0:T(8,128)(2,1)S(1)}, u32[]{:S(2)}, u32[]{:S(2)}) %collective-permute-start.18) | collective-permute-done | bytes 262176 | tf_op jit(solution)/shard_map/ppermute | solution.py:122
  161.0 15.0 %collective-permute-start.23 = (bf16[2,4,128,128]{3,2,1,0:T(8,128)(2,1)S(1)}, bf16[2,4,128,128]{3,2,1,0:T(8,128)(2,1)S(1)}, u32[]{:S(2)}, u32[]{:S(2)}) collective-permute-start(bf16[2,4,128,128]{3,2,1,0:T(8,128)(2,1)S(1)} %get-tuple-element.70), channel_id=1, source_target_pairs={{0,4},{1,5},{2,6},{3,7},{4,0},{5,1},{6,2},{7,3},{8,12},{9,13},{10,... | collective-permute-start | bytes 786440 | tf_op jit(solution)/shard_map/ppermute | solution.py:122
  177.6 11.1 %collective-permute-done.23 = bf16[2,4,128,128]{3,2,1,0:T(8,128)(2,1)S(1)} collective-permute-done((bf16[2,4,128,128]{3,2,1,0:T(8,128)(2,1)S(1)}, bf16[2,4,128,128]{3,2,1,0:T(8,128)(2,1)S(1)}, u32[]{:S(2)}, u32[]{:S(2)}) %collective-permute-start.23) | collective-permute-done | bytes 262176 | tf_op jit(solution)/shard_map/ppermute | solution.py:122
  (155 shorter events, 55.5 us)
Async XLA Ops:
  0.6 3.4 %copy-start = (bf16[128,4096]{1,0:T(8,128)(2,1)S(1)}, bf16[128,4096]{1,0:T(8,128)(2,1)}, u32[]{:S(2)}) copy-start(bf16[128,4096]{1,0:T(8,128)(2,1)} %param.18) | copy-start | bytes 3145732
  7.8 9.6 %copy-start.20 = (bf16[1,128,512]{2,1,0:T(8,128)(2,1)S(1)}, bf16[1,128,512]{2,1,0:T(8,128)(2,1)}, u32[]{:S(2)}) copy-start(bf16[1,128,512]{2,1,0:T(8,128)(2,1)} %param.16) | copy-start | bytes 393220
  7.8 19.6 %collective-permute-start = (bf16[2,4,128,128]{3,2,1,0:T(8,128)(2,1)}, bf16[2,4,128,128]{3,2,1,0:T(8,128)(2,1)}, u32[]{:S(2)}, u32[]{:S(2)}) collective-permute-start(bf16[2,4,128,128]{3,2,1,0:T(8,128)(2,1)} %get-tuple-element.82), channel_id=1, source_target_pairs={{0,1},{1,2},{2,3},{3,4},{4,5},{5,6},{6,7},{7,0},{8,9},{9,10},{10,1... | collective-permute-start | bytes 786440 | tf_op jit(solution)/shard_map/ppermute | solution.py:122
  9.1 24.0 %collective-permute-start.1 = (bf16[2,4,128,128]{3,2,1,0:T(8,128)(2,1)}, bf16[2,4,128,128]{3,2,1,0:T(8,128)(2,1)}, u32[]{:S(2)}, u32[]{:S(2)}) collective-permute-start(bf16[2,4,128,128]{3,2,1,0:T(8,128)(2,1)} %get-tuple-element.83), channel_id=1, source_target_pairs={{0,7},{1,0},{2,1},{3,2},{4,3},{5,4},{6,5},{7,6},{8,15},{9,8},{10,9... | collective-permute-start | bytes 786440 | tf_op jit(solution)/shard_map/ppermute | solution.py:122
  12.1 25.7 %collective-permute-start.2 = (bf16[2,4,128,128]{3,2,1,0:T(8,128)(2,1)}, bf16[2,4,128,128]{3,2,1,0:T(8,128)(2,1)}, u32[]{:S(2)}, u32[]{:S(2)}) collective-permute-start(bf16[2,4,128,128]{3,2,1,0:T(8,128)(2,1)} %get-tuple-element.84), channel_id=1, source_target_pairs={{0,3},{1,4},{2,5},{3,6},{4,7},{5,0},{6,1},{7,2},{8,11},{9,12},{10,... | collective-permute-start | bytes 786440 | tf_op jit(solution)/shard_map/ppermute | solution.py:122
  12.1 11.4 %copy-start.21 = (s32[8]{0:T(128)S(1)}, s32[8]{0:T(128)}, u32[]{:S(2)}) copy-start(s32[8]{0:T(128)} %param.19) | copy-start | bytes 100
  14.1 24.7 %collective-permute-start.3 = (bf16[2,4,128,128]{3,2,1,0:T(8,128)(2,1)}, bf16[2,4,128,128]{3,2,1,0:T(8,128)(2,1)S(1)}, u32[]{:S(2)}, u32[]{:S(2)}) collective-permute-start(bf16[2,4,128,128]{3,2,1,0:T(8,128)(2,1)} %get-tuple-element.86), channel_id=1, source_target_pairs={{0,5},{1,6},{2,7},{3,0},{4,1},{5,2},{6,3},{7,4},{8,13},{9,14},{10,... | collective-permute-start | bytes 786440 | tf_op jit(solution)/shard_map/ppermute | solution.py:122
  17.4 21.5 %collective-permute-start.4 = (bf16[2,4,128,128]{3,2,1,0:T(8,128)(2,1)}, bf16[2,4,128,128]{3,2,1,0:T(8,128)(2,1)S(1)}, u32[]{:S(2)}, u32[]{:S(2)}) collective-permute-start(bf16[2,4,128,128]{3,2,1,0:T(8,128)(2,1)} %get-tuple-element.87), channel_id=1, source_target_pairs={{0,2},{1,3},{2,4},{3,5},{4,6},{5,7},{6,0},{7,1},{8,10},{9,11},{10,... | collective-permute-start | bytes 786440 | tf_op jit(solution)/shard_map/ppermute | solution.py:122
  18.9 46.4 %all-to-all-start = ((bf16[8,128,128]{2,1,0:T(8,128)(2,1)}), bf16[8,128,128]{2,1,0:T(8,128)(2,1)S(1)}, u32[]{:S(2)}, u32[]{:S(2)}) async-start(bf16[8,128,128]{2,1,0:T(8,128)(2,1)} %gather_fusion), calls=%async_computation | async-start | bytes 524288 | tf_op jit(solution)/shard_map/all_to_all | solution.py:155
  27.4 21.4 %collective-permute-start.5 = (bf16[2,4,128,128]{3,2,1,0:T(8,128)(2,1)}, bf16[2,4,128,128]{3,2,1,0:T(8,128)(2,1)S(1)}, u32[]{:S(2)}, u32[]{:S(2)}) collective-permute-start(bf16[2,4,128,128]{3,2,1,0:T(8,128)(2,1)} %get-tuple-element.85), channel_id=1, source_target_pairs={{0,6},{1,7},{2,0},{3,1},{4,2},{5,3},{6,4},{7,5},{8,14},{9,15},{10,... | collective-permute-start | bytes 786440 | tf_op jit(solution)/shard_map/ppermute | solution.py:122
  33.1 30.5 %collective-permute-start.6 = (bf16[2,4,128,128]{3,2,1,0:T(8,128)(2,1)}, bf16[2,4,128,128]{3,2,1,0:T(8,128)(2,1)S(1)}, u32[]{:S(2)}, u32[]{:S(2)}) collective-permute-start(bf16[2,4,128,128]{3,2,1,0:T(8,128)(2,1)} %get-tuple-element.80), channel_id=1, source_target_pairs={{0,4},{1,5},{2,6},{3,7},{4,0},{5,1},{6,2},{7,3},{8,12},{9,13},{10,... | collective-permute-start | bytes 786440 | tf_op jit(solution)/shard_map/ppermute | solution.py:122
  74.5 3.4 %copy-start.16 = (bf16[4,8,128,128]{3,2,1,0:T(8,128)(2,1)}, bf16[4,8,128,128]{3,2,1,0:T(8,128)(2,1)S(1)}, u32[]{:S(2)}) copy-start(bf16[4,8,128,128]{3,2,1,0:T(8,128)(2,1)S(1)} %add_convert_fusion.3) | copy-start | bytes 3145732
  74.5 5.5 %collective-permute-start.7 = (bf16[4,8,128,128]{3,2,1,0:T(8,128)(2,1)S(1)}, bf16[4,8,128,128]{3,2,1,0:T(8,128)(2,1)S(1)}, u32[]{:S(2)}, u32[]{:S(2)}) collective-permute-start(bf16[4,8,128,128]{3,2,1,0:T(8,128)(2,1)S(1)} %add_convert_fusion.3), channel_id=1, source_target_pairs={{24,16},{25,17},{26,18},{27,19},{28,20},{29,21},{30,22},{31,23}} | collective-permute-start | bytes 3145736 | tf_op jit(solution)/shard_map/ppermute | solution.py:173
  82.7 29.6 %collective-permute-start.8 = (bf16[4,8,128,128]{3,2,1,0:T(8,128)(2,1)}, bf16[4,8,128,128]{3,2,1,0:T(8,128)(2,1)}, u32[]{:S(2)}, u32[]{:S(2)}) collective-permute-start(bf16[4,8,128,128]{3,2,1,0:T(8,128)(2,1)} %add_convert_fusion.2), channel_id=1, source_target_pairs={{16,8},{17,9},{18,10},{19,11},{20,12},{21,13},{22,14},{23,15}} | collective-permute-start | bytes 3145736 | tf_op jit(solution)/shard_map/ppermute | solution.py:173
  85.2 16.9 %collective-permute-start.10 = (bf16[4,128,128]{2,1,0:T(8,128)(2,1)}, bf16[4,128,128]{2,1,0:T(8,128)(2,1)}, u32[]{:S(2)}, u32[]{:S(2)}) collective-permute-start(bf16[4,128,128]{2,1,0:T(8,128)(2,1)} %get-tuple-element.96), channel_id=1, source_target_pairs={{24,25},{25,26},{26,27},{27,28},{28,29},{29,30},{30,31},{31,24}} | collective-permute-start | bytes 393224 | tf_op jit(solution)/shard_map/ppermute | solution.py:127
  87.1 18.5 %collective-permute-start.11 = (bf16[4,128,128]{2,1,0:T(8,128)(2,1)}, bf16[4,128,128]{2,1,0:T(8,128)(2,1)}, u32[]{:S(2)}, u32[]{:S(2)}) collective-permute-start(bf16[4,128,128]{2,1,0:T(8,128)(2,1)} %get-tuple-element.95), channel_id=1, source_target_pairs={{24,31},{25,24},{26,25},{27,26},{28,27},{29,28},{30,29},{31,30}} | collective-permute-start | bytes 393224 | tf_op jit(solution)/shard_map/ppermute | solution.py:127
  93.2 25.3 %collective-permute-start.12 = (bf16[4,128,128]{2,1,0:T(8,128)(2,1)}, bf16[4,128,128]{2,1,0:T(8,128)(2,1)}, u32[]{:S(2)}, u32[]{:S(2)}) collective-permute-start(bf16[4,128,128]{2,1,0:T(8,128)(2,1)} %get-tuple-element.94), channel_id=1, source_target_pairs={{24,27},{25,28},{26,29},{27,30},{28,31},{29,24},{30,25},{31,26}} | collective-permute-start | bytes 393224 | tf_op jit(solution)/shard_map/ppermute | solution.py:127
  95.1 25.9 %collective-permute-start.13 = (bf16[4,128,128]{2,1,0:T(8,128)(2,1)}, bf16[4,128,128]{2,1,0:T(8,128)(2,1)}, u32[]{:S(2)}, u32[]{:S(2)}) collective-permute-start(bf16[4,128,128]{2,1,0:T(8,128)(2,1)} %get-tuple-element.93), channel_id=1, source_target_pairs={{24,29},{25,30},{26,31},{27,24},{28,25},{29,26},{30,27},{31,28}} | collective-permute-start | bytes 393224 | tf_op jit(solution)/shard_map/ppermute | solution.py:127
  102.1 20.6 %collective-permute-start.14 = (bf16[4,128,128]{2,1,0:T(8,128)(2,1)S(1)}, bf16[4,128,128]{2,1,0:T(8,128)(2,1)S(1)}, u32[]{:S(2)}, u32[]{:S(2)}) collective-permute-start(bf16[4,128,128]{2,1,0:T(8,128)(2,1)S(1)} %get-tuple-element.92), channel_id=1, source_target_pairs={{24,26},{25,27},{26,28},{27,29},{28,30},{29,31},{30,24},{31,25}} | collective-permute-start | bytes 393224 | tf_op jit(solution)/shard_map/ppermute | solution.py:127
  105.6 17.7 %collective-permute-start.15 = (bf16[4,128,128]{2,1,0:T(8,128)(2,1)S(1)}, bf16[4,128,128]{2,1,0:T(8,128)(2,1)S(1)}, u32[]{:S(2)}, u32[]{:S(2)}) collective-permute-start(bf16[4,128,128]{2,1,0:T(8,128)(2,1)S(1)} %get-tuple-element.91), channel_id=1, source_target_pairs={{24,30},{25,31},{26,24},{27,25},{28,26},{29,27},{30,28},{31,29}} | collective-permute-start | bytes 393224 | tf_op jit(solution)/shard_map/ppermute | solution.py:127
  112.3 11.7 %collective-permute-start.16 = (bf16[4,128,128]{2,1,0:T(8,128)(2,1)S(1)}, bf16[4,128,128]{2,1,0:T(8,128)(2,1)S(1)}, u32[]{:S(2)}, u32[]{:S(2)}) collective-permute-start(bf16[4,128,128]{2,1,0:T(8,128)(2,1)S(1)} %get-tuple-element.90), channel_id=1, source_target_pairs={{24,28},{25,29},{26,30},{27,31},{28,24},{29,25},{30,26},{31,27}} | collective-permute-start | bytes 393224 | tf_op jit(solution)/shard_map/ppermute | solution.py:127
  116.8 7.9 %copy-start.3 = (bf16[2,4,1024,128]{3,2,1,0:T(8,128)(2,1)S(1)}, bf16[2,4,1024,128]{3,2,1,0:T(8,128)(2,1)}, u32[]{:S(2)}) copy-start(bf16[2,4,1024,128]{3,2,1,0:T(8,128)(2,1)} %copy-done.2) | copy-start | bytes 6291460
  118.5 7.5 %collective-permute-start.9 = (bf16[4,8,128,128]{3,2,1,0:T(8,128)(2,1)S(1)}, bf16[4,8,128,128]{3,2,1,0:T(8,128)(2,1)S(1)}, u32[]{:S(2)}, u32[]{:S(2)}) collective-permute-start(bf16[4,8,128,128]{3,2,1,0:T(8,128)(2,1)S(1)} %add_convert_fusion.1), channel_id=1, source_target_pairs={{8,0},{9,1},{10,2},{11,3},{12,4},{13,5},{14,6},{15,7}} | collective-permute-start | bytes 3145736 | tf_op jit(solution)/shard_map/ppermute | solution.py:173
  137.1 13.8 %collective-permute-start.17 = (bf16[2,4,128,128]{3,2,1,0:T(8,128)(2,1)S(1)}, bf16[2,4,128,128]{3,2,1,0:T(8,128)(2,1)S(1)}, u32[]{:S(2)}, u32[]{:S(2)}) collective-permute-start(bf16[2,4,128,128]{3,2,1,0:T(8,128)(2,1)S(1)} %get-tuple-element.72), channel_id=1, source_target_pairs={{0,1},{1,2},{2,3},{3,4},{4,5},{5,6},{6,7},{7,0},{8,9},{9,10},{10,1... | collective-permute-start | bytes 786440 | tf_op jit(solution)/shard_map/ppermute | solution.py:122
  137.2 54.7 %all-to-all-start.1 = ((f32[1024,1,128]{2,1,0:T(1,128)}), f32[1024,1,128]{2,1,0:T(1,128)}, u32[]{:S(2)}, u32[]{:S(2)}) async-start(f32[1024,1,128]{2,1,0:T(1,128)} %bitcast.30), calls=%async_computation.1 | async-start | bytes 1048576 | tf_op jit(solution)/shard_map/all_to_all | solution.py:200
  142.6 34.4 %collective-permute-start.21 = (bf16[2,4,128,128]{3,2,1,0:T(8,128)(2,1)S(1)}, bf16[2,4,128,128]{3,2,1,0:T(8,128)(2,1)S(1)}, u32[]{:S(2)}, u32[]{:S(2)}) collective-permute-start(bf16[2,4,128,128]{3,2,1,0:T(8,128)(2,1)S(1)} %get-tuple-element.77), channel_id=1, source_target_pairs={{0,2},{1,3},{2,4},{3,5},{4,6},{5,7},{6,0},{7,1},{8,10},{9,11},{10,... | collective-permute-start | bytes 786440 | tf_op jit(solution)/shard_map/ppermute | solution.py:122
  144.1 17.0 %collective-permute-start.18 = (bf16[2,4,128,128]{3,2,1,0:T(8,128)(2,1)S(1)}, bf16[2,4,128,128]{3,2,1,0:T(8,128)(2,1)S(1)}, u32[]{:S(2)}, u32[]{:S(2)}) collective-permute-start(bf16[2,4,128,128]{3,2,1,0:T(8,128)(2,1)S(1)} %get-tuple-element.73), channel_id=1, source_target_pairs={{0,7},{1,0},{2,1},{3,2},{4,3},{5,4},{6,5},{7,6},{8,15},{9,8},{10,9... | collective-permute-start | bytes 786440 | tf_op jit(solution)/shard_map/ppermute | solution.py:122
  147.1 29.3 %collective-permute-start.19 = (bf16[2,4,128,128]{3,2,1,0:T(8,128)(2,1)S(1)}, bf16[2,4,128,128]{3,2,1,0:T(8,128)(2,1)S(1)}, u32[]{:S(2)}, u32[]{:S(2)}) collective-permute-start(bf16[2,4,128,128]{3,2,1,0:T(8,128)(2,1)S(1)} %get-tuple-element.74), channel_id=1, source_target_pairs={{0,3},{1,4},{2,5},{3,6},{4,7},{5,0},{6,1},{7,2},{8,11},{9,12},{10,... | collective-permute-start | bytes 786440 | tf_op jit(solution)/shard_map/ppermute | solution.py:122
  147.1 29.6 %collective-permute-start.20 = (bf16[2,4,128,128]{3,2,1,0:T(8,128)(2,1)S(1)}, bf16[2,4,128,128]{3,2,1,0:T(8,128)(2,1)S(1)}, u32[]{:S(2)}, u32[]{:S(2)}) collective-permute-start(bf16[2,4,128,128]{3,2,1,0:T(8,128)(2,1)S(1)} %get-tuple-element.75), channel_id=1, source_target_pairs={{0,5},{1,6},{2,7},{3,0},{4,1},{5,2},{6,3},{7,4},{8,13},{9,14},{10,... | collective-permute-start | bytes 786440 | tf_op jit(solution)/shard_map/ppermute | solution.py:122
  150.9 26.4 %collective-permute-start.22 = (bf16[2,4,128,128]{3,2,1,0:T(8,128)(2,1)S(1)}, bf16[2,4,128,128]{3,2,1,0:T(8,128)(2,1)S(1)}, u32[]{:S(2)}, u32[]{:S(2)}) collective-permute-start(bf16[2,4,128,128]{3,2,1,0:T(8,128)(2,1)S(1)} %get-tuple-element.76), channel_id=1, source_target_pairs={{0,6},{1,7},{2,0},{3,1},{4,2},{5,3},{6,4},{7,5},{8,14},{9,15},{10,... | collective-permute-start | bytes 786440 | tf_op jit(solution)/shard_map/ppermute | solution.py:122
  161.0 27.7 %collective-permute-start.23 = (bf16[2,4,128,128]{3,2,1,0:T(8,128)(2,1)S(1)}, bf16[2,4,128,128]{3,2,1,0:T(8,128)(2,1)S(1)}, u32[]{:S(2)}, u32[]{:S(2)}) collective-permute-start(bf16[2,4,128,128]{3,2,1,0:T(8,128)(2,1)S(1)} %get-tuple-element.70), channel_id=1, source_target_pairs={{0,4},{1,5},{2,6},{3,7},{4,0},{5,1},{6,2},{7,3},{8,12},{9,13},{10,... | collective-permute-start | bytes 786440 | tf_op jit(solution)/shard_map/ppermute | solution.py:122
  189.4 4.5 %copy-start.1 = (bf16[128,4096]{1,0:T(8,128)(2,1)S(1)}, bf16[128,4096]{1,0:T(8,128)(2,1)}, u32[]{:S(2)}) copy-start(bf16[128,4096]{1,0:T(8,128)(2,1)} %param.18) | copy-start | bytes 3145732
  (16 other events, 25.5 us)

commit v14 on v12

--- a/solution.py
+++ b/solution.py
@@ -193,10 +193,33 @@
         key_part = grad_key.reshape(seq_len, DH)
     else:
         key_part = jnp.sum(grad_key.astype(jnp.float32), axis=0).reshape(seq_len, DH)
-    key_out = transpose_seq(key_part[:, None, :], 0, 1)
-    key_sum = jnp.sum(
-        key_out.reshape(tok_rows, kv_count, seq_ways // kv_count, DH).astype(jnp.float32), axis=2
-    )
+    if seq_ways == 8 and seq_ways // kv_count == 2:
+        parity = seq_index % 2
+        by_parity = key_part.reshape(seq_ways // 2, 2, tok_rows, DH)
+        keep = lax.dynamic_index_in_dim(by_parity, parity, axis=1, keepdims=False)
+        give = lax.dynamic_index_in_dim(by_parity, 1 - parity, axis=1, keepdims=False)
+        got = lax.ppermute(give, "seq", [(d, d ^ 1) for d in range(seq_ways)])
+        kept_sum = keep + got
+        received = []
+        for shift in range(0, seq_ways, 2):
+            block = ((seq_index + shift) % seq_ways) // 2
+            chunk = lax.dynamic_index_in_dim(kept_sum, block, axis=0, keepdims=False)
+            if shift > 0:
+                chunk = lax.ppermute(
+                    chunk, "seq", [(d, (d + shift) % seq_ways) for d in range(seq_ways)]
+                )
+            received.append(chunk)
+        heads_in = jnp.arange(kv_count)
+        order = ((seq_index - 2 * heads_in - parity) % seq_ways) // 2
+        key_sum = jnp.transpose(jnp.take(jnp.stack(received), order, axis=0), (1, 0, 2))
+    else:
+        key_out = lax.all_to_all(
+            key_part[:, None, :], "seq", split_axis=0, concat_axis=1, tiled=True
+        )
+        key_sum = jnp.sum(
+            key_out.reshape(tok_rows, kv_count, seq_ways // kv_count, DH).astype(jnp.float32),
+            axis=2,
+        )
     key_final = key_sum.astype(jnp.bfloat16).reshape(tok_rows, kv_count * DH)
     return (pair_rows[0][None], key_final[None], pair_rows[1][None])
 

time: 192 us -> 182 us (0.948)
  the two profiles are of different devices: /device:TPU:15 before, /device:TPU:3 now
where the time goes in v14:
time: 182 us; the launch traced here: 181 us
  starting transfers between devices  84.9 us (47%)
  local copies, waits for them, and re-layouts  38.5 us (21%)
  waiting for transfers between devices  30.6 us (17%)
  other arithmetic  16.8 us (9%)
  matrix products  8.83 us (5%)
    ppermute x14, starting transfers between devices, transpose_seq(): lax.ppermute(chunk, 'seq', [(s, (s + shift) % seq_ways) for s in range(se...  37.6 us
    ppermute x7, starting transfers between devices, transpose_seq(): lax.ppermute(chunk, ('pipe', 'seq'), [(base + s, base + (s + shift) % seq...  30.8 us
    ppermute x14, waiting for transfers between devices, transpose_seq(): lax.ppermute(chunk, 'seq', [(s, (s + shift) % seq_ways) for s in range(se...  21.3 us
    dynamic_update_slice x23, local copies, waits for them, and re-layouts, transpose_seq(): lax.dynamic_update_slice_in_dim(result, chunk, source * concat_size, axis...  15.4 us
    unnamed x50, local copies, waits for them, and re-layouts  10.7 us
    ppermute x3, starting transfers between devices, on_device(): lax.ppermute(chunk, 'seq', [(d, (d + shift) % seq_ways) for d in range(se...  7.6 us
    all_to_all x1, waiting for transfers between devices, on_device(): lax.all_to_all(key_rows, 'seq', split_axis=0, concat_axis=1, tiled=True)  7.01 us
    ppermute x3, starting transfers between devices, on_device(): grad_in = lax.ppermute(new_grad, 'pipe', [(sender, sender - 1)])  5.09 us
  transfers between devices with their start and end apart: 29, of which 6 were waited for; matrix products, arithmetic and copies ran while one was open for 18% of the time, Pallas kernels for 0%

profile of v14, /device:TPU:3, one launch (start us, length us, event | category | flops | bytes accessed | tf_op | source)
XLA Modules:
  0.0 181.2 jit_solution(16998043630676914245)
XLA Ops:
  0.7 1.6 copy.99
  4.0 1.6 fusion.55
  10.3 2.3 %collective-permute-start.2 = (bf16[2,4,128,128]{3,2,1,0:T(8,128)(2,1)}, bf16[2,4,128,128]{3,2,1,0:T(8,128)(2,1)}, u32[]{:S(2)}, u32[]{:S(2)}) collective-permute-start(bf16[2,4,128,128]{3,2,1,0:T(8,128)(2,1)} %get-tuple-element.84), channel_id=1, source_target_pairs={{0,3},{1,4},{2,5},{3,6},{4,7},{5,0},{6,1},{7,2},{8,11},{9,12},{10,... | collective-permute-start | bytes 786440 | tf_op jit(solution)/shard_map/ppermute | solution.py:118
  12.6 2.0 %fusion.34 = (bf16[2,4,128,128]{3,2,1,0:T(8,128)(2,1)}, bf16[2,4,128,128]{3,2,1,0:T(8,128)(2,1)}, bf16[2,4,128,128]{3,2,1,0:T(8,128)(2,1)}) fusion(s32[]{:T(128)S(6)} %select_n.416, bf16[1,32,128,128]{3,2,1,0:T(8,128)(2,1)} %bitcast.110, bf16[1,32,128,128]{3,2,1,0:T(8,128)(2,1)S(1)} %get-tuple-element.98, s32[]{:T(128)S(6)} %select_n.412, s32[]{:T(128)S(6)} %select_n.414), kind=kLoop, calls=%fused_computation.97 | loop fusion | flops 393216 | bytes 2883596 | tf_op jit(solution)/shard_map/stack | solution.py:142
  15.5 2.4 %collective-permute-start.4 = (bf16[2,4,128,128]{3,2,1,0:T(8,128)(2,1)}, bf16[2,4,128,128]{3,2,1,0:T(8,128)(2,1)S(1)}, u32[]{:S(2)}, u32[]{:S(2)}) collective-permute-start(bf16[2,4,128,128]{3,2,1,0:T(8,128)(2,1)} %get-tuple-element.87), channel_id=1, source_target_pairs={{0,5},{1,6},{2,7},{3,0},{4,1},{5,2},{6,3},{7,4},{8,13},{9,14},{10,... | collective-permute-start | bytes 786440 | tf_op jit(solution)/shard_map/ppermute | solution.py:118
  19.4 3.4 %all-to-all-start = ((bf16[8,128,128]{2,1,0:T(8,128)(2,1)}), bf16[8,128,128]{2,1,0:T(8,128)(2,1)S(1)}, u32[]{:S(2)}, u32[]{:S(2)}) async-start(bf16[8,128,128]{2,1,0:T(8,128)(2,1)} %gather_fusion), calls=%async_computation | async-start | bytes 524288 | tf_op jit(solution)/shard_map/all_to_all | solution.py:151
  24.0 3.2 %collective-permute-start.5 = (bf16[2,4,128,128]{3,2,1,0:T(8,128)(2,1)}, bf16[2,4,128,128]{3,2,1,0:T(8,128)(2,1)S(1)}, u32[]{:S(2)}, u32[]{:S(2)}) collective-permute-start(bf16[2,4,128,128]{3,2,1,0:T(8,128)(2,1)} %get-tuple-element.85), channel_id=1, source_target_pairs={{0,6},{1,7},{2,0},{3,1},{4,2},{5,3},{6,4},{7,5},{8,14},{9,15},{10,... | collective-permute-start | bytes 786440 | tf_op jit(solution)/shard_map/ppermute | solution.py:118
  30.4 11.7 %collective-permute-done.2 = bf16[2,4,128,128]{3,2,1,0:T(8,128)(2,1)} collective-permute-done((bf16[2,4,128,128]{3,2,1,0:T(8,128)(2,1)}, bf16[2,4,128,128]{3,2,1,0:T(8,128)(2,1)}, u32[]{:S(2)}, u32[]{:S(2)}) %collective-permute-start.2) | collective-permute-done | bytes 262176 | tf_op jit(solution)/shard_map/ppermute | solution.py:118
  44.8 2.9 %collective-permute-done.6 = bf16[2,4,128,128]{3,2,1,0:T(8,128)(2,1)S(1)} collective-permute-done((bf16[2,4,128,128]{3,2,1,0:T(8,128)(2,1)}, bf16[2,4,128,128]{3,2,1,0:T(8,128)(2,1)S(1)}, u32[]{:S(2)}, u32[]{:S(2)}) %collective-permute-start.6) | collective-permute-done | bytes 262176 | tf_op jit(solution)/shard_map/ppermute | solution.py:118
  49.4 7.0 %all-to-all-done = bf16[8,128,128]{2,1,0:T(8,128)(2,1)S(1)} async-done(((bf16[8,128,128]{2,1,0:T(8,128)(2,1)}), bf16[8,128,128]{2,1,0:T(8,128)(2,1)S(1)}, u32[]{:S(2)}, u32[]{:S(2)}) %all-to-all-start) | async-done | bytes 262176 | tf_op jit(solution)/shard_map/all_to_all | solution.py:151
  59.6 2.2 %fusion.56 = (f32[4,8,128]{2,1,0:T(8,128)S(1)}, f32[4,8,128,256]{3,2,1,0:T(8,128)S(1)}) fusion(f32[4,8,128,256]{3,2,1,0:T(8,128)S(1)} %fusion.3, pred[8,128,256]{2,1,0:T(8,128)(4,1)S(1)} %copy-done.19), kind=kOutput, calls=%fused_computation.191 | output fusion | flops 6291711 | bytes 8667136 | tf_op jit(solution)/shard_map/sub | solution.py:53
  65.5 2.6 %collective-permute-start.7 = (bf16[4,8,128,128]{3,2,1,0:T(8,128)(2,1)S(1)}, bf16[4,8,128,128]{3,2,1,0:T(8,128)(2,1)S(1)}, u32[]{:S(2)}, u32[]{:S(2)}) collective-permute-start(bf16[4,8,128,128]{3,2,1,0:T(8,128)(2,1)S(1)} %add_convert_fusion.3), channel_id=1, source_target_pairs={{24,16},{25,17},{26,18},{27,19},{28,20},{29,21},{30,22},{31,23}} | collective-permute-start | bytes 3145736 | tf_op jit(solution)/shard_map/ppermute | solution.py:169
  68.1 2.2 %collective-permute-done.7 = bf16[4,8,128,128]{3,2,1,0:T(8,128)(2,1)S(1)} collective-permute-done((bf16[4,8,128,128]{3,2,1,0:T(8,128)(2,1)S(1)}, bf16[4,8,128,128]{3,2,1,0:T(8,128)(2,1)S(1)}, u32[]{:S(2)}, u32[]{:S(2)}) %collective-permute-start.7) | collective-permute-done | bytes 1048608 | tf_op jit(solution)/shard_map/ppermute | solution.py:169
  73.0 1.6 collective-permute-start.8
  75.4 4.3 %collective-permute-start.10 = (bf16[4,128,128]{2,1,0:T(8,128)(2,1)}, bf16[4,128,128]{2,1,0:T(8,128)(2,1)}, u32[]{:S(2)}, u32[]{:S(2)}) collective-permute-start(bf16[4,128,128]{2,1,0:T(8,128)(2,1)} %get-tuple-element.96), channel_id=1, source_target_pairs={{24,25},{25,26},{26,27},{27,28},{28,29},{29,30},{30,31},{31,24}} | collective-permute-start | bytes 393224 | tf_op jit(solution)/shard_map/ppermute | solution.py:123
  79.7 10.5 %collective-permute-start.11 = (bf16[4,128,128]{2,1,0:T(8,128)(2,1)}, bf16[4,128,128]{2,1,0:T(8,128)(2,1)}, u32[]{:S(2)}, u32[]{:S(2)}) collective-permute-start(bf16[4,128,128]{2,1,0:T(8,128)(2,1)} %get-tuple-element.95), channel_id=1, source_target_pairs={{24,26},{25,27},{26,28},{27,29},{28,30},{29,31},{30,24},{31,25}} | collective-permute-start | bytes 393224 | tf_op jit(solution)/shard_map/ppermute | solution.py:123
  90.2 1.9 %collective-permute-start.12 = (bf16[4,128,128]{2,1,0:T(8,128)(2,1)}, bf16[4,128,128]{2,1,0:T(8,128)(2,1)}, u32[]{:S(2)}, u32[]{:S(2)}) collective-permute-start(bf16[4,128,128]{2,1,0:T(8,128)(2,1)} %get-tuple-element.94), channel_id=1, source_target_pairs={{24,27},{25,28},{26,29},{27,30},{28,31},{29,24},{30,25},{31,26}} | collective-permute-start | bytes 393224 | tf_op jit(solution)/shard_map/ppermute | solution.py:123
  92.2 2.2 %collective-permute-start.13 = (bf16[4,128,128]{2,1,0:T(8,128)(2,1)}, bf16[4,128,128]{2,1,0:T(8,128)(2,1)}, u32[]{:S(2)}, u32[]{:S(2)}) collective-permute-start(bf16[4,128,128]{2,1,0:T(8,128)(2,1)} %get-tuple-element.93), channel_id=1, source_target_pairs={{24,28},{25,29},{26,30},{27,31},{28,24},{29,25},{30,26},{31,27}} | collective-permute-start | bytes 393224 | tf_op jit(solution)/shard_map/ppermute | solution.py:123
  98.3 4.9 %collective-permute-start.14 = (bf16[4,128,128]{2,1,0:T(8,128)(2,1)S(1)}, bf16[4,128,128]{2,1,0:T(8,128)(2,1)S(1)}, u32[]{:S(2)}, u32[]{:S(2)}) collective-permute-start(bf16[4,128,128]{2,1,0:T(8,128)(2,1)S(1)} %get-tuple-element.92), channel_id=1, source_target_pairs={{24,29},{25,30},{26,31},{27,24},{28,25},{29,26},{30,27},{31,28}} | collective-permute-start | bytes 393224 | tf_op jit(solution)/shard_map/ppermute | solution.py:123
  103.2 1.6 constant_dynamic-update-slice_fusion.6
  104.8 3.9 %collective-permute-start.15 = (bf16[4,128,128]{2,1,0:T(8,128)(2,1)S(1)}, bf16[4,128,128]{2,1,0:T(8,128)(2,1)S(1)}, u32[]{:S(2)}, u32[]{:S(2)}) collective-permute-start(bf16[4,128,128]{2,1,0:T(8,128)(2,1)S(1)} %get-tuple-element.91), channel_id=1, source_target_pairs={{24,30},{25,31},{26,24},{27,25},{28,26},{29,27},{30,28},{31,29}} | collective-permute-start | bytes 393224 | tf_op jit(solution)/shard_map/ppermute | solution.py:123
  110.3 3.1 %collective-permute-start.16 = (bf16[4,128,128]{2,1,0:T(8,128)(2,1)S(1)}, bf16[4,128,128]{2,1,0:T(8,128)(2,1)S(1)}, u32[]{:S(2)}, u32[]{:S(2)}) collective-permute-start(bf16[4,128,128]{2,1,0:T(8,128)(2,1)S(1)} %get-tuple-element.90), channel_id=1, source_target_pairs={{24,31},{25,24},{26,25},{27,26},{28,27},{29,28},{30,29},{31,30}} | collective-permute-start | bytes 393224 | tf_op jit(solution)/shard_map/ppermute | solution.py:123
  113.4 2.0 %fusion.59 = f32[4,8,256,128]{3,2,1,0:T(8,128)S(1)} fusion(bf16[4,8,128,256]{3,2,1,0:T(8,128)(2,1)S(1)} %fusion.8, bf16[4,8,128,128]{3,2,1,0:T(8,128)(2,1)} %collective-permute-done.8), kind=kOutput, calls=%fused_computation.194 | convolution fusion | flops 268435456 | bytes 7340032 | tf_op jit(solution)/shard_map/hbij,hbid->hbjd/dot_general | solution.py:58
  116.0 1.7 add_convert_fusion.1
  118.6 1.6 constant_dynamic-update-slice_fusion.4
  120.2 1.6 constant_dynamic-update-slice_fusion.3
  137.3 2.8 %collective-permute-start.18 = (bf16[2,4,128,128]{3,2,1,0:T(8,128)(2,1)S(1)}, bf16[2,4,128,128]{3,2,1,0:T(8,128)(2,1)S(1)}, u32[]{:S(2)}, u32[]{:S(2)}) collective-permute-start(bf16[2,4,128,128]{3,2,1,0:T(8,128)(2,1)S(1)} %get-tuple-element.73), channel_id=1, source_target_pairs={{0,2},{1,3},{2,4},{3,5},{4,6},{5,7},{6,0},{7,1},{8,10},{9,11},{10,... | collective-permute-start | bytes 786440 | tf_op jit(solution)/shard_map/ppermute | solution.py:118
  140.7 5.2 %collective-permute-done.17 = bf16[2,4,128,128]{3,2,1,0:T(8,128)(2,1)S(1)} collective-permute-done((bf16[2,4,128,128]{3,2,1,0:T(8,128)(2,1)S(1)}, bf16[2,4,128,128]{3,2,1,0:T(8,128)(2,1)S(1)}, u32[]{:S(2)}, u32[]{:S(2)}) %collective-permute-start.17) | collective-permute-done | bytes 262176 | tf_op jit(solution)/shard_map/ppermute | solution.py:118
  145.8 7.9 %collective-permute-start.20 = (bf16[2,4,128,128]{3,2,1,0:T(8,128)(2,1)S(1)}, bf16[2,4,128,128]{3,2,1,0:T(8,128)(2,1)S(1)}, u32[]{:S(2)}, u32[]{:S(2)}) collective-permute-start(bf16[2,4,128,128]{3,2,1,0:T(8,128)(2,1)S(1)} %get-tuple-element.75), channel_id=1, source_target_pairs={{0,4},{1,5},{2,6},{3,7},{4,0},{5,1},{6,2},{7,3},{8,12},{9,13},{10,... | collective-permute-start | bytes 786440 | tf_op jit(solution)/shard_map/ppermute | solution.py:118
  154.4 12.8 %collective-permute-start.23 = (bf16[2,4,128,128]{3,2,1,0:T(8,128)(2,1)S(1)}, bf16[2,4,128,128]{3,2,1,0:T(8,128)(2,1)S(1)}, u32[]{:S(2)}, u32[]{:S(2)}) collective-permute-start(bf16[2,4,128,128]{3,2,1,0:T(8,128)(2,1)S(1)} %get-tuple-element.70), channel_id=1, source_target_pairs={{0,7},{1,0},{2,1},{3,2},{4,3},{5,4},{6,5},{7,6},{8,15},{9,8},{10,9... | collective-permute-start | bytes 786440 | tf_op jit(solution)/shard_map/ppermute | solution.py:118
  167.7 2.6 %collective-permute-start.26 = (bf16[128,128]{1,0:T(8,128)(2,1)S(1)}, bf16[128,128]{1,0:T(8,128)(2,1)S(1)}, u32[]{:S(2)}, u32[]{:S(2)}) collective-permute-start(bf16[128,128]{1,0:T(8,128)(2,1)S(1)} %get-tuple-element.101), channel_id=1, source_target_pairs={{0,4},{1,5},{2,6},{3,7},{4,0},{5,1},{6,2},{7,3},{8,12},{9,13},{10,... | collective-permute-start | bytes 98312 | tf_op jit(solution)/shard_map/ppermute | solution.py:208
  170.6 5.0 %collective-permute-start.27 = (bf16[128,128]{1,0:T(8,128)(2,1)S(1)}, bf16[128,128]{1,0:T(8,128)(2,1)S(1)}, u32[]{:S(2)}, u32[]{:S(2)}) collective-permute-start(bf16[128,128]{1,0:T(8,128)(2,1)S(1)} %get-tuple-element.100), channel_id=1, source_target_pairs={{0,6},{1,7},{2,0},{3,1},{4,2},{5,3},{6,4},{7,5},{8,14},{9,15},{10,... | collective-permute-start | bytes 98312 | tf_op jit(solution)/shard_map/ppermute | solution.py:208
  (171 shorter events, 57.6 us)
Async XLA Ops:
  7.8 10.1 %copy-start.20 = (bf16[1,128,512]{2,1,0:T(8,128)(2,1)S(1)}, bf16[1,128,512]{2,1,0:T(8,128)(2,1)}, u32[]{:S(2)}) copy-start(bf16[1,128,512]{2,1,0:T(8,128)(2,1)} %param.16) | copy-start | bytes 393220
  7.8 16.2 %collective-permute-start = (bf16[2,4,128,128]{3,2,1,0:T(8,128)(2,1)}, bf16[2,4,128,128]{3,2,1,0:T(8,128)(2,1)}, u32[]{:S(2)}, u32[]{:S(2)}) collective-permute-start(bf16[2,4,128,128]{3,2,1,0:T(8,128)(2,1)} %get-tuple-element.82), channel_id=1, source_target_pairs={{0,1},{1,2},{2,3},{3,4},{4,5},{5,6},{6,7},{7,0},{8,9},{9,10},{10,1... | collective-permute-start | bytes 786440 | tf_op jit(solution)/shard_map/ppermute | solution.py:118
  9.0 19.1 %collective-permute-start.1 = (bf16[2,4,128,128]{3,2,1,0:T(8,128)(2,1)}, bf16[2,4,128,128]{3,2,1,0:T(8,128)(2,1)}, u32[]{:S(2)}, u32[]{:S(2)}) collective-permute-start(bf16[2,4,128,128]{3,2,1,0:T(8,128)(2,1)} %get-tuple-element.83), channel_id=1, source_target_pairs={{0,2},{1,3},{2,4},{3,5},{4,6},{5,7},{6,0},{7,1},{8,10},{9,11},{10,... | collective-permute-start | bytes 786440 | tf_op jit(solution)/shard_map/ppermute | solution.py:118
  10.3 31.7 %collective-permute-start.2 = (bf16[2,4,128,128]{3,2,1,0:T(8,128)(2,1)}, bf16[2,4,128,128]{3,2,1,0:T(8,128)(2,1)}, u32[]{:S(2)}, u32[]{:S(2)}) collective-permute-start(bf16[2,4,128,128]{3,2,1,0:T(8,128)(2,1)} %get-tuple-element.84), channel_id=1, source_target_pairs={{0,3},{1,4},{2,5},{3,6},{4,7},{5,0},{6,1},{7,2},{8,11},{9,12},{10,... | collective-permute-start | bytes 786440 | tf_op jit(solution)/shard_map/ppermute | solution.py:118
  12.6 10.3 %copy-start.21 = (s32[8]{0:T(128)S(1)}, s32[8]{0:T(128)}, u32[]{:S(2)}) copy-start(s32[8]{0:T(128)} %param.19) | copy-start | bytes 100
  14.6 30.1 %collective-permute-start.3 = (bf16[2,4,128,128]{3,2,1,0:T(8,128)(2,1)}, bf16[2,4,128,128]{3,2,1,0:T(8,128)(2,1)S(1)}, u32[]{:S(2)}, u32[]{:S(2)}) collective-permute-start(bf16[2,4,128,128]{3,2,1,0:T(8,128)(2,1)} %get-tuple-element.86), channel_id=1, source_target_pairs={{0,4},{1,5},{2,6},{3,7},{4,0},{5,1},{6,2},{7,3},{8,12},{9,13},{10,... | collective-permute-start | bytes 786440 | tf_op jit(solution)/shard_map/ppermute | solution.py:118
  15.5 29.2 %collective-permute-start.4 = (bf16[2,4,128,128]{3,2,1,0:T(8,128)(2,1)}, bf16[2,4,128,128]{3,2,1,0:T(8,128)(2,1)S(1)}, u32[]{:S(2)}, u32[]{:S(2)}) collective-permute-start(bf16[2,4,128,128]{3,2,1,0:T(8,128)(2,1)} %get-tuple-element.87), channel_id=1, source_target_pairs={{0,5},{1,6},{2,7},{3,0},{4,1},{5,2},{6,3},{7,4},{8,13},{9,14},{10,... | collective-permute-start | bytes 786440 | tf_op jit(solution)/shard_map/ppermute | solution.py:118
  19.4 36.9 %all-to-all-start = ((bf16[8,128,128]{2,1,0:T(8,128)(2,1)}), bf16[8,128,128]{2,1,0:T(8,128)(2,1)S(1)}, u32[]{:S(2)}, u32[]{:S(2)}) async-start(bf16[8,128,128]{2,1,0:T(8,128)(2,1)} %gather_fusion), calls=%async_computation | async-start | bytes 524288 | tf_op jit(solution)/shard_map/all_to_all | solution.py:151
  24.0 20.8 %collective-permute-start.5 = (bf16[2,4,128,128]{3,2,1,0:T(8,128)(2,1)}, bf16[2,4,128,128]{3,2,1,0:T(8,128)(2,1)S(1)}, u32[]{:S(2)}, u32[]{:S(2)}) collective-permute-start(bf16[2,4,128,128]{3,2,1,0:T(8,128)(2,1)} %get-tuple-element.85), channel_id=1, source_target_pairs={{0,6},{1,7},{2,0},{3,1},{4,2},{5,3},{6,4},{7,5},{8,14},{9,15},{10,... | collective-permute-start | bytes 786440 | tf_op jit(solution)/shard_map/ppermute | solution.py:118
  28.1 19.5 %collective-permute-start.6 = (bf16[2,4,128,128]{3,2,1,0:T(8,128)(2,1)}, bf16[2,4,128,128]{3,2,1,0:T(8,128)(2,1)S(1)}, u32[]{:S(2)}, u32[]{:S(2)}) collective-permute-start(bf16[2,4,128,128]{3,2,1,0:T(8,128)(2,1)} %get-tuple-element.80), channel_id=1, source_target_pairs={{0,7},{1,0},{2,1},{3,2},{4,3},{5,4},{6,5},{7,6},{8,15},{9,8},{10,9... | collective-permute-start | bytes 786440 | tf_op jit(solution)/shard_map/ppermute | solution.py:118
  65.5 4.8 %collective-permute-start.7 = (bf16[4,8,128,128]{3,2,1,0:T(8,128)(2,1)S(1)}, bf16[4,8,128,128]{3,2,1,0:T(8,128)(2,1)S(1)}, u32[]{:S(2)}, u32[]{:S(2)}) collective-permute-start(bf16[4,8,128,128]{3,2,1,0:T(8,128)(2,1)S(1)} %add_convert_fusion.3), channel_id=1, source_target_pairs={{24,16},{25,17},{26,18},{27,19},{28,20},{29,21},{30,22},{31,23}} | collective-permute-start | bytes 3145736 | tf_op jit(solution)/shard_map/ppermute | solution.py:169
  73.0 37.3 %collective-permute-start.8 = (bf16[4,8,128,128]{3,2,1,0:T(8,128)(2,1)}, bf16[4,8,128,128]{3,2,1,0:T(8,128)(2,1)}, u32[]{:S(2)}, u32[]{:S(2)}) collective-permute-start(bf16[4,8,128,128]{3,2,1,0:T(8,128)(2,1)} %add_convert_fusion.2), channel_id=1, source_target_pairs={{16,8},{17,9},{18,10},{19,11},{20,12},{21,13},{22,14},{23,15}} | collective-permute-start | bytes 3145736 | tf_op jit(solution)/shard_map/ppermute | solution.py:169
  75.4 22.9 %collective-permute-start.10 = (bf16[4,128,128]{2,1,0:T(8,128)(2,1)}, bf16[4,128,128]{2,1,0:T(8,128)(2,1)}, u32[]{:S(2)}, u32[]{:S(2)}) collective-permute-start(bf16[4,128,128]{2,1,0:T(8,128)(2,1)} %get-tuple-element.96), channel_id=1, source_target_pairs={{24,25},{25,26},{26,27},{27,28},{28,29},{29,30},{30,31},{31,24}} | collective-permute-start | bytes 393224 | tf_op jit(solution)/shard_map/ppermute | solution.py:123
  79.7 25.1 %collective-permute-start.11 = (bf16[4,128,128]{2,1,0:T(8,128)(2,1)}, bf16[4,128,128]{2,1,0:T(8,128)(2,1)}, u32[]{:S(2)}, u32[]{:S(2)}) collective-permute-start(bf16[4,128,128]{2,1,0:T(8,128)(2,1)} %get-tuple-element.95), channel_id=1, source_target_pairs={{24,26},{25,27},{26,28},{27,29},{28,30},{29,31},{30,24},{31,25}} | collective-permute-start | bytes 393224 | tf_op jit(solution)/shard_map/ppermute | solution.py:123
  90.2 27.4 %collective-permute-start.12 = (bf16[4,128,128]{2,1,0:T(8,128)(2,1)}, bf16[4,128,128]{2,1,0:T(8,128)(2,1)}, u32[]{:S(2)}, u32[]{:S(2)}) collective-permute-start(bf16[4,128,128]{2,1,0:T(8,128)(2,1)} %get-tuple-element.94), channel_id=1, source_target_pairs={{24,27},{25,28},{26,29},{27,30},{28,31},{29,24},{30,25},{31,26}} | collective-permute-start | bytes 393224 | tf_op jit(solution)/shard_map/ppermute | solution.py:123
  92.2 28.0 %collective-permute-start.13 = (bf16[4,128,128]{2,1,0:T(8,128)(2,1)}, bf16[4,128,128]{2,1,0:T(8,128)(2,1)}, u32[]{:S(2)}, u32[]{:S(2)}) collective-permute-start(bf16[4,128,128]{2,1,0:T(8,128)(2,1)} %get-tuple-element.93), channel_id=1, source_target_pairs={{24,28},{25,29},{26,30},{27,31},{28,24},{29,25},{30,26},{31,27}} | collective-permute-start | bytes 393224 | tf_op jit(solution)/shard_map/ppermute | solution.py:123
  98.3 23.5 %collective-permute-start.14 = (bf16[4,128,128]{2,1,0:T(8,128)(2,1)S(1)}, bf16[4,128,128]{2,1,0:T(8,128)(2,1)S(1)}, u32[]{:S(2)}, u32[]{:S(2)}) collective-permute-start(bf16[4,128,128]{2,1,0:T(8,128)(2,1)S(1)} %get-tuple-element.92), channel_id=1, source_target_pairs={{24,29},{25,30},{26,31},{27,24},{28,25},{29,26},{30,27},{31,28}} | collective-permute-start | bytes 393224 | tf_op jit(solution)/shard_map/ppermute | solution.py:123
  104.8 17.7 %collective-permute-start.15 = (bf16[4,128,128]{2,1,0:T(8,128)(2,1)S(1)}, bf16[4,128,128]{2,1,0:T(8,128)(2,1)S(1)}, u32[]{:S(2)}, u32[]{:S(2)}) collective-permute-start(bf16[4,128,128]{2,1,0:T(8,128)(2,1)S(1)} %get-tuple-element.91), channel_id=1, source_target_pairs={{24,30},{25,31},{26,24},{27,25},{28,26},{29,27},{30,28},{31,29}} | collective-permute-start | bytes 393224 | tf_op jit(solution)/shard_map/ppermute | solution.py:123
  110.3 12.8 %collective-permute-start.16 = (bf16[4,128,128]{2,1,0:T(8,128)(2,1)S(1)}, bf16[4,128,128]{2,1,0:T(8,128)(2,1)S(1)}, u32[]{:S(2)}, u32[]{:S(2)}) collective-permute-start(bf16[4,128,128]{2,1,0:T(8,128)(2,1)S(1)} %get-tuple-element.90), channel_id=1, source_target_pairs={{24,31},{25,24},{26,25},{27,26},{28,27},{29,28},{30,29},{31,30}} | collective-permute-start | bytes 393224 | tf_op jit(solution)/shard_map/ppermute | solution.py:123
  116.0 7.8 %copy-start.3 = (bf16[2,4,1024,128]{3,2,1,0:T(8,128)(2,1)S(1)}, bf16[2,4,1024,128]{3,2,1,0:T(8,128)(2,1)}, u32[]{:S(2)}) copy-start(bf16[2,4,1024,128]{3,2,1,0:T(8,128)(2,1)} %copy-done.2) | copy-start | bytes 6291460
  117.7 7.5 %collective-permute-start.9 = (bf16[4,8,128,128]{3,2,1,0:T(8,128)(2,1)S(1)}, bf16[4,8,128,128]{3,2,1,0:T(8,128)(2,1)S(1)}, u32[]{:S(2)}, u32[]{:S(2)}) collective-permute-start(bf16[4,8,128,128]{3,2,1,0:T(8,128)(2,1)S(1)} %add_convert_fusion.1), channel_id=1, source_target_pairs={{8,0},{9,1},{10,2},{11,3},{12,4},{13,5},{14,6},{15,7}} | collective-permute-start | bytes 3145736 | tf_op jit(solution)/shard_map/ppermute | solution.py:169
  135.4 10.4 %collective-permute-start.17 = (bf16[2,4,128,128]{3,2,1,0:T(8,128)(2,1)S(1)}, bf16[2,4,128,128]{3,2,1,0:T(8,128)(2,1)S(1)}, u32[]{:S(2)}, u32[]{:S(2)}) collective-permute-start(bf16[2,4,128,128]{3,2,1,0:T(8,128)(2,1)S(1)} %get-tuple-element.72), channel_id=1, source_target_pairs={{0,1},{1,2},{2,3},{3,4},{4,5},{5,6},{6,7},{7,0},{8,9},{9,10},{10,1... | collective-permute-start | bytes 786440 | tf_op jit(solution)/shard_map/ppermute | solution.py:118
  135.8 18.6 %collective-permute-start.24 = (f32[4,128,128]{2,1,0:T(8,128)S(1)}, f32[4,128,128]{2,1,0:T(8,128)S(1)}, u32[]{:S(2)}, u32[]{:S(2)}) collective-permute-start(f32[4,128,128]{2,1,0:T(8,128)S(1)} %dynamic-slice_bitcast_fusion), channel_id=1, source_target_pairs={{0,1},{1,0},{2,3},{3,2},{4,5},{5,4},{6,7},{7,6},{8,9},{9,8},{10,11... | collective-permute-start | bytes 786440 | tf_op jit(solution)/shard_map/ppermute | solution.py:201
  136.2 34.4 %collective-permute-start.21 = (bf16[2,4,128,128]{3,2,1,0:T(8,128)(2,1)S(1)}, bf16[2,4,128,128]{3,2,1,0:T(8,128)(2,1)S(1)}, u32[]{:S(2)}, u32[]{:S(2)}) collective-permute-start(bf16[2,4,128,128]{3,2,1,0:T(8,128)(2,1)S(1)} %get-tuple-element.77), channel_id=1, source_target_pairs={{0,5},{1,6},{2,7},{3,0},{4,1},{5,2},{6,3},{7,4},{8,13},{9,14},{10,... | collective-permute-start | bytes 786440 | tf_op jit(solution)/shard_map/ppermute | solution.py:118
  137.3 16.7 %collective-permute-start.18 = (bf16[2,4,128,128]{3,2,1,0:T(8,128)(2,1)S(1)}, bf16[2,4,128,128]{3,2,1,0:T(8,128)(2,1)S(1)}, u32[]{:S(2)}, u32[]{:S(2)}) collective-permute-start(bf16[2,4,128,128]{3,2,1,0:T(8,128)(2,1)S(1)} %get-tuple-element.73), channel_id=1, source_target_pairs={{0,2},{1,3},{2,4},{3,5},{4,6},{5,7},{6,0},{7,1},{8,10},{9,11},{10,... | collective-permute-start | bytes 786440 | tf_op jit(solution)/shard_map/ppermute | solution.py:118
  140.1 27.2 %collective-permute-start.19 = (bf16[2,4,128,128]{3,2,1,0:T(8,128)(2,1)S(1)}, bf16[2,4,128,128]{3,2,1,0:T(8,128)(2,1)S(1)}, u32[]{:S(2)}, u32[]{:S(2)}) collective-permute-start(bf16[2,4,128,128]{3,2,1,0:T(8,128)(2,1)S(1)} %get-tuple-element.74), channel_id=1, source_target_pairs={{0,3},{1,4},{2,5},{3,6},{4,7},{5,0},{6,1},{7,2},{8,11},{9,12},{10,... | collective-permute-start | bytes 786440 | tf_op jit(solution)/shard_map/ppermute | solution.py:118
  145.8 21.9 %collective-permute-start.20 = (bf16[2,4,128,128]{3,2,1,0:T(8,128)(2,1)S(1)}, bf16[2,4,128,128]{3,2,1,0:T(8,128)(2,1)S(1)}, u32[]{:S(2)}, u32[]{:S(2)}) collective-permute-start(bf16[2,4,128,128]{3,2,1,0:T(8,128)(2,1)S(1)} %get-tuple-element.75), channel_id=1, source_target_pairs={{0,4},{1,5},{2,6},{3,7},{4,0},{5,1},{6,2},{7,3},{8,12},{9,13},{10,... | collective-permute-start | bytes 786440 | tf_op jit(solution)/shard_map/ppermute | solution.py:118
  154.0 21.8 %collective-permute-start.22 = (bf16[2,4,128,128]{3,2,1,0:T(8,128)(2,1)S(1)}, bf16[2,4,128,128]{3,2,1,0:T(8,128)(2,1)S(1)}, u32[]{:S(2)}, u32[]{:S(2)}) collective-permute-start(bf16[2,4,128,128]{3,2,1,0:T(8,128)(2,1)S(1)} %get-tuple-element.76), channel_id=1, source_target_pairs={{0,6},{1,7},{2,0},{3,1},{4,2},{5,3},{6,4},{7,5},{8,14},{9,15},{10,... | collective-permute-start | bytes 786440 | tf_op jit(solution)/shard_map/ppermute | solution.py:118
  154.4 21.8 %collective-permute-start.23 = (bf16[2,4,128,128]{3,2,1,0:T(8,128)(2,1)S(1)}, bf16[2,4,128,128]{3,2,1,0:T(8,128)(2,1)S(1)}, u32[]{:S(2)}, u32[]{:S(2)}) collective-permute-start(bf16[2,4,128,128]{3,2,1,0:T(8,128)(2,1)S(1)} %get-tuple-element.70), channel_id=1, source_target_pairs={{0,7},{1,0},{2,1},{3,2},{4,3},{5,4},{6,5},{7,6},{8,15},{9,8},{10,9... | collective-permute-start | bytes 786440 | tf_op jit(solution)/shard_map/ppermute | solution.py:118
  167.3 12.1 %collective-permute-start.25 = (bf16[128,128]{1,0:T(8,128)(2,1)S(1)}, bf16[128,128]{1,0:T(8,128)(2,1)S(1)}, u32[]{:S(2)}, u32[]{:S(2)}) collective-permute-start(bf16[128,128]{1,0:T(8,128)(2,1)S(1)} %get-tuple-element.102), channel_id=1, source_target_pairs={{0,2},{1,3},{2,4},{3,5},{4,6},{5,7},{6,0},{7,1},{8,10},{9,11},{10,... | collective-permute-start | bytes 98312 | tf_op jit(solution)/shard_map/ppermute | solution.py:208
  167.7 11.7 %collective-permute-start.26 = (bf16[128,128]{1,0:T(8,128)(2,1)S(1)}, bf16[128,128]{1,0:T(8,128)(2,1)S(1)}, u32[]{:S(2)}, u32[]{:S(2)}) collective-permute-start(bf16[128,128]{1,0:T(8,128)(2,1)S(1)} %get-tuple-element.101), channel_id=1, source_target_pairs={{0,4},{1,5},{2,6},{3,7},{4,0},{5,1},{6,2},{7,3},{8,12},{9,13},{10,... | collective-permute-start | bytes 98312 | tf_op jit(solution)/shard_map/ppermute | solution.py:208
  170.6 8.8 %collective-permute-start.27 = (bf16[128,128]{1,0:T(8,128)(2,1)S(1)}, bf16[128,128]{1,0:T(8,128)(2,1)S(1)}, u32[]{:S(2)}, u32[]{:S(2)}) collective-permute-start(bf16[128,128]{1,0:T(8,128)(2,1)S(1)} %get-tuple-element.100), channel_id=1, source_target_pairs={{0,6},{1,7},{2,0},{3,1},{4,2},{5,3},{6,4},{7,5},{8,14},{9,15},{10,... | collective-permute-start | bytes 98312 | tf_op jit(solution)/shard_map/ppermute | solution.py:208
  (20 other events, 39.0 us)

commit v15 on v14

--- a/solution.py
+++ b/solution.py
@@ -146,9 +146,31 @@
     last_inputs = transpose_seq(head_major(inputs[0]), 0, 1, section=last_section)
     input_heads = jnp.where(is_last, last_inputs, stacked_heads[1])
     values_both = key_pair(to_blocks(input_heads))
-    kv_pick = (jnp.arange(seq_ways) * local_heads) // group_size
-    key_rows = jnp.transpose(key_heads[0].reshape(tok_rows, kv_count, DH), (1, 0, 2))[kv_pick]
-    key_flat = lax.all_to_all(key_rows, "seq", split_axis=0, concat_axis=1, tiled=True)
+    kv_rows = jnp.transpose(key_heads[0].reshape(tok_rows, kv_count, DH), (1, 0, 2))
+    if seq_ways == 8 and seq_ways // kv_count == 2:
+        parity = seq_index % 2
+        fetched = []
+        for shift in range(0, seq_ways, 2):
+            head = ((seq_index + shift) % seq_ways) // 2
+            chunk = lax.dynamic_index_in_dim(kv_rows, head, axis=0, keepdims=False)
+            if shift > 0:
+                chunk = lax.ppermute(
+                    chunk, "seq", [(d, (d + shift) % seq_ways) for d in range(seq_ways)]
+                )
+            fetched.append(chunk)
+        mine = jnp.stack(fetched)
+        theirs = lax.ppermute(mine, "seq", [(d, d ^ 1) for d in range(seq_ways)])
+        partner = seq_index + 1 - 2 * parity
+        blocks = jnp.arange(seq_ways)
+        order = jnp.where(
+            blocks % 2 == parity,
+            ((seq_index - blocks) % seq_ways) // 2,
+            seq_ways // 2 + ((partner - blocks) % seq_ways) // 2,
+        )
+        key_flat = jnp.take(jnp.concatenate([mine, theirs]), order, axis=0).reshape(1, seq_len, DH)
+    else:
+        kv_pick = (jnp.arange(seq_ways) * local_heads) // group_size
+        key_flat = lax.all_to_all(kv_rows[kv_pick], "seq", split_axis=0, concat_axis=1, tiled=True)
     key_blocks = jnp.broadcast_to(
         key_flat.reshape(1, block_count, BLK, DH), (local_heads, block_count, BLK, DH)
     )

time: 182 us -> 182 us (level)
  waiting for transfers between devices: 30.6 us -> 26.5 us
    ppermute x0 -> x1, waiting for transfers between devices: none -> 7.75 us  [on_device(): theirs = lax.ppermute(mine, 'seq', [(d, d ^ 1) for d in range(seq_ways)])]
    all_to_all x1 -> x0, waiting for transfers between devices: 7.01 us -> none  [on_device(): lax.all_to_all(key_rows, 'seq', split_axis=0, concat_axis=1, tiled=True)]
    ppermute x14, waiting for transfers between devices: 21.3 us -> 16.5 us  [transpose_seq(): lax.ppermute(chunk, 'seq', [(s, (s + shift) % seq_ways) for s in range(se...]
    all_to_all x1 -> x0, starting transfers between devices: 3.41 us -> none  [on_device(): lax.all_to_all(key_rows, 'seq', split_axis=0, concat_axis=1, tiled=True)]
    ppermute x3 -> x6, starting transfers between devices: 7.6 us -> 10.7 us  [on_device(): lax.ppermute(chunk, 'seq', [(d, (d + shift) % seq_ways) for d in range(se...]
    ppermute x3, starting transfers between devices: 5.09 us -> 7.93 us  [on_device(): grad_in = lax.ppermute(new_grad, 'pipe', [(sender, sender - 1)])]
    ppermute x14, starting transfers between devices: 37.6 us -> 35.1 us  [transpose_seq(): lax.ppermute(chunk, 'seq', [(s, (s + shift) % seq_ways) for s in range(se...]
    another operation x1 -> x5, local copies, waits for them, and re-layouts: 0.14 us -> 2.28 us  [on_device(): key_heads[0].reshape(tok_rows, kv_count, DH)]
  transfers between devices with their start and end apart: 29 -> 32, of which waited for: 6 -> 6; matrix products, arithmetic and copies ran while one was open for 18% -> 22% of each run, Pallas kernels for 0% -> 0%
where the time goes in v15:
time: 182 us; the launch traced here: 181 us
  starting transfers between devices  86.4 us (47%)
  local copies, waits for them, and re-layouts  39.3 us (22%)
  waiting for transfers between devices  26.5 us (15%)
  other arithmetic  18 us (10%)
  matrix products  8.84 us (5%)
    ppermute x14, starting transfers between devices, transpose_seq(): lax.ppermute(chunk, 'seq', [(s, (s + shift) % seq_ways) for s in range(se...  35.1 us
    ppermute x7, starting transfers between devices, transpose_seq(): lax.ppermute(chunk, ('pipe', 'seq'), [(base + s, base + (s + shift) % seq...  31.1 us
    ppermute x14, waiting for transfers between devices, transpose_seq(): lax.ppermute(chunk, 'seq', [(s, (s + shift) % seq_ways) for s in range(se...  16.5 us
    dynamic_update_slice x23, local copies, waits for them, and re-layouts, transpose_seq(): lax.dynamic_update_slice_in_dim(result, chunk, source * concat_size, axis...  14.5 us
    unnamed x58, local copies, waits for them, and re-layouts  11.9 us
    ppermute x6, starting transfers between devices, on_device(): lax.ppermute(chunk, 'seq', [(d, (d + shift) % seq_ways) for d in range(se...  10.7 us
    ppermute x3, starting transfers between devices, on_device(): grad_in = lax.ppermute(new_grad, 'pipe', [(sender, sender - 1)])  7.93 us
    ppermute x1, waiting for transfers between devices, on_device(): theirs = lax.ppermute(mine, 'seq', [(d, d ^ 1) for d in range(seq_ways)])  7.75 us
  transfers between devices with their start and end apart: 32, of which 6 were waited for; matrix products, arithmetic and copies ran while one was open for 22% of the time, Pallas kernels for 0%

profile of v15, /device:TPU:3, one launch (start us, length us, event | category | flops | bytes accessed | tf_op | source)
XLA Modules:
  0.0 180.8 jit_solution(12664806846116415428)
XLA Ops:
  2.8 2.3 %collective-permute-start.8 = (bf16[128,128]{1,0:T(8,128)(2,1)}, bf16[128,128]{1,0:T(8,128)(2,1)S(1)}, u32[]{:S(2)}, u32[]{:S(2)}) collective-permute-start(bf16[128,128]{1,0:T(8,128)(2,1)} %bitcast.10), channel_id=1, source_target_pairs={{0,4},{1,5},{2,6},{3,7},{4,0},{5,1},{6,2},{7,3},{8,12},{9,13},{10,... | collective-permute-start | bytes 98312 | tf_op jit(solution)/shard_map/ppermute | solution.py:157
  11.1 1.6 fusion.60
  18.8 1.9 %fusion.34 = (bf16[2,4,128,128]{3,2,1,0:T(8,128)(2,1)}, bf16[2,4,128,128]{3,2,1,0:T(8,128)(2,1)}, bf16[2,4,128,128]{3,2,1,0:T(8,128)(2,1)}) fusion(s32[]{:T(128)S(6)} %select_n.533, bf16[1,32,128,128]{3,2,1,0:T(8,128)(2,1)} %bitcast.122, bf16[1,32,128,128]{3,2,1,0:T(8,128)(2,1)S(1)} %get-tuple-element.98, s32[]{:T(128)S(6)} %select_n.529, s32[]{:T(128)S(6)} %select_n.531), kind=kLoop, calls=%fused_computation.97 | loop fusion | flops 393216 | bytes 2883596 | tf_op jit(solution)/shard_map/stack | solution.py:142
  21.9 1.8 %collective-permute-start.2 = (bf16[2,4,128,128]{3,2,1,0:T(8,128)(2,1)}, bf16[2,4,128,128]{3,2,1,0:T(8,128)(2,1)S(1)}, u32[]{:S(2)}, u32[]{:S(2)}) collective-permute-start(bf16[2,4,128,128]{3,2,1,0:T(8,128)(2,1)} %get-tuple-element.84), channel_id=1, source_target_pairs={{0,3},{1,4},{2,5},{3,6},{4,7},{5,0},{6,1},{7,2},{8,11},{9,12},{10,... | collective-permute-start | bytes 786440 | tf_op jit(solution)/shard_map/ppermute | solution.py:118
  25.6 7.7 %collective-permute-done.10 = bf16[4,128,128]{2,1,0:T(8,128)(2,1)S(1)} collective-permute-done((bf16[4,128,128]{2,1,0:T(8,128)(2,1)S(1)}, bf16[4,128,128]{2,1,0:T(8,128)(2,1)S(1)}, u32[]{:S(2)}, u32[]{:S(2)}) %collective-permute-start.10) | collective-permute-done | bytes 131104 | tf_op jit(solution)/shard_map/ppermute | solution.py:162
  34.2 4.6 %collective-permute-start.5 = (bf16[2,4,128,128]{3,2,1,0:T(8,128)(2,1)S(1)}, bf16[2,4,128,128]{3,2,1,0:T(8,128)(2,1)S(1)}, u32[]{:S(2)}, u32[]{:S(2)}) collective-permute-start(bf16[2,4,128,128]{3,2,1,0:T(8,128)(2,1)S(1)} %copy-done.19), channel_id=1, source_target_pairs={{0,6},{1,7},{2,0},{3,1},{4,2},{5,3},{6,4},{7,5},{8,14},{9,15},{10,... | collective-permute-start | bytes 786440 | tf_op jit(solution)/shard_map/ppermute | solution.py:118
  40.8 7.7 %collective-permute-done.2 = bf16[2,4,128,128]{3,2,1,0:T(8,128)(2,1)S(1)} collective-permute-done((bf16[2,4,128,128]{3,2,1,0:T(8,128)(2,1)}, bf16[2,4,128,128]{3,2,1,0:T(8,128)(2,1)S(1)}, u32[]{:S(2)}, u32[]{:S(2)}) %collective-permute-start.2) | collective-permute-done | bytes 262176 | tf_op jit(solution)/shard_map/ppermute | solution.py:118
  50.1 3.2 %collective-permute-done.6 = bf16[2,4,128,128]{3,2,1,0:T(8,128)(2,1)S(1)} collective-permute-done((bf16[2,4,128,128]{3,2,1,0:T(8,128)(2,1)}, bf16[2,4,128,128]{3,2,1,0:T(8,128)(2,1)S(1)}, u32[]{:S(2)}, u32[]{:S(2)}) %collective-permute-start.6) | collective-permute-done | bytes 262176 | tf_op jit(solution)/shard_map/ppermute | solution.py:118
  57.4 2.2 %fusion.61 = (f32[4,8,128]{2,1,0:T(8,128)S(1)}, f32[4,8,128,256]{3,2,1,0:T(8,128)S(1)}) fusion(f32[4,8,128,256]{3,2,1,0:T(8,128)S(1)} %fusion.3, pred[8,128,256]{2,1,0:T(8,128)(4,1)S(1)} %copy-done.20), kind=kOutput, calls=%fused_computation.237 | output fusion | flops 6291711 | bytes 8667136 | tf_op jit(solution)/shard_map/sub | solution.py:53
  63.3 5.6 %collective-permute-start.11 = (bf16[4,8,128,128]{3,2,1,0:T(8,128)(2,1)S(1)}, bf16[4,8,128,128]{3,2,1,0:T(8,128)(2,1)S(1)}, u32[]{:S(2)}, u32[]{:S(2)}) collective-permute-start(bf16[4,8,128,128]{3,2,1,0:T(8,128)(2,1)S(1)} %add_convert_fusion.3), channel_id=1, source_target_pairs={{24,16},{25,17},{26,18},{27,19},{28,20},{29,21},{30,22},{31,23}} | collective-permute-start | bytes 3145736 | tf_op jit(solution)/shard_map/ppermute | solution.py:191
  68.9 2.2 %collective-permute-done.11 = bf16[4,8,128,128]{3,2,1,0:T(8,128)(2,1)S(1)} collective-permute-done((bf16[4,8,128,128]{3,2,1,0:T(8,128)(2,1)S(1)}, bf16[4,8,128,128]{3,2,1,0:T(8,128)(2,1)S(1)}, u32[]{:S(2)}, u32[]{:S(2)}) %collective-permute-start.11) | collective-permute-done | bytes 1048608 | tf_op jit(solution)/shard_map/ppermute | solution.py:191
  73.8 1.6 collective-permute-start.12
  76.2 6.7 %collective-permute-start.14 = (bf16[4,128,128]{2,1,0:T(8,128)(2,1)}, bf16[4,128,128]{2,1,0:T(8,128)(2,1)}, u32[]{:S(2)}, u32[]{:S(2)}) collective-permute-start(bf16[4,128,128]{2,1,0:T(8,128)(2,1)} %get-tuple-element.96), channel_id=1, source_target_pairs={{24,25},{25,26},{26,27},{27,28},{28,29},{29,30},{30,31},{31,24}} | collective-permute-start | bytes 393224 | tf_op jit(solution)/shard_map/ppermute | solution.py:123
  82.9 7.9 %collective-permute-start.15 = (bf16[4,128,128]{2,1,0:T(8,128)(2,1)}, bf16[4,128,128]{2,1,0:T(8,128)(2,1)}, u32[]{:S(2)}, u32[]{:S(2)}) collective-permute-start(bf16[4,128,128]{2,1,0:T(8,128)(2,1)} %get-tuple-element.95), channel_id=1, source_target_pairs={{24,26},{25,27},{26,28},{27,29},{28,30},{29,31},{30,24},{31,25}} | collective-permute-start | bytes 393224 | tf_op jit(solution)/shard_map/ppermute | solution.py:123
  90.8 1.9 %collective-permute-start.16 = (bf16[4,128,128]{2,1,0:T(8,128)(2,1)}, bf16[4,128,128]{2,1,0:T(8,128)(2,1)}, u32[]{:S(2)}, u32[]{:S(2)}) collective-permute-start(bf16[4,128,128]{2,1,0:T(8,128)(2,1)} %get-tuple-element.94), channel_id=1, source_target_pairs={{24,27},{25,28},{26,29},{27,30},{28,31},{29,24},{30,25},{31,26}} | collective-permute-start | bytes 393224 | tf_op jit(solution)/shard_map/ppermute | solution.py:123
  92.7 4.4 %collective-permute-start.17 = (bf16[4,128,128]{2,1,0:T(8,128)(2,1)}, bf16[4,128,128]{2,1,0:T(8,128)(2,1)}, u32[]{:S(2)}, u32[]{:S(2)}) collective-permute-start(bf16[4,128,128]{2,1,0:T(8,128)(2,1)} %get-tuple-element.93), channel_id=1, source_target_pairs={{24,28},{25,29},{26,30},{27,31},{28,24},{29,25},{30,26},{31,27}} | collective-permute-start | bytes 393224 | tf_op jit(solution)/shard_map/ppermute | solution.py:123
  100.1 5.0 %collective-permute-start.18 = (bf16[4,128,128]{2,1,0:T(8,128)(2,1)S(1)}, bf16[4,128,128]{2,1,0:T(8,128)(2,1)S(1)}, u32[]{:S(2)}, u32[]{:S(2)}) collective-permute-start(bf16[4,128,128]{2,1,0:T(8,128)(2,1)S(1)} %get-tuple-element.92), channel_id=1, source_target_pairs={{24,29},{25,30},{26,31},{27,24},{28,25},{29,26},{30,27},{31,28}} | collective-permute-start | bytes 393224 | tf_op jit(solution)/shard_map/ppermute | solution.py:123
  105.1 1.6 constant_dynamic-update-slice_fusion.6
  106.7 1.9 %collective-permute-start.19 = (bf16[4,128,128]{2,1,0:T(8,128)(2,1)S(1)}, bf16[4,128,128]{2,1,0:T(8,128)(2,1)S(1)}, u32[]{:S(2)}, u32[]{:S(2)}) collective-permute-start(bf16[4,128,128]{2,1,0:T(8,128)(2,1)S(1)} %get-tuple-element.91), channel_id=1, source_target_pairs={{24,30},{25,31},{26,24},{27,25},{28,26},{29,27},{30,28},{31,29}} | collective-permute-start | bytes 393224 | tf_op jit(solution)/shard_map/ppermute | solution.py:123
  108.6 1.6 constant_dynamic-update-slice_fusion.5
  110.2 3.3 %collective-permute-start.20 = (bf16[4,128,128]{2,1,0:T(8,128)(2,1)S(1)}, bf16[4,128,128]{2,1,0:T(8,128)(2,1)S(1)}, u32[]{:S(2)}, u32[]{:S(2)}) collective-permute-start(bf16[4,128,128]{2,1,0:T(8,128)(2,1)S(1)} %get-tuple-element.90), channel_id=1, source_target_pairs={{24,31},{25,24},{26,25},{27,26},{28,27},{29,28},{30,29},{31,30}} | collective-permute-start | bytes 393224 | tf_op jit(solution)/shard_map/ppermute | solution.py:123
  113.5 2.0 %fusion.64 = f32[4,8,256,128]{3,2,1,0:T(8,128)S(1)} fusion(bf16[4,8,128,256]{3,2,1,0:T(8,128)(2,1)S(1)} %fusion.8, bf16[4,8,128,128]{3,2,1,0:T(8,128)(2,1)} %collective-permute-done.12), kind=kOutput, calls=%fused_computation.240 | convolution fusion | flops 268435456 | bytes 7340032 | tf_op jit(solution)/shard_map/hbij,hbid->hbjd/dot_general | solution.py:58
  116.1 1.7 add_convert_fusion.1
  118.5 1.6 constant_dynamic-update-slice_fusion.4
  120.1 1.6 constant_dynamic-update-slice_fusion.3
  130.7 1.5 multiply_convert_fusion
  138.2 1.9 %collective-permute-start.22 = (bf16[2,4,128,128]{3,2,1,0:T(8,128)(2,1)S(1)}, bf16[2,4,128,128]{3,2,1,0:T(8,128)(2,1)S(1)}, u32[]{:S(2)}, u32[]{:S(2)}) collective-permute-start(bf16[2,4,128,128]{3,2,1,0:T(8,128)(2,1)S(1)} %get-tuple-element.73), channel_id=1, source_target_pairs={{0,2},{1,3},{2,4},{3,5},{4,6},{5,7},{6,0},{7,1},{8,10},{9,11},{10,... | collective-permute-start | bytes 786440 | tf_op jit(solution)/shard_map/ppermute | solution.py:118
  141.1 5.1 %collective-permute-done.21 = bf16[2,4,128,128]{3,2,1,0:T(8,128)(2,1)S(1)} collective-permute-done((bf16[2,4,128,128]{3,2,1,0:T(8,128)(2,1)S(1)}, bf16[2,4,128,128]{3,2,1,0:T(8,128)(2,1)S(1)}, u32[]{:S(2)}, u32[]{:S(2)}) %collective-permute-start.21) | collective-permute-done | bytes 262176 | tf_op jit(solution)/shard_map/ppermute | solution.py:118
  146.2 7.1 %collective-permute-start.24 = (bf16[2,4,128,128]{3,2,1,0:T(8,128)(2,1)S(1)}, bf16[2,4,128,128]{3,2,1,0:T(8,128)(2,1)S(1)}, u32[]{:S(2)}, u32[]{:S(2)}) collective-permute-start(bf16[2,4,128,128]{3,2,1,0:T(8,128)(2,1)S(1)} %get-tuple-element.75), channel_id=1, source_target_pairs={{0,4},{1,5},{2,6},{3,7},{4,0},{5,1},{6,2},{7,3},{8,12},{9,13},{10,... | collective-permute-start | bytes 786440 | tf_op jit(solution)/shard_map/ppermute | solution.py:118
  154.0 13.6 %collective-permute-start.27 = (bf16[2,4,128,128]{3,2,1,0:T(8,128)(2,1)S(1)}, bf16[2,4,128,128]{3,2,1,0:T(8,128)(2,1)S(1)}, u32[]{:S(2)}, u32[]{:S(2)}) collective-permute-start(bf16[2,4,128,128]{3,2,1,0:T(8,128)(2,1)S(1)} %get-tuple-element.70), channel_id=1, source_target_pairs={{0,7},{1,0},{2,1},{3,2},{4,3},{5,4},{6,5},{7,6},{8,15},{9,8},{10,9... | collective-permute-start | bytes 786440 | tf_op jit(solution)/shard_map/ppermute | solution.py:118
  168.1 3.1 %collective-permute-start.30 = (bf16[128,128]{1,0:T(8,128)(2,1)S(1)}, bf16[128,128]{1,0:T(8,128)(2,1)S(1)}, u32[]{:S(2)}, u32[]{:S(2)}) collective-permute-start(bf16[128,128]{1,0:T(8,128)(2,1)S(1)} %get-tuple-element.101), channel_id=1, source_target_pairs={{0,4},{1,5},{2,6},{3,7},{4,0},{5,1},{6,2},{7,3},{8,12},{9,13},{10,... | collective-permute-start | bytes 98312 | tf_op jit(solution)/shard_map/ppermute | solution.py:230
  171.5 3.7 %collective-permute-start.31 = (bf16[128,128]{1,0:T(8,128)(2,1)S(1)}, bf16[128,128]{1,0:T(8,128)(2,1)S(1)}, u32[]{:S(2)}, u32[]{:S(2)}) collective-permute-start(bf16[128,128]{1,0:T(8,128)(2,1)S(1)} %get-tuple-element.100), channel_id=1, source_target_pairs={{0,6},{1,7},{2,0},{3,1},{4,2},{5,3},{6,4},{7,5},{8,14},{9,15},{10,... | collective-permute-start | bytes 98312 | tf_op jit(solution)/shard_map/ppermute | solution.py:230
  (193 shorter events, 59.3 us)
Async XLA Ops:
  2.8 19.1 %collective-permute-start.8 = (bf16[128,128]{1,0:T(8,128)(2,1)}, bf16[128,128]{1,0:T(8,128)(2,1)S(1)}, u32[]{:S(2)}, u32[]{:S(2)}) collective-permute-start(bf16[128,128]{1,0:T(8,128)(2,1)} %bitcast.10), channel_id=1, source_target_pairs={{0,4},{1,5},{2,6},{3,7},{4,0},{5,1},{6,2},{7,3},{8,12},{9,13},{10,... | collective-permute-start | bytes 98312 | tf_op jit(solution)/shard_map/ppermute | solution.py:157
  5.8 18.0 %collective-permute-start.9 = (bf16[128,128]{1,0:T(8,128)(2,1)}, bf16[128,128]{1,0:T(8,128)(2,1)S(1)}, u32[]{:S(2)}, u32[]{:S(2)}) collective-permute-start(bf16[128,128]{1,0:T(8,128)(2,1)} %bitcast.12), channel_id=1, source_target_pairs={{0,6},{1,7},{2,0},{3,1},{4,2},{5,3},{6,4},{7,5},{8,14},{9,15},{10,... | collective-permute-start | bytes 98312 | tf_op jit(solution)/shard_map/ppermute | solution.py:157
  7.6 17.6 %collective-permute-start.7 = (bf16[128,128]{1,0:T(8,128)(2,1)}, bf16[128,128]{1,0:T(8,128)(2,1)S(1)}, u32[]{:S(2)}, u32[]{:S(2)}) collective-permute-start(bf16[128,128]{1,0:T(8,128)(2,1)} %bitcast.8), channel_id=1, source_target_pairs={{0,2},{1,3},{2,4},{3,5},{4,6},{5,7},{6,0},{7,1},{8,10},{9,11},{10,... | collective-permute-start | bytes 98312 | tf_op jit(solution)/shard_map/ppermute | solution.py:157
  14.9 19.3 %collective-permute-start = (bf16[2,4,128,128]{3,2,1,0:T(8,128)(2,1)}, bf16[2,4,128,128]{3,2,1,0:T(8,128)(2,1)}, u32[]{:S(2)}, u32[]{:S(2)}) collective-permute-start(bf16[2,4,128,128]{3,2,1,0:T(8,128)(2,1)} %get-tuple-element.82), channel_id=1, source_target_pairs={{0,1},{1,2},{2,3},{3,4},{4,5},{5,6},{6,7},{7,0},{8,9},{9,10},{10,1... | collective-permute-start | bytes 786440 | tf_op jit(solution)/shard_map/ppermute | solution.py:118
  16.1 23.6 %collective-permute-start.1 = (bf16[2,4,128,128]{3,2,1,0:T(8,128)(2,1)}, bf16[2,4,128,128]{3,2,1,0:T(8,128)(2,1)}, u32[]{:S(2)}, u32[]{:S(2)}) collective-permute-start(bf16[2,4,128,128]{3,2,1,0:T(8,128)(2,1)} %get-tuple-element.83), channel_id=1, source_target_pairs={{0,2},{1,3},{2,4},{3,5},{4,6},{5,7},{6,0},{7,1},{8,10},{9,11},{10,... | collective-permute-start | bytes 786440 | tf_op jit(solution)/shard_map/ppermute | solution.py:118
  21.9 26.6 %collective-permute-start.2 = (bf16[2,4,128,128]{3,2,1,0:T(8,128)(2,1)}, bf16[2,4,128,128]{3,2,1,0:T(8,128)(2,1)S(1)}, u32[]{:S(2)}, u32[]{:S(2)}) collective-permute-start(bf16[2,4,128,128]{3,2,1,0:T(8,128)(2,1)} %get-tuple-element.84), channel_id=1, source_target_pairs={{0,3},{1,4},{2,5},{3,6},{4,7},{5,0},{6,1},{7,2},{8,11},{9,12},{10,... | collective-permute-start | bytes 786440 | tf_op jit(solution)/shard_map/ppermute | solution.py:118
  23.8 25.2 %collective-permute-start.3 = (bf16[2,4,128,128]{3,2,1,0:T(8,128)(2,1)}, bf16[2,4,128,128]{3,2,1,0:T(8,128)(2,1)S(1)}, u32[]{:S(2)}, u32[]{:S(2)}) collective-permute-start(bf16[2,4,128,128]{3,2,1,0:T(8,128)(2,1)} %get-tuple-element.86), channel_id=1, source_target_pairs={{0,4},{1,5},{2,6},{3,7},{4,0},{5,1},{6,2},{7,3},{8,12},{9,13},{10,... | collective-permute-start | bytes 786440 | tf_op jit(solution)/shard_map/ppermute | solution.py:118
  25.2 8.2 %collective-permute-start.10 = (bf16[4,128,128]{2,1,0:T(8,128)(2,1)S(1)}, bf16[4,128,128]{2,1,0:T(8,128)(2,1)S(1)}, u32[]{:S(2)}, u32[]{:S(2)}) collective-permute-start(bf16[4,128,128]{2,1,0:T(8,128)(2,1)S(1)} %pad_maximum_fusion.11), channel_id=1, source_target_pairs={{0,1},{1,0},{2,3},{3,2},{4,5},{5,4},{6,7},{7,6},{8,9},{9,8},{10,11... | collective-permute-start | bytes 393224 | tf_op jit(solution)/shard_map/ppermute | solution.py:162
  33.4 15.7 %collective-permute-start.4 = (bf16[2,4,128,128]{3,2,1,0:T(8,128)(2,1)}, bf16[2,4,128,128]{3,2,1,0:T(8,128)(2,1)}, u32[]{:S(2)}, u32[]{:S(2)}) collective-permute-start(bf16[2,4,128,128]{3,2,1,0:T(8,128)(2,1)} %get-tuple-element.87), channel_id=1, source_target_pairs={{0,5},{1,6},{2,7},{3,0},{4,1},{5,2},{6,3},{7,4},{8,13},{9,14},{10,... | collective-permute-start | bytes 786440 | tf_op jit(solution)/shard_map/ppermute | solution.py:118
  34.2 15.9 %collective-permute-start.5 = (bf16[2,4,128,128]{3,2,1,0:T(8,128)(2,1)S(1)}, bf16[2,4,128,128]{3,2,1,0:T(8,128)(2,1)S(1)}, u32[]{:S(2)}, u32[]{:S(2)}) collective-permute-start(bf16[2,4,128,128]{3,2,1,0:T(8,128)(2,1)S(1)} %copy-done.19), channel_id=1, source_target_pairs={{0,6},{1,7},{2,0},{3,1},{4,2},{5,3},{6,4},{7,5},{8,14},{9,15},{10,... | collective-permute-start | bytes 786440 | tf_op jit(solution)/shard_map/ppermute | solution.py:118
  39.8 13.6 %collective-permute-start.6 = (bf16[2,4,128,128]{3,2,1,0:T(8,128)(2,1)}, bf16[2,4,128,128]{3,2,1,0:T(8,128)(2,1)S(1)}, u32[]{:S(2)}, u32[]{:S(2)}) collective-permute-start(bf16[2,4,128,128]{3,2,1,0:T(8,128)(2,1)} %get-tuple-element.80), channel_id=1, source_target_pairs={{0,7},{1,0},{2,1},{3,2},{4,3},{5,4},{6,5},{7,6},{8,15},{9,8},{10,9... | collective-permute-start | bytes 786440 | tf_op jit(solution)/shard_map/ppermute | solution.py:118
  63.3 7.8 %collective-permute-start.11 = (bf16[4,8,128,128]{3,2,1,0:T(8,128)(2,1)S(1)}, bf16[4,8,128,128]{3,2,1,0:T(8,128)(2,1)S(1)}, u32[]{:S(2)}, u32[]{:S(2)}) collective-permute-start(bf16[4,8,128,128]{3,2,1,0:T(8,128)(2,1)S(1)} %add_convert_fusion.3), channel_id=1, source_target_pairs={{24,16},{25,17},{26,18},{27,19},{28,20},{29,21},{30,22},{31,23}} | collective-permute-start | bytes 3145736 | tf_op jit(solution)/shard_map/ppermute | solution.py:191
  73.8 36.5 %collective-permute-start.12 = (bf16[4,8,128,128]{3,2,1,0:T(8,128)(2,1)}, bf16[4,8,128,128]{3,2,1,0:T(8,128)(2,1)}, u32[]{:S(2)}, u32[]{:S(2)}) collective-permute-start(bf16[4,8,128,128]{3,2,1,0:T(8,128)(2,1)} %add_convert_fusion.2), channel_id=1, source_target_pairs={{16,8},{17,9},{18,10},{19,11},{20,12},{21,13},{22,14},{23,15}} | collective-permute-start | bytes 3145736 | tf_op jit(solution)/shard_map/ppermute | solution.py:191
  76.2 23.9 %collective-permute-start.14 = (bf16[4,128,128]{2,1,0:T(8,128)(2,1)}, bf16[4,128,128]{2,1,0:T(8,128)(2,1)}, u32[]{:S(2)}, u32[]{:S(2)}) collective-permute-start(bf16[4,128,128]{2,1,0:T(8,128)(2,1)} %get-tuple-element.96), channel_id=1, source_target_pairs={{24,25},{25,26},{26,27},{27,28},{28,29},{29,30},{30,31},{31,24}} | collective-permute-start | bytes 393224 | tf_op jit(solution)/shard_map/ppermute | solution.py:123
  82.9 23.8 %collective-permute-start.15 = (bf16[4,128,128]{2,1,0:T(8,128)(2,1)}, bf16[4,128,128]{2,1,0:T(8,128)(2,1)}, u32[]{:S(2)}, u32[]{:S(2)}) collective-permute-start(bf16[4,128,128]{2,1,0:T(8,128)(2,1)} %get-tuple-element.95), channel_id=1, source_target_pairs={{24,26},{25,27},{26,28},{27,29},{28,30},{29,31},{30,24},{31,25}} | collective-permute-start | bytes 393224 | tf_op jit(solution)/shard_map/ppermute | solution.py:123
  90.8 27.0 %collective-permute-start.16 = (bf16[4,128,128]{2,1,0:T(8,128)(2,1)}, bf16[4,128,128]{2,1,0:T(8,128)(2,1)}, u32[]{:S(2)}, u32[]{:S(2)}) collective-permute-start(bf16[4,128,128]{2,1,0:T(8,128)(2,1)} %get-tuple-element.94), channel_id=1, source_target_pairs={{24,27},{25,28},{26,29},{27,30},{28,31},{29,24},{30,25},{31,26}} | collective-permute-start | bytes 393224 | tf_op jit(solution)/shard_map/ppermute | solution.py:123
  92.7 27.4 %collective-permute-start.17 = (bf16[4,128,128]{2,1,0:T(8,128)(2,1)}, bf16[4,128,128]{2,1,0:T(8,128)(2,1)}, u32[]{:S(2)}, u32[]{:S(2)}) collective-permute-start(bf16[4,128,128]{2,1,0:T(8,128)(2,1)} %get-tuple-element.93), channel_id=1, source_target_pairs={{24,28},{25,29},{26,30},{27,31},{28,24},{29,25},{30,26},{31,27}} | collective-permute-start | bytes 393224 | tf_op jit(solution)/shard_map/ppermute | solution.py:123
  100.1 21.6 %collective-permute-start.18 = (bf16[4,128,128]{2,1,0:T(8,128)(2,1)S(1)}, bf16[4,128,128]{2,1,0:T(8,128)(2,1)S(1)}, u32[]{:S(2)}, u32[]{:S(2)}) collective-permute-start(bf16[4,128,128]{2,1,0:T(8,128)(2,1)S(1)} %get-tuple-element.92), channel_id=1, source_target_pairs={{24,29},{25,30},{26,31},{27,24},{28,25},{29,26},{30,27},{31,28}} | collective-permute-start | bytes 393224 | tf_op jit(solution)/shard_map/ppermute | solution.py:123
  106.7 15.7 %collective-permute-start.19 = (bf16[4,128,128]{2,1,0:T(8,128)(2,1)S(1)}, bf16[4,128,128]{2,1,0:T(8,128)(2,1)S(1)}, u32[]{:S(2)}, u32[]{:S(2)}) collective-permute-start(bf16[4,128,128]{2,1,0:T(8,128)(2,1)S(1)} %get-tuple-element.91), channel_id=1, source_target_pairs={{24,30},{25,31},{26,24},{27,25},{28,26},{29,27},{30,28},{31,29}} | collective-permute-start | bytes 393224 | tf_op jit(solution)/shard_map/ppermute | solution.py:123
  110.2 12.8 %collective-permute-start.20 = (bf16[4,128,128]{2,1,0:T(8,128)(2,1)S(1)}, bf16[4,128,128]{2,1,0:T(8,128)(2,1)S(1)}, u32[]{:S(2)}, u32[]{:S(2)}) collective-permute-start(bf16[4,128,128]{2,1,0:T(8,128)(2,1)S(1)} %get-tuple-element.90), channel_id=1, source_target_pairs={{24,31},{25,24},{26,25},{27,26},{28,27},{29,28},{30,29},{31,30}} | collective-permute-start | bytes 393224 | tf_op jit(solution)/shard_map/ppermute | solution.py:123
  117.8 7.3 %collective-permute-start.13 = (bf16[4,8,128,128]{3,2,1,0:T(8,128)(2,1)S(1)}, bf16[4,8,128,128]{3,2,1,0:T(8,128)(2,1)S(1)}, u32[]{:S(2)}, u32[]{:S(2)}) collective-permute-start(bf16[4,8,128,128]{3,2,1,0:T(8,128)(2,1)S(1)} %add_convert_fusion.1), channel_id=1, source_target_pairs={{8,0},{9,1},{10,2},{11,3},{12,4},{13,5},{14,6},{15,7}} | collective-permute-start | bytes 3145736 | tf_op jit(solution)/shard_map/ppermute | solution.py:191
  135.4 10.8 %collective-permute-start.21 = (bf16[2,4,128,128]{3,2,1,0:T(8,128)(2,1)S(1)}, bf16[2,4,128,128]{3,2,1,0:T(8,128)(2,1)S(1)}, u32[]{:S(2)}, u32[]{:S(2)}) collective-permute-start(bf16[2,4,128,128]{3,2,1,0:T(8,128)(2,1)S(1)} %get-tuple-element.72), channel_id=1, source_target_pairs={{0,1},{1,2},{2,3},{3,4},{4,5},{5,6},{6,7},{7,0},{8,9},{9,10},{10,1... | collective-permute-start | bytes 786440 | tf_op jit(solution)/shard_map/ppermute | solution.py:118
  135.7 18.3 %collective-permute-start.28 = (f32[4,128,128]{2,1,0:T(8,128)S(1)}, f32[4,128,128]{2,1,0:T(8,128)S(1)}, u32[]{:S(2)}, u32[]{:S(2)}) collective-permute-start(f32[4,128,128]{2,1,0:T(8,128)S(1)} %dynamic-slice_bitcast_fusion), channel_id=1, source_target_pairs={{0,1},{1,0},{2,3},{3,2},{4,5},{5,4},{6,7},{7,6},{8,9},{9,8},{10,11... | collective-permute-start | bytes 786440 | tf_op jit(solution)/shard_map/ppermute | solution.py:223
  137.0 34.5 %collective-permute-start.25 = (bf16[2,4,128,128]{3,2,1,0:T(8,128)(2,1)S(1)}, bf16[2,4,128,128]{3,2,1,0:T(8,128)(2,1)S(1)}, u32[]{:S(2)}, u32[]{:S(2)}) collective-permute-start(bf16[2,4,128,128]{3,2,1,0:T(8,128)(2,1)S(1)} %get-tuple-element.77), channel_id=1, source_target_pairs={{0,5},{1,6},{2,7},{3,0},{4,1},{5,2},{6,3},{7,4},{8,13},{9,14},{10,... | collective-permute-start | bytes 786440 | tf_op jit(solution)/shard_map/ppermute | solution.py:118
  138.2 15.4 %collective-permute-start.22 = (bf16[2,4,128,128]{3,2,1,0:T(8,128)(2,1)S(1)}, bf16[2,4,128,128]{3,2,1,0:T(8,128)(2,1)S(1)}, u32[]{:S(2)}, u32[]{:S(2)}) collective-permute-start(bf16[2,4,128,128]{3,2,1,0:T(8,128)(2,1)S(1)} %get-tuple-element.73), channel_id=1, source_target_pairs={{0,2},{1,3},{2,4},{3,5},{4,6},{5,7},{6,0},{7,1},{8,10},{9,11},{10,... | collective-permute-start | bytes 786440 | tf_op jit(solution)/shard_map/ppermute | solution.py:118
  140.1 27.6 %collective-permute-start.23 = (bf16[2,4,128,128]{3,2,1,0:T(8,128)(2,1)S(1)}, bf16[2,4,128,128]{3,2,1,0:T(8,128)(2,1)S(1)}, u32[]{:S(2)}, u32[]{:S(2)}) collective-permute-start(bf16[2,4,128,128]{3,2,1,0:T(8,128)(2,1)S(1)} %get-tuple-element.74), channel_id=1, source_target_pairs={{0,3},{1,4},{2,5},{3,6},{4,7},{5,0},{6,1},{7,2},{8,11},{9,12},{10,... | collective-permute-start | bytes 786440 | tf_op jit(solution)/shard_map/ppermute | solution.py:118
  146.2 21.8 %collective-permute-start.24 = (bf16[2,4,128,128]{3,2,1,0:T(8,128)(2,1)S(1)}, bf16[2,4,128,128]{3,2,1,0:T(8,128)(2,1)S(1)}, u32[]{:S(2)}, u32[]{:S(2)}) collective-permute-start(bf16[2,4,128,128]{3,2,1,0:T(8,128)(2,1)S(1)} %get-tuple-element.75), channel_id=1, source_target_pairs={{0,4},{1,5},{2,6},{3,7},{4,0},{5,1},{6,2},{7,3},{8,12},{9,13},{10,... | collective-permute-start | bytes 786440 | tf_op jit(solution)/shard_map/ppermute | solution.py:118
  153.6 21.9 %collective-permute-start.26 = (bf16[2,4,128,128]{3,2,1,0:T(8,128)(2,1)S(1)}, bf16[2,4,128,128]{3,2,1,0:T(8,128)(2,1)S(1)}, u32[]{:S(2)}, u32[]{:S(2)}) collective-permute-start(bf16[2,4,128,128]{3,2,1,0:T(8,128)(2,1)S(1)} %get-tuple-element.76), channel_id=1, source_target_pairs={{0,6},{1,7},{2,0},{3,1},{4,2},{5,3},{6,4},{7,5},{8,14},{9,15},{10,... | collective-permute-start | bytes 786440 | tf_op jit(solution)/shard_map/ppermute | solution.py:118
  154.0 21.8 %collective-permute-start.27 = (bf16[2,4,128,128]{3,2,1,0:T(8,128)(2,1)S(1)}, bf16[2,4,128,128]{3,2,1,0:T(8,128)(2,1)S(1)}, u32[]{:S(2)}, u32[]{:S(2)}) collective-permute-start(bf16[2,4,128,128]{3,2,1,0:T(8,128)(2,1)S(1)} %get-tuple-element.70), channel_id=1, source_target_pairs={{0,7},{1,0},{2,1},{3,2},{4,3},{5,4},{6,5},{7,6},{8,15},{9,8},{10,9... | collective-permute-start | bytes 786440 | tf_op jit(solution)/shard_map/ppermute | solution.py:118
  167.7 11.4 %collective-permute-start.29 = (bf16[128,128]{1,0:T(8,128)(2,1)S(1)}, bf16[128,128]{1,0:T(8,128)(2,1)S(1)}, u32[]{:S(2)}, u32[]{:S(2)}) collective-permute-start(bf16[128,128]{1,0:T(8,128)(2,1)S(1)} %get-tuple-element.102), channel_id=1, source_target_pairs={{0,2},{1,3},{2,4},{3,5},{4,6},{5,7},{6,0},{7,1},{8,10},{9,11},{10,... | collective-permute-start | bytes 98312 | tf_op jit(solution)/shard_map/ppermute | solution.py:230
  168.1 11.0 %collective-permute-start.30 = (bf16[128,128]{1,0:T(8,128)(2,1)S(1)}, bf16[128,128]{1,0:T(8,128)(2,1)S(1)}, u32[]{:S(2)}, u32[]{:S(2)}) collective-permute-start(bf16[128,128]{1,0:T(8,128)(2,1)S(1)} %get-tuple-element.101), channel_id=1, source_target_pairs={{0,4},{1,5},{2,6},{3,7},{4,0},{5,1},{6,2},{7,3},{8,12},{9,13},{10,... | collective-permute-start | bytes 98312 | tf_op jit(solution)/shard_map/ppermute | solution.py:230
  171.5 7.6 %collective-permute-start.31 = (bf16[128,128]{1,0:T(8,128)(2,1)S(1)}, bf16[128,128]{1,0:T(8,128)(2,1)S(1)}, u32[]{:S(2)}, u32[]{:S(2)}) collective-permute-start(bf16[128,128]{1,0:T(8,128)(2,1)S(1)} %get-tuple-element.100), channel_id=1, source_target_pairs={{0,6},{1,7},{2,0},{3,1},{4,2},{5,3},{6,4},{7,5},{8,14},{9,15},{10,... | collective-permute-start | bytes 98312 | tf_op jit(solution)/shard_map/ppermute | solution.py:230
  (25 other events, 85.7 us)

commit v16 on v15

--- a/solution.py
+++ b/solution.py
@@ -208,9 +208,11 @@
         score_scale,
         BLK,
     )
-    pair = jnp.stack([grad_query, held_out]).reshape(2, local_heads, seq_len, DH)
-    pair_out = transpose_seq(pair, 2, 1)
-    pair_rows = jnp.transpose(pair_out, (0, 2, 1, 3)).reshape(2, tok_rows, full_width)
+    pair = jnp.transpose(
+        jnp.stack([grad_query, held_out]).reshape(2, local_heads, seq_len, DH), (0, 2, 1, 3)
+    )
+    pair_out = transpose_seq(pair, 1, 2)
+    pair_rows = pair_out.reshape(2, tok_rows, full_width)
     if local_heads == 1:
         key_part = grad_key.reshape(seq_len, DH)
     else:

time: 182 us -> 180 us (0.989)
  the two profiles are of different devices: /device:TPU:3 before, /device:TPU:15 now
where the time goes in v16:
time: 180 us; the launch traced here: 178 us
  waiting for transfers between devices  61.5 us (34%)
  starting transfers between devices  48.4 us (27%)
  local copies, waits for them, and re-layouts  39.3 us (22%)
  other arithmetic  18 us (10%)
  matrix products  8.84 us (5%)
    ppermute x14, waiting for transfers between devices, transpose_seq(): lax.ppermute(chunk, 'seq', [(s, (s + shift) % seq_ways) for s in range(se...  50 us
    ppermute x7, starting transfers between devices, transpose_seq(): lax.ppermute(chunk, ('pipe', 'seq'), [(base + s, base + (s + shift) % seq...  22 us
    dynamic_update_slice x23, local copies, waits for them, and re-layouts, transpose_seq(): lax.dynamic_update_slice_in_dim(result, chunk, source * concat_size, axis...  14.5 us
    unnamed x58, local copies, waits for them, and re-layouts  11.9 us
    ppermute x14, starting transfers between devices, transpose_seq(): lax.ppermute(chunk, 'seq', [(s, (s + shift) % seq_ways) for s in range(se...  11.5 us
    ppermute x1, waiting for transfers between devices, on_device(): theirs = lax.ppermute(mine, 'seq', [(d, d ^ 1) for d in range(seq_ways)])  9.32 us
    ppermute x6, starting transfers between devices, on_device(): lax.ppermute(chunk, 'seq', [(d, (d + shift) % seq_ways) for d in range(se...  8.13 us
    ppermute x3, starting transfers between devices, on_device(): grad_in = lax.ppermute(new_grad, 'pipe', [(sender, sender - 1)])  4.83 us
  transfers between devices with their start and end apart: 32, of which 10 were waited for; matrix products, arithmetic and copies ran while one was open for 22% of the time, Pallas kernels for 0%

profile of v16, /device:TPU:15, one launch (start us, length us, event | category | flops | bytes accessed | tf_op | source)
XLA Modules:
  0.0 177.8 jit_solution(4793662994009040325)
XLA Ops:
  2.8 2.3 %collective-permute-start.8 = (bf16[128,128]{1,0:T(8,128)(2,1)}, bf16[128,128]{1,0:T(8,128)(2,1)S(1)}, u32[]{:S(2)}, u32[]{:S(2)}) collective-permute-start(bf16[128,128]{1,0:T(8,128)(2,1)} %bitcast.10), channel_id=1, source_target_pairs={{0,4},{1,5},{2,6},{3,7},{4,0},{5,1},{6,2},{7,3},{8,12},{9,13},{10,... | collective-permute-start | bytes 98312 | tf_op jit(solution)/shard_map/ppermute | solution.py:157
  11.1 1.6 fusion.68
  14.9 2.1 %collective-permute-start.1 = (bf16[2,4,128,128]{3,2,1,0:T(8,128)(2,1)}, bf16[2,4,128,128]{3,2,1,0:T(8,128)(2,1)}, u32[]{:S(2)}, u32[]{:S(2)}) collective-permute-start(bf16[2,4,128,128]{3,2,1,0:T(8,128)(2,1)} %get-tuple-element.83), channel_id=1, source_target_pairs={{0,2},{1,3},{2,4},{3,5},{4,6},{5,7},{6,0},{7,1},{8,10},{9,11},{10,... | collective-permute-start | bytes 786440 | tf_op jit(solution)/shard_map/ppermute | solution.py:118
  18.3 1.9 %fusion.34 = (bf16[2,4,128,128]{3,2,1,0:T(8,128)(2,1)}, bf16[2,4,128,128]{3,2,1,0:T(8,128)(2,1)}, bf16[2,4,128,128]{3,2,1,0:T(8,128)(2,1)}) fusion(s32[]{:T(128)S(6)} %select_n.533, bf16[1,32,128,128]{3,2,1,0:T(8,128)(2,1)} %bitcast.137, bf16[1,32,128,128]{3,2,1,0:T(8,128)(2,1)S(1)} %get-tuple-element.96, s32[]{:T(128)S(6)} %select_n.529, s32[]{:T(128)S(6)} %select_n.531), kind=kLoop, calls=%fused_computation.97 | loop fusion | flops 393216 | bytes 2883596 | tf_op jit(solution)/shard_map/stack | solution.py:142
  24.3 9.3 %collective-permute-done.10 = bf16[4,128,128]{2,1,0:T(8,128)(2,1)S(1)} collective-permute-done((bf16[4,128,128]{2,1,0:T(8,128)(2,1)S(1)}, bf16[4,128,128]{2,1,0:T(8,128)(2,1)S(1)}, u32[]{:S(2)}, u32[]{:S(2)}) %collective-permute-start.10) | collective-permute-done | bytes 131104 | tf_op jit(solution)/shard_map/ppermute | solution.py:162
  38.6 14.7 %collective-permute-done.2 = bf16[2,4,128,128]{3,2,1,0:T(8,128)(2,1)S(1)} collective-permute-done((bf16[2,4,128,128]{3,2,1,0:T(8,128)(2,1)}, bf16[2,4,128,128]{3,2,1,0:T(8,128)(2,1)S(1)}, u32[]{:S(2)}, u32[]{:S(2)}) %collective-permute-start.2) | collective-permute-done | bytes 262176 | tf_op jit(solution)/shard_map/ppermute | solution.py:118
  53.3 5.6 %collective-permute-done.3 = bf16[2,4,128,128]{3,2,1,0:T(8,128)(2,1)S(1)} collective-permute-done((bf16[2,4,128,128]{3,2,1,0:T(8,128)(2,1)}, bf16[2,4,128,128]{3,2,1,0:T(8,128)(2,1)S(1)}, u32[]{:S(2)}, u32[]{:S(2)}) %collective-permute-start.3) | collective-permute-done | bytes 262176 | tf_op jit(solution)/shard_map/ppermute | solution.py:118
  59.9 3.5 %collective-permute-done.5 = bf16[2,4,128,128]{3,2,1,0:T(8,128)(2,1)S(1)} collective-permute-done((bf16[2,4,128,128]{3,2,1,0:T(8,128)(2,1)S(1)}, bf16[2,4,128,128]{3,2,1,0:T(8,128)(2,1)S(1)}, u32[]{:S(2)}, u32[]{:S(2)}) %collective-permute-start.5) | collective-permute-done | bytes 262176 | tf_op jit(solution)/shard_map/ppermute | solution.py:118
  68.8 2.2 %fusion.69 = (f32[4,8,128]{2,1,0:T(8,128)S(1)}, f32[4,8,128,256]{3,2,1,0:T(8,128)S(1)}) fusion(f32[4,8,128,256]{3,2,1,0:T(8,128)S(1)} %fusion.3, pred[8,128,256]{2,1,0:T(8,128)(4,1)S(1)} %copy-done.20), kind=kOutput, calls=%fused_computation.245 | output fusion | flops 6291711 | bytes 8667136 | tf_op jit(solution)/shard_map/sub | solution.py:53
  74.6 2.5 %collective-permute-start.11 = (bf16[4,8,128,128]{3,2,1,0:T(8,128)(2,1)S(1)}, bf16[4,8,128,128]{3,2,1,0:T(8,128)(2,1)S(1)}, u32[]{:S(2)}, u32[]{:S(2)}) collective-permute-start(bf16[4,8,128,128]{3,2,1,0:T(8,128)(2,1)S(1)} %add_convert_fusion.3), channel_id=1, source_target_pairs={{24,16},{25,17},{26,18},{27,19},{28,20},{29,21},{30,22},{31,23}} | collective-permute-start | bytes 3145736 | tf_op jit(solution)/shard_map/ppermute | solution.py:191
  77.1 2.2 %collective-permute-done.11 = bf16[4,8,128,128]{3,2,1,0:T(8,128)(2,1)S(1)} collective-permute-done((bf16[4,8,128,128]{3,2,1,0:T(8,128)(2,1)S(1)}, bf16[4,8,128,128]{3,2,1,0:T(8,128)(2,1)S(1)}, u32[]{:S(2)}, u32[]{:S(2)}) %collective-permute-start.11) | collective-permute-done | bytes 1048608 | tf_op jit(solution)/shard_map/ppermute | solution.py:191
  82.0 1.6 collective-permute-start.12
  84.4 1.9 %collective-permute-start.14 = (bf16[4,128,128]{2,1,0:T(8,128)(2,1)}, bf16[4,128,128]{2,1,0:T(8,128)(2,1)}, u32[]{:S(2)}, u32[]{:S(2)}) collective-permute-start(bf16[4,128,128]{2,1,0:T(8,128)(2,1)} %get-tuple-element.94), channel_id=1, source_target_pairs={{24,25},{25,26},{26,27},{27,28},{28,29},{29,30},{30,31},{31,24}} | collective-permute-start | bytes 393224 | tf_op jit(solution)/shard_map/ppermute | solution.py:123
  86.4 1.9 %collective-permute-start.15 = (bf16[4,128,128]{2,1,0:T(8,128)(2,1)}, bf16[4,128,128]{2,1,0:T(8,128)(2,1)}, u32[]{:S(2)}, u32[]{:S(2)}) collective-permute-start(bf16[4,128,128]{2,1,0:T(8,128)(2,1)} %get-tuple-element.93), channel_id=1, source_target_pairs={{24,26},{25,27},{26,28},{27,29},{28,30},{29,31},{30,24},{31,25}} | collective-permute-start | bytes 393224 | tf_op jit(solution)/shard_map/ppermute | solution.py:123
  88.3 5.4 %collective-permute-start.16 = (bf16[4,128,128]{2,1,0:T(8,128)(2,1)}, bf16[4,128,128]{2,1,0:T(8,128)(2,1)}, u32[]{:S(2)}, u32[]{:S(2)}) collective-permute-start(bf16[4,128,128]{2,1,0:T(8,128)(2,1)} %get-tuple-element.92), channel_id=1, source_target_pairs={{24,27},{25,28},{26,29},{27,30},{28,31},{29,24},{30,25},{31,26}} | collective-permute-start | bytes 393224 | tf_op jit(solution)/shard_map/ppermute | solution.py:123
  93.7 1.9 %collective-permute-start.17 = (bf16[4,128,128]{2,1,0:T(8,128)(2,1)}, bf16[4,128,128]{2,1,0:T(8,128)(2,1)}, u32[]{:S(2)}, u32[]{:S(2)}) collective-permute-start(bf16[4,128,128]{2,1,0:T(8,128)(2,1)} %get-tuple-element.91), channel_id=1, source_target_pairs={{24,28},{25,29},{26,30},{27,31},{28,24},{29,25},{30,26},{31,27}} | collective-permute-start | bytes 393224 | tf_op jit(solution)/shard_map/ppermute | solution.py:123
  98.6 3.5 %collective-permute-start.18 = (bf16[4,128,128]{2,1,0:T(8,128)(2,1)S(1)}, bf16[4,128,128]{2,1,0:T(8,128)(2,1)S(1)}, u32[]{:S(2)}, u32[]{:S(2)}) collective-permute-start(bf16[4,128,128]{2,1,0:T(8,128)(2,1)S(1)} %get-tuple-element.90), channel_id=1, source_target_pairs={{24,29},{25,30},{26,31},{27,24},{28,25},{29,26},{30,27},{31,28}} | collective-permute-start | bytes 393224 | tf_op jit(solution)/shard_map/ppermute | solution.py:123
  102.2 1.6 constant_dynamic-update-slice_fusion.6
  103.7 3.8 %collective-permute-start.19 = (bf16[4,128,128]{2,1,0:T(8,128)(2,1)S(1)}, bf16[4,128,128]{2,1,0:T(8,128)(2,1)S(1)}, u32[]{:S(2)}, u32[]{:S(2)}) collective-permute-start(bf16[4,128,128]{2,1,0:T(8,128)(2,1)S(1)} %get-tuple-element.89), channel_id=1, source_target_pairs={{24,30},{25,31},{26,24},{27,25},{28,26},{29,27},{30,28},{31,29}} | collective-permute-start | bytes 393224 | tf_op jit(solution)/shard_map/ppermute | solution.py:123
  107.6 1.6 constant_dynamic-update-slice_fusion.5
  109.2 3.5 %collective-permute-start.20 = (bf16[4,128,128]{2,1,0:T(8,128)(2,1)S(1)}, bf16[4,128,128]{2,1,0:T(8,128)(2,1)S(1)}, u32[]{:S(2)}, u32[]{:S(2)}) collective-permute-start(bf16[4,128,128]{2,1,0:T(8,128)(2,1)S(1)} %get-tuple-element.88), channel_id=1, source_target_pairs={{24,31},{25,24},{26,25},{27,26},{28,27},{29,28},{30,29},{31,30}} | collective-permute-start | bytes 393224 | tf_op jit(solution)/shard_map/ppermute | solution.py:123
  112.7 2.0 %fusion.72 = f32[4,8,256,128]{3,2,1,0:T(8,128)S(1)} fusion(bf16[4,8,128,256]{3,2,1,0:T(8,128)(2,1)S(1)} %fusion.8, bf16[4,8,128,128]{3,2,1,0:T(8,128)(2,1)} %collective-permute-done.12), kind=kOutput, calls=%fused_computation.248 | convolution fusion | flops 268435456 | bytes 7340032 | tf_op jit(solution)/shard_map/hbij,hbid->hbjd/dot_general | solution.py:58
  115.3 1.7 add_convert_fusion.1
  117.7 1.6 constant_dynamic-update-slice_fusion.4
  119.3 1.6 constant_dynamic-update-slice_fusion.3
  130.0 1.6 multiply_convert_fusion
  138.3 2.1 %collective-permute-start.23 = (bf16[2,128,4,128]{3,1,2,0:T(8,128)(2,1)S(1)}, bf16[2,128,4,128]{3,1,2,0:T(8,128)(2,1)S(1)}, u32[]{:S(2)}, u32[]{:S(2)}) collective-permute-start(bf16[2,128,4,128]{3,1,2,0:T(8,128)(2,1)S(1)} %get-tuple-element.74), channel_id=1, source_target_pairs={{0,3},{1,4},{2,5},{3,6},{4,7},{5,0},{6,1},{7,2},{8,11},{9,12},{10,... | collective-permute-start | bytes 786440 | tf_op jit(solution)/shard_map/ppermute | solution.py:118
  141.0 8.5 %collective-permute-done.21 = bf16[2,128,4,128]{3,1,2,0:T(8,128)(2,1)S(1)} collective-permute-done((bf16[2,128,4,128]{3,1,2,0:T(8,128)(2,1)S(1)}, bf16[2,128,4,128]{3,1,2,0:T(8,128)(2,1)S(1)}, u32[]{:S(2)}, u32[]{:S(2)}) %collective-permute-start.21) | collective-permute-done | bytes 262176 | tf_op jit(solution)/shard_map/ppermute | solution.py:118
  149.8 12.4 %collective-permute-done.22 = bf16[2,128,4,128]{3,1,2,0:T(8,128)(2,1)S(1)} collective-permute-done((bf16[2,128,4,128]{3,1,2,0:T(8,128)(2,1)S(1)}, bf16[2,128,4,128]{3,1,2,0:T(8,128)(2,1)S(1)}, u32[]{:S(2)}, u32[]{:S(2)}) %collective-permute-start.22) | collective-permute-done | bytes 262176 | tf_op jit(solution)/shard_map/ppermute | solution.py:118
  163.1 2.6 %collective-permute-done.23 = bf16[2,128,4,128]{3,1,2,0:T(8,128)(2,1)S(1)} collective-permute-done((bf16[2,128,4,128]{3,1,2,0:T(8,128)(2,1)S(1)}, bf16[2,128,4,128]{3,1,2,0:T(8,128)(2,1)S(1)}, u32[]{:S(2)}, u32[]{:S(2)}) %collective-permute-start.23) | collective-permute-done | bytes 262176 | tf_op jit(solution)/shard_map/ppermute | solution.py:118
  167.4 1.5 collective-permute-done.24
  168.9 2.9 %collective-permute-start.30 = (bf16[128,128]{1,0:T(8,128)(2,1)S(1)}, bf16[128,128]{1,0:T(8,128)(2,1)S(1)}, u32[]{:S(2)}, u32[]{:S(2)}) collective-permute-start(bf16[128,128]{1,0:T(8,128)(2,1)S(1)} %get-tuple-element.101), channel_id=1, source_target_pairs={{0,4},{1,5},{2,6},{3,7},{4,0},{5,1},{6,2},{7,3},{8,12},{9,13},{10,... | collective-permute-start | bytes 98312 | tf_op jit(solution)/shard_map/ppermute | solution.py:232
  (193 shorter events, 62.9 us)
Async XLA Ops:
  2.8 18.7 %collective-permute-start.8 = (bf16[128,128]{1,0:T(8,128)(2,1)}, bf16[128,128]{1,0:T(8,128)(2,1)S(1)}, u32[]{:S(2)}, u32[]{:S(2)}) collective-permute-start(bf16[128,128]{1,0:T(8,128)(2,1)} %bitcast.10), channel_id=1, source_target_pairs={{0,4},{1,5},{2,6},{3,7},{4,0},{5,1},{6,2},{7,3},{8,12},{9,13},{10,... | collective-permute-start | bytes 98312 | tf_op jit(solution)/shard_map/ppermute | solution.py:157
  5.8 17.1 %collective-permute-start.9 = (bf16[128,128]{1,0:T(8,128)(2,1)}, bf16[128,128]{1,0:T(8,128)(2,1)S(1)}, u32[]{:S(2)}, u32[]{:S(2)}) collective-permute-start(bf16[128,128]{1,0:T(8,128)(2,1)} %bitcast.12), channel_id=1, source_target_pairs={{0,6},{1,7},{2,0},{3,1},{4,2},{5,3},{6,4},{7,5},{8,14},{9,15},{10,... | collective-permute-start | bytes 98312 | tf_op jit(solution)/shard_map/ppermute | solution.py:157
  6.7 16.3 %collective-permute-start.7 = (bf16[128,128]{1,0:T(8,128)(2,1)}, bf16[128,128]{1,0:T(8,128)(2,1)S(1)}, u32[]{:S(2)}, u32[]{:S(2)}) collective-permute-start(bf16[128,128]{1,0:T(8,128)(2,1)} %bitcast.8), channel_id=1, source_target_pairs={{0,2},{1,3},{2,4},{3,5},{4,6},{5,7},{6,0},{7,1},{8,10},{9,11},{10,... | collective-permute-start | bytes 98312 | tf_op jit(solution)/shard_map/ppermute | solution.py:157
  14.9 19.5 %collective-permute-start = (bf16[2,4,128,128]{3,2,1,0:T(8,128)(2,1)}, bf16[2,4,128,128]{3,2,1,0:T(8,128)(2,1)}, u32[]{:S(2)}, u32[]{:S(2)}) collective-permute-start(bf16[2,4,128,128]{3,2,1,0:T(8,128)(2,1)} %get-tuple-element.82), channel_id=1, source_target_pairs={{0,1},{1,2},{2,3},{3,4},{4,5},{5,6},{6,7},{7,0},{8,9},{9,10},{10,1... | collective-permute-start | bytes 786440 | tf_op jit(solution)/shard_map/ppermute | solution.py:118
  14.9 21.7 %collective-permute-start.1 = (bf16[2,4,128,128]{3,2,1,0:T(8,128)(2,1)}, bf16[2,4,128,128]{3,2,1,0:T(8,128)(2,1)}, u32[]{:S(2)}, u32[]{:S(2)}) collective-permute-start(bf16[2,4,128,128]{3,2,1,0:T(8,128)(2,1)} %get-tuple-element.83), channel_id=1, source_target_pairs={{0,2},{1,3},{2,4},{3,5},{4,6},{5,7},{6,0},{7,1},{8,10},{9,11},{10,... | collective-permute-start | bytes 786440 | tf_op jit(solution)/shard_map/ppermute | solution.py:118
  21.4 31.8 %collective-permute-start.2 = (bf16[2,4,128,128]{3,2,1,0:T(8,128)(2,1)}, bf16[2,4,128,128]{3,2,1,0:T(8,128)(2,1)S(1)}, u32[]{:S(2)}, u32[]{:S(2)}) collective-permute-start(bf16[2,4,128,128]{3,2,1,0:T(8,128)(2,1)} %get-tuple-element.84), channel_id=1, source_target_pairs={{0,3},{1,4},{2,5},{3,6},{4,7},{5,0},{6,1},{7,2},{8,11},{9,12},{10,... | collective-permute-start | bytes 786440 | tf_op jit(solution)/shard_map/ppermute | solution.py:118
  22.9 36.0 %collective-permute-start.3 = (bf16[2,4,128,128]{3,2,1,0:T(8,128)(2,1)}, bf16[2,4,128,128]{3,2,1,0:T(8,128)(2,1)S(1)}, u32[]{:S(2)}, u32[]{:S(2)}) collective-permute-start(bf16[2,4,128,128]{3,2,1,0:T(8,128)(2,1)} %get-tuple-element.86), channel_id=1, source_target_pairs={{0,4},{1,5},{2,6},{3,7},{4,0},{5,1},{6,2},{7,3},{8,12},{9,13},{10,... | collective-permute-start | bytes 786440 | tf_op jit(solution)/shard_map/ppermute | solution.py:118
  23.0 10.6 %collective-permute-start.10 = (bf16[4,128,128]{2,1,0:T(8,128)(2,1)S(1)}, bf16[4,128,128]{2,1,0:T(8,128)(2,1)S(1)}, u32[]{:S(2)}, u32[]{:S(2)}) collective-permute-start(bf16[4,128,128]{2,1,0:T(8,128)(2,1)S(1)} %pad_maximum_fusion.11), channel_id=1, source_target_pairs={{0,1},{1,0},{2,3},{3,2},{4,5},{5,4},{6,7},{7,6},{8,9},{9,8},{10,11... | collective-permute-start | bytes 393224 | tf_op jit(solution)/shard_map/ppermute | solution.py:162
  33.6 25.3 %collective-permute-start.4 = (bf16[2,4,128,128]{3,2,1,0:T(8,128)(2,1)}, bf16[2,4,128,128]{3,2,1,0:T(8,128)(2,1)}, u32[]{:S(2)}, u32[]{:S(2)}) collective-permute-start(bf16[2,4,128,128]{3,2,1,0:T(8,128)(2,1)} %get-tuple-element.87), channel_id=1, source_target_pairs={{0,5},{1,6},{2,7},{3,0},{4,1},{5,2},{6,3},{7,4},{8,13},{9,14},{10,... | collective-permute-start | bytes 786440 | tf_op jit(solution)/shard_map/ppermute | solution.py:118
  34.4 29.1 %collective-permute-start.5 = (bf16[2,4,128,128]{3,2,1,0:T(8,128)(2,1)S(1)}, bf16[2,4,128,128]{3,2,1,0:T(8,128)(2,1)S(1)}, u32[]{:S(2)}, u32[]{:S(2)}) collective-permute-start(bf16[2,4,128,128]{3,2,1,0:T(8,128)(2,1)S(1)} %copy-done.19), channel_id=1, source_target_pairs={{0,6},{1,7},{2,0},{3,1},{4,2},{5,3},{6,4},{7,5},{8,14},{9,15},{10,... | collective-permute-start | bytes 786440 | tf_op jit(solution)/shard_map/ppermute | solution.py:118
  36.6 28.0 %collective-permute-start.6 = (bf16[2,4,128,128]{3,2,1,0:T(8,128)(2,1)}, bf16[2,4,128,128]{3,2,1,0:T(8,128)(2,1)S(1)}, u32[]{:S(2)}, u32[]{:S(2)}) collective-permute-start(bf16[2,4,128,128]{3,2,1,0:T(8,128)(2,1)} %get-tuple-element.80), channel_id=1, source_target_pairs={{0,7},{1,0},{2,1},{3,2},{4,3},{5,4},{6,5},{7,6},{8,15},{9,8},{10,9... | collective-permute-start | bytes 786440 | tf_op jit(solution)/shard_map/ppermute | solution.py:118
  74.6 4.7 %collective-permute-start.11 = (bf16[4,8,128,128]{3,2,1,0:T(8,128)(2,1)S(1)}, bf16[4,8,128,128]{3,2,1,0:T(8,128)(2,1)S(1)}, u32[]{:S(2)}, u32[]{:S(2)}) collective-permute-start(bf16[4,8,128,128]{3,2,1,0:T(8,128)(2,1)S(1)} %add_convert_fusion.3), channel_id=1, source_target_pairs={{24,16},{25,17},{26,18},{27,19},{28,20},{29,21},{30,22},{31,23}} | collective-permute-start | bytes 3145736 | tf_op jit(solution)/shard_map/ppermute | solution.py:191
  82.0 27.2 %collective-permute-start.12 = (bf16[4,8,128,128]{3,2,1,0:T(8,128)(2,1)}, bf16[4,8,128,128]{3,2,1,0:T(8,128)(2,1)}, u32[]{:S(2)}, u32[]{:S(2)}) collective-permute-start(bf16[4,8,128,128]{3,2,1,0:T(8,128)(2,1)} %add_convert_fusion.2), channel_id=1, source_target_pairs={{16,8},{17,9},{18,10},{19,11},{20,12},{21,13},{22,14},{23,15}} | collective-permute-start | bytes 3145736 | tf_op jit(solution)/shard_map/ppermute | solution.py:191
  84.4 14.2 %collective-permute-start.14 = (bf16[4,128,128]{2,1,0:T(8,128)(2,1)}, bf16[4,128,128]{2,1,0:T(8,128)(2,1)}, u32[]{:S(2)}, u32[]{:S(2)}) collective-permute-start(bf16[4,128,128]{2,1,0:T(8,128)(2,1)} %get-tuple-element.94), channel_id=1, source_target_pairs={{24,25},{25,26},{26,27},{27,28},{28,29},{29,30},{30,31},{31,24}} | collective-permute-start | bytes 393224 | tf_op jit(solution)/shard_map/ppermute | solution.py:123
  86.4 17.4 %collective-permute-start.15 = (bf16[4,128,128]{2,1,0:T(8,128)(2,1)}, bf16[4,128,128]{2,1,0:T(8,128)(2,1)}, u32[]{:S(2)}, u32[]{:S(2)}) collective-permute-start(bf16[4,128,128]{2,1,0:T(8,128)(2,1)} %get-tuple-element.93), channel_id=1, source_target_pairs={{24,26},{25,27},{26,28},{27,29},{28,30},{29,31},{30,24},{31,25}} | collective-permute-start | bytes 393224 | tf_op jit(solution)/shard_map/ppermute | solution.py:123
  88.3 28.7 %collective-permute-start.16 = (bf16[4,128,128]{2,1,0:T(8,128)(2,1)}, bf16[4,128,128]{2,1,0:T(8,128)(2,1)}, u32[]{:S(2)}, u32[]{:S(2)}) collective-permute-start(bf16[4,128,128]{2,1,0:T(8,128)(2,1)} %get-tuple-element.92), channel_id=1, source_target_pairs={{24,27},{25,28},{26,29},{27,30},{28,31},{29,24},{30,25},{31,26}} | collective-permute-start | bytes 393224 | tf_op jit(solution)/shard_map/ppermute | solution.py:123
  93.7 25.6 %collective-permute-start.17 = (bf16[4,128,128]{2,1,0:T(8,128)(2,1)}, bf16[4,128,128]{2,1,0:T(8,128)(2,1)}, u32[]{:S(2)}, u32[]{:S(2)}) collective-permute-start(bf16[4,128,128]{2,1,0:T(8,128)(2,1)} %get-tuple-element.91), channel_id=1, source_target_pairs={{24,28},{25,29},{26,30},{27,31},{28,24},{29,25},{30,26},{31,27}} | collective-permute-start | bytes 393224 | tf_op jit(solution)/shard_map/ppermute | solution.py:123
  98.6 22.3 %collective-permute-start.18 = (bf16[4,128,128]{2,1,0:T(8,128)(2,1)S(1)}, bf16[4,128,128]{2,1,0:T(8,128)(2,1)S(1)}, u32[]{:S(2)}, u32[]{:S(2)}) collective-permute-start(bf16[4,128,128]{2,1,0:T(8,128)(2,1)S(1)} %get-tuple-element.90), channel_id=1, source_target_pairs={{24,29},{25,30},{26,31},{27,24},{28,25},{29,26},{30,27},{31,28}} | collective-permute-start | bytes 393224 | tf_op jit(solution)/shard_map/ppermute | solution.py:123
  103.7 17.8 %collective-permute-start.19 = (bf16[4,128,128]{2,1,0:T(8,128)(2,1)S(1)}, bf16[4,128,128]{2,1,0:T(8,128)(2,1)S(1)}, u32[]{:S(2)}, u32[]{:S(2)}) collective-permute-start(bf16[4,128,128]{2,1,0:T(8,128)(2,1)S(1)} %get-tuple-element.89), channel_id=1, source_target_pairs={{24,30},{25,31},{26,24},{27,25},{28,26},{29,27},{30,28},{31,29}} | collective-permute-start | bytes 393224 | tf_op jit(solution)/shard_map/ppermute | solution.py:123
  109.2 13.1 %collective-permute-start.20 = (bf16[4,128,128]{2,1,0:T(8,128)(2,1)S(1)}, bf16[4,128,128]{2,1,0:T(8,128)(2,1)S(1)}, u32[]{:S(2)}, u32[]{:S(2)}) collective-permute-start(bf16[4,128,128]{2,1,0:T(8,128)(2,1)S(1)} %get-tuple-element.88), channel_id=1, source_target_pairs={{24,31},{25,24},{26,25},{27,26},{28,27},{29,28},{30,29},{31,30}} | collective-permute-start | bytes 393224 | tf_op jit(solution)/shard_map/ppermute | solution.py:123
  117.0 7.3 %collective-permute-start.13 = (bf16[4,8,128,128]{3,2,1,0:T(8,128)(2,1)S(1)}, bf16[4,8,128,128]{3,2,1,0:T(8,128)(2,1)S(1)}, u32[]{:S(2)}, u32[]{:S(2)}) collective-permute-start(bf16[4,8,128,128]{3,2,1,0:T(8,128)(2,1)S(1)} %add_convert_fusion.1), channel_id=1, source_target_pairs={{8,0},{9,1},{10,2},{11,3},{12,4},{13,5},{14,6},{15,7}} | collective-permute-start | bytes 3145736 | tf_op jit(solution)/shard_map/ppermute | solution.py:191
  134.6 14.9 %collective-permute-start.21 = (bf16[2,128,4,128]{3,1,2,0:T(8,128)(2,1)S(1)}, bf16[2,128,4,128]{3,1,2,0:T(8,128)(2,1)S(1)}, u32[]{:S(2)}, u32[]{:S(2)}) collective-permute-start(bf16[2,128,4,128]{3,1,2,0:T(8,128)(2,1)S(1)} %get-tuple-element.72), channel_id=1, source_target_pairs={{0,1},{1,2},{2,3},{3,4},{4,5},{5,6},{6,7},{7,0},{8,9},{9,10},{10,1... | collective-permute-start | bytes 786440 | tf_op jit(solution)/shard_map/ppermute | solution.py:118
  135.6 26.9 %collective-permute-start.28 = (f32[4,128,128]{2,1,0:T(8,128)S(1)}, f32[4,128,128]{2,1,0:T(8,128)S(1)}, u32[]{:S(2)}, u32[]{:S(2)}) collective-permute-start(f32[4,128,128]{2,1,0:T(8,128)S(1)} %dynamic-slice_bitcast_fusion), channel_id=1, source_target_pairs={{0,1},{1,0},{2,3},{3,2},{4,5},{5,4},{6,7},{7,6},{8,9},{9,8},{10,11... | collective-permute-start | bytes 786440 | tf_op jit(solution)/shard_map/ppermute | solution.py:225
  136.2 35.9 %collective-permute-start.25 = (bf16[2,128,4,128]{3,1,2,0:T(8,128)(2,1)S(1)}, bf16[2,128,4,128]{3,1,2,0:T(8,128)(2,1)S(1)}, u32[]{:S(2)}, u32[]{:S(2)}) collective-permute-start(bf16[2,128,4,128]{3,1,2,0:T(8,128)(2,1)S(1)} %get-tuple-element.77), channel_id=1, source_target_pairs={{0,5},{1,6},{2,7},{3,0},{4,1},{5,2},{6,3},{7,4},{8,13},{9,14},{10,... | collective-permute-start | bytes 786440 | tf_op jit(solution)/shard_map/ppermute | solution.py:118
  137.1 25.1 %collective-permute-start.22 = (bf16[2,128,4,128]{3,1,2,0:T(8,128)(2,1)S(1)}, bf16[2,128,4,128]{3,1,2,0:T(8,128)(2,1)S(1)}, u32[]{:S(2)}, u32[]{:S(2)}) collective-permute-start(bf16[2,128,4,128]{3,1,2,0:T(8,128)(2,1)S(1)} %get-tuple-element.73), channel_id=1, source_target_pairs={{0,2},{1,3},{2,4},{3,5},{4,6},{5,7},{6,0},{7,1},{8,10},{9,11},{10,... | collective-permute-start | bytes 786440 | tf_op jit(solution)/shard_map/ppermute | solution.py:118
  138.3 27.4 %collective-permute-start.23 = (bf16[2,128,4,128]{3,1,2,0:T(8,128)(2,1)S(1)}, bf16[2,128,4,128]{3,1,2,0:T(8,128)(2,1)S(1)}, u32[]{:S(2)}, u32[]{:S(2)}) collective-permute-start(bf16[2,128,4,128]{3,1,2,0:T(8,128)(2,1)S(1)} %get-tuple-element.74), channel_id=1, source_target_pairs={{0,3},{1,4},{2,5},{3,6},{4,7},{5,0},{6,1},{7,2},{8,11},{9,12},{10,... | collective-permute-start | bytes 786440 | tf_op jit(solution)/shard_map/ppermute | solution.py:118
  149.5 19.5 %collective-permute-start.24 = (bf16[2,128,4,128]{3,1,2,0:T(8,128)(2,1)S(1)}, bf16[2,128,4,128]{3,1,2,0:T(8,128)(2,1)S(1)}, u32[]{:S(2)}, u32[]{:S(2)}) collective-permute-start(bf16[2,128,4,128]{3,1,2,0:T(8,128)(2,1)S(1)} %get-tuple-element.75), channel_id=1, source_target_pairs={{0,4},{1,5},{2,6},{3,7},{4,0},{5,1},{6,2},{7,3},{8,12},{9,13},{10,... | collective-permute-start | bytes 786440 | tf_op jit(solution)/shard_map/ppermute | solution.py:118
  162.2 10.3 %collective-permute-start.26 = (bf16[2,128,4,128]{3,1,2,0:T(8,128)(2,1)S(1)}, bf16[2,128,4,128]{3,1,2,0:T(8,128)(2,1)S(1)}, u32[]{:S(2)}, u32[]{:S(2)}) collective-permute-start(bf16[2,128,4,128]{3,1,2,0:T(8,128)(2,1)S(1)} %get-tuple-element.76), channel_id=1, source_target_pairs={{0,6},{1,7},{2,0},{3,1},{4,2},{5,3},{6,4},{7,5},{8,14},{9,15},{10,... | collective-permute-start | bytes 786440 | tf_op jit(solution)/shard_map/ppermute | solution.py:118
  162.5 10.3 %collective-permute-start.27 = (bf16[2,128,4,128]{3,1,2,0:T(8,128)(2,1)S(1)}, bf16[2,128,4,128]{3,1,2,0:T(8,128)(2,1)S(1)}, u32[]{:S(2)}, u32[]{:S(2)}) collective-permute-start(bf16[2,128,4,128]{3,1,2,0:T(8,128)(2,1)S(1)} %get-tuple-element.70), channel_id=1, source_target_pairs={{0,7},{1,0},{2,1},{3,2},{4,3},{5,4},{6,5},{7,6},{8,15},{9,8},{10,9... | collective-permute-start | bytes 786440 | tf_op jit(solution)/shard_map/ppermute | solution.py:118
  165.7 10.3 %collective-permute-start.29 = (bf16[128,128]{1,0:T(8,128)(2,1)S(1)}, bf16[128,128]{1,0:T(8,128)(2,1)S(1)}, u32[]{:S(2)}, u32[]{:S(2)}) collective-permute-start(bf16[128,128]{1,0:T(8,128)(2,1)S(1)} %get-tuple-element.102), channel_id=1, source_target_pairs={{0,2},{1,3},{2,4},{3,5},{4,6},{5,7},{6,0},{7,1},{8,10},{9,11},{10,... | collective-permute-start | bytes 98312 | tf_op jit(solution)/shard_map/ppermute | solution.py:232
  168.9 7.1 %collective-permute-start.30 = (bf16[128,128]{1,0:T(8,128)(2,1)S(1)}, bf16[128,128]{1,0:T(8,128)(2,1)S(1)}, u32[]{:S(2)}, u32[]{:S(2)}) collective-permute-start(bf16[128,128]{1,0:T(8,128)(2,1)S(1)} %get-tuple-element.101), channel_id=1, source_target_pairs={{0,4},{1,5},{2,6},{3,7},{4,0},{5,1},{6,2},{7,3},{8,12},{9,13},{10,... | collective-permute-start | bytes 98312 | tf_op jit(solution)/shard_map/ppermute | solution.py:232
  172.1 3.9 %collective-permute-start.31 = (bf16[128,128]{1,0:T(8,128)(2,1)S(1)}, bf16[128,128]{1,0:T(8,128)(2,1)S(1)}, u32[]{:S(2)}, u32[]{:S(2)}) collective-permute-start(bf16[128,128]{1,0:T(8,128)(2,1)S(1)} %get-tuple-element.100), channel_id=1, source_target_pairs={{0,6},{1,7},{2,0},{3,1},{4,2},{5,3},{6,4},{7,5},{8,14},{9,15},{10,... | collective-permute-start | bytes 98312 | tf_op jit(solution)/shard_map/ppermute | solution.py:232
  (25 other events, 82.8 us)

commit v17 on v16

--- a/solution.py
+++ b/solution.py
@@ -102,15 +102,19 @@
 
     seq_index = lax.axis_index("seq")
 
-    def transpose_seq(value, split_axis, concat_axis, section=None):
+    def transpose_seq(value, split_axis, concat_axis, section=None, apart=False):
         if seq_ways > 8:
-            return lax.all_to_all(value, "seq", split_axis, concat_axis, tiled=True)
+            moved = lax.all_to_all(value, "seq", split_axis, concat_axis, tiled=True)
+            return [moved[i] for i in range(value.shape[0])] if apart else moved
         split_size = value.shape[split_axis] // seq_ways
         concat_size = value.shape[concat_axis]
         out_shape = list(value.shape)
         out_shape[split_axis] = split_size
         out_shape[concat_axis] = concat_size * seq_ways
-        result = jnp.zeros(out_shape, value.dtype)
+        parts = value.shape[0] if apart else 1
+        part_shape = out_shape[1:] if apart else out_shape
+        results = [jnp.zeros(part_shape, value.dtype) for _ in range(parts)]
+        part_axis = concat_axis - 1 if apart else concat_axis
         for shift in range(seq_ways):
             target = (seq_index + shift) % seq_ways
             chunk = lax.dynamic_slice_in_dim(value, target * split_size, split_size, axis=split_axis)
@@ -126,10 +130,11 @@
                     [(base + s, base + (s + shift) % seq_ways) for s in range(seq_ways)],
                 )
             source = (seq_index + seq_ways - shift) % seq_ways
-            result = lax.dynamic_update_slice_in_dim(
-                result, chunk, source * concat_size, axis=concat_axis
-            )
-        return result
+            for i in range(parts):
+                results[i] = lax.dynamic_update_slice_in_dim(
+                    results[i], chunk[i] if apart else chunk, source * concat_size, axis=part_axis
+                )
+        return results if apart else results[0]
 
     def to_blocks(head_rows):
         return head_rows.reshape(local_heads, block_count, BLK, DH)
@@ -211,8 +216,9 @@
     pair = jnp.transpose(
         jnp.stack([grad_query, held_out]).reshape(2, local_heads, seq_len, DH), (0, 2, 1, 3)
     )
-    pair_out = transpose_seq(pair, 1, 2)
-    pair_rows = pair_out.reshape(2, tok_rows, full_width)
+    pair_rows = [
+        rows.reshape(tok_rows, full_width) for rows in transpose_seq(pair, 1, 2, apart=True)
+    ]
     if local_heads == 1:
         key_part = grad_key.reshape(seq_len, DH)
     else:

time: 180 us -> 182 us (1.011)
  waiting for transfers between devices: 61.5 us -> 68.1 us
  starting transfers between devices: 48.4 us -> 45.3 us
    ppermute x1, waiting for transfers between devices: 0.01 us -> 7.32 us  [on_device(): got = lax.ppermute(give, 'seq', [(d, d ^ 1) for d in range(seq_ways)])]
    slice x3 -> x0, local copies, waits for them, and re-layouts: 2.89 us -> none  [on_device(): return (pair_rows[0][None], key_final[None], pair_rows[1][None])]
    another operation x5 -> x9, local copies, waits for them, and re-layouts: 2.28 us -> 5.07 us
    ppermute x6, starting transfers between devices: 8.13 us -> 5.42 us  [on_device(): lax.ppermute(chunk, 'seq', [(d, (d + shift) % seq_ways) for d in range(se...]
    dynamic_update_slice x23 -> x30, local copies, waits for them, and re-layouts: 14.5 us -> 14.6 us  [transpose_seq(): lax.dynamic_update_slice_in_dim(results[i], chunk[i] if apart else chunk,...]
where the time goes in v17:
time: 182 us; the launch traced here: 181 us
  waiting for transfers between devices  68.1 us (37%)
  starting transfers between devices  45.3 us (25%)
  local copies, waits for them, and re-layouts  38.5 us (21%)
  other arithmetic  18 us (10%)
  matrix products  8.81 us (5%)
  between operations  1.87 us (1%)
    ppermute x14, waiting for transfers between devices, transpose_seq(): lax.ppermute(chunk, 'seq', [(s, (s + shift) % seq_ways) for s in range(se...  49.2 us
    ppermute x7, starting transfers between devices, transpose_seq(): lax.ppermute(chunk, ('pipe', 'seq'), [(base + s, base + (s + shift) % seq...  22 us
    dynamic_update_slice x30, local copies, waits for them, and re-layouts, transpose_seq(): lax.dynamic_update_slice_in_dim(results[i], chunk[i] if apart else chunk,...  14.6 us
    ppermute x14, starting transfers between devices, transpose_seq(): lax.ppermute(chunk, 'seq', [(s, (s + shift) % seq_ways) for s in range(se...  11.8 us
    unnamed x58, local copies, waits for them, and re-layouts  11.3 us
    ppermute x1, waiting for transfers between devices, on_device(): theirs = lax.ppermute(mine, 'seq', [(d, d ^ 1) for d in range(seq_ways)])  9.32 us
    ppermute x1, waiting for transfers between devices, on_device(): got = lax.ppermute(give, 'seq', [(d, d ^ 1) for d in range(seq_ways)])  7.32 us
    ppermute x6, starting transfers between devices, on_device(): lax.ppermute(chunk, 'seq', [(d, (d + shift) % seq_ways) for d in range(se...  5.42 us
  transfers between devices with their start and end apart: 32, of which 10 were waited for; matrix products, arithmetic and copies ran while one was open for 22% of the time, Pallas kernels for 0%

profile of v17, /device:TPU:15, one launch (start us, length us, event | category | flops | bytes accessed | tf_op | source)
XLA Modules:
  0.0 180.5 jit_solution(4355403459504161426)
XLA Ops:
  2.7 2.3 %collective-permute-start.8 = (bf16[128,128]{1,0:T(8,128)(2,1)}, bf16[128,128]{1,0:T(8,128)(2,1)S(1)}, u32[]{:S(2)}, u32[]{:S(2)}) collective-permute-start(bf16[128,128]{1,0:T(8,128)(2,1)} %bitcast.10), channel_id=1, source_target_pairs={{0,4},{1,5},{2,6},{3,7},{4,0},{5,1},{6,2},{7,3},{8,12},{9,13},{10,... | collective-permute-start | bytes 98312 | tf_op jit(solution)/shard_map/ppermute | solution.py:162
  11.1 1.6 fusion.67
  14.9 2.1 %collective-permute-start.1 = (bf16[2,4,128,128]{3,2,1,0:T(8,128)(2,1)}, bf16[2,4,128,128]{3,2,1,0:T(8,128)(2,1)}, u32[]{:S(2)}, u32[]{:S(2)}) collective-permute-start(bf16[2,4,128,128]{3,2,1,0:T(8,128)(2,1)} %get-tuple-element.81), channel_id=1, source_target_pairs={{0,2},{1,3},{2,4},{3,5},{4,6},{5,7},{6,0},{7,1},{8,10},{9,11},{10,... | collective-permute-start | bytes 786440 | tf_op jit(solution)/shard_map/ppermute | solution.py:122
  18.3 2.0 %fusion.34 = (bf16[2,4,128,128]{3,2,1,0:T(8,128)(2,1)}, bf16[2,4,128,128]{3,2,1,0:T(8,128)(2,1)}, bf16[2,4,128,128]{3,2,1,0:T(8,128)(2,1)}) fusion(s32[]{:T(128)S(6)} %select_n.541, bf16[1,32,128,128]{3,2,1,0:T(8,128)(2,1)} %bitcast.165, bf16[1,32,128,128]{3,2,1,0:T(8,128)(2,1)S(1)} %get-tuple-element.94, s32[]{:T(128)S(6)} %select_n.537, s32[]{:T(128)S(6)} %select_n.539), kind=kLoop, calls=%fused_computation.97 | loop fusion | flops 393216 | bytes 2883596 | tf_op jit(solution)/shard_map/stack | solution.py:147
  24.2 9.3 %collective-permute-done.10 = bf16[4,128,128]{2,1,0:T(8,128)(2,1)S(1)} collective-permute-done((bf16[4,128,128]{2,1,0:T(8,128)(2,1)S(1)}, bf16[4,128,128]{2,1,0:T(8,128)(2,1)S(1)}, u32[]{:S(2)}, u32[]{:S(2)}) %collective-permute-start.10) | collective-permute-done | bytes 131104 | tf_op jit(solution)/shard_map/ppermute | solution.py:167
  38.5 14.8 %collective-permute-done.2 = bf16[2,4,128,128]{3,2,1,0:T(8,128)(2,1)S(1)} collective-permute-done((bf16[2,4,128,128]{3,2,1,0:T(8,128)(2,1)}, bf16[2,4,128,128]{3,2,1,0:T(8,128)(2,1)S(1)}, u32[]{:S(2)}, u32[]{:S(2)}) %collective-permute-start.2) | collective-permute-done | bytes 262176 | tf_op jit(solution)/shard_map/ppermute | solution.py:122
  53.3 5.6 %collective-permute-done.3 = bf16[2,4,128,128]{3,2,1,0:T(8,128)(2,1)S(1)} collective-permute-done((bf16[2,4,128,128]{3,2,1,0:T(8,128)(2,1)}, bf16[2,4,128,128]{3,2,1,0:T(8,128)(2,1)S(1)}, u32[]{:S(2)}, u32[]{:S(2)}) %collective-permute-start.3) | collective-permute-done | bytes 262176 | tf_op jit(solution)/shard_map/ppermute | solution.py:122
  60.0 3.5 %collective-permute-done.5 = bf16[2,4,128,128]{3,2,1,0:T(8,128)(2,1)S(1)} collective-permute-done((bf16[2,4,128,128]{3,2,1,0:T(8,128)(2,1)S(1)}, bf16[2,4,128,128]{3,2,1,0:T(8,128)(2,1)S(1)}, u32[]{:S(2)}, u32[]{:S(2)}) %collective-permute-start.5) | collective-permute-done | bytes 262176 | tf_op jit(solution)/shard_map/ppermute | solution.py:122
  68.4 2.2 %fusion.68 = (f32[4,8,128]{2,1,0:T(8,128)S(1)}, f32[4,8,128,256]{3,2,1,0:T(8,128)S(1)}) fusion(f32[4,8,128,256]{3,2,1,0:T(8,128)S(1)} %fusion.3, pred[8,128,256]{2,1,0:T(8,128)(4,1)S(1)} %copy-done.20), kind=kOutput, calls=%fused_computation.268 | output fusion | flops 6291711 | bytes 8667136 | tf_op jit(solution)/shard_map/sub | solution.py:53
  74.3 2.5 %collective-permute-start.11 = (bf16[4,8,128,128]{3,2,1,0:T(8,128)(2,1)S(1)}, bf16[4,8,128,128]{3,2,1,0:T(8,128)(2,1)S(1)}, u32[]{:S(2)}, u32[]{:S(2)}) collective-permute-start(bf16[4,8,128,128]{3,2,1,0:T(8,128)(2,1)S(1)} %add_convert_fusion.3), channel_id=1, source_target_pairs={{24,16},{25,17},{26,18},{27,19},{28,20},{29,21},{30,22},{31,23}} | collective-permute-start | bytes 3145736 | tf_op jit(solution)/shard_map/ppermute | solution.py:196
  76.8 2.2 %collective-permute-done.11 = bf16[4,8,128,128]{3,2,1,0:T(8,128)(2,1)S(1)} collective-permute-done((bf16[4,8,128,128]{3,2,1,0:T(8,128)(2,1)S(1)}, bf16[4,8,128,128]{3,2,1,0:T(8,128)(2,1)S(1)}, u32[]{:S(2)}, u32[]{:S(2)}) %collective-permute-start.11) | collective-permute-done | bytes 1048608 | tf_op jit(solution)/shard_map/ppermute | solution.py:196
  81.7 1.6 collective-permute-start.12
  84.1 1.9 %collective-permute-start.14 = (bf16[4,128,128]{2,1,0:T(8,128)(2,1)}, bf16[4,128,128]{2,1,0:T(8,128)(2,1)}, u32[]{:S(2)}, u32[]{:S(2)}) collective-permute-start(bf16[4,128,128]{2,1,0:T(8,128)(2,1)} %get-tuple-element.92), channel_id=1, source_target_pairs={{24,25},{25,26},{26,27},{27,28},{28,29},{29,30},{30,31},{31,24}} | collective-permute-start | bytes 393224 | tf_op jit(solution)/shard_map/ppermute | solution.py:127
  86.0 1.9 %collective-permute-start.15 = (bf16[4,128,128]{2,1,0:T(8,128)(2,1)}, bf16[4,128,128]{2,1,0:T(8,128)(2,1)}, u32[]{:S(2)}, u32[]{:S(2)}) collective-permute-start(bf16[4,128,128]{2,1,0:T(8,128)(2,1)} %get-tuple-element.91), channel_id=1, source_target_pairs={{24,26},{25,27},{26,28},{27,29},{28,30},{29,31},{30,24},{31,25}} | collective-permute-start | bytes 393224 | tf_op jit(solution)/shard_map/ppermute | solution.py:127
  87.9 5.4 %collective-permute-start.16 = (bf16[4,128,128]{2,1,0:T(8,128)(2,1)}, bf16[4,128,128]{2,1,0:T(8,128)(2,1)}, u32[]{:S(2)}, u32[]{:S(2)}) collective-permute-start(bf16[4,128,128]{2,1,0:T(8,128)(2,1)} %get-tuple-element.90), channel_id=1, source_target_pairs={{24,27},{25,28},{26,29},{27,30},{28,31},{29,24},{30,25},{31,26}} | collective-permute-start | bytes 393224 | tf_op jit(solution)/shard_map/ppermute | solution.py:127
  93.3 2.0 %collective-permute-start.17 = (bf16[4,128,128]{2,1,0:T(8,128)(2,1)}, bf16[4,128,128]{2,1,0:T(8,128)(2,1)}, u32[]{:S(2)}, u32[]{:S(2)}) collective-permute-start(bf16[4,128,128]{2,1,0:T(8,128)(2,1)} %get-tuple-element.89), channel_id=1, source_target_pairs={{24,28},{25,29},{26,30},{27,31},{28,24},{29,25},{30,26},{31,27}} | collective-permute-start | bytes 393224 | tf_op jit(solution)/shard_map/ppermute | solution.py:127
  98.3 3.4 %collective-permute-start.18 = (bf16[4,128,128]{2,1,0:T(8,128)(2,1)S(1)}, bf16[4,128,128]{2,1,0:T(8,128)(2,1)S(1)}, u32[]{:S(2)}, u32[]{:S(2)}) collective-permute-start(bf16[4,128,128]{2,1,0:T(8,128)(2,1)S(1)} %get-tuple-element.88), channel_id=1, source_target_pairs={{24,29},{25,30},{26,31},{27,24},{28,25},{29,26},{30,27},{31,28}} | collective-permute-start | bytes 393224 | tf_op jit(solution)/shard_map/ppermute | solution.py:127
  101.7 1.6 constant_dynamic-update-slice_fusion.6
  103.3 3.8 %collective-permute-start.19 = (bf16[4,128,128]{2,1,0:T(8,128)(2,1)S(1)}, bf16[4,128,128]{2,1,0:T(8,128)(2,1)S(1)}, u32[]{:S(2)}, u32[]{:S(2)}) collective-permute-start(bf16[4,128,128]{2,1,0:T(8,128)(2,1)S(1)} %get-tuple-element.87), channel_id=1, source_target_pairs={{24,30},{25,31},{26,24},{27,25},{28,26},{29,27},{30,28},{31,29}} | collective-permute-start | bytes 393224 | tf_op jit(solution)/shard_map/ppermute | solution.py:127
  107.2 1.6 constant_dynamic-update-slice_fusion.5
  108.7 3.5 %collective-permute-start.20 = (bf16[4,128,128]{2,1,0:T(8,128)(2,1)S(1)}, bf16[4,128,128]{2,1,0:T(8,128)(2,1)S(1)}, u32[]{:S(2)}, u32[]{:S(2)}) collective-permute-start(bf16[4,128,128]{2,1,0:T(8,128)(2,1)S(1)} %get-tuple-element.86), channel_id=1, source_target_pairs={{24,31},{25,24},{26,25},{27,26},{28,27},{29,28},{30,29},{31,30}} | collective-permute-start | bytes 393224 | tf_op jit(solution)/shard_map/ppermute | solution.py:127
  112.3 2.0 %fusion.71 = f32[4,8,256,128]{3,2,1,0:T(8,128)S(1)} fusion(bf16[4,8,128,256]{3,2,1,0:T(8,128)(2,1)S(1)} %fusion.8, bf16[4,8,128,128]{3,2,1,0:T(8,128)(2,1)} %collective-permute-done.12), kind=kOutput, calls=%fused_computation.271 | convolution fusion | flops 268435456 | bytes 7340032 | tf_op jit(solution)/shard_map/hbij,hbid->hbjd/dot_general | solution.py:58
  114.9 1.7 add_convert_fusion.1
  117.3 1.6 constant_dynamic-update-slice_fusion.4
  118.9 1.6 constant_dynamic-update-slice_fusion.3
  129.5 1.6 multiply_convert_fusion
  134.3 2.4 %collective-permute-start.23 = (bf16[2,128,4,128]{3,1,2,0:T(8,128)(2,1)S(1)}, bf16[2,128,4,128]{3,1,2,0:T(8,128)(2,1)S(1)}, u32[]{:S(2)}, u32[]{:S(2)}) collective-permute-start(bf16[2,128,4,128]{3,1,2,0:T(8,128)(2,1)S(1)} %get-tuple-element.72), channel_id=1, source_target_pairs={{0,3},{1,4},{2,5},{3,6},{4,7},{5,0},{6,1},{7,2},{8,11},{9,12},{10,... | collective-permute-start | bytes 786440 | tf_op jit(solution)/shard_map/ppermute | solution.py:122
  137.0 2.1 %collective-permute-start.25 = (bf16[2,128,4,128]{3,1,2,0:T(8,128)(2,1)S(1)}, bf16[2,128,4,128]{3,1,2,0:T(8,128)(2,1)S(1)}, u32[]{:S(2)}, u32[]{:S(2)}) collective-permute-start(bf16[2,128,4,128]{3,1,2,0:T(8,128)(2,1)S(1)} %get-tuple-element.75), channel_id=1, source_target_pairs={{0,5},{1,6},{2,7},{3,0},{4,1},{5,2},{6,3},{7,4},{8,13},{9,14},{10,... | collective-permute-start | bytes 786440 | tf_op jit(solution)/shard_map/ppermute | solution.py:122
  140.3 3.6 %collective-permute-done.21 = bf16[2,128,4,128]{3,1,2,0:T(8,128)(2,1)S(1)} collective-permute-done((bf16[2,128,4,128]{3,1,2,0:T(8,128)(2,1)S(1)}, bf16[2,128,4,128]{3,1,2,0:T(8,128)(2,1)S(1)}, u32[]{:S(2)}, u32[]{:S(2)}) %collective-permute-start.21) | collective-permute-done | bytes 262176 | tf_op jit(solution)/shard_map/ppermute | solution.py:122
  143.9 16.7 %collective-permute-done.22 = bf16[2,128,4,128]{3,1,2,0:T(8,128)(2,1)S(1)} collective-permute-done((bf16[2,128,4,128]{3,1,2,0:T(8,128)(2,1)S(1)}, bf16[2,128,4,128]{3,1,2,0:T(8,128)(2,1)S(1)}, u32[]{:S(2)}, u32[]{:S(2)}) %collective-permute-start.22) | collective-permute-done | bytes 262176 | tf_op jit(solution)/shard_map/ppermute | solution.py:122
  160.9 7.3 %collective-permute-done.28 = f32[4,128,128]{2,1,0:T(8,128)S(1)} collective-permute-done((f32[4,128,128]{2,1,0:T(8,128)S(1)}, f32[4,128,128]{2,1,0:T(8,128)S(1)}, u32[]{:S(2)}, u32[]{:S(2)}) %collective-permute-start.28) | collective-permute-done | bytes 262176 | tf_op jit(solution)/shard_map/ppermute | solution.py:231
  171.2 3.9 %collective-permute-done.27 = bf16[2,128,4,128]{3,1,2,0:T(8,128)(2,1)S(1)} collective-permute-done((bf16[2,128,4,128]{3,1,2,0:T(8,128)(2,1)S(1)}, bf16[2,128,4,128]{3,1,2,0:T(8,128)(2,1)S(1)}, u32[]{:S(2)}, u32[]{:S(2)}) %collective-permute-start.27) | collective-permute-done | bytes 262176 | tf_op jit(solution)/shard_map/ppermute | solution.py:122
  (209 shorter events, 59.6 us)
Async XLA Ops:
  2.7 18.7 %collective-permute-start.8 = (bf16[128,128]{1,0:T(8,128)(2,1)}, bf16[128,128]{1,0:T(8,128)(2,1)S(1)}, u32[]{:S(2)}, u32[]{:S(2)}) collective-permute-start(bf16[128,128]{1,0:T(8,128)(2,1)} %bitcast.10), channel_id=1, source_target_pairs={{0,4},{1,5},{2,6},{3,7},{4,0},{5,1},{6,2},{7,3},{8,12},{9,13},{10,... | collective-permute-start | bytes 98312 | tf_op jit(solution)/shard_map/ppermute | solution.py:162
  5.8 17.0 %collective-permute-start.9 = (bf16[128,128]{1,0:T(8,128)(2,1)}, bf16[128,128]{1,0:T(8,128)(2,1)S(1)}, u32[]{:S(2)}, u32[]{:S(2)}) collective-permute-start(bf16[128,128]{1,0:T(8,128)(2,1)} %bitcast.12), channel_id=1, source_target_pairs={{0,6},{1,7},{2,0},{3,1},{4,2},{5,3},{6,4},{7,5},{8,14},{9,15},{10,... | collective-permute-start | bytes 98312 | tf_op jit(solution)/shard_map/ppermute | solution.py:162
  6.7 16.3 %collective-permute-start.7 = (bf16[128,128]{1,0:T(8,128)(2,1)}, bf16[128,128]{1,0:T(8,128)(2,1)S(1)}, u32[]{:S(2)}, u32[]{:S(2)}) collective-permute-start(bf16[128,128]{1,0:T(8,128)(2,1)} %bitcast.8), channel_id=1, source_target_pairs={{0,2},{1,3},{2,4},{3,5},{4,6},{5,7},{6,0},{7,1},{8,10},{9,11},{10,... | collective-permute-start | bytes 98312 | tf_op jit(solution)/shard_map/ppermute | solution.py:162
  14.9 19.5 %collective-permute-start = (bf16[2,4,128,128]{3,2,1,0:T(8,128)(2,1)}, bf16[2,4,128,128]{3,2,1,0:T(8,128)(2,1)}, u32[]{:S(2)}, u32[]{:S(2)}) collective-permute-start(bf16[2,4,128,128]{3,2,1,0:T(8,128)(2,1)} %get-tuple-element.80), channel_id=1, source_target_pairs={{0,1},{1,2},{2,3},{3,4},{4,5},{5,6},{6,7},{7,0},{8,9},{9,10},{10,1... | collective-permute-start | bytes 786440 | tf_op jit(solution)/shard_map/ppermute | solution.py:122
  14.9 21.8 %collective-permute-start.1 = (bf16[2,4,128,128]{3,2,1,0:T(8,128)(2,1)}, bf16[2,4,128,128]{3,2,1,0:T(8,128)(2,1)}, u32[]{:S(2)}, u32[]{:S(2)}) collective-permute-start(bf16[2,4,128,128]{3,2,1,0:T(8,128)(2,1)} %get-tuple-element.81), channel_id=1, source_target_pairs={{0,2},{1,3},{2,4},{3,5},{4,6},{5,7},{6,0},{7,1},{8,10},{9,11},{10,... | collective-permute-start | bytes 786440 | tf_op jit(solution)/shard_map/ppermute | solution.py:122
  21.4 31.9 %collective-permute-start.2 = (bf16[2,4,128,128]{3,2,1,0:T(8,128)(2,1)}, bf16[2,4,128,128]{3,2,1,0:T(8,128)(2,1)S(1)}, u32[]{:S(2)}, u32[]{:S(2)}) collective-permute-start(bf16[2,4,128,128]{3,2,1,0:T(8,128)(2,1)} %get-tuple-element.82), channel_id=1, source_target_pairs={{0,3},{1,4},{2,5},{3,6},{4,7},{5,0},{6,1},{7,2},{8,11},{9,12},{10,... | collective-permute-start | bytes 786440 | tf_op jit(solution)/shard_map/ppermute | solution.py:122
  22.8 36.1 %collective-permute-start.3 = (bf16[2,4,128,128]{3,2,1,0:T(8,128)(2,1)}, bf16[2,4,128,128]{3,2,1,0:T(8,128)(2,1)S(1)}, u32[]{:S(2)}, u32[]{:S(2)}) collective-permute-start(bf16[2,4,128,128]{3,2,1,0:T(8,128)(2,1)} %get-tuple-element.84), channel_id=1, source_target_pairs={{0,4},{1,5},{2,6},{3,7},{4,0},{5,1},{6,2},{7,3},{8,12},{9,13},{10,... | collective-permute-start | bytes 786440 | tf_op jit(solution)/shard_map/ppermute | solution.py:122
  23.0 10.6 %collective-permute-start.10 = (bf16[4,128,128]{2,1,0:T(8,128)(2,1)S(1)}, bf16[4,128,128]{2,1,0:T(8,128)(2,1)S(1)}, u32[]{:S(2)}, u32[]{:S(2)}) collective-permute-start(bf16[4,128,128]{2,1,0:T(8,128)(2,1)S(1)} %pad_maximum_fusion.11), channel_id=1, source_target_pairs={{0,1},{1,0},{2,3},{3,2},{4,5},{5,4},{6,7},{7,6},{8,9},{9,8},{10,11... | collective-permute-start | bytes 393224 | tf_op jit(solution)/shard_map/ppermute | solution.py:167
  33.6 25.4 %collective-permute-start.4 = (bf16[2,4,128,128]{3,2,1,0:T(8,128)(2,1)}, bf16[2,4,128,128]{3,2,1,0:T(8,128)(2,1)}, u32[]{:S(2)}, u32[]{:S(2)}) collective-permute-start(bf16[2,4,128,128]{3,2,1,0:T(8,128)(2,1)} %get-tuple-element.85), channel_id=1, source_target_pairs={{0,5},{1,6},{2,7},{3,0},{4,1},{5,2},{6,3},{7,4},{8,13},{9,14},{10,... | collective-permute-start | bytes 786440 | tf_op jit(solution)/shard_map/ppermute | solution.py:122
  34.4 29.0 %collective-permute-start.5 = (bf16[2,4,128,128]{3,2,1,0:T(8,128)(2,1)S(1)}, bf16[2,4,128,128]{3,2,1,0:T(8,128)(2,1)S(1)}, u32[]{:S(2)}, u32[]{:S(2)}) collective-permute-start(bf16[2,4,128,128]{3,2,1,0:T(8,128)(2,1)S(1)} %copy-done.19), channel_id=1, source_target_pairs={{0,6},{1,7},{2,0},{3,1},{4,2},{5,3},{6,4},{7,5},{8,14},{9,15},{10,... | collective-permute-start | bytes 786440 | tf_op jit(solution)/shard_map/ppermute | solution.py:122
  36.7 28.0 %collective-permute-start.6 = (bf16[2,4,128,128]{3,2,1,0:T(8,128)(2,1)}, bf16[2,4,128,128]{3,2,1,0:T(8,128)(2,1)S(1)}, u32[]{:S(2)}, u32[]{:S(2)}) collective-permute-start(bf16[2,4,128,128]{3,2,1,0:T(8,128)(2,1)} %get-tuple-element.78), channel_id=1, source_target_pairs={{0,7},{1,0},{2,1},{3,2},{4,3},{5,4},{6,5},{7,6},{8,15},{9,8},{10,9... | collective-permute-start | bytes 786440 | tf_op jit(solution)/shard_map/ppermute | solution.py:122
  74.3 4.7 %collective-permute-start.11 = (bf16[4,8,128,128]{3,2,1,0:T(8,128)(2,1)S(1)}, bf16[4,8,128,128]{3,2,1,0:T(8,128)(2,1)S(1)}, u32[]{:S(2)}, u32[]{:S(2)}) collective-permute-start(bf16[4,8,128,128]{3,2,1,0:T(8,128)(2,1)S(1)} %add_convert_fusion.3), channel_id=1, source_target_pairs={{24,16},{25,17},{26,18},{27,19},{28,20},{29,21},{30,22},{31,23}} | collective-permute-start | bytes 3145736 | tf_op jit(solution)/shard_map/ppermute | solution.py:196
  81.7 27.1 %collective-permute-start.12 = (bf16[4,8,128,128]{3,2,1,0:T(8,128)(2,1)}, bf16[4,8,128,128]{3,2,1,0:T(8,128)(2,1)}, u32[]{:S(2)}, u32[]{:S(2)}) collective-permute-start(bf16[4,8,128,128]{3,2,1,0:T(8,128)(2,1)} %add_convert_fusion.2), channel_id=1, source_target_pairs={{16,8},{17,9},{18,10},{19,11},{20,12},{21,13},{22,14},{23,15}} | collective-permute-start | bytes 3145736 | tf_op jit(solution)/shard_map/ppermute | solution.py:196
  84.1 14.2 %collective-permute-start.14 = (bf16[4,128,128]{2,1,0:T(8,128)(2,1)}, bf16[4,128,128]{2,1,0:T(8,128)(2,1)}, u32[]{:S(2)}, u32[]{:S(2)}) collective-permute-start(bf16[4,128,128]{2,1,0:T(8,128)(2,1)} %get-tuple-element.92), channel_id=1, source_target_pairs={{24,25},{25,26},{26,27},{27,28},{28,29},{29,30},{30,31},{31,24}} | collective-permute-start | bytes 393224 | tf_op jit(solution)/shard_map/ppermute | solution.py:127
  86.0 17.3 %collective-permute-start.15 = (bf16[4,128,128]{2,1,0:T(8,128)(2,1)}, bf16[4,128,128]{2,1,0:T(8,128)(2,1)}, u32[]{:S(2)}, u32[]{:S(2)}) collective-permute-start(bf16[4,128,128]{2,1,0:T(8,128)(2,1)} %get-tuple-element.91), channel_id=1, source_target_pairs={{24,26},{25,27},{26,28},{27,29},{28,30},{29,31},{30,24},{31,25}} | collective-permute-start | bytes 393224 | tf_op jit(solution)/shard_map/ppermute | solution.py:127
  87.9 28.6 %collective-permute-start.16 = (bf16[4,128,128]{2,1,0:T(8,128)(2,1)}, bf16[4,128,128]{2,1,0:T(8,128)(2,1)}, u32[]{:S(2)}, u32[]{:S(2)}) collective-permute-start(bf16[4,128,128]{2,1,0:T(8,128)(2,1)} %get-tuple-element.90), channel_id=1, source_target_pairs={{24,27},{25,28},{26,29},{27,30},{28,31},{29,24},{30,25},{31,26}} | collective-permute-start | bytes 393224 | tf_op jit(solution)/shard_map/ppermute | solution.py:127
  93.3 25.6 %collective-permute-start.17 = (bf16[4,128,128]{2,1,0:T(8,128)(2,1)}, bf16[4,128,128]{2,1,0:T(8,128)(2,1)}, u32[]{:S(2)}, u32[]{:S(2)}) collective-permute-start(bf16[4,128,128]{2,1,0:T(8,128)(2,1)} %get-tuple-element.89), channel_id=1, source_target_pairs={{24,28},{25,29},{26,30},{27,31},{28,24},{29,25},{30,26},{31,27}} | collective-permute-start | bytes 393224 | tf_op jit(solution)/shard_map/ppermute | solution.py:127
  98.3 22.2 %collective-permute-start.18 = (bf16[4,128,128]{2,1,0:T(8,128)(2,1)S(1)}, bf16[4,128,128]{2,1,0:T(8,128)(2,1)S(1)}, u32[]{:S(2)}, u32[]{:S(2)}) collective-permute-start(bf16[4,128,128]{2,1,0:T(8,128)(2,1)S(1)} %get-tuple-element.88), channel_id=1, source_target_pairs={{24,29},{25,30},{26,31},{27,24},{28,25},{29,26},{30,27},{31,28}} | collective-permute-start | bytes 393224 | tf_op jit(solution)/shard_map/ppermute | solution.py:127
  103.3 17.8 %collective-permute-start.19 = (bf16[4,128,128]{2,1,0:T(8,128)(2,1)S(1)}, bf16[4,128,128]{2,1,0:T(8,128)(2,1)S(1)}, u32[]{:S(2)}, u32[]{:S(2)}) collective-permute-start(bf16[4,128,128]{2,1,0:T(8,128)(2,1)S(1)} %get-tuple-element.87), channel_id=1, source_target_pairs={{24,30},{25,31},{26,24},{27,25},{28,26},{29,27},{30,28},{31,29}} | collective-permute-start | bytes 393224 | tf_op jit(solution)/shard_map/ppermute | solution.py:127
  108.7 13.1 %collective-permute-start.20 = (bf16[4,128,128]{2,1,0:T(8,128)(2,1)S(1)}, bf16[4,128,128]{2,1,0:T(8,128)(2,1)S(1)}, u32[]{:S(2)}, u32[]{:S(2)}) collective-permute-start(bf16[4,128,128]{2,1,0:T(8,128)(2,1)S(1)} %get-tuple-element.86), channel_id=1, source_target_pairs={{24,31},{25,24},{26,25},{27,26},{28,27},{29,28},{30,29},{31,30}} | collective-permute-start | bytes 393224 | tf_op jit(solution)/shard_map/ppermute | solution.py:127
  116.6 7.3 %collective-permute-start.13 = (bf16[4,8,128,128]{3,2,1,0:T(8,128)(2,1)S(1)}, bf16[4,8,128,128]{3,2,1,0:T(8,128)(2,1)S(1)}, u32[]{:S(2)}, u32[]{:S(2)}) collective-permute-start(bf16[4,8,128,128]{3,2,1,0:T(8,128)(2,1)S(1)} %add_convert_fusion.1), channel_id=1, source_target_pairs={{8,0},{9,1},{10,2},{11,3},{12,4},{13,5},{14,6},{15,7}} | collective-permute-start | bytes 3145736 | tf_op jit(solution)/shard_map/ppermute | solution.py:196
  133.4 10.5 %collective-permute-start.21 = (bf16[2,128,4,128]{3,1,2,0:T(8,128)(2,1)S(1)}, bf16[2,128,4,128]{3,1,2,0:T(8,128)(2,1)S(1)}, u32[]{:S(2)}, u32[]{:S(2)}) collective-permute-start(bf16[2,128,4,128]{3,1,2,0:T(8,128)(2,1)S(1)} %get-tuple-element.70), channel_id=1, source_target_pairs={{0,1},{1,2},{2,3},{3,4},{4,5},{5,6},{6,7},{7,0},{8,9},{9,10},{10,1... | collective-permute-start | bytes 786440 | tf_op jit(solution)/shard_map/ppermute | solution.py:122
  134.3 26.3 %collective-permute-start.22 = (bf16[2,128,4,128]{3,1,2,0:T(8,128)(2,1)S(1)}, bf16[2,128,4,128]{3,1,2,0:T(8,128)(2,1)S(1)}, u32[]{:S(2)}, u32[]{:S(2)}) collective-permute-start(bf16[2,128,4,128]{3,1,2,0:T(8,128)(2,1)S(1)} %get-tuple-element.71), channel_id=1, source_target_pairs={{0,2},{1,3},{2,4},{3,5},{4,6},{5,7},{6,0},{7,1},{8,10},{9,11},{10,... | collective-permute-start | bytes 786440 | tf_op jit(solution)/shard_map/ppermute | solution.py:122
  134.3 34.5 %collective-permute-start.23 = (bf16[2,128,4,128]{3,1,2,0:T(8,128)(2,1)S(1)}, bf16[2,128,4,128]{3,1,2,0:T(8,128)(2,1)S(1)}, u32[]{:S(2)}, u32[]{:S(2)}) collective-permute-start(bf16[2,128,4,128]{3,1,2,0:T(8,128)(2,1)S(1)} %get-tuple-element.72), channel_id=1, source_target_pairs={{0,3},{1,4},{2,5},{3,6},{4,7},{5,0},{6,1},{7,2},{8,11},{9,12},{10,... | collective-permute-start | bytes 786440 | tf_op jit(solution)/shard_map/ppermute | solution.py:122
  136.7 32.2 %collective-permute-start.24 = (bf16[2,128,4,128]{3,1,2,0:T(8,128)(2,1)S(1)}, bf16[2,128,4,128]{3,1,2,0:T(8,128)(2,1)S(1)}, u32[]{:S(2)}, u32[]{:S(2)}) collective-permute-start(bf16[2,128,4,128]{3,1,2,0:T(8,128)(2,1)S(1)} %get-tuple-element.73), channel_id=1, source_target_pairs={{0,4},{1,5},{2,6},{3,7},{4,0},{5,1},{6,2},{7,3},{8,12},{9,13},{10,... | collective-permute-start | bytes 786440 | tf_op jit(solution)/shard_map/ppermute | solution.py:122
  137.0 33.1 %collective-permute-start.25 = (bf16[2,128,4,128]{3,1,2,0:T(8,128)(2,1)S(1)}, bf16[2,128,4,128]{3,1,2,0:T(8,128)(2,1)S(1)}, u32[]{:S(2)}, u32[]{:S(2)}) collective-permute-start(bf16[2,128,4,128]{3,1,2,0:T(8,128)(2,1)S(1)} %get-tuple-element.75), channel_id=1, source_target_pairs={{0,5},{1,6},{2,7},{3,0},{4,1},{5,2},{6,3},{7,4},{8,13},{9,14},{10,... | collective-permute-start | bytes 786440 | tf_op jit(solution)/shard_map/ppermute | solution.py:122
  143.8 27.0 %collective-permute-start.26 = (bf16[2,128,4,128]{3,1,2,0:T(8,128)(2,1)S(1)}, bf16[2,128,4,128]{3,1,2,0:T(8,128)(2,1)S(1)}, u32[]{:S(2)}, u32[]{:S(2)}) collective-permute-start(bf16[2,128,4,128]{3,1,2,0:T(8,128)(2,1)S(1)} %get-tuple-element.74), channel_id=1, source_target_pairs={{0,6},{1,7},{2,0},{3,1},{4,2},{5,3},{6,4},{7,5},{8,14},{9,15},{10,... | collective-permute-start | bytes 786440 | tf_op jit(solution)/shard_map/ppermute | solution.py:122
  160.6 7.7 %collective-permute-start.28 = (f32[4,128,128]{2,1,0:T(8,128)S(1)}, f32[4,128,128]{2,1,0:T(8,128)S(1)}, u32[]{:S(2)}, u32[]{:S(2)}) collective-permute-start(f32[4,128,128]{2,1,0:T(8,128)S(1)} %dynamic-slice_bitcast_fusion), channel_id=1, source_target_pairs={{0,1},{1,0},{2,3},{3,2},{4,5},{5,4},{6,7},{7,6},{8,9},{9,8},{10,11... | collective-permute-start | bytes 786440 | tf_op jit(solution)/shard_map/ppermute | solution.py:231
  168.3 6.8 %collective-permute-start.27 = (bf16[2,128,4,128]{3,1,2,0:T(8,128)(2,1)S(1)}, bf16[2,128,4,128]{3,1,2,0:T(8,128)(2,1)S(1)}, u32[]{:S(2)}, u32[]{:S(2)}) collective-permute-start(bf16[2,128,4,128]{3,1,2,0:T(8,128)(2,1)S(1)} %get-tuple-element.68), channel_id=1, source_target_pairs={{0,7},{1,0},{2,1},{3,2},{4,3},{5,4},{6,5},{7,6},{8,15},{9,8},{10,9... | collective-permute-start | bytes 786440 | tf_op jit(solution)/shard_map/ppermute | solution.py:122
  168.8 10.0 %collective-permute-start.29 = (bf16[128,128]{1,0:T(8,128)(2,1)S(1)}, bf16[128,128]{1,0:T(8,128)(2,1)S(1)}, u32[]{:S(2)}, u32[]{:S(2)}) collective-permute-start(bf16[128,128]{1,0:T(8,128)(2,1)S(1)} %get-tuple-element.116), channel_id=1, source_target_pairs={{0,2},{1,3},{2,4},{3,5},{4,6},{5,7},{6,0},{7,1},{8,10},{9,11},{10,... | collective-permute-start | bytes 98312 | tf_op jit(solution)/shard_map/ppermute | solution.py:238
  168.9 9.9 %collective-permute-start.30 = (bf16[128,128]{1,0:T(8,128)(2,1)S(1)}, bf16[128,128]{1,0:T(8,128)(2,1)S(1)}, u32[]{:S(2)}, u32[]{:S(2)}) collective-permute-start(bf16[128,128]{1,0:T(8,128)(2,1)S(1)} %get-tuple-element.115), channel_id=1, source_target_pairs={{0,4},{1,5},{2,6},{3,7},{4,0},{5,1},{6,2},{7,3},{8,12},{9,13},{10,... | collective-permute-start | bytes 98312 | tf_op jit(solution)/shard_map/ppermute | solution.py:238
  170.1 8.7 %collective-permute-start.31 = (bf16[128,128]{1,0:T(8,128)(2,1)S(1)}, bf16[128,128]{1,0:T(8,128)(2,1)S(1)}, u32[]{:S(2)}, u32[]{:S(2)}) collective-permute-start(bf16[128,128]{1,0:T(8,128)(2,1)S(1)} %get-tuple-element.114), channel_id=1, source_target_pairs={{0,6},{1,7},{2,0},{3,1},{4,2},{5,3},{6,4},{7,5},{8,14},{9,15},{10,... | collective-permute-start | bytes 98312 | tf_op jit(solution)/shard_map/ppermute | solution.py:238
  (25 other events, 83.2 us)

commit v18 on v16

--- a/solution.py
+++ b/solution.py
@@ -235,7 +235,7 @@
             received.append(chunk)
         heads_in = jnp.arange(kv_count)
         order = ((seq_index - 2 * heads_in - parity) % seq_ways) // 2
-        key_sum = jnp.transpose(jnp.take(jnp.stack(received), order, axis=0), (1, 0, 2))
+        key_sum = jnp.take(jnp.stack(received, axis=1), order, axis=1)
     else:
         key_out = lax.all_to_all(
             key_part[:, None, :], "seq", split_axis=0, concat_axis=1, tiled=True

time: 180 us -> 180 us (level)
  no operation moved by 1% of the time
where the time goes in v18:
time: 180 us; the launch traced here: 178 us
  waiting for transfers between devices  61.5 us (34%)
  starting transfers between devices  48.4 us (27%)
  local copies, waits for them, and re-layouts  39.9 us (22%)
  other arithmetic  17.5 us (10%)
  matrix products  8.84 us (5%)
    ppermute x14, waiting for transfers between devices, transpose_seq(): lax.ppermute(chunk, 'seq', [(s, (s + shift) % seq_ways) for s in range(se...  50 us
    ppermute x7, starting transfers between devices, transpose_seq(): lax.ppermute(chunk, ('pipe', 'seq'), [(base + s, base + (s + shift) % seq...  22 us
    dynamic_update_slice x23, local copies, waits for them, and re-layouts, transpose_seq(): lax.dynamic_update_slice_in_dim(result, chunk, source * concat_size, axis...  14.5 us
    unnamed x58, local copies, waits for them, and re-layouts  11.9 us
    ppermute x14, starting transfers between devices, transpose_seq(): lax.ppermute(chunk, 'seq', [(s, (s + shift) % seq_ways) for s in range(se...  11.5 us
    ppermute x1, waiting for transfers between devices, on_device(): theirs = lax.ppermute(mine, 'seq', [(d, d ^ 1) for d in range(seq_ways)])  9.32 us
    ppermute x6, starting transfers between devices, on_device(): lax.ppermute(chunk, 'seq', [(d, (d + shift) % seq_ways) for d in range(se...  8.13 us
    ppermute x3, starting transfers between devices, on_device(): grad_in = lax.ppermute(new_grad, 'pipe', [(sender, sender - 1)])  4.83 us
  transfers between devices with their start and end apart: 32, of which 10 were waited for; matrix products, arithmetic and copies ran while one was open for 22% of the time, Pallas kernels for 0%

profile of v18, /device:TPU:15, one launch (start us, length us, event | category | flops | bytes accessed | tf_op | source)
XLA Modules:
  0.0 177.9 jit_solution(12221573791006709009)
XLA Ops:
  2.8 2.3 %collective-permute-start.8 = (bf16[128,128]{1,0:T(8,128)(2,1)}, bf16[128,128]{1,0:T(8,128)(2,1)S(1)}, u32[]{:S(2)}, u32[]{:S(2)}) collective-permute-start(bf16[128,128]{1,0:T(8,128)(2,1)} %bitcast.10), channel_id=1, source_target_pairs={{0,4},{1,5},{2,6},{3,7},{4,0},{5,1},{6,2},{7,3},{8,12},{9,13},{10,... | collective-permute-start | bytes 98312 | tf_op jit(solution)/shard_map/ppermute | solution.py:157
  11.1 1.6 fusion.68
  14.9 2.1 %collective-permute-start.1 = (bf16[2,4,128,128]{3,2,1,0:T(8,128)(2,1)}, bf16[2,4,128,128]{3,2,1,0:T(8,128)(2,1)}, u32[]{:S(2)}, u32[]{:S(2)}) collective-permute-start(bf16[2,4,128,128]{3,2,1,0:T(8,128)(2,1)} %get-tuple-element.83), channel_id=1, source_target_pairs={{0,2},{1,3},{2,4},{3,5},{4,6},{5,7},{6,0},{7,1},{8,10},{9,11},{10,... | collective-permute-start | bytes 786440 | tf_op jit(solution)/shard_map/ppermute | solution.py:118
  18.3 1.9 %fusion.34 = (bf16[2,4,128,128]{3,2,1,0:T(8,128)(2,1)}, bf16[2,4,128,128]{3,2,1,0:T(8,128)(2,1)}, bf16[2,4,128,128]{3,2,1,0:T(8,128)(2,1)}) fusion(s32[]{:T(128)S(6)} %select_n.538, bf16[1,32,128,128]{3,2,1,0:T(8,128)(2,1)} %bitcast.143, bf16[1,32,128,128]{3,2,1,0:T(8,128)(2,1)S(1)} %get-tuple-element.96, s32[]{:T(128)S(6)} %select_n.534, s32[]{:T(128)S(6)} %select_n.536), kind=kLoop, calls=%fused_computation.97 | loop fusion | flops 393216 | bytes 2883596 | tf_op jit(solution)/shard_map/stack | solution.py:142
  24.3 9.3 %collective-permute-done.10 = bf16[4,128,128]{2,1,0:T(8,128)(2,1)S(1)} collective-permute-done((bf16[4,128,128]{2,1,0:T(8,128)(2,1)S(1)}, bf16[4,128,128]{2,1,0:T(8,128)(2,1)S(1)}, u32[]{:S(2)}, u32[]{:S(2)}) %collective-permute-start.10) | collective-permute-done | bytes 131104 | tf_op jit(solution)/shard_map/ppermute | solution.py:162
  38.6 14.7 %collective-permute-done.2 = bf16[2,4,128,128]{3,2,1,0:T(8,128)(2,1)S(1)} collective-permute-done((bf16[2,4,128,128]{3,2,1,0:T(8,128)(2,1)}, bf16[2,4,128,128]{3,2,1,0:T(8,128)(2,1)S(1)}, u32[]{:S(2)}, u32[]{:S(2)}) %collective-permute-start.2) | collective-permute-done | bytes 262176 | tf_op jit(solution)/shard_map/ppermute | solution.py:118
  53.3 5.6 %collective-permute-done.3 = bf16[2,4,128,128]{3,2,1,0:T(8,128)(2,1)S(1)} collective-permute-done((bf16[2,4,128,128]{3,2,1,0:T(8,128)(2,1)}, bf16[2,4,128,128]{3,2,1,0:T(8,128)(2,1)S(1)}, u32[]{:S(2)}, u32[]{:S(2)}) %collective-permute-start.3) | collective-permute-done | bytes 262176 | tf_op jit(solution)/shard_map/ppermute | solution.py:118
  59.9 3.5 %collective-permute-done.5 = bf16[2,4,128,128]{3,2,1,0:T(8,128)(2,1)S(1)} collective-permute-done((bf16[2,4,128,128]{3,2,1,0:T(8,128)(2,1)S(1)}, bf16[2,4,128,128]{3,2,1,0:T(8,128)(2,1)S(1)}, u32[]{:S(2)}, u32[]{:S(2)}) %collective-permute-start.5) | collective-permute-done | bytes 262176 | tf_op jit(solution)/shard_map/ppermute | solution.py:118
  68.8 2.2 %fusion.69 = (f32[4,8,128]{2,1,0:T(8,128)S(1)}, f32[4,8,128,256]{3,2,1,0:T(8,128)S(1)}) fusion(f32[4,8,128,256]{3,2,1,0:T(8,128)S(1)} %fusion.3, pred[8,128,256]{2,1,0:T(8,128)(4,1)S(1)} %copy-done.20), kind=kOutput, calls=%fused_computation.246 | output fusion | flops 6291711 | bytes 8667136 | tf_op jit(solution)/shard_map/sub | solution.py:53
  74.6 2.5 %collective-permute-start.11 = (bf16[4,8,128,128]{3,2,1,0:T(8,128)(2,1)S(1)}, bf16[4,8,128,128]{3,2,1,0:T(8,128)(2,1)S(1)}, u32[]{:S(2)}, u32[]{:S(2)}) collective-permute-start(bf16[4,8,128,128]{3,2,1,0:T(8,128)(2,1)S(1)} %add_convert_fusion.3), channel_id=1, source_target_pairs={{24,16},{25,17},{26,18},{27,19},{28,20},{29,21},{30,22},{31,23}} | collective-permute-start | bytes 3145736 | tf_op jit(solution)/shard_map/ppermute | solution.py:191
  77.1 2.2 %collective-permute-done.11 = bf16[4,8,128,128]{3,2,1,0:T(8,128)(2,1)S(1)} collective-permute-done((bf16[4,8,128,128]{3,2,1,0:T(8,128)(2,1)S(1)}, bf16[4,8,128,128]{3,2,1,0:T(8,128)(2,1)S(1)}, u32[]{:S(2)}, u32[]{:S(2)}) %collective-permute-start.11) | collective-permute-done | bytes 1048608 | tf_op jit(solution)/shard_map/ppermute | solution.py:191
  82.0 1.6 collective-permute-start.12
  84.4 1.9 %collective-permute-start.14 = (bf16[4,128,128]{2,1,0:T(8,128)(2,1)}, bf16[4,128,128]{2,1,0:T(8,128)(2,1)}, u32[]{:S(2)}, u32[]{:S(2)}) collective-permute-start(bf16[4,128,128]{2,1,0:T(8,128)(2,1)} %get-tuple-element.94), channel_id=1, source_target_pairs={{24,25},{25,26},{26,27},{27,28},{28,29},{29,30},{30,31},{31,24}} | collective-permute-start | bytes 393224 | tf_op jit(solution)/shard_map/ppermute | solution.py:123
  86.4 1.9 %collective-permute-start.15 = (bf16[4,128,128]{2,1,0:T(8,128)(2,1)}, bf16[4,128,128]{2,1,0:T(8,128)(2,1)}, u32[]{:S(2)}, u32[]{:S(2)}) collective-permute-start(bf16[4,128,128]{2,1,0:T(8,128)(2,1)} %get-tuple-element.93), channel_id=1, source_target_pairs={{24,26},{25,27},{26,28},{27,29},{28,30},{29,31},{30,24},{31,25}} | collective-permute-start | bytes 393224 | tf_op jit(solution)/shard_map/ppermute | solution.py:123
  88.3 5.4 %collective-permute-start.16 = (bf16[4,128,128]{2,1,0:T(8,128)(2,1)}, bf16[4,128,128]{2,1,0:T(8,128)(2,1)}, u32[]{:S(2)}, u32[]{:S(2)}) collective-permute-start(bf16[4,128,128]{2,1,0:T(8,128)(2,1)} %get-tuple-element.92), channel_id=1, source_target_pairs={{24,27},{25,28},{26,29},{27,30},{28,31},{29,24},{30,25},{31,26}} | collective-permute-start | bytes 393224 | tf_op jit(solution)/shard_map/ppermute | solution.py:123
  93.7 1.9 %collective-permute-start.17 = (bf16[4,128,128]{2,1,0:T(8,128)(2,1)}, bf16[4,128,128]{2,1,0:T(8,128)(2,1)}, u32[]{:S(2)}, u32[]{:S(2)}) collective-permute-start(bf16[4,128,128]{2,1,0:T(8,128)(2,1)} %get-tuple-element.91), channel_id=1, source_target_pairs={{24,28},{25,29},{26,30},{27,31},{28,24},{29,25},{30,26},{31,27}} | collective-permute-start | bytes 393224 | tf_op jit(solution)/shard_map/ppermute | solution.py:123
  98.7 3.5 %collective-permute-start.18 = (bf16[4,128,128]{2,1,0:T(8,128)(2,1)S(1)}, bf16[4,128,128]{2,1,0:T(8,128)(2,1)S(1)}, u32[]{:S(2)}, u32[]{:S(2)}) collective-permute-start(bf16[4,128,128]{2,1,0:T(8,128)(2,1)S(1)} %get-tuple-element.90), channel_id=1, source_target_pairs={{24,29},{25,30},{26,31},{27,24},{28,25},{29,26},{30,27},{31,28}} | collective-permute-start | bytes 393224 | tf_op jit(solution)/shard_map/ppermute | solution.py:123
  102.2 1.6 constant_dynamic-update-slice_fusion.6
  103.8 3.8 %collective-permute-start.19 = (bf16[4,128,128]{2,1,0:T(8,128)(2,1)S(1)}, bf16[4,128,128]{2,1,0:T(8,128)(2,1)S(1)}, u32[]{:S(2)}, u32[]{:S(2)}) collective-permute-start(bf16[4,128,128]{2,1,0:T(8,128)(2,1)S(1)} %get-tuple-element.89), channel_id=1, source_target_pairs={{24,30},{25,31},{26,24},{27,25},{28,26},{29,27},{30,28},{31,29}} | collective-permute-start | bytes 393224 | tf_op jit(solution)/shard_map/ppermute | solution.py:123
  107.7 1.6 constant_dynamic-update-slice_fusion.5
  109.2 3.5 %collective-permute-start.20 = (bf16[4,128,128]{2,1,0:T(8,128)(2,1)S(1)}, bf16[4,128,128]{2,1,0:T(8,128)(2,1)S(1)}, u32[]{:S(2)}, u32[]{:S(2)}) collective-permute-start(bf16[4,128,128]{2,1,0:T(8,128)(2,1)S(1)} %get-tuple-element.88), channel_id=1, source_target_pairs={{24,31},{25,24},{26,25},{27,26},{28,27},{29,28},{30,29},{31,30}} | collective-permute-start | bytes 393224 | tf_op jit(solution)/shard_map/ppermute | solution.py:123
  112.8 2.0 %fusion.72 = f32[4,8,256,128]{3,2,1,0:T(8,128)S(1)} fusion(bf16[4,8,128,256]{3,2,1,0:T(8,128)(2,1)S(1)} %fusion.8, bf16[4,8,128,128]{3,2,1,0:T(8,128)(2,1)} %collective-permute-done.12), kind=kOutput, calls=%fused_computation.249 | convolution fusion | flops 268435456 | bytes 7340032 | tf_op jit(solution)/shard_map/hbij,hbid->hbjd/dot_general | solution.py:58
  115.4 1.7 add_convert_fusion.1
  117.8 1.6 constant_dynamic-update-slice_fusion.4
  119.4 1.6 constant_dynamic-update-slice_fusion.3
  130.0 1.6 multiply_convert_fusion
  138.4 2.1 %collective-permute-start.23 = (bf16[2,128,4,128]{3,1,2,0:T(8,128)(2,1)S(1)}, bf16[2,128,4,128]{3,1,2,0:T(8,128)(2,1)S(1)}, u32[]{:S(2)}, u32[]{:S(2)}) collective-permute-start(bf16[2,128,4,128]{3,1,2,0:T(8,128)(2,1)S(1)} %get-tuple-element.74), channel_id=1, source_target_pairs={{0,3},{1,4},{2,5},{3,6},{4,7},{5,0},{6,1},{7,2},{8,11},{9,12},{10,... | collective-permute-start | bytes 786440 | tf_op jit(solution)/shard_map/ppermute | solution.py:118
  141.0 8.5 %collective-permute-done.21 = bf16[2,128,4,128]{3,1,2,0:T(8,128)(2,1)S(1)} collective-permute-done((bf16[2,128,4,128]{3,1,2,0:T(8,128)(2,1)S(1)}, bf16[2,128,4,128]{3,1,2,0:T(8,128)(2,1)S(1)}, u32[]{:S(2)}, u32[]{:S(2)}) %collective-permute-start.21) | collective-permute-done | bytes 262176 | tf_op jit(solution)/shard_map/ppermute | solution.py:118
  149.8 12.4 %collective-permute-done.22 = bf16[2,128,4,128]{3,1,2,0:T(8,128)(2,1)S(1)} collective-permute-done((bf16[2,128,4,128]{3,1,2,0:T(8,128)(2,1)S(1)}, bf16[2,128,4,128]{3,1,2,0:T(8,128)(2,1)S(1)}, u32[]{:S(2)}, u32[]{:S(2)}) %collective-permute-start.22) | collective-permute-done | bytes 262176 | tf_op jit(solution)/shard_map/ppermute | solution.py:118
  163.2 2.6 %collective-permute-done.23 = bf16[2,128,4,128]{3,1,2,0:T(8,128)(2,1)S(1)} collective-permute-done((bf16[2,128,4,128]{3,1,2,0:T(8,128)(2,1)S(1)}, bf16[2,128,4,128]{3,1,2,0:T(8,128)(2,1)S(1)}, u32[]{:S(2)}, u32[]{:S(2)}) %collective-permute-start.23) | collective-permute-done | bytes 262176 | tf_op jit(solution)/shard_map/ppermute | solution.py:118
  167.5 1.5 collective-permute-done.24
  169.0 2.9 %collective-permute-start.30 = (bf16[128,128]{1,0:T(8,128)(2,1)S(1)}, bf16[128,128]{1,0:T(8,128)(2,1)S(1)}, u32[]{:S(2)}, u32[]{:S(2)}) collective-permute-start(bf16[128,128]{1,0:T(8,128)(2,1)S(1)} %get-tuple-element.101), channel_id=1, source_target_pairs={{0,4},{1,5},{2,6},{3,7},{4,0},{5,1},{6,2},{7,3},{8,12},{9,13},{10,... | collective-permute-start | bytes 98312 | tf_op jit(solution)/shard_map/ppermute | solution.py:232
  (194 shorter events, 63.1 us)
Async XLA Ops:
  2.8 18.7 %collective-permute-start.8 = (bf16[128,128]{1,0:T(8,128)(2,1)}, bf16[128,128]{1,0:T(8,128)(2,1)S(1)}, u32[]{:S(2)}, u32[]{:S(2)}) collective-permute-start(bf16[128,128]{1,0:T(8,128)(2,1)} %bitcast.10), channel_id=1, source_target_pairs={{0,4},{1,5},{2,6},{3,7},{4,0},{5,1},{6,2},{7,3},{8,12},{9,13},{10,... | collective-permute-start | bytes 98312 | tf_op jit(solution)/shard_map/ppermute | solution.py:157
  5.8 17.1 %collective-permute-start.9 = (bf16[128,128]{1,0:T(8,128)(2,1)}, bf16[128,128]{1,0:T(8,128)(2,1)S(1)}, u32[]{:S(2)}, u32[]{:S(2)}) collective-permute-start(bf16[128,128]{1,0:T(8,128)(2,1)} %bitcast.12), channel_id=1, source_target_pairs={{0,6},{1,7},{2,0},{3,1},{4,2},{5,3},{6,4},{7,5},{8,14},{9,15},{10,... | collective-permute-start | bytes 98312 | tf_op jit(solution)/shard_map/ppermute | solution.py:157
  6.7 16.3 %collective-permute-start.7 = (bf16[128,128]{1,0:T(8,128)(2,1)}, bf16[128,128]{1,0:T(8,128)(2,1)S(1)}, u32[]{:S(2)}, u32[]{:S(2)}) collective-permute-start(bf16[128,128]{1,0:T(8,128)(2,1)} %bitcast.8), channel_id=1, source_target_pairs={{0,2},{1,3},{2,4},{3,5},{4,6},{5,7},{6,0},{7,1},{8,10},{9,11},{10,... | collective-permute-start | bytes 98312 | tf_op jit(solution)/shard_map/ppermute | solution.py:157
  14.9 19.5 %collective-permute-start = (bf16[2,4,128,128]{3,2,1,0:T(8,128)(2,1)}, bf16[2,4,128,128]{3,2,1,0:T(8,128)(2,1)}, u32[]{:S(2)}, u32[]{:S(2)}) collective-permute-start(bf16[2,4,128,128]{3,2,1,0:T(8,128)(2,1)} %get-tuple-element.82), channel_id=1, source_target_pairs={{0,1},{1,2},{2,3},{3,4},{4,5},{5,6},{6,7},{7,0},{8,9},{9,10},{10,1... | collective-permute-start | bytes 786440 | tf_op jit(solution)/shard_map/ppermute | solution.py:118
  14.9 21.7 %collective-permute-start.1 = (bf16[2,4,128,128]{3,2,1,0:T(8,128)(2,1)}, bf16[2,4,128,128]{3,2,1,0:T(8,128)(2,1)}, u32[]{:S(2)}, u32[]{:S(2)}) collective-permute-start(bf16[2,4,128,128]{3,2,1,0:T(8,128)(2,1)} %get-tuple-element.83), channel_id=1, source_target_pairs={{0,2},{1,3},{2,4},{3,5},{4,6},{5,7},{6,0},{7,1},{8,10},{9,11},{10,... | collective-permute-start | bytes 786440 | tf_op jit(solution)/shard_map/ppermute | solution.py:118
  21.4 31.8 %collective-permute-start.2 = (bf16[2,4,128,128]{3,2,1,0:T(8,128)(2,1)}, bf16[2,4,128,128]{3,2,1,0:T(8,128)(2,1)S(1)}, u32[]{:S(2)}, u32[]{:S(2)}) collective-permute-start(bf16[2,4,128,128]{3,2,1,0:T(8,128)(2,1)} %get-tuple-element.84), channel_id=1, source_target_pairs={{0,3},{1,4},{2,5},{3,6},{4,7},{5,0},{6,1},{7,2},{8,11},{9,12},{10,... | collective-permute-start | bytes 786440 | tf_op jit(solution)/shard_map/ppermute | solution.py:118
  22.9 36.0 %collective-permute-start.3 = (bf16[2,4,128,128]{3,2,1,0:T(8,128)(2,1)}, bf16[2,4,128,128]{3,2,1,0:T(8,128)(2,1)S(1)}, u32[]{:S(2)}, u32[]{:S(2)}) collective-permute-start(bf16[2,4,128,128]{3,2,1,0:T(8,128)(2,1)} %get-tuple-element.86), channel_id=1, source_target_pairs={{0,4},{1,5},{2,6},{3,7},{4,0},{5,1},{6,2},{7,3},{8,12},{9,13},{10,... | collective-permute-start | bytes 786440 | tf_op jit(solution)/shard_map/ppermute | solution.py:118
  23.0 10.6 %collective-permute-start.10 = (bf16[4,128,128]{2,1,0:T(8,128)(2,1)S(1)}, bf16[4,128,128]{2,1,0:T(8,128)(2,1)S(1)}, u32[]{:S(2)}, u32[]{:S(2)}) collective-permute-start(bf16[4,128,128]{2,1,0:T(8,128)(2,1)S(1)} %pad_maximum_fusion.11), channel_id=1, source_target_pairs={{0,1},{1,0},{2,3},{3,2},{4,5},{5,4},{6,7},{7,6},{8,9},{9,8},{10,11... | collective-permute-start | bytes 393224 | tf_op jit(solution)/shard_map/ppermute | solution.py:162
  33.6 25.3 %collective-permute-start.4 = (bf16[2,4,128,128]{3,2,1,0:T(8,128)(2,1)}, bf16[2,4,128,128]{3,2,1,0:T(8,128)(2,1)}, u32[]{:S(2)}, u32[]{:S(2)}) collective-permute-start(bf16[2,4,128,128]{3,2,1,0:T(8,128)(2,1)} %get-tuple-element.87), channel_id=1, source_target_pairs={{0,5},{1,6},{2,7},{3,0},{4,1},{5,2},{6,3},{7,4},{8,13},{9,14},{10,... | collective-permute-start | bytes 786440 | tf_op jit(solution)/shard_map/ppermute | solution.py:118
  34.4 29.1 %collective-permute-start.5 = (bf16[2,4,128,128]{3,2,1,0:T(8,128)(2,1)S(1)}, bf16[2,4,128,128]{3,2,1,0:T(8,128)(2,1)S(1)}, u32[]{:S(2)}, u32[]{:S(2)}) collective-permute-start(bf16[2,4,128,128]{3,2,1,0:T(8,128)(2,1)S(1)} %copy-done.19), channel_id=1, source_target_pairs={{0,6},{1,7},{2,0},{3,1},{4,2},{5,3},{6,4},{7,5},{8,14},{9,15},{10,... | collective-permute-start | bytes 786440 | tf_op jit(solution)/shard_map/ppermute | solution.py:118
  36.6 28.0 %collective-permute-start.6 = (bf16[2,4,128,128]{3,2,1,0:T(8,128)(2,1)}, bf16[2,4,128,128]{3,2,1,0:T(8,128)(2,1)S(1)}, u32[]{:S(2)}, u32[]{:S(2)}) collective-permute-start(bf16[2,4,128,128]{3,2,1,0:T(8,128)(2,1)} %get-tuple-element.80), channel_id=1, source_target_pairs={{0,7},{1,0},{2,1},{3,2},{4,3},{5,4},{6,5},{7,6},{8,15},{9,8},{10,9... | collective-permute-start | bytes 786440 | tf_op jit(solution)/shard_map/ppermute | solution.py:118
  74.6 4.7 %collective-permute-start.11 = (bf16[4,8,128,128]{3,2,1,0:T(8,128)(2,1)S(1)}, bf16[4,8,128,128]{3,2,1,0:T(8,128)(2,1)S(1)}, u32[]{:S(2)}, u32[]{:S(2)}) collective-permute-start(bf16[4,8,128,128]{3,2,1,0:T(8,128)(2,1)S(1)} %add_convert_fusion.3), channel_id=1, source_target_pairs={{24,16},{25,17},{26,18},{27,19},{28,20},{29,21},{30,22},{31,23}} | collective-permute-start | bytes 3145736 | tf_op jit(solution)/shard_map/ppermute | solution.py:191
  82.0 27.3 %collective-permute-start.12 = (bf16[4,8,128,128]{3,2,1,0:T(8,128)(2,1)}, bf16[4,8,128,128]{3,2,1,0:T(8,128)(2,1)}, u32[]{:S(2)}, u32[]{:S(2)}) collective-permute-start(bf16[4,8,128,128]{3,2,1,0:T(8,128)(2,1)} %add_convert_fusion.2), channel_id=1, source_target_pairs={{16,8},{17,9},{18,10},{19,11},{20,12},{21,13},{22,14},{23,15}} | collective-permute-start | bytes 3145736 | tf_op jit(solution)/shard_map/ppermute | solution.py:191
  84.4 14.3 %collective-permute-start.14 = (bf16[4,128,128]{2,1,0:T(8,128)(2,1)}, bf16[4,128,128]{2,1,0:T(8,128)(2,1)}, u32[]{:S(2)}, u32[]{:S(2)}) collective-permute-start(bf16[4,128,128]{2,1,0:T(8,128)(2,1)} %get-tuple-element.94), channel_id=1, source_target_pairs={{24,25},{25,26},{26,27},{27,28},{28,29},{29,30},{30,31},{31,24}} | collective-permute-start | bytes 393224 | tf_op jit(solution)/shard_map/ppermute | solution.py:123
  86.4 17.5 %collective-permute-start.15 = (bf16[4,128,128]{2,1,0:T(8,128)(2,1)}, bf16[4,128,128]{2,1,0:T(8,128)(2,1)}, u32[]{:S(2)}, u32[]{:S(2)}) collective-permute-start(bf16[4,128,128]{2,1,0:T(8,128)(2,1)} %get-tuple-element.93), channel_id=1, source_target_pairs={{24,26},{25,27},{26,28},{27,29},{28,30},{29,31},{30,24},{31,25}} | collective-permute-start | bytes 393224 | tf_op jit(solution)/shard_map/ppermute | solution.py:123
  88.3 28.8 %collective-permute-start.16 = (bf16[4,128,128]{2,1,0:T(8,128)(2,1)}, bf16[4,128,128]{2,1,0:T(8,128)(2,1)}, u32[]{:S(2)}, u32[]{:S(2)}) collective-permute-start(bf16[4,128,128]{2,1,0:T(8,128)(2,1)} %get-tuple-element.92), channel_id=1, source_target_pairs={{24,27},{25,28},{26,29},{27,30},{28,31},{29,24},{30,25},{31,26}} | collective-permute-start | bytes 393224 | tf_op jit(solution)/shard_map/ppermute | solution.py:123
  93.7 25.7 %collective-permute-start.17 = (bf16[4,128,128]{2,1,0:T(8,128)(2,1)}, bf16[4,128,128]{2,1,0:T(8,128)(2,1)}, u32[]{:S(2)}, u32[]{:S(2)}) collective-permute-start(bf16[4,128,128]{2,1,0:T(8,128)(2,1)} %get-tuple-element.91), channel_id=1, source_target_pairs={{24,28},{25,29},{26,30},{27,31},{28,24},{29,25},{30,26},{31,27}} | collective-permute-start | bytes 393224 | tf_op jit(solution)/shard_map/ppermute | solution.py:123
  98.7 22.3 %collective-permute-start.18 = (bf16[4,128,128]{2,1,0:T(8,128)(2,1)S(1)}, bf16[4,128,128]{2,1,0:T(8,128)(2,1)S(1)}, u32[]{:S(2)}, u32[]{:S(2)}) collective-permute-start(bf16[4,128,128]{2,1,0:T(8,128)(2,1)S(1)} %get-tuple-element.90), channel_id=1, source_target_pairs={{24,29},{25,30},{26,31},{27,24},{28,25},{29,26},{30,27},{31,28}} | collective-permute-start | bytes 393224 | tf_op jit(solution)/shard_map/ppermute | solution.py:123
  103.8 17.8 %collective-permute-start.19 = (bf16[4,128,128]{2,1,0:T(8,128)(2,1)S(1)}, bf16[4,128,128]{2,1,0:T(8,128)(2,1)S(1)}, u32[]{:S(2)}, u32[]{:S(2)}) collective-permute-start(bf16[4,128,128]{2,1,0:T(8,128)(2,1)S(1)} %get-tuple-element.89), channel_id=1, source_target_pairs={{24,30},{25,31},{26,24},{27,25},{28,26},{29,27},{30,28},{31,29}} | collective-permute-start | bytes 393224 | tf_op jit(solution)/shard_map/ppermute | solution.py:123
  109.2 13.1 %collective-permute-start.20 = (bf16[4,128,128]{2,1,0:T(8,128)(2,1)S(1)}, bf16[4,128,128]{2,1,0:T(8,128)(2,1)S(1)}, u32[]{:S(2)}, u32[]{:S(2)}) collective-permute-start(bf16[4,128,128]{2,1,0:T(8,128)(2,1)S(1)} %get-tuple-element.88), channel_id=1, source_target_pairs={{24,31},{25,24},{26,25},{27,26},{28,27},{29,28},{30,29},{31,30}} | collective-permute-start | bytes 393224 | tf_op jit(solution)/shard_map/ppermute | solution.py:123
  117.1 7.3 %collective-permute-start.13 = (bf16[4,8,128,128]{3,2,1,0:T(8,128)(2,1)S(1)}, bf16[4,8,128,128]{3,2,1,0:T(8,128)(2,1)S(1)}, u32[]{:S(2)}, u32[]{:S(2)}) collective-permute-start(bf16[4,8,128,128]{3,2,1,0:T(8,128)(2,1)S(1)} %add_convert_fusion.1), channel_id=1, source_target_pairs={{8,0},{9,1},{10,2},{11,3},{12,4},{13,5},{14,6},{15,7}} | collective-permute-start | bytes 3145736 | tf_op jit(solution)/shard_map/ppermute | solution.py:191
  134.7 14.9 %collective-permute-start.21 = (bf16[2,128,4,128]{3,1,2,0:T(8,128)(2,1)S(1)}, bf16[2,128,4,128]{3,1,2,0:T(8,128)(2,1)S(1)}, u32[]{:S(2)}, u32[]{:S(2)}) collective-permute-start(bf16[2,128,4,128]{3,1,2,0:T(8,128)(2,1)S(1)} %get-tuple-element.72), channel_id=1, source_target_pairs={{0,1},{1,2},{2,3},{3,4},{4,5},{5,6},{6,7},{7,0},{8,9},{9,10},{10,1... | collective-permute-start | bytes 786440 | tf_op jit(solution)/shard_map/ppermute | solution.py:118
  135.7 26.9 %collective-permute-start.28 = (f32[4,128,128]{2,1,0:T(8,128)S(1)}, f32[4,128,128]{2,1,0:T(8,128)S(1)}, u32[]{:S(2)}, u32[]{:S(2)}) collective-permute-start(f32[4,128,128]{2,1,0:T(8,128)S(1)} %dynamic-slice_bitcast_fusion), channel_id=1, source_target_pairs={{0,1},{1,0},{2,3},{3,2},{4,5},{5,4},{6,7},{7,6},{8,9},{9,8},{10,11... | collective-permute-start | bytes 786440 | tf_op jit(solution)/shard_map/ppermute | solution.py:225
  136.3 35.9 %collective-permute-start.25 = (bf16[2,128,4,128]{3,1,2,0:T(8,128)(2,1)S(1)}, bf16[2,128,4,128]{3,1,2,0:T(8,128)(2,1)S(1)}, u32[]{:S(2)}, u32[]{:S(2)}) collective-permute-start(bf16[2,128,4,128]{3,1,2,0:T(8,128)(2,1)S(1)} %get-tuple-element.77), channel_id=1, source_target_pairs={{0,5},{1,6},{2,7},{3,0},{4,1},{5,2},{6,3},{7,4},{8,13},{9,14},{10,... | collective-permute-start | bytes 786440 | tf_op jit(solution)/shard_map/ppermute | solution.py:118
  137.2 25.1 %collective-permute-start.22 = (bf16[2,128,4,128]{3,1,2,0:T(8,128)(2,1)S(1)}, bf16[2,128,4,128]{3,1,2,0:T(8,128)(2,1)S(1)}, u32[]{:S(2)}, u32[]{:S(2)}) collective-permute-start(bf16[2,128,4,128]{3,1,2,0:T(8,128)(2,1)S(1)} %get-tuple-element.73), channel_id=1, source_target_pairs={{0,2},{1,3},{2,4},{3,5},{4,6},{5,7},{6,0},{7,1},{8,10},{9,11},{10,... | collective-permute-start | bytes 786440 | tf_op jit(solution)/shard_map/ppermute | solution.py:118
  138.4 27.4 %collective-permute-start.23 = (bf16[2,128,4,128]{3,1,2,0:T(8,128)(2,1)S(1)}, bf16[2,128,4,128]{3,1,2,0:T(8,128)(2,1)S(1)}, u32[]{:S(2)}, u32[]{:S(2)}) collective-permute-start(bf16[2,128,4,128]{3,1,2,0:T(8,128)(2,1)S(1)} %get-tuple-element.74), channel_id=1, source_target_pairs={{0,3},{1,4},{2,5},{3,6},{4,7},{5,0},{6,1},{7,2},{8,11},{9,12},{10,... | collective-permute-start | bytes 786440 | tf_op jit(solution)/shard_map/ppermute | solution.py:118
  149.5 19.5 %collective-permute-start.24 = (bf16[2,128,4,128]{3,1,2,0:T(8,128)(2,1)S(1)}, bf16[2,128,4,128]{3,1,2,0:T(8,128)(2,1)S(1)}, u32[]{:S(2)}, u32[]{:S(2)}) collective-permute-start(bf16[2,128,4,128]{3,1,2,0:T(8,128)(2,1)S(1)} %get-tuple-element.75), channel_id=1, source_target_pairs={{0,4},{1,5},{2,6},{3,7},{4,0},{5,1},{6,2},{7,3},{8,12},{9,13},{10,... | collective-permute-start | bytes 786440 | tf_op jit(solution)/shard_map/ppermute | solution.py:118
  162.3 10.3 %collective-permute-start.26 = (bf16[2,128,4,128]{3,1,2,0:T(8,128)(2,1)S(1)}, bf16[2,128,4,128]{3,1,2,0:T(8,128)(2,1)S(1)}, u32[]{:S(2)}, u32[]{:S(2)}) collective-permute-start(bf16[2,128,4,128]{3,1,2,0:T(8,128)(2,1)S(1)} %get-tuple-element.76), channel_id=1, source_target_pairs={{0,6},{1,7},{2,0},{3,1},{4,2},{5,3},{6,4},{7,5},{8,14},{9,15},{10,... | collective-permute-start | bytes 786440 | tf_op jit(solution)/shard_map/ppermute | solution.py:118
  162.6 10.3 %collective-permute-start.27 = (bf16[2,128,4,128]{3,1,2,0:T(8,128)(2,1)S(1)}, bf16[2,128,4,128]{3,1,2,0:T(8,128)(2,1)S(1)}, u32[]{:S(2)}, u32[]{:S(2)}) collective-permute-start(bf16[2,128,4,128]{3,1,2,0:T(8,128)(2,1)S(1)} %get-tuple-element.70), channel_id=1, source_target_pairs={{0,7},{1,0},{2,1},{3,2},{4,3},{5,4},{6,5},{7,6},{8,15},{9,8},{10,9... | collective-permute-start | bytes 786440 | tf_op jit(solution)/shard_map/ppermute | solution.py:118
  165.8 10.3 %collective-permute-start.29 = (bf16[128,128]{1,0:T(8,128)(2,1)S(1)}, bf16[128,128]{1,0:T(8,128)(2,1)S(1)}, u32[]{:S(2)}, u32[]{:S(2)}) collective-permute-start(bf16[128,128]{1,0:T(8,128)(2,1)S(1)} %get-tuple-element.102), channel_id=1, source_target_pairs={{0,2},{1,3},{2,4},{3,5},{4,6},{5,7},{6,0},{7,1},{8,10},{9,11},{10,... | collective-permute-start | bytes 98312 | tf_op jit(solution)/shard_map/ppermute | solution.py:232
  169.0 7.1 %collective-permute-start.30 = (bf16[128,128]{1,0:T(8,128)(2,1)S(1)}, bf16[128,128]{1,0:T(8,128)(2,1)S(1)}, u32[]{:S(2)}, u32[]{:S(2)}) collective-permute-start(bf16[128,128]{1,0:T(8,128)(2,1)S(1)} %get-tuple-element.101), channel_id=1, source_target_pairs={{0,4},{1,5},{2,6},{3,7},{4,0},{5,1},{6,2},{7,3},{8,12},{9,13},{10,... | collective-permute-start | bytes 98312 | tf_op jit(solution)/shard_map/ppermute | solution.py:232
  172.2 3.9 %collective-permute-start.31 = (bf16[128,128]{1,0:T(8,128)(2,1)S(1)}, bf16[128,128]{1,0:T(8,128)(2,1)S(1)}, u32[]{:S(2)}, u32[]{:S(2)}) collective-permute-start(bf16[128,128]{1,0:T(8,128)(2,1)S(1)} %get-tuple-element.100), channel_id=1, source_target_pairs={{0,6},{1,7},{2,0},{3,1},{4,2},{5,3},{6,4},{7,5},{8,14},{9,15},{10,... | collective-permute-start | bytes 98312 | tf_op jit(solution)/shard_map/ppermute | solution.py:232
  (25 other events, 83.0 us)
